TPU v7x, 32 devices: a whole 2x2x4 slice. The times are simulated.
32 devices in a mesh: groups: 2 (over y), lon: 8 (over z, x), lat: 2 (over core).
Axes of the slice: x: 2, y: 2, z: 4, core: 2. Of those that a mesh axis runs over, the one named last changes fastest.
Arguments:
- acts: bfloat16 [4, 96, 256, 256], P('groups', 'lat', 'lon'), parts along dimension 0, may hold values from -6 to 6
- rates: int32 [256], replicated, may hold values from 1 to 4, as said below
- dw_kernel: bfloat16 [9, 256], replicated, may hold values from -2 to 2
- pw_weight: bfloat16 [256, 256], replicated, may hold values from -0.375 to 0.375
- head_weight: bfloat16 [256, 227], replicated, may hold values from -0.375 to 0.375
- teacher_tiles: bfloat16 [512, 8, 227], P(('groups', 'lon', 'lat')), parts along dimension 0, may hold values from -6 to 6
- tile_dest: int32 [512, 1], P(('groups', 'lon', 'lat')), parts along dimension 0, may hold values from 0 to 15; in each aligned block of 16 rows (0 to 15, 16 to 31, ...) at most 2 rows name the same one
- tile_start: int32 [512], P(('groups', 'lon', 'lat')), parts along dimension 0, may hold values from 0 to 3064, as said below
- tile_count: int32 [512], P(('groups', 'lon', 'lat')), parts along dimension 0, may hold values from 1 to 8
Outputs:
- grad_dw: float32 [18, 256], P('groups'), parts along dimension 0
- grad_pw: float32 [512, 256], P('groups'), parts along dimension 0
- grad_head: float32 [512, 227], P('groups'), parts along dimension 0
- mse: float32 [2], P('groups'), parts along dimension 0
There are 2 independent parts, one for each index of `groups`. A program takes and returns all parts, laid end to end along the dimension named above; an argument that names none is the same for every part. Nothing has to cross between parts.
Inputs may be any that keep to these rules, and one draw needn't show every extreme that they name: The channels form 4 contiguous groups of 64 channels; all channels of a group share one rate, and the groups take the rates 1 to 4, each once, in an order that varies. `tile_dest`: among the 16 tiles of one teacher partition no destination is named more than 2 times. A tile's 8 cells lie in one row of one sample of its destination's block: tile_start mod 32 is at most 24.
All inputs are finite; a program needn't handle non-finite values.
Results may differ from a plain program's by a relative error of at most 0.0045.
Values may be sent and summed in bfloat16 or wider, within the bound.
No kernel may reach another device: no remote copies, remote signals or barrier semaphores. Data moves between devices by JAX's collectives and lax.ppermute only.
A program may use at most 64 MiB of HBM per device.

v0:
```python
import jax
import jax.numpy as jnp
from jax import lax
from jax.sharding import PartitionSpec as P

DMAX = 4
TILE = 8
CAP = 2


def padded_2(cells, sides, width, closed):
    for axis, dim in sides:
        count = lax.axis_size(axis)
        ends = count if closed else count - 1
        head = lax.slice_in_dim(cells, 0, width, axis=dim)
        tail = lax.slice_in_dim(cells, cells.shape[dim] - width, cells.shape[dim], axis=dim)
        cells = jnp.concatenate(
            [
                lax.ppermute(tail, axis, [(i, (i + 1) % count) for i in range(ends)]),
                cells,
                lax.ppermute(head, axis, [((i + 1) % count, i) for i in range(ends)]),
            ],
            axis=dim,
        )
    return cells


def tap_window(group_in, rate, tap_index, band_rows, block_cols):
    row_start = DMAX + (tap_index // 3 - 1) * rate
    col_start = DMAX + (tap_index % 3 - 1) * rate
    zero = jnp.int32(0)
    sizes = (group_in.shape[0], band_rows, block_cols, group_in.shape[3])
    return lax.dynamic_slice(group_in, (zero, row_start, col_start, zero), sizes)


def dilated(padded, kernel, rates, band_rows, block_cols):
    width = padded.shape[-1]
    group_width = width // DMAX
    outputs = []
    for group in range(DMAX):
        low = group * group_width
        group_in = padded[..., low : low + group_width]
        rate = rates[low]
        accum_sum = None
        for tap_index in range(9):
            window = tap_window(group_in, rate, tap_index, band_rows, block_cols)
            term = window.astype(jnp.float32) * kernel[tap_index, low : low + group_width]
            accum_sum = term if accum_sum is None else accum_sum + term
        outputs.append(accum_sum)
    return jnp.concatenate(outputs, axis=-1)


def dilated_grad(padded, grad_z, rates, band_rows, block_cols):
    width = padded.shape[-1]
    group_width = width // DMAX
    columns = []
    for group in range(DMAX):
        low = group * group_width
        group_in = padded[..., low : low + group_width]
        group_grad = grad_z[..., low : low + group_width]
        rate = rates[low]
        tap_sums = []
        for tap_index in range(9):
            window = tap_window(group_in, rate, tap_index, band_rows, block_cols)
            tap_sums.append(
                jnp.sum((window.astype(jnp.float32) * group_grad).reshape(-1, group_width), axis=0)
            )
        columns.append(jnp.stack(tap_sums, axis=0))
    return jnp.concatenate(columns, axis=1)


def local(
    acts, rates, dw_kernel, pw_weight, head_weight, teacher_tiles, tile_dest, tile_start, tile_count
):
    micro_batch, band_rows, block_cols, width = acts.shape
    teach_width = head_weight.shape[1]
    lat_index = lax.axis_index("lat")
    lat_count = lax.axis_size("lat")
    lon_count = lax.axis_size("lon")
    devices = lon_count * lat_count
    lon_padded = padded_2(acts, (("lon", 2),), DMAX, True)
    padded = padded_2(lon_padded, (("lat", 1),), DMAX, False)
    kernel = dw_kernel.astype(jnp.float32)
    depthwise_out = dilated(padded, kernel, rates, band_rows, block_cols).astype(jnp.bfloat16)
    depth_flat = depthwise_out.reshape(-1, width)
    preact = jnp.dot(depth_flat, pw_weight, preferred_element_type=jnp.float32)
    block_flat = (acts.reshape(-1, width).astype(jnp.float32) + jax.nn.silu(preact)).astype(
        jnp.bfloat16
    )
    tiles_here = teacher_tiles.shape[0]
    destination = tile_dest[:, 0]
    positions = jnp.arange(tiles_here, dtype=jnp.int32)
    same_dest = destination[:, None] == destination[None, :]
    earlier = positions[:, None] > positions[None, :]
    slot_rank = jnp.sum((same_dest & earlier).astype(jnp.int32), axis=1)
    slot_index = destination * CAP + slot_rank
    send_tiles = (
        jnp.zeros((devices * CAP, TILE, teach_width), jnp.bfloat16)
        .at[slot_index]
        .set(teacher_tiles)
    )
    send_start = jnp.zeros((devices * CAP,), jnp.int32).at[slot_index].set(tile_start)
    send_count = jnp.zeros((devices * CAP,), jnp.int32).at[slot_index].set(tile_count)
    recv_tiles, recv_start, recv_count = (
        lax.all_to_all(send_tiles, ("lon", "lat"), split_axis=0, concat_axis=0, tiled=True),
        lax.all_to_all(send_start, ("lon", "lat"), split_axis=0, concat_axis=0, tiled=True),
        lax.all_to_all(send_count, ("lon", "lat"), split_axis=0, concat_axis=0, tiled=True),
    )
    offsets = jnp.arange(TILE, dtype=jnp.int32)
    cell_index = recv_start[:, None] + offsets[None, :]
    is_valid = offsets[None, :] < recv_count[:, None]
    inner_row = recv_start // block_cols % band_rows
    glob_row = lat_index * band_rows + inner_row
    area_weight = jnp.cos(
        jnp.pi * ((glob_row.astype(jnp.float32) + 0.5) / (band_rows * lat_count) - 0.5)
    )
    row_weight = jnp.where(is_valid, area_weight[:, None], jnp.float32(0.0)) / jnp.float32(
        devices * tiles_here * TILE
    )
    row_weight = row_weight.reshape(-1, 1)
    cell_flat = cell_index.reshape(-1)
    y_rows = block_flat[cell_flat]
    predicted = jnp.dot(y_rows, head_weight, preferred_element_type=jnp.float32)
    residual = predicted - recv_tiles.reshape(-1, teach_width).astype(jnp.float32)
    loss_sum = jnp.sum(row_weight * residual * residual)
    grad_pred = (2.0 * row_weight * residual).astype(jnp.bfloat16)
    grad_head = lax.dot_general(
        y_rows, grad_pred, (((0,), (0,)), ((), ())), preferred_element_type=jnp.float32
    )
    grad_rows = jnp.dot(grad_pred, head_weight.T, preferred_element_type=jnp.float32)
    grad_y = jnp.zeros((block_flat.shape[0], width), jnp.float32).at[cell_flat].add(grad_rows)
    sigmoid_u = jax.nn.sigmoid(preact)
    grad_u = (grad_y * sigmoid_u * (1.0 + preact * (1.0 - sigmoid_u))).astype(jnp.bfloat16)
    grad_pw = lax.dot_general(
        depth_flat, grad_u, (((0,), (0,)), ((), ())), preferred_element_type=jnp.float32
    )
    grad_z = jnp.dot(grad_u, pw_weight.T, preferred_element_type=jnp.float32).reshape(
        micro_batch, band_rows, block_cols, width
    )
    grad_dw = dilated_grad(padded, grad_z, rates, band_rows, block_cols)
    grad_dw, grad_pw, grad_head, loss_sum = lax.psum(
        (grad_dw, grad_pw, grad_head, loss_sum), ("lon", "lat")
    )
    return (grad_dw, grad_pw, grad_head, (loss_sum / teach_width).reshape(1))


def solution(mesh):
    in_specs = (
        P("groups", "lat", "lon", None),
        P(),
        P(),
        P(),
        P(),
        P(("groups", "lon", "lat"), None, None),
        P(("groups", "lon", "lat"), None),
        P(("groups", "lon", "lat")),
        P(("groups", "lon", "lat")),
    )
    out_specs = (P("groups", None), P("groups", None), P("groups", None), P("groups"))
    return jax.shard_map(local, mesh=mesh, in_specs=in_specs, out_specs=out_specs, check_vma=False)
```

profile of v0, /device:TPU:0, one launch (start us, length us, event | category | flops | bytes accessed | tf_op | source)
XLA Modules:
  0.0 211.7 jit_solution(15716888762554736010)
XLA Ops:
  10.3 7.4 %all-to-all-start.1 = ((s32[16,2,1]{1,2,0:T(1,128)}), s32[16,2,1]{1,2,0:T(1,128)S(1)}, u32[]{:S(2)}, u32[]{:S(2)}) async-start(s32[16,2,1]{1,2,0:T(1,128)} %bitcast.8), calls=%async_computation.1 | async-start | bytes 16384 | tf_op jit(solution)/shard_map/all_to_all | solution.py:107
  18.9 2.0 collective-permute-start
  20.9 2.8 %collective-permute-start.1 = (bf16[2,48,4,256]{3,2,1,0:T(4,128)(2,1)S(1)}, bf16[2,48,4,256]{3,2,1,0:T(4,128)(2,1)S(1)}, u32[]{:S(2)}, u32[]{:S(2)}) collective-permute-start(bf16[2,48,4,256]{3,2,1,0:T(4,128)(2,1)S(1)} %get-tuple-element.71), channel_id=1, source_target_pairs={{2,0},{4,2},{6,4},{8,6},{10,8},{12,10},{14,12},{0,14},{3,1},{5,3},... | collective-permute-start | bytes 589832 | tf_op jit(solution)/shard_map/ppermute | solution.py:21
  38.7 3.5 %all-to-all-start = ((s32[16,2,1]{1,2,0:T(1,128)}), s32[16,2,1]{1,2,0:T(1,128)S(1)}, u32[]{:S(2)}, u32[]{:S(2)}) async-start(s32[16,2,1]{1,2,0:T(1,128)} %bitcast.6), calls=%async_computation | async-start | bytes 16384 | tf_op jit(solution)/shard_map/all_to_all | solution.py:106
  42.8 2.3 %scatter_fusion = bf16[32,8,227]{2,1,0:T(8,128)(2,1)} fusion(bf16[32,8,227]{2,1,0:T(8,128)(2,1)} %broadcast_in_dim.15, s32[16]{0:T(128)S(1)} %fusion.86, bf16[16,8,227]{2,1,0:T(8,128)(2,1)} %param.14), kind=kCustom, calls=%fused_computation.3 | custom fusion | bytes 174400 | tf_op jit(solution)/shard_map/scatter | solution.py:100
  46.4 2.0 all-to-all-done
  48.5 4.0 %all-to-all-start.2 = ((bf16[32,8,227]{2,1,0:T(8,128)(2,1)}), bf16[32,8,227]{2,1,0:T(8,128)(2,1)S(1)}, u32[]{:S(2)}, u32[]{:S(2)}) async-start(bf16[32,8,227]{2,1,0:T(8,128)(2,1)} %scatter_fusion), calls=%async_computation.2 | async-start | bytes 262144 | tf_op jit(solution)/shard_map/all_to_all | solution.py:105
  53.9 2.3 %collective-permute-start.2 = (bf16[2,4,40,256]{3,2,1,0:T(8,128)(2,1)S(1)}, bf16[2,4,40,256]{3,2,1,0:T(8,128)(2,1)S(1)}, u32[]{:S(2)}, u32[]{:S(2)}) collective-permute-start(bf16[2,4,40,256]{3,2,1,0:T(8,128)(2,1)S(1)} %get-tuple-element.68), channel_id=1, source_target_pairs={{0,1},{2,3},{4,5},{6,7},{8,9},{10,11},{12,13},{14,15},{16,17},{18,... | collective-permute-start | bytes 491528 | tf_op jit(solution)/shard_map/ppermute | solution.py:19
  57.6 2.8 %all-to-all-done.2 = bf16[32,8,227]{2,1,0:T(8,128)(2,1)S(1)} async-done(((bf16[32,8,227]{2,1,0:T(8,128)(2,1)}), bf16[32,8,227]{2,1,0:T(8,128)(2,1)S(1)}, u32[]{:S(2)}, u32[]{:S(2)}) %all-to-all-start.2) | async-done | bytes 116256 | tf_op jit(solution)/shard_map/all_to_all | solution.py:105
  63.4 3.5 %fusion.9 = bf16[2,48,32,64]{3,2,1,0:T(8,128)(2,1)S(1)} fusion(f32[64]{0:T(128)S(1)} %get-tuple-element.101, f32[64]{0:T(128)S(1)} %get-tuple-element.102, f32[64]{0:T(128)S(1)} %get-tuple-element.103, f32[64]{0:T(128)S(1)} %get-tuple-element.104, f32[64]{0:T(128)S(1)} %get-tuple-element.105, f32[64]{0:T(128)S(1)} %get-tuple-element.106, ...), kind=kLoop, calls=%fused_computation.90 | loop fusion | flops 5308416 | bytes 3934480 | tf_op jit(solution)/shard_map/convert.9
  67.0 3.1 %fusion.63 = bf16[2,48,32,64]{3,2,1,0:T(8,128)(2,1)S(1)} fusion(f32[64]{0:T(128)S(1)} %copy-done.22, f32[64]{0:T(128)S(1)} %copy-done.23, f32[64]{0:T(128)S(1)} %copy-done.24, f32[64]{0:T(128)S(1)} %copy-done.25, f32[64]{0:T(128)S(1)} %copy-done.26, f32[64]{0:T(128)S(1)} %copy-done.27, f32[64]{0:T(128)S(1)} %copy-done.28, f32[64]{0:T(128)S(1)} %copy-done.29, ...), kind=kLoop, calls=%fused_computation.144 | loop fusion | flops 5308416 | bytes 3934480 | tf_op jit(solution)/shard_map/convert.6
  70.2 3.5 %fusion.45 = bf16[2,48,32,64]{3,2,1,0:T(8,128)(2,1)S(1)} fusion(f32[64]{0:T(128)S(1)} %get-tuple-element.82, f32[64]{0:T(128)S(1)} %get-tuple-element.83, f32[64]{0:T(128)S(1)} %get-tuple-element.84, f32[64]{0:T(128)S(1)} %get-tuple-element.85, f32[64]{0:T(128)S(1)} %get-tuple-element.86, f32[64]{0:T(128)S(1)} %copy-done.18, f32[64]{0:T(128)S(1)} %copy-done.19, ...), kind=kLoop, calls=%fused_computation.126 | loop fusion | flops 5308416 | bytes 3934480 | tf_op jit(solution)/shard_map/convert.7
  73.7 3.3 %fusion.27 = bf16[2,48,32,64]{3,2,1,0:T(8,128)(2,1)S(1)} fusion(f32[64]{0:T(128)S(1)} %get-tuple-element.92, f32[64]{0:T(128)S(1)} %get-tuple-element.93, f32[64]{0:T(128)S(1)} %get-tuple-element.94, f32[64]{0:T(128)S(1)} %get-tuple-element.95, f32[64]{0:T(128)S(1)} %get-tuple-element.96, f32[64]{0:T(128)S(1)} %get-tuple-element.97, ...), kind=kLoop, calls=%fused_computation.108 | loop fusion | flops 5308416 | bytes 3934480 | tf_op jit(solution)/shard_map/convert.8
  77.1 3.4 %fusion = (bf16[3072,256]{1,0:T(8,128)(2,1)}, f32[3072,256]{1,0:T(8,128)}) fusion(bf16[2,48,32,256]{3,2,1,0:T(8,128)(2,1)S(1)} %copy-done.7, bf16[256,256]{1,0:T(8,128)(2,1)S(1)} %copy-done, bf16[3072,64]{1,0:T(8,128)(2,1)S(1)} %bitcast.171, bf16[3072,64]{1,0:T(8,128)(2,1)S(1)} %bitcast.173, bf16[3072,64]{1,0:T(8,128)(2,1)S(1)} %bitcast.175, ...), kind=kOutput, calls=%fused_computation.6 | convolution fusion | flops 414449664 | bytes 7995392 | tf_op jit(solution)/shard_map/dot_general | solution.py:86
  80.5 2.6 %gather_fusion = bf16[256,256]{1,0:T(8,128)(2,1)S(1)} fusion(bf16[3072,256]{1,0:T(8,128)(2,1)} %get-tuple-element.114, s32[1024]{0:T(1024)S(1)} %pad_clamp_fusion), kind=kCustom, calls=%fused_computation | custom fusion | bytes 263168 | tf_op jit(solution)/shard_map/gather | solution.py:122
  85.0 3.8 %scatter_custom_fusion.3 = f32[3072,256]{1,0:T(8,128)} fusion(s32[256]{0:T(256)S(1)} %bitcast.178, f32[256,256]{1,0:T(8,128)S(1)} %fusion.77, f32[]{:T(128)} %constant.101.clone.1), kind=kCustom, calls=%fused_computation.155 | custom fusion | flops 65536 | bytes 3145732 | tf_op jit(solution)/shard_map/scatter-add | solution.py:131
  88.8 4.0 %multiply_convert_fusion = bf16[3072,256]{1,0:T(8,128)(2,1)S(1)} fusion(f32[3072,256]{1,0:T(8,128)} %get-tuple-element.115, f32[3072,256]{1,0:T(8,128)} %scatter_custom_fusion.3), kind=kLoop, calls=%fused_computation.7 | loop fusion | flops 7077888 | bytes 7864320 | tf_op jit(solution)/shard_map/convert_element_type | solution.py:133
  94.1 2.2 %fusion.91 = f32[256,256]{1,0:T(8,128)} fusion(bf16[3072,256]{1,0:T(8,128)(2,1)S(1)} %multiply_convert_fusion, bf16[3072,64]{1,0:T(8,128)(2,1)S(1)} %bitcast.172, bf16[3072,64]{1,0:T(8,128)(2,1)S(1)} %bitcast.174, bf16[3072,64]{1,0:T(8,128)(2,1)S(1)} %bitcast.176, bf16[3072,64]{1,0:T(8,128)(2,1)S(1)} %bitcast.170), kind=kOutput, calls=%fused_computation.232 | convolution fusion | flops 408944640 | bytes 3407872 | tf_op jit(solution)/shard_map/dot_general | solution.py:134
  96.2 2.2 %fusion.96 = f32[3072,256]{1,0:T(8,128)S(1)} fusion(bf16[3072,256]{1,0:T(8,128)(2,1)} %copy-done.8, bf16[256,256]{1,0:T(8,128)(2,1)S(1)} %copy-done), kind=kOutput, calls=%fused_computation.237 | convolution fusion | flops 402653184 | bytes 4849664 | tf_op jit(solution)/shard_map/dot_general | solution.py:137
  100.1 10.6 %fusion.18 = (f32[64]{0:T(128)S(1)}, f32[64]{0:T(128)S(1)}, f32[64]{0:T(128)S(1)}, f32[64]{0:T(128)S(1)}, f32[64]{0:T(128)S(1)}, /*index=5*/f32[64]{0:T(128)S(1)...) fusion(f32[2,48,32,256]{3,2,1,0:T(8,128)S(1)} %bitcast.167, ...), kind=kLoop, calls=%fused_computation.99 | loop fusion | flops 14154240 | bytes 11802672 | tf_op jit(solution)/shard_map/reduce_sum | solution.py:66
  110.7 7.1 %fusion.36 = (f32[64]{0:T(128)S(1)}, f32[64]{0:T(128)S(1)}, f32[64]{0:T(128)S(1)}, f32[64]{0:T(128)S(1)}, f32[64]{0:T(128)S(1)}, /*index=5*/f32[64]{0:T(128)S(1)...) fusion(f32[2,48,32,256]{3,2,1,0:T(8,128)} %bitcast.168, ...), kind=kLoop, calls=%fused_computation.117 | loop fusion | flops 7077120 | bytes 7867408 | tf_op jit(solution)/shard_map/reduce_sum | solution.py:66
  118.0 60.9 %all-reduce = (f32[9,256]{1,0:T(8,128)}, f32[]{:T(128)}) all-reduce(f32[9,256]{1,0:T(8,128)S(1)} %pad_maximum_fusion.5, f32[]{:T(128)} %get-tuple-element.116), channel_id=1, replica_groups=mesh['groups'=2,'lon'=8,'lat'=2] {'lon','lat'}, use_global_device_ids=true, to_apply=%region_41.42 | all-reduce | flops 2305 | bytes 18440 | tf_op jit(solution)/shard_map/psum | solution.py:141
  179.5 20.9 %all-reduce.4.cloned.1.call-done = (f32[256,256]{1,0:T(8,128)}, f32[256,227]{0,1:T(8,128)}) async-done(((f32[256,256]{1,0:T(8,128)}, f32[256,227]{0,1:T(8,128)}), (f32[256,256]{1,0:T(8,128)}, f32[256,227]{0,1:T(8,128)})) %all-reduce.4.cloned.1.call-update) | async-done | bytes 494608 | tf_op jit(solution)/shard_map/psum | solution.py:141
  200.4 1.7 copy.23
  (111 shorter events, 23.1 us)
Async XLA Ops:
  7.2 69.9 %copy-start = (bf16[256,256]{1,0:T(8,128)(2,1)S(1)}, bf16[256,256]{1,0:T(8,128)(2,1)}, u32[]{:S(2)}) copy-start(bf16[256,256]{1,0:T(8,128)(2,1)} %param.12) | copy-start | bytes 393220
  7.2 46.6 %copy-start.6 = (bf16[2,48,32,256]{3,2,1,0:T(8,128)(2,1)S(1)}, bf16[2,48,32,256]{3,2,1,0:T(8,128)(2,1)}, u32[]{:S(2)}) copy-start(bf16[2,48,32,256]{3,2,1,0:T(8,128)(2,1)} %param.9) | copy-start | bytes 4718596
  10.3 28.4 %all-to-all-start.1 = ((s32[16,2,1]{1,2,0:T(1,128)}), s32[16,2,1]{1,2,0:T(1,128)S(1)}, u32[]{:S(2)}, u32[]{:S(2)}) async-start(s32[16,2,1]{1,2,0:T(1,128)} %bitcast.8), calls=%async_computation.1 | async-start | bytes 16384 | tf_op jit(solution)/shard_map/all_to_all | solution.py:107
  18.9 34.8 %collective-permute-start = (bf16[2,48,4,256]{3,2,1,0:T(4,128)(2,1)S(1)}, bf16[2,48,4,256]{3,2,1,0:T(4,128)(2,1)S(1)}, u32[]{:S(2)}, u32[]{:S(2)}) collective-permute-start(bf16[2,48,4,256]{3,2,1,0:T(4,128)(2,1)S(1)} %get-tuple-element.70), channel_id=1, source_target_pairs={{0,2},{2,4},{4,6},{6,8},{8,10},{10,12},{12,14},{14,0},{1,3},{3,5},... | collective-permute-start | bytes 589832 | tf_op jit(solution)/shard_map/ppermute | solution.py:19
  20.9 32.8 %collective-permute-start.1 = (bf16[2,48,4,256]{3,2,1,0:T(4,128)(2,1)S(1)}, bf16[2,48,4,256]{3,2,1,0:T(4,128)(2,1)S(1)}, u32[]{:S(2)}, u32[]{:S(2)}) collective-permute-start(bf16[2,48,4,256]{3,2,1,0:T(4,128)(2,1)S(1)} %get-tuple-element.71), channel_id=1, source_target_pairs={{2,0},{4,2},{6,4},{8,6},{10,8},{12,10},{14,12},{0,14},{3,1},{5,3},... | collective-permute-start | bytes 589832 | tf_op jit(solution)/shard_map/ppermute | solution.py:21
  38.7 9.8 %all-to-all-start = ((s32[16,2,1]{1,2,0:T(1,128)}), s32[16,2,1]{1,2,0:T(1,128)S(1)}, u32[]{:S(2)}, u32[]{:S(2)}) async-start(s32[16,2,1]{1,2,0:T(1,128)} %bitcast.6), calls=%async_computation | async-start | bytes 16384 | tf_op jit(solution)/shard_map/all_to_all | solution.py:106
  48.5 11.9 %all-to-all-start.2 = ((bf16[32,8,227]{2,1,0:T(8,128)(2,1)}), bf16[32,8,227]{2,1,0:T(8,128)(2,1)S(1)}, u32[]{:S(2)}, u32[]{:S(2)}) async-start(bf16[32,8,227]{2,1,0:T(8,128)(2,1)} %scatter_fusion), calls=%async_computation.2 | async-start | bytes 262144 | tf_op jit(solution)/shard_map/all_to_all | solution.py:105
  52.4 148.0 %all-reduce.4.cloned.1.call-start = ((), (), s32[]{:S(2)}) async-start(), calls=%async_computation.3 | async-start | bytes 999424 | tf_op jit(solution)/shard_map/psum | solution.py:141
  53.9 6.6 %collective-permute-start.2 = (bf16[2,4,40,256]{3,2,1,0:T(8,128)(2,1)S(1)}, bf16[2,4,40,256]{3,2,1,0:T(8,128)(2,1)S(1)}, u32[]{:S(2)}, u32[]{:S(2)}) collective-permute-start(bf16[2,4,40,256]{3,2,1,0:T(8,128)(2,1)S(1)} %get-tuple-element.68), channel_id=1, source_target_pairs={{0,1},{2,3},{4,5},{6,7},{8,9},{10,11},{12,13},{14,15},{16,17},{18,... | collective-permute-start | bytes 491528 | tf_op jit(solution)/shard_map/ppermute | solution.py:19
  56.3 4.3 %collective-permute-start.3 = (bf16[2,4,40,256]{3,2,1,0:T(8,128)(2,1)S(1)}, bf16[2,4,40,256]{3,2,1,0:T(8,128)(2,1)S(1)}, u32[]{:S(2)}, u32[]{:S(2)}) collective-permute-start(bf16[2,4,40,256]{3,2,1,0:T(8,128)(2,1)S(1)} %get-tuple-element.69), channel_id=1, source_target_pairs={{1,0},{3,2},{5,4},{7,6},{9,8},{11,10},{13,12},{15,14},{17,16},{19,... | collective-permute-start | bytes 491528 | tf_op jit(solution)/shard_map/ppermute | solution.py:21
  63.0 3.9 %copy-start.1 = (bf16[2,56,40,64]{3,2,1,0:T(8,128)(2,1)}, bf16[2,56,40,64]{3,2,1,0:T(8,128)(2,1)S(1)}, u32[]{:S(2)}) copy-start(bf16[2,56,40,64]{3,2,1,0:T(8,128)(2,1)S(1)} %get-tuple-element.65) | copy-start | bytes 1720324
  63.0 7.2 %copy-start.3 = (bf16[2,56,40,64]{3,2,1,0:T(8,128)(2,1)}, bf16[2,56,40,64]{3,2,1,0:T(8,128)(2,1)S(1)}, u32[]{:S(2)}) copy-start(bf16[2,56,40,64]{3,2,1,0:T(8,128)(2,1)S(1)} %get-tuple-element.66) | copy-start | bytes 1720324
  63.4 3.6 %copy-start.25 = (f32[64]{0:T(128)S(1)}, f32[64]{0:T(128)}, u32[]{:S(2)}) copy-start(f32[64]{0:T(128)} %get-tuple-element.76) | copy-start | bytes 772
  63.4 3.6 %copy-start.26 = (f32[64]{0:T(128)S(1)}, f32[64]{0:T(128)}, u32[]{:S(2)}) copy-start(f32[64]{0:T(128)} %get-tuple-element.77) | copy-start | bytes 772
  63.4 3.6 %copy-start.27 = (f32[64]{0:T(128)S(1)}, f32[64]{0:T(128)}, u32[]{:S(2)}) copy-start(f32[64]{0:T(128)} %get-tuple-element.78) | copy-start | bytes 772
  66.9 10.1 %copy-start.9 = (bf16[2,48,32,64]{3,2,1,0:T(8,128)(2,1)}, bf16[2,48,32,64]{3,2,1,0:T(8,128)(2,1)S(1)}, u32[]{:S(2)}) copy-start(bf16[2,48,32,64]{3,2,1,0:T(8,128)(2,1)S(1)} %fusion.9) | copy-start | bytes 1179652
  70.2 6.9 %copy-start.11 = (bf16[2,48,32,64]{3,2,1,0:T(8,128)(2,1)}, bf16[2,48,32,64]{3,2,1,0:T(8,128)(2,1)S(1)}, u32[]{:S(2)}) copy-start(bf16[2,48,32,64]{3,2,1,0:T(8,128)(2,1)S(1)} %fusion.63) | copy-start | bytes 1179652
  77.1 6.0 %copy-start.17 = (bf16[256,227]{0,1:T(8,128)(2,1)S(1)}, bf16[256,227]{0,1:T(8,128)(2,1)}, u32[]{:S(2)}) copy-start(bf16[256,227]{0,1:T(8,128)(2,1)} %param.13) | copy-start | bytes 348676
  88.8 5.2 %copy-start.10 = (bf16[2,48,32,64]{3,2,1,0:T(8,128)(2,1)S(1)}, bf16[2,48,32,64]{3,2,1,0:T(8,128)(2,1)}, u32[]{:S(2)}) copy-start(bf16[2,48,32,64]{3,2,1,0:T(8,128)(2,1)} %copy-done.9) | copy-start | bytes 1179652
  88.8 5.2 %copy-start.12 = (bf16[2,48,32,64]{3,2,1,0:T(8,128)(2,1)S(1)}, bf16[2,48,32,64]{3,2,1,0:T(8,128)(2,1)}, u32[]{:S(2)}) copy-start(bf16[2,48,32,64]{3,2,1,0:T(8,128)(2,1)} %copy-done.11) | copy-start | bytes 1179652
  88.8 5.2 %copy-start.14 = (bf16[2,48,32,64]{3,2,1,0:T(8,128)(2,1)S(1)}, bf16[2,48,32,64]{3,2,1,0:T(8,128)(2,1)}, u32[]{:S(2)}) copy-start(bf16[2,48,32,64]{3,2,1,0:T(8,128)(2,1)} %copy-done.13) | copy-start | bytes 1179652
  88.8 5.2 %copy-start.16 = (bf16[2,48,32,64]{3,2,1,0:T(8,128)(2,1)S(1)}, bf16[2,48,32,64]{3,2,1,0:T(8,128)(2,1)}, u32[]{:S(2)}) copy-start(bf16[2,48,32,64]{3,2,1,0:T(8,128)(2,1)} %copy-done.15) | copy-start | bytes 1179652
  96.2 3.8 %copy-start.2 = (bf16[2,56,40,64]{3,2,1,0:T(8,128)(2,1)S(1)}, bf16[2,56,40,64]{3,2,1,0:T(8,128)(2,1)}, u32[]{:S(2)}) copy-start(bf16[2,56,40,64]{3,2,1,0:T(8,128)(2,1)} %copy-done.1) | copy-start | bytes 1720324
  96.2 3.8 %copy-start.4 = (bf16[2,56,40,64]{3,2,1,0:T(8,128)(2,1)S(1)}, bf16[2,56,40,64]{3,2,1,0:T(8,128)(2,1)}, u32[]{:S(2)}) copy-start(bf16[2,56,40,64]{3,2,1,0:T(8,128)(2,1)} %copy-done.3) | copy-start | bytes 1720324
  (16 other events, 46.6 us)
Sparse Core Ops, SparseCore 0:
  110.8 89.5 all-reduce.3
where the time goes:
time: 213 us; the launch traced here: 212 us
  blocking collectives  60.9 us (29%)
  other arithmetic  44.4 us (21%)
  between operations  27 us (13%)
  waiting for transfers between devices  25.8 us (12%)
  starting transfers between devices  23.2 us (11%)
  local copies, waits for them, and re-layouts  20.8 us (10%)
  matrix products  9.66 us (5%)
    psum x1, blocking collectives, local(): lax.psum((grad_dw, grad_pw, grad_head, loss_sum), ('lon', 'lat'))  60.9 us
    psum x1, waiting for transfers between devices, local(): lax.psum((grad_dw, grad_pw, grad_head, loss_sum), ('lon', 'lat'))  20.9 us
    reduce_sum x2, other arithmetic, dilated_grad(): jnp.sum((window.astype(jnp.float32) * group_grad).reshape(-1, group_width...  17.7 us
    another operation x4, other arithmetic  13.4 us
    all_to_all x1, starting transfers between devices, local(): lax.all_to_all(send_count, ('lon', 'lat'), split_axis=0, concat_axis=0, t...  7.36 us
    unnamed x66, local copies, waits for them, and re-layouts  6.59 us
    ppermute x2, starting transfers between devices, padded_2(): lax.ppermute(tail, axis, [(i, (i + 1) % count) for i in range(ends)])  4.29 us
  transfers between devices with their start and end apart: 8, of which 3 were waited for; matrix products, arithmetic and copies ran while one was open for 9% of the time, Pallas kernels for 0%

commit v1 on v0

--- a/solution.py
+++ b/solution.py
@@ -6,6 +6,59 @@
 DMAX = 4
 TILE = 8
 CAP = 2
+
+
+LANES = 128
+
+
+def halve(x, axis, bit):
+    count = lax.axis_size(axis)
+    rows = x.shape[0] // 2
+    upper = (lax.axis_index(axis) // bit) % 2
+    keep = lax.dynamic_slice_in_dim(x, upper * rows, rows, 0)
+    send = lax.dynamic_slice_in_dim(x, (1 - upper) * rows, rows, 0)
+    return keep + lax.ppermute(send, axis, [(i, i ^ bit) for i in range(count)])
+
+
+def double(x, axis, bit):
+    count = lax.axis_size(axis)
+    rows = x.shape[0]
+    upper = (lax.axis_index(axis) // bit) % 2
+    got = lax.ppermute(x, axis, [(i, i ^ bit) for i in range(count)])
+    whole = jnp.zeros((2 * rows,) + x.shape[1:], x.dtype)
+    whole = lax.dynamic_update_slice_in_dim(whole, x, upper * rows, 0)
+    return lax.dynamic_update_slice_in_dim(whole, got, (1 - upper) * rows, 0)
+
+
+def packed_sum(values, axes):
+    steps = []
+    rest = []
+    for axis in axes:
+        count = lax.axis_size(axis)
+        if count & (count - 1):
+            rest.append(axis)
+            continue
+        bit = 1
+        while bit < count:
+            steps.append((axis, bit))
+            bit *= 2
+    flat = jnp.concatenate([jnp.ravel(v).astype(jnp.float32) for v in values])
+    unit = 8 * LANES * (2 ** len(steps))
+    total = -(-flat.shape[0] // unit) * unit
+    x = jnp.pad(flat, (0, total - flat.shape[0])).reshape(-1, LANES)
+    for axis, bit in steps:
+        x = halve(x, axis, bit)
+    if rest:
+        x = lax.psum(x, tuple(rest))
+    for axis, bit in reversed(steps):
+        x = double(x, axis, bit)
+    flat = x.reshape(-1)
+    out = []
+    offset = 0
+    for v in values:
+        out.append(flat[offset : offset + v.size].reshape(v.shape))
+        offset += v.size
+    return tuple(out)
 
 
 def padded_2(cells, sides, width, closed):
@@ -138,8 +191,8 @@
         micro_batch, band_rows, block_cols, width
     )
     grad_dw = dilated_grad(padded, grad_z, rates, band_rows, block_cols)
-    grad_dw, grad_pw, grad_head, loss_sum = lax.psum(
-        (grad_dw, grad_pw, grad_head, loss_sum), ("lon", "lat")
+    grad_dw, grad_pw, grad_head, loss_sum = packed_sum(
+        (grad_dw, grad_pw, grad_head, loss_sum), ("lat", "lon")
     )
     return (grad_dw, grad_pw, grad_head, (loss_sum / teach_width).reshape(1))
 

time: 213 us -> 145 us (0.68)
  blocking collectives: 60.9 us -> 0 us
  between operations: 27 us -> 13.2 us
  waiting for transfers between devices: 25.8 us -> 36.3 us
  starting transfers between devices: 23.2 us -> 26.5 us
  matrix products: 9.66 us -> 6.76 us
    psum x1 -> x0, blocking collectives: 60.9 us -> none  [local(): lax.psum((grad_dw, grad_pw, grad_head, loss_sum), ('lon', 'lat'))]
    ppermute x0 -> x8, waiting for transfers between devices: none -> 28.3 us  [the longest x4 14.3 us: halve(): return keep + lax.ppermute(send, axis, [(i, i ^ bit) for i in range(count)])]
    psum x1 -> x0, waiting for transfers between devices: 20.9 us -> none  [local(): lax.psum((grad_dw, grad_pw, grad_head, loss_sum), ('lon', 'lat'))]
    all_to_all x1, waiting for transfers between devices: 0.01 us -> 4.82 us  [local(): lax.all_to_all(send_count, ('lon', 'lat'), split_axis=0, concat_axis=0, t...]
    unnamed x66 -> x36, local copies, waits for them, and re-layouts: 6.59 us -> 2.18 us
    ppermute x0 -> x8, starting transfers between devices: none -> 3.94 us  [the longest x4 2.17 us: halve(): return keep + lax.ppermute(send, axis, [(i, i ^ bit) for i in range(count)])]
    reduce_sum x2, other arithmetic: 17.7 us -> 15.4 us  [dilated_grad(): jnp.sum((window.astype(jnp.float32) * group_grad).reshape(-1, group_width...]
  transfers between devices with their start and end apart: 8 -> 15, of which waited for: 3 -> 10; matrix products, arithmetic and copies ran while one was open for 9% -> 8% of each run, Pallas kernels for 0% -> 0%
where the time goes in v1:
time: 145 us; the launch traced here: 144 us
  other arithmetic  42.7 us (29%)
  waiting for transfers between devices  36.3 us (25%)
  starting transfers between devices  26.5 us (18%)
  local copies, waits for them, and re-layouts  18.7 us (13%)
  between operations  13.2 us (9%)
  matrix products  6.76 us (5%)
    reduce_sum x2, other arithmetic, dilated_grad(): jnp.sum((window.astype(jnp.float32) * group_grad).reshape(-1, group_width...  15.4 us
    ppermute x4, waiting for transfers between devices, halve(): return keep + lax.ppermute(send, axis, [(i, i ^ bit) for i in range(count)])  14.3 us
    ppermute x4, waiting for transfers between devices, double(): got = lax.ppermute(x, axis, [(i, i ^ bit) for i in range(count)])  14 us
    another operation x4, other arithmetic  13.4 us
    all_to_all x1, starting transfers between devices, local(): lax.all_to_all(send_count, ('lon', 'lat'), split_axis=0, concat_axis=0, t...  5.97 us
    ppermute x2, starting transfers between devices, padded_2(): lax.ppermute(tail, axis, [(i, (i + 1) % count) for i in range(ends)])  5.19 us
    all_to_all x1, waiting for transfers between devices, local(): lax.all_to_all(send_count, ('lon', 'lat'), split_axis=0, concat_axis=0, t...  4.82 us
    ppermute x2, starting transfers between devices, padded_2(): lax.ppermute(head, axis, [((i + 1) % count, i) for i in range(ends)])  4.4 us
  transfers between devices with their start and end apart: 15, of which 10 were waited for; matrix products, arithmetic and copies ran while one was open for 8% of the time, Pallas kernels for 0%

profile of v1, /device:TPU:0, one launch (start us, length us, event | category | flops | bytes accessed | tf_op | source)
XLA Modules:
  0.0 144.2 jit_solution(947118813523149761)
XLA Ops:
  2.1 3.0 %collective-permute-start = (bf16[2,48,4,256]{3,2,1,0:T(4,128)(2,1)S(1)}, bf16[2,48,4,256]{3,2,1,0:T(4,128)(2,1)S(1)}, u32[]{:S(2)}, u32[]{:S(2)}) collective-permute-start(bf16[2,48,4,256]{3,2,1,0:T(4,128)(2,1)S(1)} %get-tuple-element.80), channel_id=1, source_target_pairs={{0,2},{2,4},{4,6},{6,8},{8,10},{10,12},{12,14},{14,0},{1,3},{3,5},... | collective-permute-start | bytes 589832 | tf_op jit(solution)/shard_map/ppermute | solution.py:72
  5.1 3.1 %collective-permute-start.1 = (bf16[2,48,4,256]{3,2,1,0:T(4,128)(2,1)S(1)}, bf16[2,48,4,256]{3,2,1,0:T(4,128)(2,1)S(1)}, u32[]{:S(2)}, u32[]{:S(2)}) collective-permute-start(bf16[2,48,4,256]{3,2,1,0:T(4,128)(2,1)S(1)} %get-tuple-element.81), channel_id=1, source_target_pairs={{2,0},{4,2},{6,4},{8,6},{10,8},{12,10},{14,12},{0,14},{3,1},{5,3},... | collective-permute-start | bytes 589832 | tf_op jit(solution)/shard_map/ppermute | solution.py:74
  11.2 3.5 %all-to-all-start = ((s32[16,2,1]{1,2,0:T(1,128)}), s32[16,2,1]{1,2,0:T(1,128)S(1)}, u32[]{:S(2)}, u32[]{:S(2)}) async-start(s32[16,2,1]{1,2,0:T(1,128)} %bitcast.6), calls=%async_computation | async-start | bytes 16384 | tf_op jit(solution)/shard_map/all_to_all | solution.py:159
  29.2 2.3 %scatter_fusion = bf16[32,8,227]{2,1,0:T(8,128)(2,1)} fusion(bf16[32,8,227]{2,1,0:T(8,128)(2,1)} %broadcast_in_dim.49, s32[16]{0:T(128)S(1)} %fusion.87, bf16[16,8,227]{2,1,0:T(8,128)(2,1)} %param.14), kind=kCustom, calls=%fused_computation.3 | custom fusion | bytes 174400 | tf_op jit(solution)/shard_map/scatter | solution.py:153
  31.5 6.0 %all-to-all-start.1 = ((s32[16,2,1]{1,2,0:T(1,128)}), s32[16,2,1]{1,2,0:T(1,128)S(1)}, u32[]{:S(2)}, u32[]{:S(2)}) async-start(s32[16,2,1]{1,2,0:T(1,128)} %bitcast.8), calls=%async_computation.1 | async-start | bytes 16384 | tf_op jit(solution)/shard_map/all_to_all | solution.py:160
  39.0 4.8 %all-to-all-done.1 = s32[16,2,1]{1,2,0:T(1,128)S(1)} async-done(((s32[16,2,1]{1,2,0:T(1,128)}), s32[16,2,1]{1,2,0:T(1,128)S(1)}, u32[]{:S(2)}, u32[]{:S(2)}) %all-to-all-start.1) | async-done | bytes 160 | tf_op jit(solution)/shard_map/all_to_all | solution.py:160
  43.8 3.5 %all-to-all-start.2 = ((bf16[32,8,227]{2,1,0:T(8,128)(2,1)}), bf16[32,8,227]{2,1,0:T(8,128)(2,1)S(1)}, u32[]{:S(2)}, u32[]{:S(2)}) async-start(bf16[32,8,227]{2,1,0:T(8,128)(2,1)} %scatter_fusion), calls=%async_computation.2 | async-start | bytes 262144 | tf_op jit(solution)/shard_map/all_to_all | solution.py:158
  52.0 3.2 %all-to-all-done.2 = bf16[32,8,227]{2,1,0:T(8,128)(2,1)S(1)} async-done(((bf16[32,8,227]{2,1,0:T(8,128)(2,1)}), bf16[32,8,227]{2,1,0:T(8,128)(2,1)S(1)}, u32[]{:S(2)}, u32[]{:S(2)}) %all-to-all-start.2) | async-done | bytes 116256 | tf_op jit(solution)/shard_map/all_to_all | solution.py:158
  58.2 3.5 %fusion.45 = bf16[2,48,32,64]{3,2,1,0:T(8,128)(2,1)S(1)} fusion(f32[64]{0:T(128)S(1)} %get-tuple-element.92, f32[64]{0:T(128)S(1)} %get-tuple-element.93, f32[64]{0:T(128)S(1)} %get-tuple-element.94, f32[64]{0:T(128)S(1)} %get-tuple-element.95, f32[64]{0:T(128)S(1)} %get-tuple-element.96, f32[64]{0:T(128)S(1)} %get-tuple-element.97, ...), kind=kLoop, calls=%fused_computation.126 | loop fusion | flops 5308416 | bytes 3934480 | tf_op jit(solution)/shard_map/convert.7
  61.7 3.1 %fusion.63 = bf16[2,48,32,64]{3,2,1,0:T(8,128)(2,1)S(1)} fusion(f32[64]{0:T(128)S(1)} %get-tuple-element.83, f32[64]{0:T(128)S(1)} %get-tuple-element.84, f32[64]{0:T(128)S(1)} %get-tuple-element.85, f32[64]{0:T(128)S(1)} %get-tuple-element.86, f32[64]{0:T(128)S(1)} %get-tuple-element.87, f32[64]{0:T(128)S(1)} %get-tuple-element.88, ...), kind=kLoop, calls=%fused_computation.144 | loop fusion | flops 5308416 | bytes 3934480 | tf_op jit(solution)/shard_map/convert.6
  64.8 3.5 %fusion.9 = bf16[2,48,32,64]{3,2,1,0:T(8,128)(2,1)S(1)} fusion(f32[64]{0:T(128)S(1)} %get-tuple-element.111, f32[64]{0:T(128)S(1)} %get-tuple-element.112, f32[64]{0:T(128)S(1)} %get-tuple-element.113, f32[64]{0:T(128)S(1)} %get-tuple-element.114, f32[64]{0:T(128)S(1)} %get-tuple-element.115, f32[64]{0:T(128)S(1)} %get-tuple-element.116, ...), kind=kLoop, calls=%fused_computation.90 | loop fusion | flops 5308416 | bytes 3934480 | tf_op jit(solution)/shard_map/convert.9
  68.3 3.3 %fusion.27 = bf16[2,48,32,64]{3,2,1,0:T(8,128)(2,1)S(1)} fusion(f32[64]{0:T(128)S(1)} %get-tuple-element.102, f32[64]{0:T(128)S(1)} %get-tuple-element.103, f32[64]{0:T(128)S(1)} %get-tuple-element.104, f32[64]{0:T(128)S(1)} %get-tuple-element.105, f32[64]{0:T(128)S(1)} %get-tuple-element.106, f32[64]{0:T(128)S(1)} %get-tuple-element.107, ...), kind=kLoop, calls=%fused_computation.108 | loop fusion | flops 5308416 | bytes 3934480 | tf_op jit(solution)/shard_map/convert.8
  71.7 3.4 %fusion = (bf16[3072,256]{1,0:T(8,128)(2,1)}, f32[3072,256]{1,0:T(8,128)}) fusion(bf16[2,48,32,256]{3,2,1,0:T(8,128)(2,1)S(1)} %copy-done.6, bf16[256,256]{1,0:T(8,128)(2,1)S(1)} %copy-done, bf16[3072,64]{1,0:T(8,128)(2,1)S(1)} %bitcast.176, bf16[3072,64]{1,0:T(8,128)(2,1)S(1)} %bitcast.174, bf16[3072,64]{1,0:T(8,128)(2,1)S(1)} %bitcast.180, ...), kind=kOutput, calls=%fused_computation.6 | convolution fusion | flops 414449664 | bytes 7995392 | tf_op jit(solution)/shard_map/dot_general | solution.py:139
  75.0 2.6 %gather_fusion = bf16[256,256]{1,0:T(8,128)(2,1)S(1)} fusion(bf16[3072,256]{1,0:T(8,128)(2,1)} %get-tuple-element.124, s32[1024]{0:T(1024)S(1)} %pad_clamp_fusion), kind=kCustom, calls=%fused_computation | custom fusion | bytes 263168 | tf_op jit(solution)/shard_map/gather | solution.py:175
  78.7 3.8 %scatter_custom_fusion.3 = f32[3072,256]{1,0:T(8,128)} fusion(s32[256]{0:T(256)S(1)} %bitcast.183, f32[256,256]{1,0:T(8,128)S(1)} %fusion.78, f32[]{:T(128)} %constant.182.clone.1), kind=kCustom, calls=%fused_computation.155 | custom fusion | flops 65536 | bytes 3145732 | tf_op jit(solution)/shard_map/scatter-add | solution.py:184
  82.5 3.9 %multiply_convert_fusion = bf16[3072,256]{1,0:T(8,128)(2,1)S(1)} fusion(f32[3072,256]{1,0:T(8,128)} %get-tuple-element.125, f32[3072,256]{1,0:T(8,128)} %scatter_custom_fusion.3), kind=kLoop, calls=%fused_computation.7 | loop fusion | flops 7077888 | bytes 7864320 | tf_op jit(solution)/shard_map/convert_element_type | solution.py:186
  87.8 5.1 %fusion.36 = (f32[64]{0:T(128)S(1)}, f32[64]{0:T(128)S(1)}, f32[64]{0:T(128)S(1)}, f32[64]{0:T(128)S(1)}, f32[64]{0:T(128)S(1)}, /*index=5*/f32[64]{0:T(128)S(1)...) fusion(f32[2,48,32,256]{3,2,1,0:T(8,128)S(1)} %bitcast.170, ...), kind=kLoop, calls=%fused_computation.117 | loop fusion | flops 7077120 | bytes 7867408 | tf_op jit(solution)/shard_map/reduce_sum | solution.py:119
  93.0 10.3 %fusion.18 = (f32[64]{0:T(128)S(1)}, f32[64]{0:T(128)S(1)}, f32[64]{0:T(128)S(1)}, f32[64]{0:T(128)S(1)}, f32[64]{0:T(128)S(1)}, /*index=5*/f32[64]{0:T(128)S(1)...) fusion(f32[2,48,32,256]{3,2,1,0:T(8,128)S(1)} %bitcast.171, ...), kind=kLoop, calls=%fused_computation.99 | loop fusion | flops 14154240 | bytes 11802672 | tf_op jit(solution)/shard_map/reduce_sum | solution.py:119
  108.6 5.2 %collective-permute-done.5 = f32[256,128]{1,0:T(8,128)S(1)} collective-permute-done((f32[256,128]{1,0:T(8,128)S(1)}, f32[256,128]{1,0:T(8,128)S(1)}, u32[]{:S(2)}, u32[]{:S(2)}) %collective-permute-start.5) | collective-permute-done | bytes 131104 | tf_op jit(solution)/shard_map/ppermute | solution.py:20
  114.3 3.9 %collective-permute-done.6 = f32[128,128]{1,0:T(8,128)S(1)} collective-permute-done((f32[128,128]{1,0:T(8,128)S(1)}, f32[128,128]{1,0:T(8,128)S(1)}, u32[]{:S(2)}, u32[]{:S(2)}) %collective-permute-start.6) | collective-permute-done | bytes 65568 | tf_op jit(solution)/shard_map/ppermute | solution.py:20
  119.6 3.7 %collective-permute-done.7 = f32[64,128]{1,0:T(8,128)S(1)} collective-permute-done((f32[64,128]{1,0:T(8,128)S(1)}, f32[64,128]{1,0:T(8,128)S(1)}, u32[]{:S(2)}, u32[]{:S(2)}) %collective-permute-start.7) | collective-permute-done | bytes 32800 | tf_op jit(solution)/shard_map/ppermute | solution.py:20
  124.5 3.8 %collective-permute-done.8 = f32[64,128]{1,0:T(8,128)S(1)} collective-permute-done((f32[64,128]{1,0:T(8,128)S(1)}, f32[64,128]{1,0:T(8,128)S(1)}, u32[]{:S(2)}, u32[]{:S(2)}) %collective-permute-start.8) | collective-permute-done | bytes 32800 | tf_op jit(solution)/shard_map/ppermute | solution.py:27
  128.8 3.8 %collective-permute-done.9 = f32[128,128]{1,0:T(8,128)S(1)} collective-permute-done((f32[128,128]{1,0:T(8,128)S(1)}, f32[128,128]{1,0:T(8,128)S(1)}, u32[]{:S(2)}, u32[]{:S(2)}) %collective-permute-start.9) | collective-permute-done | bytes 65568 | tf_op jit(solution)/shard_map/ppermute | solution.py:27
  132.7 4.9 %collective-permute-done.10 = f32[256,128]{1,0:T(8,128)S(1)} collective-permute-done((f32[256,128]{1,0:T(8,128)S(1)}, f32[256,128]{1,0:T(8,128)S(1)}, u32[]{:S(2)}, u32[]{:S(2)}) %collective-permute-start.10) | collective-permute-done | bytes 131104 | tf_op jit(solution)/shard_map/ppermute | solution.py:27
  (122 shorter events, 33.8 us)
Async XLA Ops:
  0.6 71.0 %copy-start = (bf16[256,256]{1,0:T(8,128)(2,1)S(1)}, bf16[256,256]{1,0:T(8,128)(2,1)}, u32[]{:S(2)}) copy-start(bf16[256,256]{1,0:T(8,128)(2,1)} %param.12) | copy-start | bytes 393220
  0.6 47.7 %copy-start.5 = (bf16[2,48,32,256]{3,2,1,0:T(8,128)(2,1)S(1)}, bf16[2,48,32,256]{3,2,1,0:T(8,128)(2,1)}, u32[]{:S(2)}) copy-start(bf16[2,48,32,256]{3,2,1,0:T(8,128)(2,1)} %param.9) | copy-start | bytes 4718596
  2.1 46.3 %collective-permute-start = (bf16[2,48,4,256]{3,2,1,0:T(4,128)(2,1)S(1)}, bf16[2,48,4,256]{3,2,1,0:T(4,128)(2,1)S(1)}, u32[]{:S(2)}, u32[]{:S(2)}) collective-permute-start(bf16[2,48,4,256]{3,2,1,0:T(4,128)(2,1)S(1)} %get-tuple-element.80), channel_id=1, source_target_pairs={{0,2},{2,4},{4,6},{6,8},{8,10},{10,12},{12,14},{14,0},{1,3},{3,5},... | collective-permute-start | bytes 589832 | tf_op jit(solution)/shard_map/ppermute | solution.py:72
  5.1 43.3 %collective-permute-start.1 = (bf16[2,48,4,256]{3,2,1,0:T(4,128)(2,1)S(1)}, bf16[2,48,4,256]{3,2,1,0:T(4,128)(2,1)S(1)}, u32[]{:S(2)}, u32[]{:S(2)}) collective-permute-start(bf16[2,48,4,256]{3,2,1,0:T(4,128)(2,1)S(1)} %get-tuple-element.81), channel_id=1, source_target_pairs={{2,0},{4,2},{6,4},{8,6},{10,8},{12,10},{14,12},{0,14},{3,1},{5,3},... | collective-permute-start | bytes 589832 | tf_op jit(solution)/shard_map/ppermute | solution.py:74
  11.2 20.3 %all-to-all-start = ((s32[16,2,1]{1,2,0:T(1,128)}), s32[16,2,1]{1,2,0:T(1,128)S(1)}, u32[]{:S(2)}, u32[]{:S(2)}) async-start(s32[16,2,1]{1,2,0:T(1,128)} %bitcast.6), calls=%async_computation | async-start | bytes 16384 | tf_op jit(solution)/shard_map/all_to_all | solution.py:159
  31.5 12.3 %all-to-all-start.1 = ((s32[16,2,1]{1,2,0:T(1,128)}), s32[16,2,1]{1,2,0:T(1,128)S(1)}, u32[]{:S(2)}, u32[]{:S(2)}) async-start(s32[16,2,1]{1,2,0:T(1,128)} %bitcast.8), calls=%async_computation.1 | async-start | bytes 16384 | tf_op jit(solution)/shard_map/all_to_all | solution.py:160
  43.8 11.4 %all-to-all-start.2 = ((bf16[32,8,227]{2,1,0:T(8,128)(2,1)}), bf16[32,8,227]{2,1,0:T(8,128)(2,1)S(1)}, u32[]{:S(2)}, u32[]{:S(2)}) async-start(bf16[32,8,227]{2,1,0:T(8,128)(2,1)} %scatter_fusion), calls=%async_computation.2 | async-start | bytes 262144 | tf_op jit(solution)/shard_map/all_to_all | solution.py:158
  48.5 6.8 %collective-permute-start.2 = (bf16[2,4,40,256]{3,2,1,0:T(8,128)(2,1)S(1)}, bf16[2,4,40,256]{3,2,1,0:T(8,128)(2,1)S(1)}, u32[]{:S(2)}, u32[]{:S(2)}) collective-permute-start(bf16[2,4,40,256]{3,2,1,0:T(8,128)(2,1)S(1)} %get-tuple-element.78), channel_id=1, source_target_pairs={{0,1},{2,3},{4,5},{6,7},{8,9},{10,11},{12,13},{14,15},{16,17},{18,... | collective-permute-start | bytes 491528 | tf_op jit(solution)/shard_map/ppermute | solution.py:72
  50.7 4.6 %collective-permute-start.3 = (bf16[2,4,40,256]{3,2,1,0:T(8,128)(2,1)S(1)}, bf16[2,4,40,256]{3,2,1,0:T(8,128)(2,1)S(1)}, u32[]{:S(2)}, u32[]{:S(2)}) collective-permute-start(bf16[2,4,40,256]{3,2,1,0:T(8,128)(2,1)S(1)} %get-tuple-element.79), channel_id=1, source_target_pairs={{1,0},{3,2},{5,4},{7,6},{9,8},{11,10},{13,12},{15,14},{17,16},{19,... | collective-permute-start | bytes 491528 | tf_op jit(solution)/shard_map/ppermute | solution.py:74
  61.6 10.0 %copy-start.8 = (bf16[2,48,32,64]{3,2,1,0:T(8,128)(2,1)}, bf16[2,48,32,64]{3,2,1,0:T(8,128)(2,1)S(1)}, u32[]{:S(2)}) copy-start(bf16[2,48,32,64]{3,2,1,0:T(8,128)(2,1)S(1)} %fusion.45) | copy-start | bytes 1179652
  64.8 6.8 %copy-start.10 = (bf16[2,48,32,64]{3,2,1,0:T(8,128)(2,1)}, bf16[2,48,32,64]{3,2,1,0:T(8,128)(2,1)S(1)}, u32[]{:S(2)}) copy-start(bf16[2,48,32,64]{3,2,1,0:T(8,128)(2,1)S(1)} %fusion.63) | copy-start | bytes 1179652
  71.6 6.0 %copy-start.16 = (bf16[256,227]{0,1:T(8,128)(2,1)S(1)}, bf16[256,227]{0,1:T(8,128)(2,1)}, u32[]{:S(2)}) copy-start(bf16[256,227]{0,1:T(8,128)(2,1)} %param.13) | copy-start | bytes 348676
  93.0 10.4 %copy-start.9 = (bf16[2,48,32,64]{3,2,1,0:T(8,128)(2,1)S(1)}, bf16[2,48,32,64]{3,2,1,0:T(8,128)(2,1)}, u32[]{:S(2)}) copy-start(bf16[2,48,32,64]{3,2,1,0:T(8,128)(2,1)} %copy-done.8) | copy-start | bytes 1179652
  93.0 10.4 %copy-start.11 = (bf16[2,48,32,64]{3,2,1,0:T(8,128)(2,1)S(1)}, bf16[2,48,32,64]{3,2,1,0:T(8,128)(2,1)}, u32[]{:S(2)}) copy-start(bf16[2,48,32,64]{3,2,1,0:T(8,128)(2,1)} %copy-done.10) | copy-start | bytes 1179652
  93.0 10.4 %copy-start.13 = (bf16[2,48,32,64]{3,2,1,0:T(8,128)(2,1)S(1)}, bf16[2,48,32,64]{3,2,1,0:T(8,128)(2,1)}, u32[]{:S(2)}) copy-start(bf16[2,48,32,64]{3,2,1,0:T(8,128)(2,1)} %copy-done.12) | copy-start | bytes 1179652
  93.0 10.4 %copy-start.15 = (bf16[2,48,32,64]{3,2,1,0:T(8,128)(2,1)S(1)}, bf16[2,48,32,64]{3,2,1,0:T(8,128)(2,1)}, u32[]{:S(2)}) copy-start(bf16[2,48,32,64]{3,2,1,0:T(8,128)(2,1)} %copy-done.14) | copy-start | bytes 1179652
  106.6 1.6 %collective-permute-start.4 = (f32[512,128]{1,0:T(8,128)S(1)}, f32[512,128]{1,0:T(8,128)S(1)}, u32[]{:S(2)}, u32[]{:S(2)}) collective-permute-start(f32[512,128]{1,0:T(8,128)S(1)} %constant_dynamic-slice_fusion.3), channel_id=1, source_target_pairs={{0,1},{1,0},{2,3},{3,2},{4,5},{5,4},{6,7},{7,6},{8,9},{9,8},{10,11... | collective-permute-start | bytes 786440 | tf_op jit(solution)/shard_map/ppermute | solution.py:20
  108.2 5.6 %collective-permute-start.5 = (f32[256,128]{1,0:T(8,128)S(1)}, f32[256,128]{1,0:T(8,128)S(1)}, u32[]{:S(2)}, u32[]{:S(2)}) collective-permute-start(f32[256,128]{1,0:T(8,128)S(1)} %constant_dynamic-slice_fusion.2), channel_id=1, source_target_pairs={{0,2},{2,0},{4,6},{6,4},{8,10},{10,8},{12,14},{14,12},{1,3},{3,1},... | collective-permute-start | bytes 393224 | tf_op jit(solution)/shard_map/ppermute | solution.py:20
  113.9 4.3 %collective-permute-start.6 = (f32[128,128]{1,0:T(8,128)S(1)}, f32[128,128]{1,0:T(8,128)S(1)}, u32[]{:S(2)}, u32[]{:S(2)}) collective-permute-start(f32[128,128]{1,0:T(8,128)S(1)} %constant_dynamic-slice_fusion.1), channel_id=1, source_target_pairs={{0,4},{2,6},{4,0},{6,2},{8,12},{10,14},{12,8},{14,10},{1,5},{3,7},... | collective-permute-start | bytes 196616 | tf_op jit(solution)/shard_map/ppermute | solution.py:20
  118.2 5.0 %collective-permute-start.7 = (f32[64,128]{1,0:T(8,128)S(1)}, f32[64,128]{1,0:T(8,128)S(1)}, u32[]{:S(2)}, u32[]{:S(2)}) collective-permute-start(f32[64,128]{1,0:T(8,128)S(1)} %constant_dynamic-slice_fusion), channel_id=1, source_target_pairs={{0,8},{2,10},{4,12},{6,14},{8,0},{10,2},{12,4},{14,6},{1,9},{3,11}... | collective-permute-start | bytes 98312 | tf_op jit(solution)/shard_map/ppermute | solution.py:20
  123.3 5.1 %collective-permute-start.8 = (f32[64,128]{1,0:T(8,128)S(1)}, f32[64,128]{1,0:T(8,128)S(1)}, u32[]{:S(2)}, u32[]{:S(2)}) collective-permute-start(f32[64,128]{1,0:T(8,128)S(1)} %get-tuple-element.53), channel_id=1, source_target_pairs={{0,8},{2,10},{4,12},{6,14},{8,0},{10,2},{12,4},{14,6},{1,9},{3,11}... | collective-permute-start | bytes 98312 | tf_op jit(solution)/shard_map/ppermute | solution.py:27
  128.3 4.3 %collective-permute-start.9 = (f32[128,128]{1,0:T(8,128)S(1)}, f32[128,128]{1,0:T(8,128)S(1)}, u32[]{:S(2)}, u32[]{:S(2)}) collective-permute-start(f32[128,128]{1,0:T(8,128)S(1)} %constant_dynamic-update-slice_fusion.6), channel_id=1, source_target_pairs={{0,4},{2,6},{4,0},{6,2},{8,12},{10,14},{12,8},{14,10},{1,5},{3,7},... | collective-permute-start | bytes 196616 | tf_op jit(solution)/shard_map/ppermute | solution.py:27
  132.6 5.0 %collective-permute-start.10 = (f32[256,128]{1,0:T(8,128)S(1)}, f32[256,128]{1,0:T(8,128)S(1)}, u32[]{:S(2)}, u32[]{:S(2)}) collective-permute-start(f32[256,128]{1,0:T(8,128)S(1)} %constant_dynamic-update-slice_fusion.4), channel_id=1, source_target_pairs={{0,2},{2,0},{4,6},{6,4},{8,10},{10,8},{12,14},{14,12},{1,3},{3,1},... | collective-permute-start | bytes 393224 | tf_op jit(solution)/shard_map/ppermute | solution.py:27
  137.7 1.6 %collective-permute-start.11 = (f32[512,128]{1,0:T(8,128)S(1)}, f32[512,128]{1,0:T(8,128)S(1)}, u32[]{:S(2)}, u32[]{:S(2)}) collective-permute-start(f32[512,128]{1,0:T(8,128)S(1)} %constant_dynamic-update-slice_fusion.2), channel_id=1, source_target_pairs={{0,1},{1,0},{2,3},{3,2},{4,5},{5,4},{6,7},{7,6},{8,9},{9,8},{10,11... | collective-permute-start | bytes 786440 | tf_op jit(solution)/shard_map/ppermute | solution.py:27
  (8 other events, 27.5 us)

commit v2 on v1

--- a/solution.py
+++ b/solution.py
@@ -6,6 +6,7 @@
 DMAX = 4
 TILE = 8
 CAP = 2
+CHUNK = 32
 
 
 LANES = 128
@@ -78,50 +79,6 @@
     return cells
 
 
-def tap_window(group_in, rate, tap_index, band_rows, block_cols):
-    row_start = DMAX + (tap_index // 3 - 1) * rate
-    col_start = DMAX + (tap_index % 3 - 1) * rate
-    zero = jnp.int32(0)
-    sizes = (group_in.shape[0], band_rows, block_cols, group_in.shape[3])
-    return lax.dynamic_slice(group_in, (zero, row_start, col_start, zero), sizes)
-
-
-def dilated(padded, kernel, rates, band_rows, block_cols):
-    width = padded.shape[-1]
-    group_width = width // DMAX
-    outputs = []
-    for group in range(DMAX):
-        low = group * group_width
-        group_in = padded[..., low : low + group_width]
-        rate = rates[low]
-        accum_sum = None
-        for tap_index in range(9):
-            window = tap_window(group_in, rate, tap_index, band_rows, block_cols)
-            term = window.astype(jnp.float32) * kernel[tap_index, low : low + group_width]
-            accum_sum = term if accum_sum is None else accum_sum + term
-        outputs.append(accum_sum)
-    return jnp.concatenate(outputs, axis=-1)
-
-
-def dilated_grad(padded, grad_z, rates, band_rows, block_cols):
-    width = padded.shape[-1]
-    group_width = width // DMAX
-    columns = []
-    for group in range(DMAX):
-        low = group * group_width
-        group_in = padded[..., low : low + group_width]
-        group_grad = grad_z[..., low : low + group_width]
-        rate = rates[low]
-        tap_sums = []
-        for tap_index in range(9):
-            window = tap_window(group_in, rate, tap_index, band_rows, block_cols)
-            tap_sums.append(
-                jnp.sum((window.astype(jnp.float32) * group_grad).reshape(-1, group_width), axis=0)
-            )
-        columns.append(jnp.stack(tap_sums, axis=0))
-    return jnp.concatenate(columns, axis=1)
-
-
 def local(
     acts, rates, dw_kernel, pw_weight, head_weight, teacher_tiles, tile_dest, tile_start, tile_count
 ):
@@ -133,13 +90,6 @@
     devices = lon_count * lat_count
     lon_padded = padded_2(acts, (("lon", 2),), DMAX, True)
     padded = padded_2(lon_padded, (("lat", 1),), DMAX, False)
-    kernel = dw_kernel.astype(jnp.float32)
-    depthwise_out = dilated(padded, kernel, rates, band_rows, block_cols).astype(jnp.bfloat16)
-    depth_flat = depthwise_out.reshape(-1, width)
-    preact = jnp.dot(depth_flat, pw_weight, preferred_element_type=jnp.float32)
-    block_flat = (acts.reshape(-1, width).astype(jnp.float32) + jax.nn.silu(preact)).astype(
-        jnp.bfloat16
-    )
     tiles_here = teacher_tiles.shape[0]
     destination = tile_dest[:, 0]
     positions = jnp.arange(tiles_here, dtype=jnp.int32)
@@ -160,9 +110,10 @@
         lax.all_to_all(send_count, ("lon", "lat"), split_axis=0, concat_axis=0, tiled=True),
     )
     offsets = jnp.arange(TILE, dtype=jnp.int32)
-    cell_index = recv_start[:, None] + offsets[None, :]
     is_valid = offsets[None, :] < recv_count[:, None]
+    sample_of = recv_start // (block_cols * band_rows)
     inner_row = recv_start // block_cols % band_rows
+    first_col = recv_start % block_cols
     glob_row = lat_index * band_rows + inner_row
     area_weight = jnp.cos(
         jnp.pi * ((glob_row.astype(jnp.float32) + 0.5) / (band_rows * lat_count) - 0.5)
@@ -170,27 +121,121 @@
     row_weight = jnp.where(is_valid, area_weight[:, None], jnp.float32(0.0)) / jnp.float32(
         devices * tiles_here * TILE
     )
-    row_weight = row_weight.reshape(-1, 1)
-    cell_flat = cell_index.reshape(-1)
-    y_rows = block_flat[cell_flat]
-    predicted = jnp.dot(y_rows, head_weight, preferred_element_type=jnp.float32)
-    residual = predicted - recv_tiles.reshape(-1, teach_width).astype(jnp.float32)
-    loss_sum = jnp.sum(row_weight * residual * residual)
-    grad_pred = (2.0 * row_weight * residual).astype(jnp.bfloat16)
-    grad_head = lax.dot_general(
-        y_rows, grad_pred, (((0,), (0,)), ((), ())), preferred_element_type=jnp.float32
-    )
-    grad_rows = jnp.dot(grad_pred, head_weight.T, preferred_element_type=jnp.float32)
-    grad_y = jnp.zeros((block_flat.shape[0], width), jnp.float32).at[cell_flat].add(grad_rows)
+    kernel = dw_kernel.astype(jnp.float32)
+    onehot = (
+        rates[None, :] == jnp.arange(1, DMAX + 1, dtype=jnp.int32)[:, None]
+    ).astype(jnp.float32)
+    span = 2 * DMAX + 1
+    reach = TILE + 2 * DMAX
+
+    def gather_windows(place):
+        b, h, w = place
+        return jax.vmap(
+            lambda b, h, w: lax.dynamic_slice(
+                padded, (b, h, w, jnp.int32(0)), (1, span, reach, width)
+            )[0]
+        )(b, h, w)
+
+    def shifted(source, row_shift, col_shift):
+        return source[:, DMAX + row_shift, DMAX + col_shift : DMAX + col_shift + TILE, :].astype(
+            jnp.float32
+        )
+
+    def forward(windows, tiles, weight):
+        center = shifted(windows, 0, 0)
+        accum_sum = center * kernel[4]
+        for dilation in range(1, DMAX + 1):
+            for tap_index in range(9):
+                if tap_index == 4:
+                    continue
+                row_shift = (tap_index // 3 - 1) * dilation
+                col_shift = (tap_index % 3 - 1) * dilation
+                accum_sum = accum_sum + kernel[tap_index] * onehot[dilation - 1] * shifted(
+                    windows, row_shift, col_shift
+                )
+        depth_flat = accum_sum.astype(jnp.bfloat16).reshape(-1, width)
+        preact = jnp.dot(depth_flat, pw_weight, preferred_element_type=jnp.float32)
+        y_rows = (center.reshape(-1, width) + jax.nn.silu(preact)).astype(jnp.bfloat16)
+        weight = weight.reshape(-1, 1)
+        predicted = jnp.dot(y_rows, head_weight, preferred_element_type=jnp.float32)
+        residual = predicted - tiles.reshape(-1, teach_width).astype(jnp.float32)
+        loss_part = jnp.sum(weight * residual * residual)
+        grad_pred = (2.0 * weight * residual).astype(jnp.bfloat16)
+        head_part = lax.dot_general(
+            y_rows, grad_pred, (((0,), (0,)), ((), ())), preferred_element_type=jnp.float32
+        )
+        grad_rows = jnp.dot(grad_pred, head_weight.T, preferred_element_type=jnp.float32)
+        return depth_flat, preact, grad_rows, loss_part, head_part
+
+    def backward(windows, depth_flat, grad_u):
+        pw_part = lax.dot_general(
+            depth_flat, grad_u, (((0,), (0,)), ((), ())), preferred_element_type=jnp.float32
+        )
+        grad_z = jnp.dot(grad_u, pw_weight.T, preferred_element_type=jnp.float32)
+        grad_z = grad_z.reshape(windows.shape[0], TILE, width)
+        tap_sums = []
+        for tap_index in range(9):
+            if tap_index == 4:
+                part = shifted(windows, 0, 0) * grad_z
+                tap_sums.append(jnp.sum(part.reshape(-1, width), axis=0))
+                continue
+            tap_sum = jnp.zeros((width,), jnp.float32)
+            for dilation in range(1, DMAX + 1):
+                row_shift = (tap_index // 3 - 1) * dilation
+                col_shift = (tap_index % 3 - 1) * dilation
+                part = shifted(windows, row_shift, col_shift) * grad_z
+                part = jnp.sum(part.reshape(-1, width), axis=0)
+                tap_sum = tap_sum + onehot[dilation - 1] * part
+            tap_sums.append(tap_sum)
+        return pw_part, jnp.stack(tap_sums, axis=0)
+
+    slots = recv_start.shape[0]
+    chunk = min(slots, CHUNK)
+    chunks = slots // chunk
+    place = (sample_of, inner_row, first_col)
+    if chunks == 1:
+        windows = gather_windows(place)
+        depth_flat, preact, grad_rows, loss_sum, grad_head = forward(
+            windows, recv_tiles, row_weight
+        )
+    else:
+        split = lambda v: v.reshape((chunks, chunk) + v.shape[1:])
+        outs = lax.map(
+            lambda xs: forward(gather_windows(xs[0]), xs[1], xs[2]),
+            (tuple(split(v) for v in place), split(recv_tiles), split(row_weight)),
+        )
+        depth_flat, preact, grad_rows = (v.reshape((-1, width)) for v in outs[:3])
+        loss_sum, grad_head = jnp.sum(outs[3]), jnp.sum(outs[4], axis=0)
+    cell = (recv_start[:, None] + offsets[None, :]).reshape(-1)
+    row_ids = jnp.arange(cell.shape[0], dtype=jnp.int32)
+    if cell.shape[0] <= 512:
+        same_cell = cell[:, None] == cell[None, :]
+        grad_y = jnp.dot(
+            same_cell.astype(jnp.float32),
+            grad_rows,
+            precision=lax.Precision.HIGHEST,
+            preferred_element_type=jnp.float32,
+        )
+        repeated = jnp.any(same_cell & (row_ids[None, :] < row_ids[:, None]), axis=1)
+    else:
+        cells_here = micro_batch * band_rows * block_cols
+        grid = jnp.zeros((cells_here, width), jnp.float32).at[cell].add(grad_rows)
+        grad_y = grid[cell]
+        owner = jnp.full((cells_here,), cell.shape[0], jnp.int32).at[cell].min(row_ids)
+        repeated = owner[cell] != row_ids
     sigmoid_u = jax.nn.sigmoid(preact)
     grad_u = (grad_y * sigmoid_u * (1.0 + preact * (1.0 - sigmoid_u))).astype(jnp.bfloat16)
-    grad_pw = lax.dot_general(
-        depth_flat, grad_u, (((0,), (0,)), ((), ())), preferred_element_type=jnp.float32
-    )
-    grad_z = jnp.dot(grad_u, pw_weight.T, preferred_element_type=jnp.float32).reshape(
-        micro_batch, band_rows, block_cols, width
-    )
-    grad_dw = dilated_grad(padded, grad_z, rates, band_rows, block_cols)
+    grad_u = jnp.where(repeated[:, None], jnp.zeros_like(grad_u), grad_u)
+    if chunks == 1:
+        windows_again, grad_u = lax.optimization_barrier((windows, grad_u))
+        grad_pw, grad_dw = backward(windows_again, depth_flat, grad_u)
+    else:
+        rows_split = lambda v: v.reshape((chunks, chunk * TILE) + v.shape[1:])
+        outs = lax.map(
+            lambda xs: backward(gather_windows(xs[0]), xs[1], xs[2]),
+            (tuple(split(v) for v in place), rows_split(depth_flat), rows_split(grad_u)),
+        )
+        grad_pw, grad_dw = jnp.sum(outs[0], axis=0), jnp.sum(outs[1], axis=0)
     grad_dw, grad_pw, grad_head, loss_sum = packed_sum(
         (grad_dw, grad_pw, grad_head, loss_sum), ("lat", "lon")
     )

time: 145 us -> 117 us (0.81)
  other arithmetic: 42.7 us -> 21.1 us
  waiting for transfers between devices: 36.3 us -> 25.8 us
  between operations: 13.2 us -> 3.02 us
  starting transfers between devices: 26.5 us -> 35.5 us
  local copies, waits for them, and re-layouts: 18.7 us -> 24.2 us
    another operation x4 -> x0, other arithmetic: 13.4 us -> none
    reduce_sum x2 -> x1, other arithmetic: 15.4 us -> 2.86 us  [backward(): part = jnp.sum(part.reshape(-1, width), axis=0)]
    ppermute x4, waiting for transfers between devices: 14 us -> 9.17 us  [double(): got = lax.ppermute(x, axis, [(i, i ^ bit) for i in range(count)])]
    ppermute x4, starting transfers between devices: 1.77 us -> 6.55 us  [double(): got = lax.ppermute(x, axis, [(i, i ^ bit) for i in range(count)])]
    convert_element_type x2 -> x7, other arithmetic: 3.92 us -> 8.53 us  [the longest x1 3.9 us: forward(): depth_flat = accum_sum.astype(jnp.bfloat16).reshape(-1, width)]
    ppermute x4, waiting for transfers between devices: 14.3 us -> 10 us  [halve(): return keep + lax.ppermute(send, axis, [(i, i ^ bit) for i in range(count)])]
    ppermute x4, starting transfers between devices: 2.17 us -> 6.39 us  [halve(): return keep + lax.ppermute(send, axis, [(i, i ^ bit) for i in range(count)])]
    scatter-add x1 -> x0, other arithmetic: 3.8 us -> none  [local(): jnp.zeros((block_flat.shape[0], width), jnp.float32).at[cell_flat]]
  transfers between devices with their start and end apart: 15 -> 15, of which waited for: 10 -> 10; matrix products, arithmetic and copies ran while one was open for 8% -> 12% of each run, Pallas kernels for 0% -> 0%
where the time goes in v2:
time: 117 us; the launch traced here: 116 us
  starting transfers between devices  35.5 us (30%)
  waiting for transfers between devices  25.8 us (22%)
  local copies, waits for them, and re-layouts  24.2 us (21%)
  other arithmetic  21.1 us (18%)
  matrix products  6.25 us (5%)
  between operations  3.02 us (3%)
    ppermute x4, waiting for transfers between devices, halve(): return keep + lax.ppermute(send, axis, [(i, i ^ bit) for i in range(count)])  10 us
    ppermute x4, waiting for transfers between devices, double(): got = lax.ppermute(x, axis, [(i, i ^ bit) for i in range(count)])  9.17 us
    ppermute x4, starting transfers between devices, double(): got = lax.ppermute(x, axis, [(i, i ^ bit) for i in range(count)])  6.55 us
    ppermute x4, starting transfers between devices, halve(): return keep + lax.ppermute(send, axis, [(i, i ^ bit) for i in range(count)])  6.39 us
    all_to_all x1, starting transfers between devices, local(): lax.all_to_all(send_count, ('lon', 'lat'), split_axis=0, concat_axis=0, t...  5.97 us
    gather x1, local copies, waits for them, and re-layouts, gather_windows(): lax.dynamic_slice(padded, (b, h, w, jnp.int32(0)), (1, span, reach, width))  5.73 us
    ppermute x2, starting transfers between devices, padded_2(): lax.ppermute(tail, axis, [(i, (i + 1) % count) for i in range(ends)])  5.19 us
    all_to_all x1, waiting for transfers between devices, local(): lax.all_to_all(send_count, ('lon', 'lat'), split_axis=0, concat_axis=0, t...  4.82 us
  transfers between devices with their start and end apart: 15, of which 10 were waited for; matrix products, arithmetic and copies ran while one was open for 12% of the time, Pallas kernels for 0%

profile of v2, /device:TPU:0, one launch (start us, length us, event | category | flops | bytes accessed | tf_op | source)
XLA Modules:
  0.0 115.9 jit_solution(8399155437256331963)
XLA Ops:
  2.3 3.0 %collective-permute-start = (bf16[2,48,4,256]{3,0,2,1:T(2,128)(2,1)S(1)}, bf16[2,48,4,256]{3,0,2,1:T(2,128)(2,1)S(1)}, u32[]{:S(2)}, u32[]{:S(2)}) collective-permute-start(bf16[2,48,4,256]{3,0,2,1:T(2,128)(2,1)S(1)} %copy.360), channel_id=1, source_target_pairs={{0,2},{2,4},{4,6},{6,8},{8,10},{10,12},{12,14},{14,0},{1,3},{3,5},... | collective-permute-start | bytes 589832 | tf_op jit(solution)/shard_map/ppermute | solution.py:73
  5.5 3.1 %collective-permute-start.1 = (bf16[2,48,4,256]{3,0,2,1:T(2,128)(2,1)S(1)}, bf16[2,48,4,256]{3,0,2,1:T(2,128)(2,1)S(1)}, u32[]{:S(2)}, u32[]{:S(2)}) collective-permute-start(bf16[2,48,4,256]{3,0,2,1:T(2,128)(2,1)S(1)} %copy.361), channel_id=1, source_target_pairs={{2,0},{4,2},{6,4},{8,6},{10,8},{12,10},{14,12},{0,14},{3,1},{5,3},... | collective-permute-start | bytes 589832 | tf_op jit(solution)/shard_map/ppermute | solution.py:75
  11.6 3.5 %all-to-all-start = ((s32[16,2,1]{1,2,0:T(1,128)}), s32[16,2,1]{1,2,0:T(1,128)S(1)}, u32[]{:S(2)}, u32[]{:S(2)}) async-start(s32[16,2,1]{1,2,0:T(1,128)} %bitcast.3), calls=%async_computation | async-start | bytes 16384 | tf_op jit(solution)/shard_map/all_to_all | solution.py:109
  19.4 2.3 %scatter_fusion = bf16[32,8,227]{2,1,0:T(8,128)(2,1)} fusion(bf16[32,8,227]{2,1,0:T(8,128)(2,1)} %broadcast_in_dim.37, s32[16]{0:T(128)S(1)} %fusion.86, bf16[16,8,227]{2,1,0:T(8,128)(2,1)} %param.14), kind=kCustom, calls=%fused_computation.3 | custom fusion | bytes 174400 | tf_op jit(solution)/shard_map/scatter | solution.py:103
  21.7 6.0 %all-to-all-start.1 = ((s32[16,2,1]{1,2,0:T(1,128)}), s32[16,2,1]{1,2,0:T(1,128)S(1)}, u32[]{:S(2)}, u32[]{:S(2)}) async-start(s32[16,2,1]{1,2,0:T(1,128)} %bitcast.5), calls=%async_computation.1 | async-start | bytes 16384 | tf_op jit(solution)/shard_map/all_to_all | solution.py:110
  29.2 4.8 %all-to-all-done.1 = s32[16,2,1]{1,2,0:T(1,128)S(1)} async-done(((s32[16,2,1]{1,2,0:T(1,128)}), s32[16,2,1]{1,2,0:T(1,128)S(1)}, u32[]{:S(2)}, u32[]{:S(2)}) %all-to-all-start.1) | async-done | bytes 160 | tf_op jit(solution)/shard_map/all_to_all | solution.py:110
  34.0 3.5 %all-to-all-start.2 = ((bf16[32,8,227]{2,1,0:T(8,128)(2,1)}), bf16[32,8,227]{2,1,0:T(8,128)(2,1)S(1)}, u32[]{:S(2)}, u32[]{:S(2)}) async-start(bf16[32,8,227]{2,1,0:T(8,128)(2,1)} %scatter_fusion), calls=%async_computation.2 | async-start | bytes 262144 | tf_op jit(solution)/shard_map/all_to_all | solution.py:108
  42.5 2.2 %collective-permute-start.2 = (bf16[2,4,40,256]{3,0,2,1:T(2,128)(2,1)S(1)}, bf16[2,4,40,256]{3,0,2,1:T(2,128)(2,1)S(1)}, u32[]{:S(2)}, u32[]{:S(2)}) collective-permute-start(bf16[2,4,40,256]{3,0,2,1:T(2,128)(2,1)S(1)} %get-tuple-element.121), channel_id=1, source_target_pairs={{0,1},{2,3},{4,5},{6,7},{8,9},{10,11},{12,13},{14,15},{16,17},{18,... | collective-permute-start | bytes 491528 | tf_op jit(solution)/shard_map/ppermute | solution.py:73
  46.2 1.8 %collective-permute-done.3 = bf16[2,4,40,256]{3,0,2,1:T(2,128)(2,1)S(1)} collective-permute-done((bf16[2,4,40,256]{3,0,2,1:T(2,128)(2,1)S(1)}, bf16[2,4,40,256]{3,0,2,1:T(2,128)(2,1)S(1)}, u32[]{:S(2)}, u32[]{:S(2)}) %collective-permute-start.3) | collective-permute-done | bytes 163872 | tf_op jit(solution)/shard_map/ppermute | solution.py:75
  48.0 4.8 %pad_maximum_fusion = bf16[2,56,40,256]{3,0,2,1:T(2,128)(2,1)S(1)} fusion(bf16[2,4,40,256]{3,0,2,1:T(2,128)(2,1)S(1)} %collective-permute-done.3, bf16[2,48,40,256]{3,0,2,1:T(2,128)(2,1)} %copy-done.2, bf16[2,4,40,256]{3,0,2,1:T(2,128)(2,1)S(1)} %collective-permute-done.2), kind=kLoop, calls=%fused_computation.4 | loop fusion | flops 2293760 | bytes 4587520 | tf_op jit(solution)/shard_map/concatenate | solution.py:71
  52.7 5.7 %gather_fusion = bf16[32,9,16,256]{3,0,2,1:T(8,128)(2,1)} fusion(bf16[2,56,40,256]{3,0,2,1:T(2,128)(2,1)S(1)} %pad_maximum_fusion, s32[32]{0:T(128)S(1)} %fusion.95), kind=kCustom, calls=%fused_computation | custom fusion | bytes 4719104 | tf_op jit(solution)/shard_map/vmap()/gather | solution.py:134
  58.5 2.5 %slice_convert_fusion.20 = (f32[32,1,8,256]{3,0,2,1:T(8,128)S(1)}, f32[32,1,8,256]{3,0,2,1:T(8,128)S(1)}, f32[32,1,8,256]{3,0,2,1:T(8,128)S(1)}, f32[32,1,8,256]...) fusion(bf16[32,9,16,256]{3,0,2,1:T(8,128)(2,1)} %gather_fusion), kind=kLoop, calls=%fused_computation.179 | loop fusion | flops 1245184 | bytes 7471104 | tf_op jit(solution)/shard_map/convert_element_type | solution.py:140
  63.1 3.9 %fusion.39 = bf16[256,256]{1,0:T(8,128)(2,1)S(1)} fusion(f32[32,1,8,256]{3,2,0,1:T(8,128)S(1)} %copy.242, f32[32,1,8,256]{3,2,0,1:T(8,128)S(1)} %copy.241, f32[32,1,8,256]{3,2,0,1:T(8,128)S(1)} %copy.240, f32[32,1,8,256]{3,2,0,1:T(8,128)S(1)} %copy.239, f32[32,1,8,256]{3,2,0,1:T(8,128)S(1)} %copy.238, f32[32,1,8,256]{3,2,0,1:T(8,128)S(1)} %copy.237, ...), kind=kLoop, calls=%fused_computation.87 | loop fusion | flops 4325376 | bytes 8815616 | tf_op jit(solution)/shard_map/convert_element_type | solution.py:156
  70.1 4.1 %fusion.8 = (f32[256]{0:T(256)S(1)}, f32[256]{0:T(256)S(1)}, f32[256]{0:T(256)S(1)}, f32[256]{0:T(256)S(1)}, f32[256]{0:T(256)S(1)}, /*index=5*/f32[256]{0:T(256...) fusion(f32[32,1,8,256]{3,0,2,1:T(8,128)S(1)} %get-tuple-element, ...), kind=kOutput, calls=%fused_computation.26 | convolution fusion | flops 35909120 | bytes 5261312 | tf_op jit(solution)/shard_map/dot_general | solution.py:174
  74.2 2.9 %fusion.25 = (f32[256]{0:T(256)S(1)}, f32[256]{0:T(256)S(1)}, f32[256]{0:T(256)S(1)}, f32[256]{0:T(256)S(1)}, f32[256]{0:T(256)S(1)}, /*index=5*/f32[256]{0:T(25...) fusion(f32[256,256]{1,0:T(8,128)S(1)} %get-tuple-element.171, ...), kind=kLoop, calls=%fused_computation.60 | loop fusion | flops 1962240 | bytes 4209664 | tf_op jit(solution)/shard_map/reduce_sum | solution.py:187
  81.9 3.9 %collective-permute-done.5 = f32[256,128]{1,0:T(8,128)S(1)} collective-permute-done((f32[256,128]{1,0:T(8,128)S(1)}, f32[256,128]{1,0:T(8,128)S(1)}, u32[]{:S(2)}, u32[]{:S(2)}) %collective-permute-start.5) | collective-permute-done | bytes 131104 | tf_op jit(solution)/shard_map/ppermute | solution.py:21
  87.5 2.6 %collective-permute-done.6 = f32[128,128]{1,0:T(8,128)S(1)} collective-permute-done((f32[128,128]{1,0:T(8,128)S(1)}, f32[128,128]{1,0:T(8,128)S(1)}, u32[]{:S(2)}, u32[]{:S(2)}) %collective-permute-start.6) | collective-permute-done | bytes 65568 | tf_op jit(solution)/shard_map/ppermute | solution.py:21
  90.1 2.7 %collective-permute-start.7 = (f32[64,128]{1,0:T(8,128)S(1)}, f32[64,128]{1,0:T(8,128)S(1)}, u32[]{:S(2)}, u32[]{:S(2)}) collective-permute-start(f32[64,128]{1,0:T(8,128)S(1)} %constant_dynamic-slice_fusion), channel_id=1, source_target_pairs={{0,8},{2,10},{4,12},{6,14},{8,0},{10,2},{12,4},{14,6},{1,9},{3,11}... | collective-permute-start | bytes 98312 | tf_op jit(solution)/shard_map/ppermute | solution.py:21
  92.8 2.2 %collective-permute-done.7 = f32[64,128]{1,0:T(8,128)S(1)} collective-permute-done((f32[64,128]{1,0:T(8,128)S(1)}, f32[64,128]{1,0:T(8,128)S(1)}, u32[]{:S(2)}, u32[]{:S(2)}) %collective-permute-start.7) | collective-permute-done | bytes 32800 | tf_op jit(solution)/shard_map/ppermute | solution.py:21
  95.0 2.7 %collective-permute-start.8 = (f32[64,128]{1,0:T(8,128)S(1)}, f32[64,128]{1,0:T(8,128)S(1)}, u32[]{:S(2)}, u32[]{:S(2)}) collective-permute-start(f32[64,128]{1,0:T(8,128)S(1)} %get-tuple-element.54), channel_id=1, source_target_pairs={{0,8},{2,10},{4,12},{6,14},{8,0},{10,2},{12,4},{14,6},{1,9},{3,11}... | collective-permute-start | bytes 98312 | tf_op jit(solution)/shard_map/ppermute | solution.py:28
  97.8 2.2 %collective-permute-done.8 = f32[64,128]{1,0:T(8,128)S(1)} collective-permute-done((f32[64,128]{1,0:T(8,128)S(1)}, f32[64,128]{1,0:T(8,128)S(1)}, u32[]{:S(2)}, u32[]{:S(2)}) %collective-permute-start.8) | collective-permute-done | bytes 32800 | tf_op jit(solution)/shard_map/ppermute | solution.py:28
  99.9 2.1 %collective-permute-start.9 = (f32[128,128]{1,0:T(8,128)S(1)}, f32[128,128]{1,0:T(8,128)S(1)}, u32[]{:S(2)}, u32[]{:S(2)}) collective-permute-start(f32[128,128]{1,0:T(8,128)S(1)} %constant_dynamic-update-slice_fusion.9), channel_id=1, source_target_pairs={{0,4},{2,6},{4,0},{6,2},{8,12},{10,14},{12,8},{14,10},{1,5},{3,7},... | collective-permute-start | bytes 196616 | tf_op jit(solution)/shard_map/ppermute | solution.py:28
  102.1 2.2 %collective-permute-done.9 = f32[128,128]{1,0:T(8,128)S(1)} collective-permute-done((f32[128,128]{1,0:T(8,128)S(1)}, f32[128,128]{1,0:T(8,128)S(1)}, u32[]{:S(2)}, u32[]{:S(2)}) %collective-permute-start.9) | collective-permute-done | bytes 65568 | tf_op jit(solution)/shard_map/ppermute | solution.py:28
  106.0 3.4 %collective-permute-done.10 = f32[256,128]{1,0:T(8,128)S(1)} collective-permute-done((f32[256,128]{1,0:T(8,128)S(1)}, f32[256,128]{1,0:T(8,128)S(1)}, u32[]{:S(2)}, u32[]{:S(2)}) %collective-permute-start.10) | collective-permute-done | bytes 131104 | tf_op jit(solution)/shard_map/ppermute | solution.py:28
  (116 shorter events, 34.9 us)
Async XLA Ops:
  0.6 66.4 %copy-start = (bf16[256,256]{1,0:T(8,128)(2,1)S(1)}, bf16[256,256]{1,0:T(8,128)(2,1)}, u32[]{:S(2)}) copy-start(bf16[256,256]{1,0:T(8,128)(2,1)} %param.12) | copy-start | bytes 393220
  0.6 38.4 %copy-start.3 = (bf16[2,48,32,256]{3,2,1,0:T(8,128)(2,1)S(1)}, bf16[2,48,32,256]{3,2,1,0:T(8,128)(2,1)}, u32[]{:S(2)}) copy-start(bf16[2,48,32,256]{3,2,1,0:T(8,128)(2,1)} %param.9) | copy-start | bytes 4718596
  2.3 36.6 %collective-permute-start = (bf16[2,48,4,256]{3,0,2,1:T(2,128)(2,1)S(1)}, bf16[2,48,4,256]{3,0,2,1:T(2,128)(2,1)S(1)}, u32[]{:S(2)}, u32[]{:S(2)}) collective-permute-start(bf16[2,48,4,256]{3,0,2,1:T(2,128)(2,1)S(1)} %copy.360), channel_id=1, source_target_pairs={{0,2},{2,4},{4,6},{6,8},{8,10},{10,12},{12,14},{14,0},{1,3},{3,5},... | collective-permute-start | bytes 589832 | tf_op jit(solution)/shard_map/ppermute | solution.py:73
  5.5 35.3 %collective-permute-start.1 = (bf16[2,48,4,256]{3,0,2,1:T(2,128)(2,1)S(1)}, bf16[2,48,4,256]{3,0,2,1:T(2,128)(2,1)S(1)}, u32[]{:S(2)}, u32[]{:S(2)}) collective-permute-start(bf16[2,48,4,256]{3,0,2,1:T(2,128)(2,1)S(1)} %copy.361), channel_id=1, source_target_pairs={{2,0},{4,2},{6,4},{8,6},{10,8},{12,10},{14,12},{0,14},{3,1},{5,3},... | collective-permute-start | bytes 589832 | tf_op jit(solution)/shard_map/ppermute | solution.py:75
  11.6 10.1 %all-to-all-start = ((s32[16,2,1]{1,2,0:T(1,128)}), s32[16,2,1]{1,2,0:T(1,128)S(1)}, u32[]{:S(2)}, u32[]{:S(2)}) async-start(s32[16,2,1]{1,2,0:T(1,128)} %bitcast.3), calls=%async_computation | async-start | bytes 16384 | tf_op jit(solution)/shard_map/all_to_all | solution.py:109
  21.7 12.3 %all-to-all-start.1 = ((s32[16,2,1]{1,2,0:T(1,128)}), s32[16,2,1]{1,2,0:T(1,128)S(1)}, u32[]{:S(2)}, u32[]{:S(2)}) async-start(s32[16,2,1]{1,2,0:T(1,128)} %bitcast.5), calls=%async_computation.1 | async-start | bytes 16384 | tf_op jit(solution)/shard_map/all_to_all | solution.py:110
  34.0 12.0 %all-to-all-start.2 = ((bf16[32,8,227]{2,1,0:T(8,128)(2,1)}), bf16[32,8,227]{2,1,0:T(8,128)(2,1)S(1)}, u32[]{:S(2)}, u32[]{:S(2)}) async-start(bf16[32,8,227]{2,1,0:T(8,128)(2,1)} %scatter_fusion), calls=%async_computation.2 | async-start | bytes 262144 | tf_op jit(solution)/shard_map/all_to_all | solution.py:108
  41.0 1.3 %copy-start.2 = (bf16[2,48,40,256]{3,0,2,1:T(2,128)(2,1)}, bf16[2,48,40,256]{3,0,2,1:T(2,128)(2,1)S(1)}, u32[]{:S(2)}) copy-start(bf16[2,48,40,256]{3,0,2,1:T(2,128)(2,1)S(1)} %constant_dynamic-update-slice_fusion) | copy-start | bytes 5898244
  42.5 3.7 %collective-permute-start.2 = (bf16[2,4,40,256]{3,0,2,1:T(2,128)(2,1)S(1)}, bf16[2,4,40,256]{3,0,2,1:T(2,128)(2,1)S(1)}, u32[]{:S(2)}, u32[]{:S(2)}) collective-permute-start(bf16[2,4,40,256]{3,0,2,1:T(2,128)(2,1)S(1)} %get-tuple-element.121), channel_id=1, source_target_pairs={{0,1},{2,3},{4,5},{6,7},{8,9},{10,11},{12,13},{14,15},{16,17},{18,... | collective-permute-start | bytes 491528 | tf_op jit(solution)/shard_map/ppermute | solution.py:73
  44.7 3.3 %collective-permute-start.3 = (bf16[2,4,40,256]{3,0,2,1:T(2,128)(2,1)S(1)}, bf16[2,4,40,256]{3,0,2,1:T(2,128)(2,1)S(1)}, u32[]{:S(2)}, u32[]{:S(2)}) collective-permute-start(bf16[2,4,40,256]{3,0,2,1:T(2,128)(2,1)S(1)} %get-tuple-element.122), channel_id=1, source_target_pairs={{1,0},{3,2},{5,4},{7,6},{9,8},{11,10},{13,12},{15,14},{17,16},{19,... | collective-permute-start | bytes 491528 | tf_op jit(solution)/shard_map/ppermute | solution.py:75
  58.5 2.5 %copy-start.1 = (bf16[32,9,16,256]{3,0,2,1:T(8,128)(2,1)S(1)}, bf16[32,9,16,256]{3,0,2,1:T(8,128)(2,1)}, u32[]{:S(2)}) copy-start(bf16[32,9,16,256]{3,0,2,1:T(8,128)(2,1)} %gather_fusion) | copy-start | bytes 7077892
  63.1 4.2 %copy-start.4 = (bf16[256,227]{0,1:T(8,128)(2,1)S(1)}, bf16[256,227]{0,1:T(8,128)(2,1)}, u32[]{:S(2)}) copy-start(bf16[256,227]{0,1:T(8,128)(2,1)} %param.13) | copy-start | bytes 348676
  78.5 1.6 %collective-permute-start.4 = (f32[512,128]{1,0:T(8,128)S(1)}, f32[512,128]{1,0:T(8,128)S(1)}, u32[]{:S(2)}, u32[]{:S(2)}) collective-permute-start(f32[512,128]{1,0:T(8,128)S(1)} %constant_dynamic-slice_fusion.3), channel_id=1, source_target_pairs={{0,1},{1,0},{2,3},{3,2},{4,5},{5,4},{6,7},{7,6},{8,9},{9,8},{10,11... | collective-permute-start | bytes 786440 | tf_op jit(solution)/shard_map/ppermute | solution.py:21
  80.1 5.6 %collective-permute-start.5 = (f32[256,128]{1,0:T(8,128)S(1)}, f32[256,128]{1,0:T(8,128)S(1)}, u32[]{:S(2)}, u32[]{:S(2)}) collective-permute-start(f32[256,128]{1,0:T(8,128)S(1)} %constant_dynamic-slice_fusion.2), channel_id=1, source_target_pairs={{0,2},{2,0},{4,6},{6,4},{8,10},{10,8},{12,14},{14,12},{1,3},{3,1},... | collective-permute-start | bytes 393224 | tf_op jit(solution)/shard_map/ppermute | solution.py:21
  85.8 4.3 %collective-permute-start.6 = (f32[128,128]{1,0:T(8,128)S(1)}, f32[128,128]{1,0:T(8,128)S(1)}, u32[]{:S(2)}, u32[]{:S(2)}) collective-permute-start(f32[128,128]{1,0:T(8,128)S(1)} %constant_dynamic-slice_fusion.1), channel_id=1, source_target_pairs={{0,4},{2,6},{4,0},{6,2},{8,12},{10,14},{12,8},{14,10},{1,5},{3,7},... | collective-permute-start | bytes 196616 | tf_op jit(solution)/shard_map/ppermute | solution.py:21
  90.1 4.9 %collective-permute-start.7 = (f32[64,128]{1,0:T(8,128)S(1)}, f32[64,128]{1,0:T(8,128)S(1)}, u32[]{:S(2)}, u32[]{:S(2)}) collective-permute-start(f32[64,128]{1,0:T(8,128)S(1)} %constant_dynamic-slice_fusion), channel_id=1, source_target_pairs={{0,8},{2,10},{4,12},{6,14},{8,0},{10,2},{12,4},{14,6},{1,9},{3,11}... | collective-permute-start | bytes 98312 | tf_op jit(solution)/shard_map/ppermute | solution.py:21
  95.0 4.9 %collective-permute-start.8 = (f32[64,128]{1,0:T(8,128)S(1)}, f32[64,128]{1,0:T(8,128)S(1)}, u32[]{:S(2)}, u32[]{:S(2)}) collective-permute-start(f32[64,128]{1,0:T(8,128)S(1)} %get-tuple-element.54), channel_id=1, source_target_pairs={{0,8},{2,10},{4,12},{6,14},{8,0},{10,2},{12,4},{14,6},{1,9},{3,11}... | collective-permute-start | bytes 98312 | tf_op jit(solution)/shard_map/ppermute | solution.py:28
  99.9 4.4 %collective-permute-start.9 = (f32[128,128]{1,0:T(8,128)S(1)}, f32[128,128]{1,0:T(8,128)S(1)}, u32[]{:S(2)}, u32[]{:S(2)}) collective-permute-start(f32[128,128]{1,0:T(8,128)S(1)} %constant_dynamic-update-slice_fusion.9), channel_id=1, source_target_pairs={{0,4},{2,6},{4,0},{6,2},{8,12},{10,14},{12,8},{14,10},{1,5},{3,7},... | collective-permute-start | bytes 196616 | tf_op jit(solution)/shard_map/ppermute | solution.py:28
  104.3 5.0 %collective-permute-start.10 = (f32[256,128]{1,0:T(8,128)S(1)}, f32[256,128]{1,0:T(8,128)S(1)}, u32[]{:S(2)}, u32[]{:S(2)}) collective-permute-start(f32[256,128]{1,0:T(8,128)S(1)} %constant_dynamic-update-slice_fusion.7), channel_id=1, source_target_pairs={{0,2},{2,0},{4,6},{6,4},{8,10},{10,8},{12,14},{14,12},{1,3},{3,1},... | collective-permute-start | bytes 393224 | tf_op jit(solution)/shard_map/ppermute | solution.py:28
  109.4 1.6 %collective-permute-start.11 = (f32[512,128]{1,0:T(8,128)S(1)}, f32[512,128]{1,0:T(8,128)S(1)}, u32[]{:S(2)}, u32[]{:S(2)}) collective-permute-start(f32[512,128]{1,0:T(8,128)S(1)} %constant_dynamic-update-slice_fusion.5), channel_id=1, source_target_pairs={{0,1},{1,0},{2,3},{3,2},{4,5},{5,4},{6,7},{7,6},{8,9},{9,8},{10,11... | collective-permute-start | bytes 786440 | tf_op jit(solution)/shard_map/ppermute | solution.py:28

commit v3 on v2

--- a/solution.py
+++ b/solution.py
@@ -97,18 +97,30 @@
     earlier = positions[:, None] > positions[None, :]
     slot_rank = jnp.sum((same_dest & earlier).astype(jnp.int32), axis=1)
     slot_index = destination * CAP + slot_rank
-    send_tiles = (
-        jnp.zeros((devices * CAP, TILE, teach_width), jnp.bfloat16)
-        .at[slot_index]
-        .set(teacher_tiles)
-    )
-    send_start = jnp.zeros((devices * CAP,), jnp.int32).at[slot_index].set(tile_start)
-    send_count = jnp.zeros((devices * CAP,), jnp.int32).at[slot_index].set(tile_count)
-    recv_tiles, recv_start, recv_count = (
-        lax.all_to_all(send_tiles, ("lon", "lat"), split_axis=0, concat_axis=0, tiled=True),
-        lax.all_to_all(send_start, ("lon", "lat"), split_axis=0, concat_axis=0, tiled=True),
-        lax.all_to_all(send_count, ("lon", "lat"), split_axis=0, concat_axis=0, tiled=True),
-    )
+    slots = devices * CAP
+    base = 64
+    column = jnp.zeros((tiles_here, TILE, 1), jnp.float32)
+    column = column.at[:, 0, 0].set((tile_start // base).astype(jnp.float32))
+    column = column.at[:, 1, 0].set((tile_start % base).astype(jnp.float32))
+    column = column.at[:, 2, 0].set(tile_count.astype(jnp.float32))
+    packed = jnp.concatenate([teacher_tiles, column.astype(jnp.bfloat16)], axis=2)
+    chooser = (slot_index[None, :] == jnp.arange(slots, dtype=jnp.int32)[:, None]).astype(
+        jnp.bfloat16
+    )
+    send = jnp.dot(
+        chooser, packed.reshape(tiles_here, -1), preferred_element_type=jnp.float32
+    ).astype(jnp.bfloat16)
+    recv = lax.all_to_all(
+        send.reshape(slots, TILE, teach_width + 1),
+        ("lon", "lat"),
+        split_axis=0,
+        concat_axis=0,
+        tiled=True,
+    )
+    recv_tiles = recv[:, :, :teach_width]
+    meta = recv[:, :3, teach_width].astype(jnp.int32)
+    recv_start = meta[:, 0] * base + meta[:, 1]
+    recv_count = meta[:, 2]
     offsets = jnp.arange(TILE, dtype=jnp.int32)
     is_valid = offsets[None, :] < recv_count[:, None]
     sample_of = recv_start // (block_cols * band_rows)

time: 117 us -> 104 us (0.89)
  starting transfers between devices: 35.5 us -> 26.9 us
  local copies, waits for them, and re-layouts: 24.2 us -> 18.1 us
  waiting for transfers between devices: 25.8 us -> 27.6 us
    ppermute x2, waiting for transfers between devices: 0.01 us -> 5.92 us  [padded_2(): lax.ppermute(tail, axis, [(i, (i + 1) % count) for i in range(ends)])]
    all_to_all x3 -> x1, starting transfers between devices: 13 us -> 7.36 us  [local(): lax.all_to_all(send.reshape(slots, TILE, teach_width + 1), ('lon', 'lat')...]
    all_to_all x3 -> x1, waiting for transfers between devices: 4.83 us -> 0.01 us  [local(): lax.all_to_all(send.reshape(slots, TILE, teach_width + 1), ('lon', 'lat')...]
    scatter x3 -> x1, local copies, waits for them, and re-layouts: 3.79 us -> 0.01 us  [local(): column = column.at[:, 0, 0].set((tile_start // base).astype(jnp.float32))]
    all_to_all x4 -> x0, local copies, waits for them, and re-layouts: 1.98 us -> none  [the longest x3 1.29 us: local(): lax.all_to_all(send_start, ('lon', 'lat'), split_axis=0, concat_axis=0, t...]
    ppermute x2, starting transfers between devices: 5.19 us -> 3.28 us  [padded_2(): lax.ppermute(tail, axis, [(i, (i + 1) % count) for i in range(ends)])]
    all_to_all x2 -> x0, other arithmetic: 1.34 us -> none  [the longest x1 0.67 us: local(): lax.all_to_all(send_count, ('lon', 'lat'), split_axis=0, concat_axis=0, t...]
    scatter x0 -> x2, other arithmetic: none -> 1.33 us  [the longest x1 0.67 us: local(): column = column.at[:, 1, 0].set((tile_start % base).astype(jnp.float32))]
  transfers between devices with their start and end apart: 15 -> 13, of which waited for: 10 -> 11; matrix products, arithmetic and copies ran while one was open for 12% -> 5% of each run, Pallas kernels for 0% -> 0%
where the time goes in v3:
time: 104 us
  waiting for transfers between devices  27.6 us (27%)
  starting transfers between devices  26.9 us (26%)
  other arithmetic  21.5 us (21%)
  local copies, waits for them, and re-layouts  18.1 us (17%)
  matrix products  6.43 us (6%)
  between operations  3.01 us (3%)
    ppermute x4, waiting for transfers between devices, halve(): return keep + lax.ppermute(send, axis, [(i, i ^ bit) for i in range(count)])  10.7 us
    ppermute x4, waiting for transfers between devices, double(): got = lax.ppermute(x, axis, [(i, i ^ bit) for i in range(count)])  9.6 us
    all_to_all x1, starting transfers between devices, local(): lax.all_to_all(send.reshape(slots, TILE, teach_width + 1), ('lon', 'lat')...  7.36 us
    ppermute x4, starting transfers between devices, halve(): return keep + lax.ppermute(send, axis, [(i, i ^ bit) for i in range(count)])  6.15 us
    ppermute x4, starting transfers between devices, double(): got = lax.ppermute(x, axis, [(i, i ^ bit) for i in range(count)])  6.01 us
    ppermute x2, waiting for transfers between devices, padded_2(): lax.ppermute(tail, axis, [(i, (i + 1) % count) for i in range(ends)])  5.92 us
    gather x1, local copies, waits for them, and re-layouts, gather_windows(): lax.dynamic_slice(padded, (b, h, w, jnp.int32(0)), (1, span, reach, width))  5.73 us
    concatenate x1, other arithmetic, padded_2(): jnp.concatenate([lax.ppermute(tail, axis, [(i, (i + 1) % count) for i in...  4.77 us
  transfers between devices with their start and end apart: 13, of which 11 were waited for; matrix products, arithmetic and copies ran while one was open for 5% of the time, Pallas kernels for 0%

profile of v3, /device:TPU:0, one launch (start us, length us, event | category | flops | bytes accessed | tf_op | source)
XLA Modules:
  0.0 103.6 jit_solution(17140606188739827613)
XLA Ops:
  6.7 7.4 %all-to-all-start = ((bf16[32,8,228]{2,1,0:T(8,128)(2,1)}), bf16[32,8,228]{2,1,0:T(8,128)(2,1)S(1)}, u32[]{:S(2)}, u32[]{:S(2)}) async-start(bf16[32,8,228]{2,1,0:T(8,128)(2,1)} %reshape.832), calls=%async_computation | async-start | bytes 262144 | tf_op jit(solution)/shard_map/all_to_all | solution.py:113
  15.5 2.0 %collective-permute-start = (bf16[2,48,4,256]{3,0,2,1:T(2,128)(2,1)S(1)}, bf16[2,48,4,256]{3,0,2,1:T(2,128)(2,1)S(1)}, u32[]{:S(2)}, u32[]{:S(2)}) collective-permute-start(bf16[2,48,4,256]{3,0,2,1:T(2,128)(2,1)S(1)} %copy.519), channel_id=1, source_target_pairs={{0,2},{2,4},{4,6},{6,8},{8,10},{10,12},{12,14},{14,0},{1,3},{3,5},... | collective-permute-start | bytes 589832 | tf_op jit(solution)/shard_map/ppermute | solution.py:73
  17.7 2.9 %collective-permute-start.1 = (bf16[2,48,4,256]{3,0,2,1:T(2,128)(2,1)S(1)}, bf16[2,48,4,256]{3,0,2,1:T(2,128)(2,1)S(1)}, u32[]{:S(2)}, u32[]{:S(2)}) collective-permute-start(bf16[2,48,4,256]{3,0,2,1:T(2,128)(2,1)S(1)} %copy.520), channel_id=1, source_target_pairs={{2,0},{4,2},{6,4},{8,6},{10,8},{12,10},{14,12},{0,14},{3,1},{5,3},... | collective-permute-start | bytes 589832 | tf_op jit(solution)/shard_map/ppermute | solution.py:75
  20.8 5.9 %collective-permute-done = bf16[2,48,4,256]{3,0,2,1:T(2,128)(2,1)S(1)} collective-permute-done((bf16[2,48,4,256]{3,0,2,1:T(2,128)(2,1)S(1)}, bf16[2,48,4,256]{3,0,2,1:T(2,128)(2,1)S(1)}, u32[]{:S(2)}, u32[]{:S(2)}) %collective-permute-start) | collective-permute-done | bytes 196640 | tf_op jit(solution)/shard_map/ppermute | solution.py:73
  26.8 1.7 %constant_dynamic-update-slice_fusion.1 = bf16[2,48,40,256]{3,0,2,1:T(2,128)(2,1)S(1)} fusion(bf16[2,48,40,256]{3,0,2,1:T(2,128)(2,1)S(1)} %constant_dynamic-update-slice_fusion.2, bf16[2,48,32,256]{3,2,1,0:T(8,128)(2,1)S(1)} %copy-done.3), kind=kLoop, calls=%fused_computation.240 | loop fusion | bytes 3145728
  35.3 4.8 %pad_maximum_fusion = bf16[2,56,40,256]{3,0,2,1:T(2,128)(2,1)S(1)} fusion(bf16[2,4,40,256]{3,0,2,1:T(2,128)(2,1)S(1)} %collective-permute-done.3, bf16[2,48,40,256]{3,0,2,1:T(2,128)(2,1)} %copy-done.2, bf16[2,4,40,256]{3,0,2,1:T(2,128)(2,1)S(1)} %collective-permute-done.2), kind=kLoop, calls=%fused_computation.1 | loop fusion | flops 2293760 | bytes 4587520 | tf_op jit(solution)/shard_map/concatenate | solution.py:71
  40.1 5.7 %gather_fusion = bf16[32,9,16,256]{3,0,2,1:T(8,128)(2,1)} fusion(bf16[2,56,40,256]{3,0,2,1:T(2,128)(2,1)S(1)} %pad_maximum_fusion, s32[32]{0:T(128)S(1)} %fusion.91), kind=kCustom, calls=%fused_computation | custom fusion | bytes 4719104 | tf_op jit(solution)/shard_map/vmap()/gather | solution.py:146
  45.9 2.5 %slice_convert_fusion.20 = (f32[32,1,8,256]{3,0,2,1:T(8,128)S(1)}, f32[32,1,8,256]{3,0,2,1:T(8,128)S(1)}, f32[32,1,8,256]{3,0,2,1:T(8,128)S(1)}, f32[32,1,8,256]...) fusion(bf16[32,9,16,256]{3,0,2,1:T(8,128)(2,1)} %gather_fusion), kind=kLoop, calls=%fused_computation.179 | loop fusion | flops 1245184 | bytes 7471104 | tf_op jit(solution)/shard_map/convert_element_type | solution.py:152
  50.5 3.9 %fusion.39 = bf16[256,256]{1,0:T(8,128)(2,1)S(1)} fusion(f32[32,1,8,256]{3,2,0,1:T(8,128)S(1)} %copy.397, f32[32,1,8,256]{3,2,0,1:T(8,128)S(1)} %copy.396, f32[32,1,8,256]{3,2,0,1:T(8,128)S(1)} %copy.395, f32[32,1,8,256]{3,2,0,1:T(8,128)S(1)} %copy.394, f32[32,1,8,256]{3,2,0,1:T(8,128)S(1)} %copy.393, f32[32,1,8,256]{3,2,0,1:T(8,128)S(1)} %copy.392, ...), kind=kLoop, calls=%fused_computation.85 | loop fusion | flops 4325376 | bytes 8815616 | tf_op jit(solution)/shard_map/convert_element_type | solution.py:168
  57.5 4.1 %fusion.8 = (f32[256]{0:T(256)S(1)}, f32[256]{0:T(256)S(1)}, f32[256]{0:T(256)S(1)}, f32[256]{0:T(256)S(1)}, f32[256]{0:T(256)S(1)}, /*index=5*/f32[256]{0:T(256...) fusion(f32[32,1,8,256]{3,0,2,1:T(8,128)S(1)} %get-tuple-element, ...), kind=kOutput, calls=%fused_computation.24 | convolution fusion | flops 35909120 | bytes 5261312 | tf_op jit(solution)/shard_map/dot_general | solution.py:186
  61.6 2.9 %fusion.25 = (f32[256]{0:T(256)S(1)}, f32[256]{0:T(256)S(1)}, f32[256]{0:T(256)S(1)}, f32[256]{0:T(256)S(1)}, f32[256]{0:T(256)S(1)}, /*index=5*/f32[256]{0:T(25...) fusion(f32[256,256]{1,0:T(8,128)S(1)} %get-tuple-element.218, ...), kind=kLoop, calls=%fused_computation.58 | loop fusion | flops 1962240 | bytes 4209664 | tf_op jit(solution)/shard_map/reduce_sum | solution.py:199
  67.5 2.1 %collective-permute-start.5 = (f32[256,128]{1,0:T(8,128)S(1)}, f32[256,128]{1,0:T(8,128)S(1)}, u32[]{:S(2)}, u32[]{:S(2)}) collective-permute-start(f32[256,128]{1,0:T(8,128)S(1)} %constant_dynamic-slice_fusion.2), channel_id=1, source_target_pairs={{0,2},{2,0},{4,6},{6,4},{8,10},{10,8},{12,14},{14,12},{1,3},{3,1},... | collective-permute-start | bytes 393224 | tf_op jit(solution)/shard_map/ppermute | solution.py:21
  69.6 3.9 %collective-permute-done.5 = f32[256,128]{1,0:T(8,128)S(1)} collective-permute-done((f32[256,128]{1,0:T(8,128)S(1)}, f32[256,128]{1,0:T(8,128)S(1)}, u32[]{:S(2)}, u32[]{:S(2)}) %collective-permute-start.5) | collective-permute-done | bytes 131104 | tf_op jit(solution)/shard_map/ppermute | solution.py:21
  73.6 1.5 %collective-permute-start.6 = (f32[128,128]{1,0:T(8,128)S(1)}, f32[128,128]{1,0:T(8,128)S(1)}, u32[]{:S(2)}, u32[]{:S(2)}) collective-permute-start(f32[128,128]{1,0:T(8,128)S(1)} %constant_dynamic-slice_fusion.1), channel_id=1, source_target_pairs={{0,4},{2,6},{4,0},{6,2},{8,12},{10,14},{12,8},{14,10},{1,5},{3,7},... | collective-permute-start | bytes 196616 | tf_op jit(solution)/shard_map/ppermute | solution.py:21
  75.1 2.8 %collective-permute-done.6 = f32[128,128]{1,0:T(8,128)S(1)} collective-permute-done((f32[128,128]{1,0:T(8,128)S(1)}, f32[128,128]{1,0:T(8,128)S(1)}, u32[]{:S(2)}, u32[]{:S(2)}) %collective-permute-start.6) | collective-permute-done | bytes 65568 | tf_op jit(solution)/shard_map/ppermute | solution.py:21
  77.9 2.2 %collective-permute-start.7 = (f32[64,128]{1,0:T(8,128)S(1)}, f32[64,128]{1,0:T(8,128)S(1)}, u32[]{:S(2)}, u32[]{:S(2)}) collective-permute-start(f32[64,128]{1,0:T(8,128)S(1)} %constant_dynamic-slice_fusion), channel_id=1, source_target_pairs={{0,8},{2,10},{4,12},{6,14},{8,0},{10,2},{12,4},{14,6},{1,9},{3,11}... | collective-permute-start | bytes 98312 | tf_op jit(solution)/shard_map/ppermute | solution.py:21
  80.2 2.6 %collective-permute-done.7 = f32[64,128]{1,0:T(8,128)S(1)} collective-permute-done((f32[64,128]{1,0:T(8,128)S(1)}, f32[64,128]{1,0:T(8,128)S(1)}, u32[]{:S(2)}, u32[]{:S(2)}) %collective-permute-start.7) | collective-permute-done | bytes 32800 | tf_op jit(solution)/shard_map/ppermute | solution.py:21
  82.8 2.3 %collective-permute-start.8 = (f32[64,128]{1,0:T(8,128)S(1)}, f32[64,128]{1,0:T(8,128)S(1)}, u32[]{:S(2)}, u32[]{:S(2)}) collective-permute-start(f32[64,128]{1,0:T(8,128)S(1)} %get-tuple-element.98), channel_id=1, source_target_pairs={{0,8},{2,10},{4,12},{6,14},{8,0},{10,2},{12,4},{14,6},{1,9},{3,11}... | collective-permute-start | bytes 98312 | tf_op jit(solution)/shard_map/ppermute | solution.py:28
  85.2 2.5 %collective-permute-done.8 = f32[64,128]{1,0:T(8,128)S(1)} collective-permute-done((f32[64,128]{1,0:T(8,128)S(1)}, f32[64,128]{1,0:T(8,128)S(1)}, u32[]{:S(2)}, u32[]{:S(2)}) %collective-permute-start.8) | collective-permute-done | bytes 32800 | tf_op jit(solution)/shard_map/ppermute | solution.py:28
  87.7 1.8 %collective-permute-start.9 = (f32[128,128]{1,0:T(8,128)S(1)}, f32[128,128]{1,0:T(8,128)S(1)}, u32[]{:S(2)}, u32[]{:S(2)}) collective-permute-start(f32[128,128]{1,0:T(8,128)S(1)} %constant_dynamic-update-slice_fusion.9), channel_id=1, source_target_pairs={{0,4},{2,6},{4,0},{6,2},{8,12},{10,14},{12,8},{14,10},{1,5},{3,7},... | collective-permute-start | bytes 196616 | tf_op jit(solution)/shard_map/ppermute | solution.py:28
  89.5 2.4 %collective-permute-done.9 = f32[128,128]{1,0:T(8,128)S(1)} collective-permute-done((f32[128,128]{1,0:T(8,128)S(1)}, f32[128,128]{1,0:T(8,128)S(1)}, u32[]{:S(2)}, u32[]{:S(2)}) %collective-permute-start.9) | collective-permute-done | bytes 65568 | tf_op jit(solution)/shard_map/ppermute | solution.py:28
  92.0 1.8 %collective-permute-start.10 = (f32[256,128]{1,0:T(8,128)S(1)}, f32[256,128]{1,0:T(8,128)S(1)}, u32[]{:S(2)}, u32[]{:S(2)}) collective-permute-start(f32[256,128]{1,0:T(8,128)S(1)} %constant_dynamic-update-slice_fusion.7), channel_id=1, source_target_pairs={{0,2},{2,0},{4,6},{6,4},{8,10},{10,8},{12,14},{14,12},{1,3},{3,1},... | collective-permute-start | bytes 393224 | tf_op jit(solution)/shard_map/ppermute | solution.py:28
  93.8 3.2 %collective-permute-done.10 = f32[256,128]{1,0:T(8,128)S(1)} collective-permute-done((f32[256,128]{1,0:T(8,128)S(1)}, f32[256,128]{1,0:T(8,128)S(1)}, u32[]{:S(2)}, u32[]{:S(2)}) %collective-permute-start.10) | collective-permute-done | bytes 131104 | tf_op jit(solution)/shard_map/ppermute | solution.py:28
  97.2 1.4 %collective-permute-done.11 = f32[512,128]{1,0:T(8,128)S(1)} collective-permute-done((f32[512,128]{1,0:T(8,128)S(1)}, f32[512,128]{1,0:T(8,128)S(1)}, u32[]{:S(2)}, u32[]{:S(2)}) %collective-permute-start.11) | collective-permute-done | bytes 262176 | tf_op jit(solution)/shard_map/ppermute | solution.py:28
  (117 shorter events, 26.1 us)
Async XLA Ops:
  0.6 53.8 %copy-start = (bf16[256,256]{1,0:T(8,128)(2,1)S(1)}, bf16[256,256]{1,0:T(8,128)(2,1)}, u32[]{:S(2)}) copy-start(bf16[256,256]{1,0:T(8,128)(2,1)} %param.18) | copy-start | bytes 393220
  0.6 26.2 %copy-start.3 = (bf16[2,48,32,256]{3,2,1,0:T(8,128)(2,1)S(1)}, bf16[2,48,32,256]{3,2,1,0:T(8,128)(2,1)}, u32[]{:S(2)}) copy-start(bf16[2,48,32,256]{3,2,1,0:T(8,128)(2,1)} %param.15) | copy-start | bytes 4718596
  0.7 19.9 %copy-start.5 = (bf16[9,256]{1,0:T(8,128)(2,1)S(1)}, bf16[9,256]{1,0:T(8,128)(2,1)}, u32[]{:S(2)}) copy-start(bf16[9,256]{1,0:T(8,128)(2,1)} %param.17) | copy-start | bytes 13828
  0.7 19.9 %copy-start.6 = (s32[256]{0:T(256)S(1)}, s32[256]{0:T(256)}, u32[]{:S(2)}) copy-start(s32[256]{0:T(256)} %param.16) | copy-start | bytes 3076
  6.7 26.7 %all-to-all-start = ((bf16[32,8,228]{2,1,0:T(8,128)(2,1)}), bf16[32,8,228]{2,1,0:T(8,128)(2,1)S(1)}, u32[]{:S(2)}, u32[]{:S(2)}) async-start(bf16[32,8,228]{2,1,0:T(8,128)(2,1)} %reshape.832), calls=%async_computation | async-start | bytes 262144 | tf_op jit(solution)/shard_map/all_to_all | solution.py:113
  15.5 11.2 %collective-permute-start = (bf16[2,48,4,256]{3,0,2,1:T(2,128)(2,1)S(1)}, bf16[2,48,4,256]{3,0,2,1:T(2,128)(2,1)S(1)}, u32[]{:S(2)}, u32[]{:S(2)}) collective-permute-start(bf16[2,48,4,256]{3,0,2,1:T(2,128)(2,1)S(1)} %copy.519), channel_id=1, source_target_pairs={{0,2},{2,4},{4,6},{6,8},{8,10},{10,12},{12,14},{14,0},{1,3},{3,5},... | collective-permute-start | bytes 589832 | tf_op jit(solution)/shard_map/ppermute | solution.py:73
  17.7 11.4 %collective-permute-start.1 = (bf16[2,48,4,256]{3,0,2,1:T(2,128)(2,1)S(1)}, bf16[2,48,4,256]{3,0,2,1:T(2,128)(2,1)S(1)}, u32[]{:S(2)}, u32[]{:S(2)}) collective-permute-start(bf16[2,48,4,256]{3,0,2,1:T(2,128)(2,1)S(1)} %copy.520), channel_id=1, source_target_pairs={{2,0},{4,2},{6,4},{8,6},{10,8},{12,10},{14,12},{0,14},{3,1},{5,3},... | collective-permute-start | bytes 589832 | tf_op jit(solution)/shard_map/ppermute | solution.py:75
  29.2 1.3 %copy-start.2 = (bf16[2,48,40,256]{3,0,2,1:T(2,128)(2,1)}, bf16[2,48,40,256]{3,0,2,1:T(2,128)(2,1)S(1)}, u32[]{:S(2)}) copy-start(bf16[2,48,40,256]{3,0,2,1:T(2,128)(2,1)S(1)} %constant_dynamic-update-slice_fusion) | copy-start | bytes 5898244
  30.8 3.7 %collective-permute-start.2 = (bf16[2,4,40,256]{3,0,2,1:T(2,128)(2,1)S(1)}, bf16[2,4,40,256]{3,0,2,1:T(2,128)(2,1)S(1)}, u32[]{:S(2)}, u32[]{:S(2)}) collective-permute-start(bf16[2,4,40,256]{3,0,2,1:T(2,128)(2,1)S(1)} %get-tuple-element.168), channel_id=1, source_target_pairs={{0,1},{2,3},{4,5},{6,7},{8,9},{10,11},{12,13},{14,15},{16,17},{18,... | collective-permute-start | bytes 491528 | tf_op jit(solution)/shard_map/ppermute | solution.py:73
  32.1 3.3 %collective-permute-start.3 = (bf16[2,4,40,256]{3,0,2,1:T(2,128)(2,1)S(1)}, bf16[2,4,40,256]{3,0,2,1:T(2,128)(2,1)S(1)}, u32[]{:S(2)}, u32[]{:S(2)}) collective-permute-start(bf16[2,4,40,256]{3,0,2,1:T(2,128)(2,1)S(1)} %get-tuple-element.169), channel_id=1, source_target_pairs={{1,0},{3,2},{5,4},{7,6},{9,8},{11,10},{13,12},{15,14},{17,16},{19,... | collective-permute-start | bytes 491528 | tf_op jit(solution)/shard_map/ppermute | solution.py:75
  45.9 2.5 %copy-start.1 = (bf16[32,9,16,256]{3,0,2,1:T(8,128)(2,1)S(1)}, bf16[32,9,16,256]{3,0,2,1:T(8,128)(2,1)}, u32[]{:S(2)}) copy-start(bf16[32,9,16,256]{3,0,2,1:T(8,128)(2,1)} %gather_fusion) | copy-start | bytes 7077892
  50.5 4.2 %copy-start.4 = (bf16[256,227]{0,1:T(8,128)(2,1)S(1)}, bf16[256,227]{0,1:T(8,128)(2,1)}, u32[]{:S(2)}) copy-start(bf16[256,227]{0,1:T(8,128)(2,1)} %param.19) | copy-start | bytes 348676
  65.9 1.6 %collective-permute-start.4 = (f32[512,128]{1,0:T(8,128)S(1)}, f32[512,128]{1,0:T(8,128)S(1)}, u32[]{:S(2)}, u32[]{:S(2)}) collective-permute-start(f32[512,128]{1,0:T(8,128)S(1)} %constant_dynamic-slice_fusion.3), channel_id=1, source_target_pairs={{0,1},{1,0},{2,3},{3,2},{4,5},{5,4},{6,7},{7,6},{8,9},{9,8},{10,11... | collective-permute-start | bytes 786440 | tf_op jit(solution)/shard_map/ppermute | solution.py:21
  67.5 6.0 %collective-permute-start.5 = (f32[256,128]{1,0:T(8,128)S(1)}, f32[256,128]{1,0:T(8,128)S(1)}, u32[]{:S(2)}, u32[]{:S(2)}) collective-permute-start(f32[256,128]{1,0:T(8,128)S(1)} %constant_dynamic-slice_fusion.2), channel_id=1, source_target_pairs={{0,2},{2,0},{4,6},{6,4},{8,10},{10,8},{12,14},{14,12},{1,3},{3,1},... | collective-permute-start | bytes 393224 | tf_op jit(solution)/shard_map/ppermute | solution.py:21
  73.6 4.3 %collective-permute-start.6 = (f32[128,128]{1,0:T(8,128)S(1)}, f32[128,128]{1,0:T(8,128)S(1)}, u32[]{:S(2)}, u32[]{:S(2)}) collective-permute-start(f32[128,128]{1,0:T(8,128)S(1)} %constant_dynamic-slice_fusion.1), channel_id=1, source_target_pairs={{0,4},{2,6},{4,0},{6,2},{8,12},{10,14},{12,8},{14,10},{1,5},{3,7},... | collective-permute-start | bytes 196616 | tf_op jit(solution)/shard_map/ppermute | solution.py:21
  77.9 4.9 %collective-permute-start.7 = (f32[64,128]{1,0:T(8,128)S(1)}, f32[64,128]{1,0:T(8,128)S(1)}, u32[]{:S(2)}, u32[]{:S(2)}) collective-permute-start(f32[64,128]{1,0:T(8,128)S(1)} %constant_dynamic-slice_fusion), channel_id=1, source_target_pairs={{0,8},{2,10},{4,12},{6,14},{8,0},{10,2},{12,4},{14,6},{1,9},{3,11}... | collective-permute-start | bytes 98312 | tf_op jit(solution)/shard_map/ppermute | solution.py:21
  82.8 4.9 %collective-permute-start.8 = (f32[64,128]{1,0:T(8,128)S(1)}, f32[64,128]{1,0:T(8,128)S(1)}, u32[]{:S(2)}, u32[]{:S(2)}) collective-permute-start(f32[64,128]{1,0:T(8,128)S(1)} %get-tuple-element.98), channel_id=1, source_target_pairs={{0,8},{2,10},{4,12},{6,14},{8,0},{10,2},{12,4},{14,6},{1,9},{3,11}... | collective-permute-start | bytes 98312 | tf_op jit(solution)/shard_map/ppermute | solution.py:28
  87.7 4.3 %collective-permute-start.9 = (f32[128,128]{1,0:T(8,128)S(1)}, f32[128,128]{1,0:T(8,128)S(1)}, u32[]{:S(2)}, u32[]{:S(2)}) collective-permute-start(f32[128,128]{1,0:T(8,128)S(1)} %constant_dynamic-update-slice_fusion.9), channel_id=1, source_target_pairs={{0,4},{2,6},{4,0},{6,2},{8,12},{10,14},{12,8},{14,10},{1,5},{3,7},... | collective-permute-start | bytes 196616 | tf_op jit(solution)/shard_map/ppermute | solution.py:28
  92.0 5.0 %collective-permute-start.10 = (f32[256,128]{1,0:T(8,128)S(1)}, f32[256,128]{1,0:T(8,128)S(1)}, u32[]{:S(2)}, u32[]{:S(2)}) collective-permute-start(f32[256,128]{1,0:T(8,128)S(1)} %constant_dynamic-update-slice_fusion.7), channel_id=1, source_target_pairs={{0,2},{2,0},{4,6},{6,4},{8,10},{10,8},{12,14},{14,12},{1,3},{3,1},... | collective-permute-start | bytes 393224 | tf_op jit(solution)/shard_map/ppermute | solution.py:28
  97.0 1.6 %collective-permute-start.11 = (f32[512,128]{1,0:T(8,128)S(1)}, f32[512,128]{1,0:T(8,128)S(1)}, u32[]{:S(2)}, u32[]{:S(2)}) collective-permute-start(f32[512,128]{1,0:T(8,128)S(1)} %constant_dynamic-update-slice_fusion.5), channel_id=1, source_target_pairs={{0,1},{1,0},{2,3},{3,2},{4,5},{5,4},{6,7},{7,6},{8,9},{9,8},{10,11... | collective-permute-start | bytes 786440 | tf_op jit(solution)/shard_map/ppermute | solution.py:28

commit v4 on v3

--- a/solution.py
+++ b/solution.py
@@ -29,6 +29,19 @@
     whole = jnp.zeros((2 * rows,) + x.shape[1:], x.dtype)
     whole = lax.dynamic_update_slice_in_dim(whole, x, upper * rows, 0)
     return lax.dynamic_update_slice_in_dim(whole, got, (1 - upper) * rows, 0)
+
+
+def exchange_sum(x, axes):
+    for axis in axes:
+        count = lax.axis_size(axis)
+        if count & (count - 1):
+            x = lax.psum(x, axis)
+            continue
+        bit = 1
+        while bit < count:
+            x = x + lax.ppermute(x, axis, [(i, i ^ bit) for i in range(count)])
+            bit *= 2
+    return x
 
 
 def packed_sum(values, axes):
@@ -248,9 +261,8 @@
             (tuple(split(v) for v in place), rows_split(depth_flat), rows_split(grad_u)),
         )
         grad_pw, grad_dw = jnp.sum(outs[0], axis=0), jnp.sum(outs[1], axis=0)
-    grad_dw, grad_pw, grad_head, loss_sum = packed_sum(
-        (grad_dw, grad_pw, grad_head, loss_sum), ("lat", "lon")
-    )
+    grad_pw, grad_head, loss_sum = packed_sum((grad_pw, grad_head, loss_sum), ("lat", "lon"))
+    grad_dw = exchange_sum(grad_dw, ("lat", "lon"))
     return (grad_dw, grad_pw, grad_head, (loss_sum / teach_width).reshape(1))
 
 

time: 104 us -> 112 us (1.077)
  starting transfers between devices: 26.9 us -> 32.9 us
  waiting for transfers between devices: 27.6 us -> 29.3 us
    ppermute x0 -> x4, waiting for transfers between devices: none -> 7.39 us  [exchange_sum(): x = x + lax.ppermute(x, axis, [(i, i ^ bit) for i in range(count)])]
    ppermute x0 -> x4, starting transfers between devices: none -> 6.21 us  [exchange_sum(): x = x + lax.ppermute(x, axis, [(i, i ^ bit) for i in range(count)])]
    ppermute x4, waiting for transfers between devices: 10.7 us -> 6.1 us  [halve(): return keep + lax.ppermute(send, axis, [(i, i ^ bit) for i in range(count)])]
  transfers between devices with their start and end apart: 13 -> 17, of which waited for: 11 -> 12; matrix products, arithmetic and copies ran while one was open for 5% -> 12% of each run, Pallas kernels for 0% -> 0%
where the time goes in v4:
time: 112 us; the launch traced here: 111 us
  starting transfers between devices  32.9 us (29%)
  waiting for transfers between devices  29.3 us (26%)
  other arithmetic  22.2 us (20%)
  local copies, waits for them, and re-layouts  17.5 us (16%)
  matrix products  6.11 us (5%)
  between operations  3.11 us (3%)
    ppermute x4, waiting for transfers between devices, double(): got = lax.ppermute(x, axis, [(i, i ^ bit) for i in range(count)])  8.54 us
    ppermute x4, waiting for transfers between devices, exchange_sum(): x = x + lax.ppermute(x, axis, [(i, i ^ bit) for i in range(count)])  7.39 us
    all_to_all x1, starting transfers between devices, local(): lax.all_to_all(send.reshape(slots, TILE, teach_width + 1), ('lon', 'lat')...  7.36 us
    ppermute x4, starting transfers between devices, halve(): return keep + lax.ppermute(send, axis, [(i, i ^ bit) for i in range(count)])  6.36 us
    ppermute x4, starting transfers between devices, exchange_sum(): x = x + lax.ppermute(x, axis, [(i, i ^ bit) for i in range(count)])  6.21 us
    ppermute x4, waiting for transfers between devices, halve(): return keep + lax.ppermute(send, axis, [(i, i ^ bit) for i in range(count)])  6.1 us
    ppermute x2, waiting for transfers between devices, padded_2(): lax.ppermute(tail, axis, [(i, (i + 1) % count) for i in range(ends)])  5.84 us
    gather x1, local copies, waits for them, and re-layouts, gather_windows(): lax.dynamic_slice(padded, (b, h, w, jnp.int32(0)), (1, span, reach, width))  5.74 us
  transfers between devices with their start and end apart: 17, of which 12 were waited for; matrix products, arithmetic and copies ran while one was open for 12% of the time, Pallas kernels for 0%

profile of v4, /device:TPU:0, one launch (start us, length us, event | category | flops | bytes accessed | tf_op | source)
XLA Modules:
  0.0 111.2 jit_solution(18196360812503907481)
XLA Ops:
  6.7 7.4 %all-to-all-start = ((bf16[32,8,228]{2,1,0:T(8,128)(2,1)}), bf16[32,8,228]{2,1,0:T(8,128)(2,1)S(1)}, u32[]{:S(2)}, u32[]{:S(2)}) async-start(bf16[32,8,228]{2,1,0:T(8,128)(2,1)} %reshape.824), calls=%async_computation | async-start | bytes 262144 | tf_op jit(solution)/shard_map/all_to_all | solution.py:126
  15.5 2.0 %collective-permute-start = (bf16[2,48,4,256]{3,0,2,1:T(2,128)(2,1)S(1)}, bf16[2,48,4,256]{3,0,2,1:T(2,128)(2,1)S(1)}, u32[]{:S(2)}, u32[]{:S(2)}) collective-permute-start(bf16[2,48,4,256]{3,0,2,1:T(2,128)(2,1)S(1)} %copy.519), channel_id=1, source_target_pairs={{0,2},{2,4},{4,6},{6,8},{8,10},{10,12},{12,14},{14,0},{1,3},{3,5},... | collective-permute-start | bytes 589832 | tf_op jit(solution)/shard_map/ppermute | solution.py:86
  17.7 2.9 %collective-permute-start.1 = (bf16[2,48,4,256]{3,0,2,1:T(2,128)(2,1)S(1)}, bf16[2,48,4,256]{3,0,2,1:T(2,128)(2,1)S(1)}, u32[]{:S(2)}, u32[]{:S(2)}) collective-permute-start(bf16[2,48,4,256]{3,0,2,1:T(2,128)(2,1)S(1)} %copy.520), channel_id=1, source_target_pairs={{2,0},{4,2},{6,4},{8,6},{10,8},{12,10},{14,12},{0,14},{3,1},{5,3},... | collective-permute-start | bytes 589832 | tf_op jit(solution)/shard_map/ppermute | solution.py:88
  20.8 5.8 %collective-permute-done = bf16[2,48,4,256]{3,0,2,1:T(2,128)(2,1)S(1)} collective-permute-done((bf16[2,48,4,256]{3,0,2,1:T(2,128)(2,1)S(1)}, bf16[2,48,4,256]{3,0,2,1:T(2,128)(2,1)S(1)}, u32[]{:S(2)}, u32[]{:S(2)}) %collective-permute-start) | collective-permute-done | bytes 196640 | tf_op jit(solution)/shard_map/ppermute | solution.py:86
  35.3 4.8 %pad_maximum_fusion = bf16[2,56,40,256]{3,0,2,1:T(2,128)(2,1)S(1)} fusion(bf16[2,4,40,256]{3,0,2,1:T(2,128)(2,1)S(1)} %collective-permute-done.3, bf16[2,48,40,256]{3,0,2,1:T(2,128)(2,1)} %copy-done.2, bf16[2,4,40,256]{3,0,2,1:T(2,128)(2,1)S(1)} %collective-permute-done.2), kind=kLoop, calls=%fused_computation.1 | loop fusion | flops 2293760 | bytes 4587520 | tf_op jit(solution)/shard_map/concatenate | solution.py:84
  40.1 5.7 %gather_fusion = bf16[32,9,16,256]{3,0,2,1:T(8,128)(2,1)} fusion(bf16[2,56,40,256]{3,0,2,1:T(2,128)(2,1)S(1)} %pad_maximum_fusion, s32[32]{0:T(128)S(1)} %fusion.91), kind=kCustom, calls=%fused_computation | custom fusion | bytes 4719104 | tf_op jit(solution)/shard_map/vmap()/gather | solution.py:159
  45.9 2.5 %slice_convert_fusion.20 = (f32[32,1,8,256]{3,0,2,1:T(8,128)S(1)}, f32[32,1,8,256]{3,0,2,1:T(8,128)S(1)}, f32[32,1,8,256]{3,0,2,1:T(8,128)S(1)}, f32[32,1,8,256]...) fusion(bf16[32,9,16,256]{3,0,2,1:T(8,128)(2,1)} %gather_fusion), kind=kLoop, calls=%fused_computation.178 | loop fusion | flops 1245184 | bytes 7471104 | tf_op jit(solution)/shard_map/convert_element_type | solution.py:165
  50.5 3.9 %fusion.39 = bf16[256,256]{1,0:T(8,128)(2,1)S(1)} fusion(f32[32,1,8,256]{3,2,0,1:T(8,128)S(1)} %copy.397, f32[32,1,8,256]{3,2,0,1:T(8,128)S(1)} %copy.396, f32[32,1,8,256]{3,2,0,1:T(8,128)S(1)} %copy.395, f32[32,1,8,256]{3,2,0,1:T(8,128)S(1)} %copy.394, f32[32,1,8,256]{3,2,0,1:T(8,128)S(1)} %copy.393, f32[32,1,8,256]{3,2,0,1:T(8,128)S(1)} %copy.392, ...), kind=kLoop, calls=%fused_computation.84 | loop fusion | flops 4325376 | bytes 8815616 | tf_op jit(solution)/shard_map/convert_element_type | solution.py:181
  59.0 3.8 %fusion.8 = (f32[256]{0:T(256)S(1)}, f32[256]{0:T(256)S(1)}, f32[256]{0:T(256)S(1)}, f32[256]{0:T(256)S(1)}, f32[256]{0:T(256)S(1)}, /*index=5*/f32[256]{0:T(256...) fusion(f32[32,1,8,256]{3,0,2,1:T(8,128)S(1)} %get-tuple-element, ...), kind=kOutput, calls=%fused_computation.23 | convolution fusion | flops 35909120 | bytes 5261312 | tf_op jit(solution)/shard_map/dot_general | solution.py:199
  62.9 2.1 %collective-permute-start.9 = (f32[256,128]{1,0:T(8,128)S(1)}, f32[256,128]{1,0:T(8,128)S(1)}, u32[]{:S(2)}, u32[]{:S(2)}) collective-permute-start(f32[256,128]{1,0:T(8,128)S(1)} %constant_dynamic-slice_fusion.2), channel_id=1, source_target_pairs={{0,2},{2,0},{4,6},{6,4},{8,10},{10,8},{12,14},{14,12},{1,3},{3,1},... | collective-permute-start | bytes 393224 | tf_op jit(solution)/shard_map/ppermute | solution.py:21
  65.4 3.5 %collective-permute-done.9 = f32[256,128]{1,0:T(8,128)S(1)} collective-permute-done((f32[256,128]{1,0:T(8,128)S(1)}, f32[256,128]{1,0:T(8,128)S(1)}, u32[]{:S(2)}, u32[]{:S(2)}) %collective-permute-start.9) | collective-permute-done | bytes 131104 | tf_op jit(solution)/shard_map/ppermute | solution.py:21
  70.4 2.8 %fusion.25 = (f32[256]{0:T(256)S(1)}, f32[256]{0:T(256)S(1)}, f32[256]{0:T(256)S(1)}, f32[256]{0:T(256)S(1)}, f32[256]{0:T(256)S(1)}, /*index=5*/f32[256]{0:T(25...) fusion(f32[256,256]{1,0:T(8,128)S(1)} %get-tuple-element.216, ...), kind=kLoop, calls=%fused_computation.57 | loop fusion | flops 1962240 | bytes 4209664 | tf_op jit(solution)/shard_map/reduce_sum | solution.py:212
  73.3 2.2 %collective-permute-start.11 = (f32[64,128]{1,0:T(8,128)S(1)}, f32[64,128]{1,0:T(8,128)S(1)}, u32[]{:S(2)}, u32[]{:S(2)}) collective-permute-start(f32[64,128]{1,0:T(8,128)S(1)} %constant_dynamic-slice_fusion), channel_id=1, source_target_pairs={{0,8},{2,10},{4,12},{6,14},{8,0},{10,2},{12,4},{14,6},{1,9},{3,11}... | collective-permute-start | bytes 98312 | tf_op jit(solution)/shard_map/ppermute | solution.py:21
  75.6 2.6 %collective-permute-done.11 = f32[64,128]{1,0:T(8,128)S(1)} collective-permute-done((f32[64,128]{1,0:T(8,128)S(1)}, f32[64,128]{1,0:T(8,128)S(1)}, u32[]{:S(2)}, u32[]{:S(2)}) %collective-permute-start.11) | collective-permute-done | bytes 32800 | tf_op jit(solution)/shard_map/ppermute | solution.py:21
  78.2 2.3 %collective-permute-start.12 = (f32[64,128]{1,0:T(8,128)S(1)}, f32[64,128]{1,0:T(8,128)S(1)}, u32[]{:S(2)}, u32[]{:S(2)}) collective-permute-start(f32[64,128]{1,0:T(8,128)S(1)} %get-tuple-element.98), channel_id=1, source_target_pairs={{0,8},{2,10},{4,12},{6,14},{8,0},{10,2},{12,4},{14,6},{1,9},{3,11}... | collective-permute-start | bytes 98312 | tf_op jit(solution)/shard_map/ppermute | solution.py:28
  80.5 2.6 %collective-permute-done.12 = f32[64,128]{1,0:T(8,128)S(1)} collective-permute-done((f32[64,128]{1,0:T(8,128)S(1)}, f32[64,128]{1,0:T(8,128)S(1)}, u32[]{:S(2)}, u32[]{:S(2)}) %collective-permute-start.12) | collective-permute-done | bytes 32800 | tf_op jit(solution)/shard_map/ppermute | solution.py:28
  84.5 2.8 %collective-permute-done.13 = f32[128,128]{1,0:T(8,128)S(1)} collective-permute-done((f32[128,128]{1,0:T(8,128)S(1)}, f32[128,128]{1,0:T(8,128)S(1)}, u32[]{:S(2)}, u32[]{:S(2)}) %collective-permute-start.13) | collective-permute-done | bytes 65568 | tf_op jit(solution)/shard_map/ppermute | solution.py:28
  87.4 1.8 %collective-permute-start.14 = (f32[256,128]{1,0:T(8,128)S(1)}, f32[256,128]{1,0:T(8,128)S(1)}, u32[]{:S(2)}, u32[]{:S(2)}) collective-permute-start(f32[256,128]{1,0:T(8,128)S(1)} %constant_dynamic-update-slice_fusion.7), channel_id=1, source_target_pairs={{0,2},{2,0},{4,6},{6,4},{8,10},{10,8},{12,14},{14,12},{1,3},{3,1},... | collective-permute-start | bytes 393224 | tf_op jit(solution)/shard_map/ppermute | solution.py:28
  89.2 3.2 %collective-permute-done.14 = f32[256,128]{1,0:T(8,128)S(1)} collective-permute-done((f32[256,128]{1,0:T(8,128)S(1)}, f32[256,128]{1,0:T(8,128)S(1)}, u32[]{:S(2)}, u32[]{:S(2)}) %collective-permute-start.14) | collective-permute-done | bytes 131104 | tf_op jit(solution)/shard_map/ppermute | solution.py:28
  94.1 1.7 %collective-permute-start.5 = (f32[9,256]{1,0:T(8,128)S(1)}, f32[9,256]{1,0:T(8,128)S(1)}, u32[]{:S(2)}, u32[]{:S(2)}) collective-permute-start(f32[9,256]{1,0:T(8,128)S(1)} %add.511), channel_id=1, source_target_pairs={{0,2},{2,0},{4,6},{6,4},{8,10},{10,8},{12,14},{14,12},{1,3},{3,1},... | collective-permute-start | bytes 27656 | tf_op jit(solution)/shard_map/ppermute | solution.py:42
  95.8 2.0 %collective-permute-done.5 = f32[9,256]{1,0:T(8,128)S(1)} collective-permute-done((f32[9,256]{1,0:T(8,128)S(1)}, f32[9,256]{1,0:T(8,128)S(1)}, u32[]{:S(2)}, u32[]{:S(2)}) %collective-permute-start.5) | collective-permute-done | bytes 9248 | tf_op jit(solution)/shard_map/ppermute | solution.py:42
  99.2 2.3 %collective-permute-done.6 = f32[9,256]{1,0:T(8,128)S(1)} collective-permute-done((f32[9,256]{1,0:T(8,128)S(1)}, f32[9,256]{1,0:T(8,128)S(1)}, u32[]{:S(2)}, u32[]{:S(2)}) %collective-permute-start.6) | collective-permute-done | bytes 9248 | tf_op jit(solution)/shard_map/ppermute | solution.py:42
  101.5 2.5 %collective-permute-start.7 = (f32[9,256]{1,0:T(8,128)S(1)}, f32[9,256]{1,0:T(8,128)S(1)}, u32[]{:S(2)}, u32[]{:S(2)}) collective-permute-start(f32[9,256]{1,0:T(8,128)S(1)} %add.513), channel_id=1, source_target_pairs={{0,8},{2,10},{4,12},{6,14},{8,0},{10,2},{12,4},{14,6},{1,9},{3,11}... | collective-permute-start | bytes 27656 | tf_op jit(solution)/shard_map/ppermute | solution.py:42
  104.1 2.1 %collective-permute-done.7 = f32[9,256]{1,0:T(8,128)S(1)} collective-permute-done((f32[9,256]{1,0:T(8,128)S(1)}, f32[9,256]{1,0:T(8,128)S(1)}, u32[]{:S(2)}, u32[]{:S(2)}) %collective-permute-start.7) | collective-permute-done | bytes 9248 | tf_op jit(solution)/shard_map/ppermute | solution.py:42
  (126 shorter events, 32.7 us)
Async XLA Ops:
  0.6 53.7 %copy-start = (bf16[256,256]{1,0:T(8,128)(2,1)S(1)}, bf16[256,256]{1,0:T(8,128)(2,1)}, u32[]{:S(2)}) copy-start(bf16[256,256]{1,0:T(8,128)(2,1)} %param.18) | copy-start | bytes 393220
  0.6 26.2 %copy-start.3 = (bf16[2,48,32,256]{3,2,1,0:T(8,128)(2,1)S(1)}, bf16[2,48,32,256]{3,2,1,0:T(8,128)(2,1)}, u32[]{:S(2)}) copy-start(bf16[2,48,32,256]{3,2,1,0:T(8,128)(2,1)} %param.15) | copy-start | bytes 4718596
  0.7 19.9 %copy-start.5 = (bf16[9,256]{1,0:T(8,128)(2,1)S(1)}, bf16[9,256]{1,0:T(8,128)(2,1)}, u32[]{:S(2)}) copy-start(bf16[9,256]{1,0:T(8,128)(2,1)} %param.17) | copy-start | bytes 13828
  0.7 19.9 %copy-start.6 = (s32[256]{0:T(256)S(1)}, s32[256]{0:T(256)}, u32[]{:S(2)}) copy-start(s32[256]{0:T(256)} %param.16) | copy-start | bytes 3076
  6.7 26.7 %all-to-all-start = ((bf16[32,8,228]{2,1,0:T(8,128)(2,1)}), bf16[32,8,228]{2,1,0:T(8,128)(2,1)S(1)}, u32[]{:S(2)}, u32[]{:S(2)}) async-start(bf16[32,8,228]{2,1,0:T(8,128)(2,1)} %reshape.824), calls=%async_computation | async-start | bytes 262144 | tf_op jit(solution)/shard_map/all_to_all | solution.py:126
  15.5 11.2 %collective-permute-start = (bf16[2,48,4,256]{3,0,2,1:T(2,128)(2,1)S(1)}, bf16[2,48,4,256]{3,0,2,1:T(2,128)(2,1)S(1)}, u32[]{:S(2)}, u32[]{:S(2)}) collective-permute-start(bf16[2,48,4,256]{3,0,2,1:T(2,128)(2,1)S(1)} %copy.519), channel_id=1, source_target_pairs={{0,2},{2,4},{4,6},{6,8},{8,10},{10,12},{12,14},{14,0},{1,3},{3,5},... | collective-permute-start | bytes 589832 | tf_op jit(solution)/shard_map/ppermute | solution.py:86
  17.7 11.4 %collective-permute-start.1 = (bf16[2,48,4,256]{3,0,2,1:T(2,128)(2,1)S(1)}, bf16[2,48,4,256]{3,0,2,1:T(2,128)(2,1)S(1)}, u32[]{:S(2)}, u32[]{:S(2)}) collective-permute-start(bf16[2,48,4,256]{3,0,2,1:T(2,128)(2,1)S(1)} %copy.520), channel_id=1, source_target_pairs={{2,0},{4,2},{6,4},{8,6},{10,8},{12,10},{14,12},{0,14},{3,1},{5,3},... | collective-permute-start | bytes 589832 | tf_op jit(solution)/shard_map/ppermute | solution.py:88
  29.2 1.3 %copy-start.2 = (bf16[2,48,40,256]{3,0,2,1:T(2,128)(2,1)}, bf16[2,48,40,256]{3,0,2,1:T(2,128)(2,1)S(1)}, u32[]{:S(2)}) copy-start(bf16[2,48,40,256]{3,0,2,1:T(2,128)(2,1)S(1)} %constant_dynamic-update-slice_fusion) | copy-start | bytes 5898244
  30.7 3.7 %collective-permute-start.2 = (bf16[2,4,40,256]{3,0,2,1:T(2,128)(2,1)S(1)}, bf16[2,4,40,256]{3,0,2,1:T(2,128)(2,1)S(1)}, u32[]{:S(2)}, u32[]{:S(2)}) collective-permute-start(bf16[2,4,40,256]{3,0,2,1:T(2,128)(2,1)S(1)} %get-tuple-element.168), channel_id=1, source_target_pairs={{0,1},{2,3},{4,5},{6,7},{8,9},{10,11},{12,13},{14,15},{16,17},{18,... | collective-permute-start | bytes 491528 | tf_op jit(solution)/shard_map/ppermute | solution.py:86
  32.0 3.3 %collective-permute-start.3 = (bf16[2,4,40,256]{3,0,2,1:T(2,128)(2,1)S(1)}, bf16[2,4,40,256]{3,0,2,1:T(2,128)(2,1)S(1)}, u32[]{:S(2)}, u32[]{:S(2)}) collective-permute-start(bf16[2,4,40,256]{3,0,2,1:T(2,128)(2,1)S(1)} %get-tuple-element.169), channel_id=1, source_target_pairs={{1,0},{3,2},{5,4},{7,6},{9,8},{11,10},{13,12},{15,14},{17,16},{19,... | collective-permute-start | bytes 491528 | tf_op jit(solution)/shard_map/ppermute | solution.py:88
  45.9 2.5 %copy-start.1 = (bf16[32,9,16,256]{3,0,2,1:T(8,128)(2,1)S(1)}, bf16[32,9,16,256]{3,0,2,1:T(8,128)(2,1)}, u32[]{:S(2)}) copy-start(bf16[32,9,16,256]{3,0,2,1:T(8,128)(2,1)} %gather_fusion) | copy-start | bytes 7077892
  50.5 4.2 %copy-start.4 = (bf16[256,227]{0,1:T(8,128)(2,1)S(1)}, bf16[256,227]{0,1:T(8,128)(2,1)}, u32[]{:S(2)}) copy-start(bf16[256,227]{0,1:T(8,128)(2,1)} %param.19) | copy-start | bytes 348676
  57.8 5.0 %collective-permute-start.8 = (f32[512,128]{1,0:T(8,128)S(1)}, f32[512,128]{1,0:T(8,128)S(1)}, u32[]{:S(2)}, u32[]{:S(2)}) collective-permute-start(f32[512,128]{1,0:T(8,128)S(1)} %constant_dynamic-slice_fusion.3), channel_id=1, source_target_pairs={{0,1},{1,0},{2,3},{3,2},{4,5},{5,4},{6,7},{7,6},{8,9},{9,8},{10,11... | collective-permute-start | bytes 786440 | tf_op jit(solution)/shard_map/ppermute | solution.py:21
  62.9 6.0 %collective-permute-start.9 = (f32[256,128]{1,0:T(8,128)S(1)}, f32[256,128]{1,0:T(8,128)S(1)}, u32[]{:S(2)}, u32[]{:S(2)}) collective-permute-start(f32[256,128]{1,0:T(8,128)S(1)} %constant_dynamic-slice_fusion.2), channel_id=1, source_target_pairs={{0,2},{2,0},{4,6},{6,4},{8,10},{10,8},{12,14},{14,12},{1,3},{3,1},... | collective-permute-start | bytes 393224 | tf_op jit(solution)/shard_map/ppermute | solution.py:21
  68.9 4.3 %collective-permute-start.10 = (f32[128,128]{1,0:T(8,128)S(1)}, f32[128,128]{1,0:T(8,128)S(1)}, u32[]{:S(2)}, u32[]{:S(2)}) collective-permute-start(f32[128,128]{1,0:T(8,128)S(1)} %constant_dynamic-slice_fusion.1), channel_id=1, source_target_pairs={{0,4},{2,6},{4,0},{6,2},{8,12},{10,14},{12,8},{14,10},{1,5},{3,7},... | collective-permute-start | bytes 196616 | tf_op jit(solution)/shard_map/ppermute | solution.py:21
  73.3 4.9 %collective-permute-start.11 = (f32[64,128]{1,0:T(8,128)S(1)}, f32[64,128]{1,0:T(8,128)S(1)}, u32[]{:S(2)}, u32[]{:S(2)}) collective-permute-start(f32[64,128]{1,0:T(8,128)S(1)} %constant_dynamic-slice_fusion), channel_id=1, source_target_pairs={{0,8},{2,10},{4,12},{6,14},{8,0},{10,2},{12,4},{14,6},{1,9},{3,11}... | collective-permute-start | bytes 98312 | tf_op jit(solution)/shard_map/ppermute | solution.py:21
  78.2 4.9 %collective-permute-start.12 = (f32[64,128]{1,0:T(8,128)S(1)}, f32[64,128]{1,0:T(8,128)S(1)}, u32[]{:S(2)}, u32[]{:S(2)}) collective-permute-start(f32[64,128]{1,0:T(8,128)S(1)} %get-tuple-element.98), channel_id=1, source_target_pairs={{0,8},{2,10},{4,12},{6,14},{8,0},{10,2},{12,4},{14,6},{1,9},{3,11}... | collective-permute-start | bytes 98312 | tf_op jit(solution)/shard_map/ppermute | solution.py:28
  83.1 4.3 %collective-permute-start.13 = (f32[128,128]{1,0:T(8,128)S(1)}, f32[128,128]{1,0:T(8,128)S(1)}, u32[]{:S(2)}, u32[]{:S(2)}) collective-permute-start(f32[128,128]{1,0:T(8,128)S(1)} %constant_dynamic-update-slice_fusion.9), channel_id=1, source_target_pairs={{0,4},{2,6},{4,0},{6,2},{8,12},{10,14},{12,8},{14,10},{1,5},{3,7},... | collective-permute-start | bytes 196616 | tf_op jit(solution)/shard_map/ppermute | solution.py:28
  87.4 5.0 %collective-permute-start.14 = (f32[256,128]{1,0:T(8,128)S(1)}, f32[256,128]{1,0:T(8,128)S(1)}, u32[]{:S(2)}, u32[]{:S(2)}) collective-permute-start(f32[256,128]{1,0:T(8,128)S(1)} %constant_dynamic-update-slice_fusion.7), channel_id=1, source_target_pairs={{0,2},{2,0},{4,6},{6,4},{8,10},{10,8},{12,14},{14,12},{1,3},{3,1},... | collective-permute-start | bytes 393224 | tf_op jit(solution)/shard_map/ppermute | solution.py:28
  92.4 14.4 %collective-permute-start.15 = (f32[512,128]{1,0:T(8,128)S(1)}, f32[512,128]{1,0:T(8,128)S(1)}, u32[]{:S(2)}, u32[]{:S(2)}) collective-permute-start(f32[512,128]{1,0:T(8,128)S(1)} %constant_dynamic-update-slice_fusion.5), channel_id=1, source_target_pairs={{0,1},{1,0},{2,3},{3,2},{4,5},{5,4},{6,7},{7,6},{8,9},{9,8},{10,11... | collective-permute-start | bytes 786440 | tf_op jit(solution)/shard_map/ppermute | solution.py:28
  92.6 1.5 %collective-permute-start.4 = (f32[9,256]{1,0:T(8,128)S(1)}, f32[9,256]{1,0:T(8,128)S(1)}, u32[]{:S(2)}, u32[]{:S(2)}) collective-permute-start(f32[9,256]{1,0:T(8,128)S(1)} %stack.5), channel_id=1, source_target_pairs={{0,1},{1,0},{2,3},{3,2},{4,5},{5,4},{6,7},{7,6},{8,9},{9,8},{10,11... | collective-permute-start | bytes 27656 | tf_op jit(solution)/shard_map/ppermute | solution.py:42
  94.1 3.7 %collective-permute-start.5 = (f32[9,256]{1,0:T(8,128)S(1)}, f32[9,256]{1,0:T(8,128)S(1)}, u32[]{:S(2)}, u32[]{:S(2)}) collective-permute-start(f32[9,256]{1,0:T(8,128)S(1)} %add.511), channel_id=1, source_target_pairs={{0,2},{2,0},{4,6},{6,4},{8,10},{10,8},{12,14},{14,12},{1,3},{3,1},... | collective-permute-start | bytes 27656 | tf_op jit(solution)/shard_map/ppermute | solution.py:42
  97.8 3.7 %collective-permute-start.6 = (f32[9,256]{1,0:T(8,128)S(1)}, f32[9,256]{1,0:T(8,128)S(1)}, u32[]{:S(2)}, u32[]{:S(2)}) collective-permute-start(f32[9,256]{1,0:T(8,128)S(1)} %add.512), channel_id=1, source_target_pairs={{0,4},{2,6},{4,0},{6,2},{8,12},{10,14},{12,8},{14,10},{1,5},{3,7},... | collective-permute-start | bytes 27656 | tf_op jit(solution)/shard_map/ppermute | solution.py:42
  101.5 4.6 %collective-permute-start.7 = (f32[9,256]{1,0:T(8,128)S(1)}, f32[9,256]{1,0:T(8,128)S(1)}, u32[]{:S(2)}, u32[]{:S(2)}) collective-permute-start(f32[9,256]{1,0:T(8,128)S(1)} %add.513), channel_id=1, source_target_pairs={{0,8},{2,10},{4,12},{6,14},{8,0},{10,2},{12,4},{14,6},{1,9},{3,11}... | collective-permute-start | bytes 27656 | tf_op jit(solution)/shard_map/ppermute | solution.py:42

commit v5 on v3

--- a/solution.py
+++ b/solution.py
@@ -31,7 +31,23 @@
     return lax.dynamic_update_slice_in_dim(whole, got, (1 - upper) * rows, 0)
 
 
-def packed_sum(values, axes):
+def as_rows(values, unit):
+    flat = jnp.concatenate([jnp.ravel(v).astype(jnp.float32) for v in values])
+    total = -(-flat.shape[0] // unit) * unit
+    return jnp.pad(flat, (0, total - flat.shape[0])).reshape(-1, LANES)
+
+
+def from_rows(x, values):
+    flat = x.reshape(-1)
+    out = []
+    offset = 0
+    for v in values:
+        out.append(flat[offset : offset + v.size].reshape(v.shape))
+        offset += v.size
+    return tuple(out)
+
+
+def packed_sum(values, axes, late):
     steps = []
     rest = []
     for axis in axes:
@@ -43,23 +59,24 @@
         while bit < count:
             steps.append((axis, bit))
             bit *= 2
-    flat = jnp.concatenate([jnp.ravel(v).astype(jnp.float32) for v in values])
-    unit = 8 * LANES * (2 ** len(steps))
-    total = -(-flat.shape[0] // unit) * unit
-    x = jnp.pad(flat, (0, total - flat.shape[0])).reshape(-1, LANES)
+    x = as_rows(values, 8 * LANES * (2 ** len(steps)))
     for axis, bit in steps:
         x = halve(x, axis, bit)
+    extra = as_rows((late,), 8 * LANES)
     if rest:
-        x = lax.psum(x, tuple(rest))
+        x, extra = lax.psum((x, extra), tuple(rest))
     for axis, bit in reversed(steps):
-        x = double(x, axis, bit)
-    flat = x.reshape(-1)
-    out = []
-    offset = 0
-    for v in values:
-        out.append(flat[offset : offset + v.size].reshape(v.shape))
-        offset += v.size
-    return tuple(out)
+        count = lax.axis_size(axis)
+        rows = x.shape[0]
+        upper = (lax.axis_index(axis) // bit) % 2
+        got = lax.ppermute(
+            jnp.concatenate([x, extra]), axis, [(i, i ^ bit) for i in range(count)]
+        )
+        extra = extra + got[rows:]
+        whole = jnp.zeros((2 * rows,) + x.shape[1:], x.dtype)
+        whole = lax.dynamic_update_slice_in_dim(whole, x, upper * rows, 0)
+        x = lax.dynamic_update_slice_in_dim(whole, got[:rows], (1 - upper) * rows, 0)
+    return from_rows(x, values), from_rows(extra, (late,))[0]
 
 
 def padded_2(cells, sides, width, closed):
@@ -248,8 +265,8 @@
             (tuple(split(v) for v in place), rows_split(depth_flat), rows_split(grad_u)),
         )
         grad_pw, grad_dw = jnp.sum(outs[0], axis=0), jnp.sum(outs[1], axis=0)
-    grad_dw, grad_pw, grad_head, loss_sum = packed_sum(
-        (grad_dw, grad_pw, grad_head, loss_sum), ("lat", "lon")
+    (grad_pw, grad_head, loss_sum), grad_dw = packed_sum(
+        (grad_pw, grad_head, loss_sum), ("lat", "lon"), grad_dw
     )
     return (grad_dw, grad_pw, grad_head, (loss_sum / teach_width).reshape(1))
 

time: 104 us -> 111 us (1.067)
  other arithmetic: 21.5 us -> 25.2 us
  local copies, waits for them, and re-layouts: 18.1 us -> 20.7 us
  matrix products: 6.43 us -> 7.96 us
    convert_element_type x4, other arithmetic: 3.86 us -> 6.45 us  [shifted(): source[:, DMAX + row_shift, DMAX + col_shift:DMAX + col_shift + TILE, :]]
    reshape x5 -> x6, local copies, waits for them, and re-layouts: 2.1 us -> 3.74 us  [the longest x2 2 us: as_rows(): flat = jnp.concatenate([jnp.ravel(v).astype(jnp.float32) for v in values])]
    ppermute x4, waiting for transfers between devices: 10.7 us -> 9.3 us  [halve(): return keep + lax.ppermute(send, axis, [(i, i ^ bit) for i in range(count)])]
    unnamed x22 -> x52, local copies, waits for them, and re-layouts: 4.62 us -> 5.61 us
  transfers between devices with their start and end apart: 13 -> 13, of which waited for: 11 -> 10; matrix products, arithmetic and copies ran while one was open for 5% -> 12% of each run, Pallas kernels for 0% -> 0%
where the time goes in v5:
time: 111 us
  starting transfers between devices  26.9 us (24%)
  waiting for transfers between devices  26.8 us (24%)
  other arithmetic  25.2 us (23%)
  local copies, waits for them, and re-layouts  20.7 us (19%)
  matrix products  7.96 us (7%)
  between operations  3.31 us (3%)
    ppermute x4, waiting for transfers between devices, packed_sum(): lax.ppermute(jnp.concatenate([x, extra]), axis, [(i, i ^ bit) for i in ra...  10.3 us
    ppermute x4, waiting for transfers between devices, halve(): return keep + lax.ppermute(send, axis, [(i, i ^ bit) for i in range(count)])  9.3 us
    all_to_all x1, starting transfers between devices, local(): lax.all_to_all(send.reshape(slots, TILE, teach_width + 1), ('lon', 'lat')...  7.36 us
    convert_element_type x4, other arithmetic, shifted(): source[:, DMAX + row_shift, DMAX + col_shift:DMAX + col_shift + TILE, :]  6.45 us
    ppermute x4, starting transfers between devices, halve(): return keep + lax.ppermute(send, axis, [(i, i ^ bit) for i in range(count)])  6.17 us
    ppermute x4, starting transfers between devices, packed_sum(): lax.ppermute(jnp.concatenate([x, extra]), axis, [(i, i ^ bit) for i in ra...  5.95 us
    ppermute x2, waiting for transfers between devices, padded_2(): lax.ppermute(tail, axis, [(i, (i + 1) % count) for i in range(ends)])  5.84 us
    gather x1, local copies, waits for them, and re-layouts, gather_windows(): lax.dynamic_slice(padded, (b, h, w, jnp.int32(0)), (1, span, reach, width))  5.74 us
  transfers between devices with their start and end apart: 13, of which 10 were waited for; matrix products, arithmetic and copies ran while one was open for 12% of the time, Pallas kernels for 0%

profile of v5, /device:TPU:0, one launch (start us, length us, event | category | flops | bytes accessed | tf_op | source)
XLA Modules:
  0.0 110.9 jit_solution(17655293664966810717)
XLA Ops:
  6.7 7.4 %all-to-all-start = ((bf16[32,8,228]{2,1,0:T(8,128)(2,1)}), bf16[32,8,228]{2,1,0:T(8,128)(2,1)S(1)}, u32[]{:S(2)}, u32[]{:S(2)}) async-start(bf16[32,8,228]{2,1,0:T(8,128)(2,1)} %reshape.836), calls=%async_computation | async-start | bytes 262144 | tf_op jit(solution)/shard_map/all_to_all | solution.py:130
  15.5 2.0 %collective-permute-start = (bf16[2,48,4,256]{3,0,2,1:T(2,128)(2,1)S(1)}, bf16[2,48,4,256]{3,0,2,1:T(2,128)(2,1)S(1)}, u32[]{:S(2)}, u32[]{:S(2)}) collective-permute-start(bf16[2,48,4,256]{3,0,2,1:T(2,128)(2,1)S(1)} %copy.519), channel_id=1, source_target_pairs={{0,2},{2,4},{4,6},{6,8},{8,10},{10,12},{12,14},{14,0},{1,3},{3,5},... | collective-permute-start | bytes 589832 | tf_op jit(solution)/shard_map/ppermute | solution.py:90
  17.7 2.9 %collective-permute-start.1 = (bf16[2,48,4,256]{3,0,2,1:T(2,128)(2,1)S(1)}, bf16[2,48,4,256]{3,0,2,1:T(2,128)(2,1)S(1)}, u32[]{:S(2)}, u32[]{:S(2)}) collective-permute-start(bf16[2,48,4,256]{3,0,2,1:T(2,128)(2,1)S(1)} %copy.520), channel_id=1, source_target_pairs={{2,0},{4,2},{6,4},{8,6},{10,8},{12,10},{14,12},{0,14},{3,1},{5,3},... | collective-permute-start | bytes 589832 | tf_op jit(solution)/shard_map/ppermute | solution.py:92
  20.8 5.8 %collective-permute-done = bf16[2,48,4,256]{3,0,2,1:T(2,128)(2,1)S(1)} collective-permute-done((bf16[2,48,4,256]{3,0,2,1:T(2,128)(2,1)S(1)}, bf16[2,48,4,256]{3,0,2,1:T(2,128)(2,1)S(1)}, u32[]{:S(2)}, u32[]{:S(2)}) %collective-permute-start) | collective-permute-done | bytes 196640 | tf_op jit(solution)/shard_map/ppermute | solution.py:90
  35.3 4.8 %pad_maximum_fusion = bf16[2,56,40,256]{3,0,2,1:T(2,128)(2,1)S(1)} fusion(bf16[2,4,40,256]{3,0,2,1:T(2,128)(2,1)S(1)} %collective-permute-done.3, bf16[2,48,40,256]{3,0,2,1:T(2,128)(2,1)} %copy-done.2, bf16[2,4,40,256]{3,0,2,1:T(2,128)(2,1)S(1)} %collective-permute-done.2), kind=kLoop, calls=%fused_computation.1 | loop fusion | flops 2293760 | bytes 4587520 | tf_op jit(solution)/shard_map/concatenate | solution.py:88
  40.1 5.7 %gather_fusion = bf16[32,9,16,256]{3,0,2,1:T(8,128)(2,1)} fusion(bf16[2,56,40,256]{3,0,2,1:T(2,128)(2,1)S(1)} %pad_maximum_fusion, s32[32]{0:T(128)S(1)} %fusion.91), kind=kCustom, calls=%fused_computation | custom fusion | bytes 4719104 | tf_op jit(solution)/shard_map/vmap()/gather | solution.py:163
  45.9 2.5 %slice_convert_fusion.20 = (f32[32,1,8,256]{3,0,2,1:T(8,128)S(1)}, f32[32,1,8,256]{3,0,2,1:T(8,128)S(1)}, f32[32,1,8,256]{3,0,2,1:T(8,128)S(1)}, f32[32,1,8,256]...) fusion(bf16[32,9,16,256]{3,0,2,1:T(8,128)(2,1)} %gather_fusion), kind=kLoop, calls=%fused_computation.182 | loop fusion | flops 1245184 | bytes 7471104 | tf_op jit(solution)/shard_map/convert_element_type | solution.py:169
  50.5 3.9 %fusion.39 = bf16[256,256]{1,0:T(8,128)(2,1)S(1)} fusion(f32[32,1,8,256]{3,2,0,1:T(8,128)S(1)} %copy.397, f32[32,1,8,256]{3,2,0,1:T(8,128)S(1)} %copy.396, f32[32,1,8,256]{3,2,0,1:T(8,128)S(1)} %copy.395, f32[32,1,8,256]{3,2,0,1:T(8,128)S(1)} %copy.394, f32[32,1,8,256]{3,2,0,1:T(8,128)S(1)} %copy.393, f32[32,1,8,256]{3,2,0,1:T(8,128)S(1)} %copy.392, ...), kind=kLoop, calls=%fused_computation.86 | loop fusion | flops 4325376 | bytes 8815616 | tf_op jit(solution)/shard_map/convert_element_type | solution.py:185
  58.7 1.9 %slice_convert_fusion.65 = (f32[32,1,8,256]{3,0,2,1:T(8,128)}, f32[32,1,8,256]{3,0,2,1:T(8,128)}, f32[32,1,8,256]{3,0,2,1:T(8,128)}, f32[32,1,8,256]{3,0,2,1:T(8...) fusion(bf16[32,9,16,256]{3,0,2,1:T(8,128)(2,1)S(1)} %copy-done.1), kind=kLoop, calls=%fused_computation.228 | loop fusion | flops 917504 | bytes 5505024 | tf_op jit(solution)/shard_map/convert_element_type | solution.py:169
  61.9 2.0 %reshape.840 = f32[58112]{0:T(1024)} reshape(f32[256,227]{1,0:T(8,128)} %fusion.77) | data formatting | bytes 464896 | tf_op jit(solution)/shard_map/reshape | solution.py:35
  63.9 1.8 %fusion.3 = f32[1024,128]{1,0:T(8,128)S(1)} fusion(f32[1]{0:T(128)} %bitcast.142, f32[58112]{0:T(1024)} %reshape.840, f32[65536]{0:T(1024)} %bitcast.448), kind=kLoop, calls=%fused_computation.10 | loop fusion | flops 786432 | bytes 1018884 | tf_op jit(solution)/shard_map/reshape | solution.py:37
  66.1 4.9 %fusion.8 = (f32[256]{0:T(256)S(1)}, f32[256]{0:T(256)S(1)}, f32[256]{0:T(256)S(1)}, f32[256]{0:T(256)S(1)}, f32[256]{0:T(256)S(1)}, /*index=5*/f32[256]{0:T(256...) fusion(f32[32,1,8,256]{3,0,2,1:T(8,128)S(1)} %get-tuple-element, ...), kind=kOutput, calls=%fused_computation.25 | convolution fusion | flops 35909120 | bytes 5261312 | tf_op jit(solution)/shard_map/dot_general | solution.py:203
  71.2 2.9 %fusion.25 = (f32[256]{0:T(256)S(1)}, f32[256]{0:T(256)S(1)}, f32[256]{0:T(256)S(1)}, f32[256]{0:T(256)S(1)}, f32[256]{0:T(256)S(1)}, /*index=5*/f32[256]{0:T(25...) fusion(f32[256,256]{1,0:T(8,128)S(1)} %get-tuple-element.216, ...), kind=kLoop, calls=%fused_computation.59 | loop fusion | flops 1962240 | bytes 4209664 | tf_op jit(solution)/shard_map/reduce_sum | solution.py:216
  74.2 2.1 %collective-permute-start.5 = (f32[256,128]{1,0:T(8,128)S(1)}, f32[256,128]{1,0:T(8,128)S(1)}, u32[]{:S(2)}, u32[]{:S(2)}) collective-permute-start(f32[256,128]{1,0:T(8,128)S(1)} %constant_dynamic-slice_fusion.2), channel_id=1, source_target_pairs={{0,2},{2,0},{4,6},{6,4},{8,10},{10,8},{12,14},{14,12},{1,3},{3,1},... | collective-permute-start | bytes 393224 | tf_op jit(solution)/shard_map/ppermute | solution.py:21
  76.3 3.9 %collective-permute-done.5 = f32[256,128]{1,0:T(8,128)S(1)} collective-permute-done((f32[256,128]{1,0:T(8,128)S(1)}, f32[256,128]{1,0:T(8,128)S(1)}, u32[]{:S(2)}, u32[]{:S(2)}) %collective-permute-start.5) | collective-permute-done | bytes 131104 | tf_op jit(solution)/shard_map/ppermute | solution.py:21
  81.8 2.8 %collective-permute-done.6 = f32[128,128]{1,0:T(8,128)S(1)} collective-permute-done((f32[128,128]{1,0:T(8,128)S(1)}, f32[128,128]{1,0:T(8,128)S(1)}, u32[]{:S(2)}, u32[]{:S(2)}) %collective-permute-start.6) | collective-permute-done | bytes 65568 | tf_op jit(solution)/shard_map/ppermute | solution.py:21
  84.6 2.3 %collective-permute-start.7 = (f32[64,128]{1,0:T(8,128)S(1)}, f32[64,128]{1,0:T(8,128)S(1)}, u32[]{:S(2)}, u32[]{:S(2)}) collective-permute-start(f32[64,128]{1,0:T(8,128)S(1)} %constant_dynamic-slice_fusion), channel_id=1, source_target_pairs={{0,8},{2,10},{4,12},{6,14},{8,0},{10,2},{12,4},{14,6},{1,9},{3,11}... | collective-permute-start | bytes 98312 | tf_op jit(solution)/shard_map/ppermute | solution.py:21
  86.8 2.6 %collective-permute-done.7 = f32[64,128]{1,0:T(8,128)S(1)} collective-permute-done((f32[64,128]{1,0:T(8,128)S(1)}, f32[64,128]{1,0:T(8,128)S(1)}, u32[]{:S(2)}, u32[]{:S(2)}) %collective-permute-start.7) | collective-permute-done | bytes 32800 | tf_op jit(solution)/shard_map/ppermute | solution.py:21
  89.5 2.3 %collective-permute-start.8 = (f32[88,128]{1,0:T(8,128)S(1)}, f32[88,128]{1,0:T(8,128)S(1)}, u32[]{:S(2)}, u32[]{:S(2)}) collective-permute-start(f32[88,128]{1,0:T(8,128)S(1)} %pad_maximum_fusion.5), channel_id=1, source_target_pairs={{0,8},{2,10},{4,12},{6,14},{8,0},{10,2},{12,4},{14,6},{1,9},{3,11}... | collective-permute-start | bytes 135176 | tf_op jit(solution)/shard_map/ppermute | solution.py:72
  91.8 2.8 %collective-permute-done.8 = f32[88,128]{1,0:T(8,128)S(1)} collective-permute-done((f32[88,128]{1,0:T(8,128)S(1)}, f32[88,128]{1,0:T(8,128)S(1)}, u32[]{:S(2)}, u32[]{:S(2)}) %collective-permute-start.8) | collective-permute-done | bytes 45088 | tf_op jit(solution)/shard_map/ppermute | solution.py:72
  94.6 1.7 %collective-permute-start.9 = (f32[152,128]{1,0:T(8,128)S(1)}, f32[152,128]{1,0:T(8,128)S(1)}, u32[]{:S(2)}, u32[]{:S(2)}) collective-permute-start(f32[152,128]{1,0:T(8,128)S(1)} %pad_maximum_fusion.3), channel_id=1, source_target_pairs={{0,4},{2,6},{4,0},{6,2},{8,12},{10,14},{12,8},{14,10},{1,5},{3,7},... | collective-permute-start | bytes 233480 | tf_op jit(solution)/shard_map/ppermute | solution.py:72
  96.4 2.7 %collective-permute-done.9 = f32[152,128]{1,0:T(8,128)S(1)} collective-permute-done((f32[152,128]{1,0:T(8,128)S(1)}, f32[152,128]{1,0:T(8,128)S(1)}, u32[]{:S(2)}, u32[]{:S(2)}) %collective-permute-start.9) | collective-permute-done | bytes 77856 | tf_op jit(solution)/shard_map/ppermute | solution.py:72
  99.1 1.8 %collective-permute-start.10 = (f32[280,128]{1,0:T(8,128)S(1)}, f32[280,128]{1,0:T(8,128)S(1)}, u32[]{:S(2)}, u32[]{:S(2)}) collective-permute-start(f32[280,128]{1,0:T(8,128)S(1)} %pad_maximum_fusion.2), channel_id=1, source_target_pairs={{0,2},{2,0},{4,6},{6,4},{8,10},{10,8},{12,14},{14,12},{1,3},{3,1},... | collective-permute-start | bytes 430088 | tf_op jit(solution)/shard_map/ppermute | solution.py:72
  101.0 3.3 %collective-permute-done.10 = f32[280,128]{1,0:T(8,128)S(1)} collective-permute-done((f32[280,128]{1,0:T(8,128)S(1)}, f32[280,128]{1,0:T(8,128)S(1)}, u32[]{:S(2)}, u32[]{:S(2)}) %collective-permute-start.10) | collective-permute-done | bytes 143392 | tf_op jit(solution)/shard_map/ppermute | solution.py:72
  (156 shorter events, 31.0 us)
Async XLA Ops:
  0.6 53.7 %copy-start = (bf16[256,256]{1,0:T(8,128)(2,1)S(1)}, bf16[256,256]{1,0:T(8,128)(2,1)}, u32[]{:S(2)}) copy-start(bf16[256,256]{1,0:T(8,128)(2,1)} %param.18) | copy-start | bytes 393220
  0.6 26.2 %copy-start.3 = (bf16[2,48,32,256]{3,2,1,0:T(8,128)(2,1)S(1)}, bf16[2,48,32,256]{3,2,1,0:T(8,128)(2,1)}, u32[]{:S(2)}) copy-start(bf16[2,48,32,256]{3,2,1,0:T(8,128)(2,1)} %param.15) | copy-start | bytes 4718596
  0.7 19.9 %copy-start.20 = (bf16[9,256]{1,0:T(8,128)(2,1)S(1)}, bf16[9,256]{1,0:T(8,128)(2,1)}, u32[]{:S(2)}) copy-start(bf16[9,256]{1,0:T(8,128)(2,1)} %param.17) | copy-start | bytes 13828
  0.7 19.9 %copy-start.21 = (s32[256]{0:T(256)S(1)}, s32[256]{0:T(256)}, u32[]{:S(2)}) copy-start(s32[256]{0:T(256)} %param.16) | copy-start | bytes 3076
  6.7 26.7 %all-to-all-start = ((bf16[32,8,228]{2,1,0:T(8,128)(2,1)}), bf16[32,8,228]{2,1,0:T(8,128)(2,1)S(1)}, u32[]{:S(2)}, u32[]{:S(2)}) async-start(bf16[32,8,228]{2,1,0:T(8,128)(2,1)} %reshape.836), calls=%async_computation | async-start | bytes 262144 | tf_op jit(solution)/shard_map/all_to_all | solution.py:130
  15.5 11.2 %collective-permute-start = (bf16[2,48,4,256]{3,0,2,1:T(2,128)(2,1)S(1)}, bf16[2,48,4,256]{3,0,2,1:T(2,128)(2,1)S(1)}, u32[]{:S(2)}, u32[]{:S(2)}) collective-permute-start(bf16[2,48,4,256]{3,0,2,1:T(2,128)(2,1)S(1)} %copy.519), channel_id=1, source_target_pairs={{0,2},{2,4},{4,6},{6,8},{8,10},{10,12},{12,14},{14,0},{1,3},{3,5},... | collective-permute-start | bytes 589832 | tf_op jit(solution)/shard_map/ppermute | solution.py:90
  17.7 11.4 %collective-permute-start.1 = (bf16[2,48,4,256]{3,0,2,1:T(2,128)(2,1)S(1)}, bf16[2,48,4,256]{3,0,2,1:T(2,128)(2,1)S(1)}, u32[]{:S(2)}, u32[]{:S(2)}) collective-permute-start(bf16[2,48,4,256]{3,0,2,1:T(2,128)(2,1)S(1)} %copy.520), channel_id=1, source_target_pairs={{2,0},{4,2},{6,4},{8,6},{10,8},{12,10},{14,12},{0,14},{3,1},{5,3},... | collective-permute-start | bytes 589832 | tf_op jit(solution)/shard_map/ppermute | solution.py:92
  30.7 3.7 %collective-permute-start.2 = (bf16[2,4,40,256]{3,0,2,1:T(2,128)(2,1)S(1)}, bf16[2,4,40,256]{3,0,2,1:T(2,128)(2,1)S(1)}, u32[]{:S(2)}, u32[]{:S(2)}) collective-permute-start(bf16[2,4,40,256]{3,0,2,1:T(2,128)(2,1)S(1)} %get-tuple-element.168), channel_id=1, source_target_pairs={{0,1},{2,3},{4,5},{6,7},{8,9},{10,11},{12,13},{14,15},{16,17},{18,... | collective-permute-start | bytes 491528 | tf_op jit(solution)/shard_map/ppermute | solution.py:90
  32.0 3.3 %collective-permute-start.3 = (bf16[2,4,40,256]{3,0,2,1:T(2,128)(2,1)S(1)}, bf16[2,4,40,256]{3,0,2,1:T(2,128)(2,1)S(1)}, u32[]{:S(2)}, u32[]{:S(2)}) collective-permute-start(bf16[2,4,40,256]{3,0,2,1:T(2,128)(2,1)S(1)} %get-tuple-element.169), channel_id=1, source_target_pairs={{1,0},{3,2},{5,4},{7,6},{9,8},{11,10},{13,12},{15,14},{17,16},{19,... | collective-permute-start | bytes 491528 | tf_op jit(solution)/shard_map/ppermute | solution.py:92
  65.7 8.4 %collective-permute-start.4 = (f32[512,128]{1,0:T(8,128)S(1)}, f32[512,128]{1,0:T(8,128)S(1)}, u32[]{:S(2)}, u32[]{:S(2)}) collective-permute-start(f32[512,128]{1,0:T(8,128)S(1)} %constant_dynamic-slice_fusion.3), channel_id=1, source_target_pairs={{0,1},{1,0},{2,3},{3,2},{4,5},{5,4},{6,7},{7,6},{8,9},{9,8},{10,11... | collective-permute-start | bytes 786440 | tf_op jit(solution)/shard_map/ppermute | solution.py:21
  66.0 5.1 %copy-start.8 = (f32[32,1,8,256]{3,0,2,1:T(8,128)S(1)}, f32[32,1,8,256]{3,0,2,1:T(8,128)}, u32[]{:S(2)}) copy-start(f32[32,1,8,256]{3,0,2,1:T(8,128)} %get-tuple-element.125) | copy-start | bytes 786436
  66.0 5.1 %copy-start.9 = (f32[32,1,8,256]{3,0,2,1:T(8,128)S(1)}, f32[32,1,8,256]{3,0,2,1:T(8,128)}, u32[]{:S(2)}) copy-start(f32[32,1,8,256]{3,0,2,1:T(8,128)} %get-tuple-element.126) | copy-start | bytes 786436
  66.0 5.1 %copy-start.10 = (f32[32,1,8,256]{3,0,2,1:T(8,128)S(1)}, f32[32,1,8,256]{3,0,2,1:T(8,128)}, u32[]{:S(2)}) copy-start(f32[32,1,8,256]{3,0,2,1:T(8,128)} %get-tuple-element.127) | copy-start | bytes 786436
  66.0 5.1 %copy-start.11 = (f32[32,1,8,256]{3,0,2,1:T(8,128)S(1)}, f32[32,1,8,256]{3,0,2,1:T(8,128)}, u32[]{:S(2)}) copy-start(f32[32,1,8,256]{3,0,2,1:T(8,128)} %get-tuple-element.128) | copy-start | bytes 786436
  66.1 5.1 %copy-start.12 = (f32[32,1,8,256]{3,0,2,1:T(8,128)S(1)}, f32[32,1,8,256]{3,0,2,1:T(8,128)}, u32[]{:S(2)}) copy-start(f32[32,1,8,256]{3,0,2,1:T(8,128)} %get-tuple-element.129) | copy-start | bytes 786436
  66.1 5.1 %copy-start.13 = (f32[32,1,8,256]{3,0,2,1:T(8,128)S(1)}, f32[32,1,8,256]{3,0,2,1:T(8,128)}, u32[]{:S(2)}) copy-start(f32[32,1,8,256]{3,0,2,1:T(8,128)} %get-tuple-element.130) | copy-start | bytes 786436
  66.1 5.1 %copy-start.14 = (f32[32,1,8,256]{3,0,2,1:T(8,128)S(1)}, f32[32,1,8,256]{3,0,2,1:T(8,128)}, u32[]{:S(2)}) copy-start(f32[32,1,8,256]{3,0,2,1:T(8,128)} %get-tuple-element.131) | copy-start | bytes 786436
  74.2 6.0 %collective-permute-start.5 = (f32[256,128]{1,0:T(8,128)S(1)}, f32[256,128]{1,0:T(8,128)S(1)}, u32[]{:S(2)}, u32[]{:S(2)}) collective-permute-start(f32[256,128]{1,0:T(8,128)S(1)} %constant_dynamic-slice_fusion.2), channel_id=1, source_target_pairs={{0,2},{2,0},{4,6},{6,4},{8,10},{10,8},{12,14},{14,12},{1,3},{3,1},... | collective-permute-start | bytes 393224 | tf_op jit(solution)/shard_map/ppermute | solution.py:21
  80.2 4.3 %collective-permute-start.6 = (f32[128,128]{1,0:T(8,128)S(1)}, f32[128,128]{1,0:T(8,128)S(1)}, u32[]{:S(2)}, u32[]{:S(2)}) collective-permute-start(f32[128,128]{1,0:T(8,128)S(1)} %constant_dynamic-slice_fusion.1), channel_id=1, source_target_pairs={{0,4},{2,6},{4,0},{6,2},{8,12},{10,14},{12,8},{14,10},{1,5},{3,7},... | collective-permute-start | bytes 196616 | tf_op jit(solution)/shard_map/ppermute | solution.py:21
  84.6 4.9 %collective-permute-start.7 = (f32[64,128]{1,0:T(8,128)S(1)}, f32[64,128]{1,0:T(8,128)S(1)}, u32[]{:S(2)}, u32[]{:S(2)}) collective-permute-start(f32[64,128]{1,0:T(8,128)S(1)} %constant_dynamic-slice_fusion), channel_id=1, source_target_pairs={{0,8},{2,10},{4,12},{6,14},{8,0},{10,2},{12,4},{14,6},{1,9},{3,11}... | collective-permute-start | bytes 98312 | tf_op jit(solution)/shard_map/ppermute | solution.py:21
  89.5 5.1 %collective-permute-start.8 = (f32[88,128]{1,0:T(8,128)S(1)}, f32[88,128]{1,0:T(8,128)S(1)}, u32[]{:S(2)}, u32[]{:S(2)}) collective-permute-start(f32[88,128]{1,0:T(8,128)S(1)} %pad_maximum_fusion.5), channel_id=1, source_target_pairs={{0,8},{2,10},{4,12},{6,14},{8,0},{10,2},{12,4},{14,6},{1,9},{3,11}... | collective-permute-start | bytes 135176 | tf_op jit(solution)/shard_map/ppermute | solution.py:72
  94.6 4.5 %collective-permute-start.9 = (f32[152,128]{1,0:T(8,128)S(1)}, f32[152,128]{1,0:T(8,128)S(1)}, u32[]{:S(2)}, u32[]{:S(2)}) collective-permute-start(f32[152,128]{1,0:T(8,128)S(1)} %pad_maximum_fusion.3), channel_id=1, source_target_pairs={{0,4},{2,6},{4,0},{6,2},{8,12},{10,14},{12,8},{14,10},{1,5},{3,7},... | collective-permute-start | bytes 233480 | tf_op jit(solution)/shard_map/ppermute | solution.py:72
  99.1 5.2 %collective-permute-start.10 = (f32[280,128]{1,0:T(8,128)S(1)}, f32[280,128]{1,0:T(8,128)S(1)}, u32[]{:S(2)}, u32[]{:S(2)}) collective-permute-start(f32[280,128]{1,0:T(8,128)S(1)} %pad_maximum_fusion.2), channel_id=1, source_target_pairs={{0,2},{2,0},{4,6},{6,4},{8,10},{10,8},{12,14},{14,12},{1,3},{3,1},... | collective-permute-start | bytes 430088 | tf_op jit(solution)/shard_map/ppermute | solution.py:72
  104.4 1.6 %collective-permute-start.11 = (f32[536,128]{1,0:T(8,128)S(1)}, f32[536,128]{1,0:T(8,128)S(1)}, u32[]{:S(2)}, u32[]{:S(2)}) collective-permute-start(f32[536,128]{1,0:T(8,128)S(1)} %pad_maximum_fusion.1), channel_id=1, source_target_pairs={{0,1},{1,0},{2,3},{3,2},{4,5},{5,4},{6,7},{7,6},{8,9},{9,8},{10,11... | collective-permute-start | bytes 823304 | tf_op jit(solution)/shard_map/ppermute | solution.py:72
  (11 other events, 47.0 us)

commit v6 on v3

--- a/solution.py
+++ b/solution.py
@@ -62,6 +62,42 @@
     return tuple(out)
 
 
+def halo_padded(cells, width):
+    lon_count = lax.axis_size("lon")
+    lat_count = lax.axis_size("lat")
+    both = ("lon", "lat")
+
+    def flat(lon, lat):
+        return lon * lat_count + lat
+
+    def send(piece, lon_step, lat_step):
+        pairs = []
+        for lon in range(lon_count):
+            for lat in range(lat_count):
+                to_lat = lat + lat_step
+                if 0 <= to_lat < lat_count:
+                    pairs.append((flat(lon, lat), flat((lon + lon_step) % lon_count, to_lat)))
+        return lax.ppermute(piece, both, pairs)
+
+    rows, cols = cells.shape[1], cells.shape[2]
+    top = lambda v: v[:, :width]
+    bottom = lambda v: v[:, rows - width :]
+    left = lambda v: v[:, :, :width]
+    right = lambda v: v[:, :, cols - width :]
+    west = send(right(cells), 1, 0)
+    east = send(left(cells), -1, 0)
+    north = send(bottom(cells), 0, 1)
+    south = send(top(cells), 0, -1)
+    north_west = send(right(bottom(cells)), 1, 1)
+    north_east = send(left(bottom(cells)), -1, 1)
+    south_west = send(right(top(cells)), 1, -1)
+    south_east = send(left(top(cells)), -1, -1)
+    upper = jnp.concatenate([north_west, north, north_east], axis=2)
+    middle = jnp.concatenate([west, cells, east], axis=2)
+    lower = jnp.concatenate([south_west, south, south_east], axis=2)
+    return jnp.concatenate([upper, middle, lower], axis=1)
+
+
 def padded_2(cells, sides, width, closed):
     for axis, dim in sides:
         count = lax.axis_size(axis)
@@ -88,8 +124,7 @@
     lat_count = lax.axis_size("lat")
     lon_count = lax.axis_size("lon")
     devices = lon_count * lat_count
-    lon_padded = padded_2(acts, (("lon", 2),), DMAX, True)
-    padded = padded_2(lon_padded, (("lat", 1),), DMAX, False)
+    padded = halo_padded(acts, DMAX)
     tiles_here = teacher_tiles.shape[0]
     destination = tile_dest[:, 0]
     positions = jnp.arange(tiles_here, dtype=jnp.int32)

time: 104 us -> 144 us (1.38)
  other arithmetic: 21.5 us -> 46.1 us
  local copies, waits for them, and re-layouts: 18.1 us -> 29 us
  starting transfers between devices: 26.9 us -> 30.2 us
  waiting for transfers between devices: 27.6 us -> 29.1 us
    concatenate x1, other arithmetic: 4.77 us -> 21.9 us  [halo_padded(): return jnp.concatenate([upper, middle, lower], axis=1)]
    ppermute x4 -> x8, starting transfers between devices: 7.42 us -> 19 us  [send(): return lax.ppermute(piece, both, pairs)]
    convert_element_type x10, local copies, waits for them, and re-layouts: 1.57 us -> 8.64 us  [shifted(): source[:, DMAX + row_shift, DMAX + col_shift:DMAX + col_shift + TILE, :]]
    ppermute x4 -> x8, waiting for transfers between devices: 7.36 us -> 0.75 us  [send(): return lax.ppermute(piece, both, pairs)]
    ppermute x4, waiting for transfers between devices: 9.6 us -> 14 us  [double(): got = lax.ppermute(x, axis, [(i, i ^ bit) for i in range(count)])]
    ppermute x4, starting transfers between devices: 6.01 us -> 1.97 us  [double(): got = lax.ppermute(x, axis, [(i, i ^ bit) for i in range(count)])]
    ppermute x4, waiting for transfers between devices: 10.7 us -> 14.4 us  [halve(): return keep + lax.ppermute(send, axis, [(i, i ^ bit) for i in range(count)])]
    ppermute x4, starting transfers between devices: 6.15 us -> 2.59 us  [halve(): return keep + lax.ppermute(send, axis, [(i, i ^ bit) for i in range(count)])]
  transfers between devices with their start and end apart: 13 -> 17, of which waited for: 11 -> 9; matrix products, arithmetic and copies ran while one was open for 5% -> 19% of each run, Pallas kernels for 0% -> 0%
where the time goes in v6:
time: 144 us
  other arithmetic  46.1 us (32%)
  starting transfers between devices  30.2 us (21%)
  waiting for transfers between devices  29.1 us (20%)
  local copies, waits for them, and re-layouts  29 us (20%)
  matrix products  6.1 us (4%)
  between operations  3.12 us (2%)
    concatenate x1, other arithmetic, halo_padded(): return jnp.concatenate([upper, middle, lower], axis=1)  21.9 us
    ppermute x8, starting transfers between devices, send(): return lax.ppermute(piece, both, pairs)  19 us
    ppermute x4, waiting for transfers between devices, halve(): return keep + lax.ppermute(send, axis, [(i, i ^ bit) for i in range(count)])  14.4 us
    ppermute x4, waiting for transfers between devices, double(): got = lax.ppermute(x, axis, [(i, i ^ bit) for i in range(count)])  14 us
    convert_element_type x10, local copies, waits for them, and re-layouts, shifted(): source[:, DMAX + row_shift, DMAX + col_shift:DMAX + col_shift + TILE, :]  8.64 us
    convert_element_type x1, other arithmetic, forward(): depth_flat = accum_sum.astype(jnp.bfloat16).reshape(-1, width)  7.16 us
    all_to_all x1, starting transfers between devices, local(): lax.all_to_all(send.reshape(slots, TILE, teach_width + 1), ('lon', 'lat')...  6.69 us
    convert_element_type x4, other arithmetic, shifted(): source[:, DMAX + row_shift, DMAX + col_shift:DMAX + col_shift + TILE, :]  6.42 us
  transfers between devices with their start and end apart: 17, of which 9 were waited for; matrix products, arithmetic and copies ran while one was open for 19% of the time, Pallas kernels for 0%

profile of v6, /device:TPU:0, one launch (start us, length us, event | category | flops | bytes accessed | tf_op | source)
XLA Modules:
  0.0 143.6 jit_solution(1214898495417210753)
XLA Ops:
  0.7 3.1 %copy.413 = bf16[2,48,32,256]{3,0,2,1:T(2,128)(2,1)S(1)} copy(bf16[2,48,32,256]{3,2,1,0:T(8,128)(2,1)} %param.15) | data formatting | bytes 3145728 | tf_op args[0]
  3.9 4.3 %collective-permute-start = (bf16[2,4,4,256]{3,0,2,1:T(2,128)(2,1)S(1)}, bf16[2,4,4,256]{3,0,2,1:T(2,128)(2,1)S(1)}, u32[]{:S(2)}, u32[]{:S(2)}) collective-permute-start(bf16[2,4,4,256]{3,0,2,1:T(2,128)(2,1)S(1)} %get-tuple-element.168), channel_id=1, source_target_pairs={{0,3},{2,5},{4,7},{6,9},{8,11},{10,13},{12,15},{14,1},{16,19},{18,... | collective-permute-start | bytes 49160 | tf_op jit(solution)/shard_map/ppermute | solution.py:80
  8.2 4.3 %collective-permute-start.2 = (bf16[2,4,4,256]{3,0,2,1:T(2,128)(2,1)S(1)}, bf16[2,4,4,256]{3,0,2,1:T(2,128)(2,1)S(1)}, u32[]{:S(2)}, u32[]{:S(2)}) collective-permute-start(bf16[2,4,4,256]{3,0,2,1:T(2,128)(2,1)S(1)} %get-tuple-element.171), channel_id=1, source_target_pairs={{0,15},{2,1},{4,3},{6,5},{8,7},{10,9},{12,11},{14,13},{16,31},{18,... | collective-permute-start | bytes 49160 | tf_op jit(solution)/shard_map/ppermute | solution.py:80
  17.2 6.7 %all-to-all-start = ((bf16[32,8,228]{2,1,0:T(8,128)(2,1)}), bf16[32,8,228]{2,1,0:T(8,128)(2,1)S(1)}, u32[]{:S(2)}, u32[]{:S(2)}) async-start(bf16[32,8,228]{2,1,0:T(8,128)(2,1)} %reshape.832), calls=%async_computation | async-start | bytes 262144 | tf_op jit(solution)/shard_map/all_to_all | solution.py:148
  26.1 4.7 %collective-permute-start.4 = (bf16[2,48,4,256]{3,0,2,1:T(2,128)(2,1)S(1)}, bf16[2,48,4,256]{3,0,2,1:T(2,128)(2,1)S(1)}, u32[]{:S(2)}, u32[]{:S(2)}) collective-permute-start(bf16[2,48,4,256]{3,0,2,1:T(2,128)(2,1)S(1)} %get-tuple-element.175), channel_id=1, source_target_pairs={{0,14},{1,15},{2,0},{3,1},{4,2},{5,3},{6,4},{7,5},{8,6},{9,7},{10,... | collective-permute-start | bytes 589832 | tf_op jit(solution)/shard_map/ppermute | solution.py:80
  30.8 1.8 %collective-permute-start.1 = (bf16[2,4,32,256]{3,0,2,1:T(2,128)(2,1)S(1)}, bf16[2,4,32,256]{3,0,2,1:T(2,128)(2,1)S(1)}, u32[]{:S(2)}, u32[]{:S(2)}) collective-permute-start(bf16[2,4,32,256]{3,0,2,1:T(2,128)(2,1)S(1)} %get-tuple-element.172), channel_id=1, source_target_pairs={{0,1},{2,3},{4,5},{6,7},{8,9},{10,11},{12,13},{14,15},{16,17},{18,... | collective-permute-start | bytes 393224 | tf_op jit(solution)/shard_map/ppermute | solution.py:80
  35.8 21.9 %maximum_maximum_fusion = bf16[2,56,40,256]{3,0,2,1:T(2,128)(2,1)S(1)} fusion(bf16[2,4,4,256]{3,0,2,1:T(2,128)(2,1)S(1)} %collective-permute-done.7, bf16[2,4,32,256]{3,0,2,1:T(2,128)(2,1)S(1)} %collective-permute-done.6, bf16[2,4,4,256]{3,0,2,1:T(2,128)(2,1)S(1)} %collective-permute-done.5, bf16[2,48,4,256]{3,0,2,1:T(2,128)(2,1)S(1)} %collective-permute-done.4, ...), kind=kLoop, calls=%fused_computation.1 | loop fusion | flops 9175040 | bytes 4587520 | tf_op jit(solution)/shard_map/concatenate | solution.py:98
  58.5 5.7 %gather_fusion = bf16[32,9,16,256]{3,0,2,1:T(8,128)(2,1)} fusion(bf16[2,56,40,256]{3,0,2,1:T(2,128)(2,1)S(1)} %maximum_maximum_fusion, s32[32]{0:T(128)S(1)} %fusion.91), kind=kCustom, calls=%fused_computation | custom fusion | bytes 4719104 | tf_op jit(solution)/shard_map/vmap()/gather | solution.py:181
  64.3 3.9 %slice_convert_fusion.20 = (f32[32,1,8,256]{3,0,2,1:T(8,128)S(1)}, f32[32,1,8,256]{3,0,2,1:T(8,128)S(1)}, f32[32,1,8,256]{3,0,2,1:T(8,128)S(1)}, f32[32,1,8,256]...) fusion(bf16[32,9,16,256]{3,0,2,1:T(8,128)(2,1)} %gather_fusion), kind=kLoop, calls=%fused_computation.179 | loop fusion | flops 1245184 | bytes 7471104 | tf_op jit(solution)/shard_map/convert_element_type | solution.py:187
  80.1 1.6 %fusion.74 = f32[256,227]{1,0:T(8,128)} fusion(bf16[32,8,228]{2,1,0:T(8,128)(2,1)} %copy-done.6), kind=kLoop, calls=%fused_computation.158 | loop fusion | flops 58112 | bytes 348672 | tf_op jit(solution)/shard_map/convert_element_type | solution.py:208
  81.7 1.8 %copy.457 = f32[256,227]{0,1:T(8,128)} copy(f32[256,227]{1,0:T(8,128)} %fusion.74) | data formatting | bytes 464896 | tf_op jit(solution)/shard_map/convert_element_type | solution.py:208
  84.3 1.3 iota_add_fusion
  86.6 7.2 %fusion.39 = bf16[256,256]{1,0:T(8,128)(2,1)S(1)} fusion(f32[32,1,8,256]{3,2,0,1:T(8,128)} %copy.433, f32[32,1,8,256]{3,2,0,1:T(8,128)} %copy.432, f32[32,1,8,256]{3,2,0,1:T(8,128)} %copy.431, f32[32,1,8,256]{3,2,0,1:T(8,128)} %copy.430, f32[32,1,8,256]{3,2,0,1:T(8,128)} %copy.429, f32[32,1,8,256]{3,2,0,1:T(8,128)} %copy.428, f32[32,1,8,256]{3,2,0,1:T(8,128)} %copy.427, ...), kind=kLoop, calls=%fused_computation.85 | loop fusion | flops 4325376 | bytes 8815616 | tf_op jit(solution)/shard_map/convert_element_type | solution.py:203
  97.3 3.8 %fusion.8 = (f32[256]{0:T(256)S(1)}, f32[256]{0:T(256)S(1)}, f32[256]{0:T(256)S(1)}, f32[256]{0:T(256)S(1)}, f32[256]{0:T(256)S(1)}, /*index=5*/f32[256]{0:T(256...) fusion(f32[32,1,8,256]{3,0,2,1:T(8,128)S(1)} %get-tuple-element, ...), kind=kOutput, calls=%fused_computation.24 | convolution fusion | flops 35909120 | bytes 5261312 | tf_op jit(solution)/shard_map/dot_general | solution.py:221
  101.1 2.9 %fusion.25 = (f32[256]{0:T(256)S(1)}, f32[256]{0:T(256)S(1)}, f32[256]{0:T(256)S(1)}, f32[256]{0:T(256)S(1)}, f32[256]{0:T(256)S(1)}, /*index=5*/f32[256]{0:T(25...) fusion(f32[256,256]{1,0:T(8,128)S(1)} %get-tuple-element.222, ...), kind=kLoop, calls=%fused_computation.58 | loop fusion | flops 1962240 | bytes 4209664 | tf_op jit(solution)/shard_map/reduce_sum | solution.py:234
  107.4 5.6 %collective-permute-done.9 = f32[256,128]{1,0:T(8,128)S(1)} collective-permute-done((f32[256,128]{1,0:T(8,128)S(1)}, f32[256,128]{1,0:T(8,128)S(1)}, u32[]{:S(2)}, u32[]{:S(2)}) %collective-permute-start.9) | collective-permute-done | bytes 131104 | tf_op jit(solution)/shard_map/ppermute | solution.py:21
  113.1 4.2 %collective-permute-done.10 = f32[128,128]{1,0:T(8,128)S(1)} collective-permute-done((f32[128,128]{1,0:T(8,128)S(1)}, f32[128,128]{1,0:T(8,128)S(1)}, u32[]{:S(2)}, u32[]{:S(2)}) %collective-permute-start.10) | collective-permute-done | bytes 65568 | tf_op jit(solution)/shard_map/ppermute | solution.py:21
  117.3 1.7 %collective-permute-start.11 = (f32[64,128]{1,0:T(8,128)S(1)}, f32[64,128]{1,0:T(8,128)S(1)}, u32[]{:S(2)}, u32[]{:S(2)}) collective-permute-start(f32[64,128]{1,0:T(8,128)S(1)} %constant_dynamic-slice_fusion), channel_id=1, source_target_pairs={{0,8},{2,10},{4,12},{6,14},{8,0},{10,2},{12,4},{14,6},{1,9},{3,11}... | collective-permute-start | bytes 98312 | tf_op jit(solution)/shard_map/ppermute | solution.py:21
  119.1 3.5 %collective-permute-done.11 = f32[64,128]{1,0:T(8,128)S(1)} collective-permute-done((f32[64,128]{1,0:T(8,128)S(1)}, f32[64,128]{1,0:T(8,128)S(1)}, u32[]{:S(2)}, u32[]{:S(2)}) %collective-permute-start.11) | collective-permute-done | bytes 32800 | tf_op jit(solution)/shard_map/ppermute | solution.py:21
  122.6 1.4 collective-permute-start.12
  124.0 3.8 %collective-permute-done.12 = f32[64,128]{1,0:T(8,128)S(1)} collective-permute-done((f32[64,128]{1,0:T(8,128)S(1)}, f32[64,128]{1,0:T(8,128)S(1)}, u32[]{:S(2)}, u32[]{:S(2)}) %collective-permute-start.12) | collective-permute-done | bytes 32800 | tf_op jit(solution)/shard_map/ppermute | solution.py:28
  128.1 4.0 %collective-permute-done.13 = f32[128,128]{1,0:T(8,128)S(1)} collective-permute-done((f32[128,128]{1,0:T(8,128)S(1)}, f32[128,128]{1,0:T(8,128)S(1)}, u32[]{:S(2)}, u32[]{:S(2)}) %collective-permute-start.13) | collective-permute-done | bytes 65568 | tf_op jit(solution)/shard_map/ppermute | solution.py:28
  132.3 4.8 %collective-permute-done.14 = f32[256,128]{1,0:T(8,128)S(1)} collective-permute-done((f32[256,128]{1,0:T(8,128)S(1)}, f32[256,128]{1,0:T(8,128)S(1)}, u32[]{:S(2)}, u32[]{:S(2)}) %collective-permute-start.14) | collective-permute-done | bytes 131104 | tf_op jit(solution)/shard_map/ppermute | solution.py:28
  137.2 1.4 %collective-permute-done.15 = f32[512,128]{1,0:T(8,128)S(1)} collective-permute-done((f32[512,128]{1,0:T(8,128)S(1)}, f32[512,128]{1,0:T(8,128)S(1)}, u32[]{:S(2)}, u32[]{:S(2)}) %collective-permute-start.15) | collective-permute-done | bytes 262176 | tf_op jit(solution)/shard_map/ppermute | solution.py:28
  (140 shorter events, 35.3 us)
Async XLA Ops:
  0.6 93.2 %copy-start = (bf16[256,256]{1,0:T(8,128)(2,1)S(1)}, bf16[256,256]{1,0:T(8,128)(2,1)}, u32[]{:S(2)}) copy-start(bf16[256,256]{1,0:T(8,128)(2,1)} %param.18) | copy-start | bytes 393220
  0.7 14.9 %copy-start.14 = (s32[16]{0:T(128)S(1)}, s32[16]{0:T(128)}, u32[]{:S(2)}) copy-start(s32[16]{0:T(128)} %param.23) | copy-start | bytes 196
  0.7 15.0 %copy-start.8 = (bf16[16,8,227]{2,1,0:T(8,128)(2,1)S(1)}, bf16[16,8,227]{2,1,0:T(8,128)(2,1)}, u32[]{:S(2)}) copy-start(bf16[16,8,227]{2,1,0:T(8,128)(2,1)} %param.20) | copy-start | bytes 174340
  0.7 15.2 %copy-start.15 = (s32[16,1]{0,1:T(1,128)S(1)}, s32[16,1]{0,1:T(1,128)}, u32[]{:S(2)}) copy-start(s32[16,1]{0,1:T(1,128)} %param.21) | copy-start | bytes 196
  0.7 23.4 %copy-start.9 = (bf16[9,256]{1,0:T(8,128)(2,1)S(1)}, bf16[9,256]{1,0:T(8,128)(2,1)}, u32[]{:S(2)}) copy-start(bf16[9,256]{1,0:T(8,128)(2,1)} %param.17) | copy-start | bytes 13828
  0.7 23.4 %copy-start.12 = (s32[256]{0:T(256)S(1)}, s32[256]{0:T(256)}, u32[]{:S(2)}) copy-start(s32[256]{0:T(256)} %param.16) | copy-start | bytes 3076
  3.8 32.0 %copy-start.2 = (bf16[2,48,32,256]{3,0,2,1:T(2,128)(2,1)}, bf16[2,48,32,256]{3,0,2,1:T(2,128)(2,1)S(1)}, u32[]{:S(2)}) copy-start(bf16[2,48,32,256]{3,0,2,1:T(2,128)(2,1)S(1)} %copy.413) | copy-start | bytes 4718596
  3.9 22.2 %collective-permute-start = (bf16[2,4,4,256]{3,0,2,1:T(2,128)(2,1)S(1)}, bf16[2,4,4,256]{3,0,2,1:T(2,128)(2,1)S(1)}, u32[]{:S(2)}, u32[]{:S(2)}) collective-permute-start(bf16[2,4,4,256]{3,0,2,1:T(2,128)(2,1)S(1)} %get-tuple-element.168), channel_id=1, source_target_pairs={{0,3},{2,5},{4,7},{6,9},{8,11},{10,13},{12,15},{14,1},{16,19},{18,... | collective-permute-start | bytes 49160 | tf_op jit(solution)/shard_map/ppermute | solution.py:80
  8.2 22.6 %collective-permute-start.2 = (bf16[2,4,4,256]{3,0,2,1:T(2,128)(2,1)S(1)}, bf16[2,4,4,256]{3,0,2,1:T(2,128)(2,1)S(1)}, u32[]{:S(2)}, u32[]{:S(2)}) collective-permute-start(bf16[2,4,4,256]{3,0,2,1:T(2,128)(2,1)S(1)} %get-tuple-element.171), channel_id=1, source_target_pairs={{0,15},{2,1},{4,3},{6,5},{8,7},{10,9},{12,11},{14,13},{16,31},{18,... | collective-permute-start | bytes 49160 | tf_op jit(solution)/shard_map/ppermute | solution.py:80
  12.5 20.0 %collective-permute-start.5 = (bf16[2,4,4,256]{3,0,2,1:T(2,128)(2,1)S(1)}, bf16[2,4,4,256]{3,0,2,1:T(2,128)(2,1)S(1)}, u32[]{:S(2)}, u32[]{:S(2)}) collective-permute-start(bf16[2,4,4,256]{3,0,2,1:T(2,128)(2,1)S(1)} %get-tuple-element.170), channel_id=1, source_target_pairs={{1,2},{3,4},{5,6},{7,8},{9,10},{11,12},{13,14},{15,0},{17,18},{19,... | collective-permute-start | bytes 49160 | tf_op jit(solution)/shard_map/ppermute | solution.py:80
  13.8 21.2 %collective-permute-start.7 = (bf16[2,4,4,256]{3,0,2,1:T(2,128)(2,1)S(1)}, bf16[2,4,4,256]{3,0,2,1:T(2,128)(2,1)S(1)}, u32[]{:S(2)}, u32[]{:S(2)}) collective-permute-start(bf16[2,4,4,256]{3,0,2,1:T(2,128)(2,1)S(1)} %get-tuple-element.169), channel_id=1, source_target_pairs={{1,14},{3,0},{5,2},{7,4},{9,6},{11,8},{13,10},{15,12},{17,30},{19,... | collective-permute-start | bytes 49160 | tf_op jit(solution)/shard_map/ppermute | solution.py:80
  15.4 20.4 %collective-permute-start.3 = (bf16[2,48,4,256]{3,0,2,1:T(2,128)(2,1)S(1)}, bf16[2,48,4,256]{3,0,2,1:T(2,128)(2,1)S(1)}, u32[]{:S(2)}, u32[]{:S(2)}) collective-permute-start(bf16[2,48,4,256]{3,0,2,1:T(2,128)(2,1)S(1)} %get-tuple-element.174), channel_id=1, source_target_pairs={{0,2},{1,3},{2,4},{3,5},{4,6},{5,7},{6,8},{7,9},{8,10},{9,11},{10,... | collective-permute-start | bytes 589832 | tf_op jit(solution)/shard_map/ppermute | solution.py:80
  17.2 40.5 %all-to-all-start = ((bf16[32,8,228]{2,1,0:T(8,128)(2,1)}), bf16[32,8,228]{2,1,0:T(8,128)(2,1)S(1)}, u32[]{:S(2)}, u32[]{:S(2)}) async-start(bf16[32,8,228]{2,1,0:T(8,128)(2,1)} %reshape.832), calls=%async_computation | async-start | bytes 262144 | tf_op jit(solution)/shard_map/all_to_all | solution.py:148
  26.1 9.7 %collective-permute-start.4 = (bf16[2,48,4,256]{3,0,2,1:T(2,128)(2,1)S(1)}, bf16[2,48,4,256]{3,0,2,1:T(2,128)(2,1)S(1)}, u32[]{:S(2)}, u32[]{:S(2)}) collective-permute-start(bf16[2,48,4,256]{3,0,2,1:T(2,128)(2,1)S(1)} %get-tuple-element.175), channel_id=1, source_target_pairs={{0,14},{1,15},{2,0},{3,1},{4,2},{5,3},{6,4},{7,5},{8,6},{9,7},{10,... | collective-permute-start | bytes 589832 | tf_op jit(solution)/shard_map/ppermute | solution.py:80
  30.8 4.3 %collective-permute-start.1 = (bf16[2,4,32,256]{3,0,2,1:T(2,128)(2,1)S(1)}, bf16[2,4,32,256]{3,0,2,1:T(2,128)(2,1)S(1)}, u32[]{:S(2)}, u32[]{:S(2)}) collective-permute-start(bf16[2,4,32,256]{3,0,2,1:T(2,128)(2,1)S(1)} %get-tuple-element.172), channel_id=1, source_target_pairs={{0,1},{2,3},{4,5},{6,7},{8,9},{10,11},{12,13},{14,15},{16,17},{18,... | collective-permute-start | bytes 393224 | tf_op jit(solution)/shard_map/ppermute | solution.py:80
  32.5 3.2 %collective-permute-start.6 = (bf16[2,4,32,256]{3,0,2,1:T(2,128)(2,1)S(1)}, bf16[2,4,32,256]{3,0,2,1:T(2,128)(2,1)S(1)}, u32[]{:S(2)}, u32[]{:S(2)}) collective-permute-start(bf16[2,4,32,256]{3,0,2,1:T(2,128)(2,1)S(1)} %get-tuple-element.173), channel_id=1, source_target_pairs={{1,0},{3,2},{5,4},{7,6},{9,8},{11,10},{13,12},{15,14},{17,16},{19,... | collective-permute-start | bytes 393224 | tf_op jit(solution)/shard_map/ppermute | solution.py:80
  105.4 1.7 %collective-permute-start.8 = (f32[512,128]{1,0:T(8,128)S(1)}, f32[512,128]{1,0:T(8,128)S(1)}, u32[]{:S(2)}, u32[]{:S(2)}) collective-permute-start(f32[512,128]{1,0:T(8,128)S(1)} %constant_dynamic-slice_fusion.3), channel_id=1, source_target_pairs={{0,1},{1,0},{2,3},{3,2},{4,5},{5,4},{6,7},{7,6},{8,9},{9,8},{10,11... | collective-permute-start | bytes 786440 | tf_op jit(solution)/shard_map/ppermute | solution.py:21
  107.1 5.8 %collective-permute-start.9 = (f32[256,128]{1,0:T(8,128)S(1)}, f32[256,128]{1,0:T(8,128)S(1)}, u32[]{:S(2)}, u32[]{:S(2)}) collective-permute-start(f32[256,128]{1,0:T(8,128)S(1)} %constant_dynamic-slice_fusion.2), channel_id=1, source_target_pairs={{0,2},{2,0},{4,6},{6,4},{8,10},{10,8},{12,14},{14,12},{1,3},{3,1},... | collective-permute-start | bytes 393224 | tf_op jit(solution)/shard_map/ppermute | solution.py:21
  112.9 4.3 %collective-permute-start.10 = (f32[128,128]{1,0:T(8,128)S(1)}, f32[128,128]{1,0:T(8,128)S(1)}, u32[]{:S(2)}, u32[]{:S(2)}) collective-permute-start(f32[128,128]{1,0:T(8,128)S(1)} %constant_dynamic-slice_fusion.1), channel_id=1, source_target_pairs={{0,4},{2,6},{4,0},{6,2},{8,12},{10,14},{12,8},{14,10},{1,5},{3,7},... | collective-permute-start | bytes 196616 | tf_op jit(solution)/shard_map/ppermute | solution.py:21
  117.3 5.2 %collective-permute-start.11 = (f32[64,128]{1,0:T(8,128)S(1)}, f32[64,128]{1,0:T(8,128)S(1)}, u32[]{:S(2)}, u32[]{:S(2)}) collective-permute-start(f32[64,128]{1,0:T(8,128)S(1)} %constant_dynamic-slice_fusion), channel_id=1, source_target_pairs={{0,8},{2,10},{4,12},{6,14},{8,0},{10,2},{12,4},{14,6},{1,9},{3,11}... | collective-permute-start | bytes 98312 | tf_op jit(solution)/shard_map/ppermute | solution.py:21
  122.6 5.2 %collective-permute-start.12 = (f32[64,128]{1,0:T(8,128)S(1)}, f32[64,128]{1,0:T(8,128)S(1)}, u32[]{:S(2)}, u32[]{:S(2)}) collective-permute-start(f32[64,128]{1,0:T(8,128)S(1)} %get-tuple-element.98), channel_id=1, source_target_pairs={{0,8},{2,10},{4,12},{6,14},{8,0},{10,2},{12,4},{14,6},{1,9},{3,11}... | collective-permute-start | bytes 98312 | tf_op jit(solution)/shard_map/ppermute | solution.py:28
  127.8 4.3 %collective-permute-start.13 = (f32[128,128]{1,0:T(8,128)S(1)}, f32[128,128]{1,0:T(8,128)S(1)}, u32[]{:S(2)}, u32[]{:S(2)}) collective-permute-start(f32[128,128]{1,0:T(8,128)S(1)} %constant_dynamic-update-slice_fusion.6), channel_id=1, source_target_pairs={{0,4},{2,6},{4,0},{6,2},{8,12},{10,14},{12,8},{14,10},{1,5},{3,7},... | collective-permute-start | bytes 196616 | tf_op jit(solution)/shard_map/ppermute | solution.py:28
  132.0 5.0 %collective-permute-start.14 = (f32[256,128]{1,0:T(8,128)S(1)}, f32[256,128]{1,0:T(8,128)S(1)}, u32[]{:S(2)}, u32[]{:S(2)}) collective-permute-start(f32[256,128]{1,0:T(8,128)S(1)} %constant_dynamic-update-slice_fusion.4), channel_id=1, source_target_pairs={{0,2},{2,0},{4,6},{6,4},{8,10},{10,8},{12,14},{14,12},{1,3},{3,1},... | collective-permute-start | bytes 393224 | tf_op jit(solution)/shard_map/ppermute | solution.py:28
  137.1 1.6 %collective-permute-start.15 = (f32[512,128]{1,0:T(8,128)S(1)}, f32[512,128]{1,0:T(8,128)S(1)}, u32[]{:S(2)}, u32[]{:S(2)}) collective-permute-start(f32[512,128]{1,0:T(8,128)S(1)} %constant_dynamic-update-slice_fusion.2), channel_id=1, source_target_pairs={{0,1},{1,0},{2,3},{3,2},{4,5},{5,4},{6,7},{7,6},{8,9},{9,8},{10,11... | collective-permute-start | bytes 786440 | tf_op jit(solution)/shard_map/ppermute | solution.py:28
  (9 other events, 57.4 us)

commit v7 on v3

--- a/solution.py
+++ b/solution.py
@@ -140,13 +140,16 @@
     span = 2 * DMAX + 1
     reach = TILE + 2 * DMAX
 
+    padded_rows = padded.reshape((-1,) + padded.shape[2:])
+    rows_per_sample = padded.shape[1]
+
     def gather_windows(place):
         b, h, w = place
         return jax.vmap(
-            lambda b, h, w: lax.dynamic_slice(
-                padded, (b, h, w, jnp.int32(0)), (1, span, reach, width)
-            )[0]
-        )(b, h, w)
+            lambda row, w: lax.dynamic_slice(
+                padded_rows, (row, w, jnp.int32(0)), (span, reach, width)
+            )
+        )(b * rows_per_sample + h, w)
 
     def shifted(source, row_shift, col_shift):
         return source[:, DMAX + row_shift, DMAX + col_shift : DMAX + col_shift + TILE, :].astype(

time: 104 us -> 177 us (1.70); the launches traced: 104 us -> 175 us
  local copies, waits for them, and re-layouts: 18.1 us -> 97.9 us
  other arithmetic: 21.5 us -> 16.8 us
  matrix products: 6.43 us -> 3.14 us
    gather x1 -> x96, local copies, waits for them, and re-layouts: 5.73 us -> 90.2 us  [gather_windows(): lax.dynamic_slice(padded, (b, h, w, jnp.int32(0)), (1, span, reach, width))]
    ppermute x2, waiting for transfers between devices: 5.92 us -> 1.82 us  [padded_2(): lax.ppermute(tail, axis, [(i, (i + 1) % count) for i in range(ends)])]
    convert_element_type x4 -> x0, other arithmetic: 3.86 us -> none  [shifted(): source[:, DMAX + row_shift, DMAX + col_shift:DMAX + col_shift + TILE, :]]
    unnamed x22 -> x70, local copies, waits for them, and re-layouts: 4.62 us -> 1.2 us
    dot_general x1, matrix products: 4.11 us -> 0.84 us  [backward(): grad_z = jnp.dot(grad_u, pw_weight.T, preferred_element_type=jnp.float32)]
    convert_element_type x1, other arithmetic: 3.9 us -> 1.21 us  [forward(): depth_flat = accum_sum.astype(jnp.bfloat16).reshape(-1, width)]
    mul x4, other arithmetic: 0.05 us -> 2.46 us  [forward(): kernel[tap_index] * onehot[dilation - 1]]
    reduce_sum x1, other arithmetic: 2.86 us -> 0.6 us  [backward(): part = jnp.sum(part.reshape(-1, width), axis=0)]
where the time goes in v7:
time: 177 us; the launch traced here: 175 us
  local copies, waits for them, and re-layouts  97.9 us (55%)
  starting transfers between devices  26.7 us (15%)
  waiting for transfers between devices  26.3 us (15%)
  other arithmetic  16.8 us (9%)
  between operations  3.28 us (2%)
  matrix products  3.14 us (2%)
    gather x96, local copies, waits for them, and re-layouts  90.2 us
    ppermute x4, waiting for transfers between devices, halve(): return keep + lax.ppermute(send, axis, [(i, i ^ bit) for i in range(count)])  11.1 us
    ppermute x4, waiting for transfers between devices, double(): got = lax.ppermute(x, axis, [(i, i ^ bit) for i in range(count)])  10.4 us
    all_to_all x1, starting transfers between devices, local(): lax.all_to_all(send.reshape(slots, TILE, teach_width + 1), ('lon', 'lat')...  7.36 us
    ppermute x4, starting transfers between devices, halve(): return keep + lax.ppermute(send, axis, [(i, i ^ bit) for i in range(count)])  6.08 us
    ppermute x4, starting transfers between devices, double(): got = lax.ppermute(x, axis, [(i, i ^ bit) for i in range(count)])  5.3 us
    ppermute x2, starting transfers between devices, padded_2(): lax.ppermute(head, axis, [((i + 1) % count, i) for i in range(ends)])  4.08 us
    ppermute x2, starting transfers between devices, padded_2(): lax.ppermute(tail, axis, [(i, (i + 1) % count) for i in range(ends)])  3.92 us
  transfers between devices with their start and end apart: 13, of which 11 were waited for; matrix products, arithmetic and copies ran while one was open for 5% of the time, Pallas kernels for 0%

profile of v7, /device:TPU:0, one launch (start us, length us, event | category | flops | bytes accessed | tf_op | source)
XLA Modules:
  0.0 174.7 jit_solution(13153565615968848747)
XLA Ops:
  6.5 7.4 %all-to-all-start = ((bf16[32,8,228]{2,1,0:T(8,128)(2,1)}), bf16[32,8,228]{2,1,0:T(8,128)(2,1)S(1)}, u32[]{:S(2)}, u32[]{:S(2)}) async-start(bf16[32,8,228]{2,1,0:T(8,128)(2,1)} %reshape.836), calls=%async_computation | async-start | bytes 262144 | tf_op jit(solution)/shard_map/all_to_all | solution.py:113
  17.1 2.8 %collective-permute-start.1 = (bf16[2,48,4,256]{3,2,1,0:T(4,128)(2,1)S(1)}, bf16[2,48,4,256]{3,2,1,0:T(4,128)(2,1)S(1)}, u32[]{:S(2)}, u32[]{:S(2)}) collective-permute-start(bf16[2,48,4,256]{3,2,1,0:T(4,128)(2,1)S(1)} %get-tuple-element.123), channel_id=1, source_target_pairs={{2,0},{4,2},{6,4},{8,6},{10,8},{12,10},{14,12},{0,14},{3,1},{5,3},... | collective-permute-start | bytes 589832 | tf_op jit(solution)/shard_map/ppermute | solution.py:75
  35.9 3.4 %pad_maximum_fusion = bf16[2,56,40,256]{3,2,1,0:T(8,128)(2,1)} fusion(bf16[2,4,40,256]{3,2,1,0:T(8,128)(2,1)} %collective-permute-done.3, bf16[2,48,4,256]{3,2,1,0:T(4,128)(2,1)S(1)} %collective-permute-done.1, bf16[2,48,32,256]{3,2,1,0:T(8,128)(2,1)} %param.15, bf16[2,48,4,256]{3,2,1,0:T(4,128)(2,1)S(1)} %collective-permute-done, ...), kind=kLoop, calls=%fused_computation.2 | loop fusion | flops 11468800 | bytes 4587520 | tf_op jit(solution)/shard_map/concatenate | solution.py:71
  39.3 90.8 %while.4 = (s32[]{:T(128)}, bf16[112,40,256]{2,1,0:T(8,128)(2,1)}, s32[32,3]{0,1:T(4,128)S(1)}, bf16[32,9,16,256]{3,2,1,0:T(8,128)(2,1)S(1)}, s32[]{:T(128)}) while((s32[]{:T(128)}, bf16[112,40,256]{2,1,0:T(8,128)(2,1)}, s32[32,3]{0,1:T(4,128)S(1)}, bf16[32,9,16,256]{3,2,1,0:T(8,128)(2,1)S(1)}, s32[]{:T(128)}) %tuple.117), condition=%wide.while_cond.3, body=%wide.while_body.3.sunk | while | flops 2 | bytes 147573 | solution.py:149
  39.9 2.2 %bitcast_dynamic-update-slice_fusion.2 = bf16[32,9,16,256]{3,2,1,0:T(8,128)(2,1)S(1)} fusion(bf16[32,9,16,256]{3,2,1,0:T(8,128)(2,1)S(1)} %get-tuple-element.208, s32[]{:T(128)} %get-tuple-element.205, bf16[112,40,256]{2,1,0:T(8,128)(2,1)} %get-tuple-element.211, s32[]{:T(128)} %bitcast.318, s32[]{:T(128)} %bitcast.319), kind=kLoop, calls=%fused_computation.clone.1 | loop fusion | bytes 147468 | tf_op jit(solution)/shard_map/vmap()/gather
  42.7 2.2 %bitcast_dynamic-update-slice_fusion.2 = bf16[32,9,16,256]{3,2,1,0:T(8,128)(2,1)S(1)} fusion(bf16[32,9,16,256]{3,2,1,0:T(8,128)(2,1)S(1)} %get-tuple-element.208, s32[]{:T(128)} %get-tuple-element.205, bf16[112,40,256]{2,1,0:T(8,128)(2,1)} %get-tuple-element.211, s32[]{:T(128)} %bitcast.318, s32[]{:T(128)} %bitcast.319), kind=kLoop, calls=%fused_computation.clone.1 | loop fusion | bytes 147468 | tf_op jit(solution)/shard_map/vmap()/gather
  45.5 2.2 %bitcast_dynamic-update-slice_fusion.2 = bf16[32,9,16,256]{3,2,1,0:T(8,128)(2,1)S(1)} fusion(bf16[32,9,16,256]{3,2,1,0:T(8,128)(2,1)S(1)} %get-tuple-element.208, s32[]{:T(128)} %get-tuple-element.205, bf16[112,40,256]{2,1,0:T(8,128)(2,1)} %get-tuple-element.211, s32[]{:T(128)} %bitcast.318, s32[]{:T(128)} %bitcast.319), kind=kLoop, calls=%fused_computation.clone.1 | loop fusion | bytes 147468 | tf_op jit(solution)/shard_map/vmap()/gather
  48.4 2.2 %bitcast_dynamic-update-slice_fusion.2 = bf16[32,9,16,256]{3,2,1,0:T(8,128)(2,1)S(1)} fusion(bf16[32,9,16,256]{3,2,1,0:T(8,128)(2,1)S(1)} %get-tuple-element.208, s32[]{:T(128)} %get-tuple-element.205, bf16[112,40,256]{2,1,0:T(8,128)(2,1)} %get-tuple-element.211, s32[]{:T(128)} %bitcast.318, s32[]{:T(128)} %bitcast.319), kind=kLoop, calls=%fused_computation.clone.1 | loop fusion | bytes 147468 | tf_op jit(solution)/shard_map/vmap()/gather
  51.2 2.2 %bitcast_dynamic-update-slice_fusion.2 = bf16[32,9,16,256]{3,2,1,0:T(8,128)(2,1)S(1)} fusion(bf16[32,9,16,256]{3,2,1,0:T(8,128)(2,1)S(1)} %get-tuple-element.208, s32[]{:T(128)} %get-tuple-element.205, bf16[112,40,256]{2,1,0:T(8,128)(2,1)} %get-tuple-element.211, s32[]{:T(128)} %bitcast.318, s32[]{:T(128)} %bitcast.319), kind=kLoop, calls=%fused_computation.clone.1 | loop fusion | bytes 147468 | tf_op jit(solution)/shard_map/vmap()/gather
  54.1 2.2 %bitcast_dynamic-update-slice_fusion.2 = bf16[32,9,16,256]{3,2,1,0:T(8,128)(2,1)S(1)} fusion(bf16[32,9,16,256]{3,2,1,0:T(8,128)(2,1)S(1)} %get-tuple-element.208, s32[]{:T(128)} %get-tuple-element.205, bf16[112,40,256]{2,1,0:T(8,128)(2,1)} %get-tuple-element.211, s32[]{:T(128)} %bitcast.318, s32[]{:T(128)} %bitcast.319), kind=kLoop, calls=%fused_computation.clone.1 | loop fusion | bytes 147468 | tf_op jit(solution)/shard_map/vmap()/gather
  56.9 2.2 %bitcast_dynamic-update-slice_fusion.2 = bf16[32,9,16,256]{3,2,1,0:T(8,128)(2,1)S(1)} fusion(bf16[32,9,16,256]{3,2,1,0:T(8,128)(2,1)S(1)} %get-tuple-element.208, s32[]{:T(128)} %get-tuple-element.205, bf16[112,40,256]{2,1,0:T(8,128)(2,1)} %get-tuple-element.211, s32[]{:T(128)} %bitcast.318, s32[]{:T(128)} %bitcast.319), kind=kLoop, calls=%fused_computation.clone.1 | loop fusion | bytes 147468 | tf_op jit(solution)/shard_map/vmap()/gather
  59.7 2.2 %bitcast_dynamic-update-slice_fusion.2 = bf16[32,9,16,256]{3,2,1,0:T(8,128)(2,1)S(1)} fusion(bf16[32,9,16,256]{3,2,1,0:T(8,128)(2,1)S(1)} %get-tuple-element.208, s32[]{:T(128)} %get-tuple-element.205, bf16[112,40,256]{2,1,0:T(8,128)(2,1)} %get-tuple-element.211, s32[]{:T(128)} %bitcast.318, s32[]{:T(128)} %bitcast.319), kind=kLoop, calls=%fused_computation.clone.1 | loop fusion | bytes 147468 | tf_op jit(solution)/shard_map/vmap()/gather
  62.6 2.2 %bitcast_dynamic-update-slice_fusion.2 = bf16[32,9,16,256]{3,2,1,0:T(8,128)(2,1)S(1)} fusion(bf16[32,9,16,256]{3,2,1,0:T(8,128)(2,1)S(1)} %get-tuple-element.208, s32[]{:T(128)} %get-tuple-element.205, bf16[112,40,256]{2,1,0:T(8,128)(2,1)} %get-tuple-element.211, s32[]{:T(128)} %bitcast.318, s32[]{:T(128)} %bitcast.319), kind=kLoop, calls=%fused_computation.clone.1 | loop fusion | bytes 147468 | tf_op jit(solution)/shard_map/vmap()/gather
  65.4 2.2 %bitcast_dynamic-update-slice_fusion.2 = bf16[32,9,16,256]{3,2,1,0:T(8,128)(2,1)S(1)} fusion(bf16[32,9,16,256]{3,2,1,0:T(8,128)(2,1)S(1)} %get-tuple-element.208, s32[]{:T(128)} %get-tuple-element.205, bf16[112,40,256]{2,1,0:T(8,128)(2,1)} %get-tuple-element.211, s32[]{:T(128)} %bitcast.318, s32[]{:T(128)} %bitcast.319), kind=kLoop, calls=%fused_computation.clone.1 | loop fusion | bytes 147468 | tf_op jit(solution)/shard_map/vmap()/gather
  68.2 2.2 %bitcast_dynamic-update-slice_fusion.2 = bf16[32,9,16,256]{3,2,1,0:T(8,128)(2,1)S(1)} fusion(bf16[32,9,16,256]{3,2,1,0:T(8,128)(2,1)S(1)} %get-tuple-element.208, s32[]{:T(128)} %get-tuple-element.205, bf16[112,40,256]{2,1,0:T(8,128)(2,1)} %get-tuple-element.211, s32[]{:T(128)} %bitcast.318, s32[]{:T(128)} %bitcast.319), kind=kLoop, calls=%fused_computation.clone.1 | loop fusion | bytes 147468 | tf_op jit(solution)/shard_map/vmap()/gather
  71.1 2.2 %bitcast_dynamic-update-slice_fusion.2 = bf16[32,9,16,256]{3,2,1,0:T(8,128)(2,1)S(1)} fusion(bf16[32,9,16,256]{3,2,1,0:T(8,128)(2,1)S(1)} %get-tuple-element.208, s32[]{:T(128)} %get-tuple-element.205, bf16[112,40,256]{2,1,0:T(8,128)(2,1)} %get-tuple-element.211, s32[]{:T(128)} %bitcast.318, s32[]{:T(128)} %bitcast.319), kind=kLoop, calls=%fused_computation.clone.1 | loop fusion | bytes 147468 | tf_op jit(solution)/shard_map/vmap()/gather
  73.9 2.2 %bitcast_dynamic-update-slice_fusion.2 = bf16[32,9,16,256]{3,2,1,0:T(8,128)(2,1)S(1)} fusion(bf16[32,9,16,256]{3,2,1,0:T(8,128)(2,1)S(1)} %get-tuple-element.208, s32[]{:T(128)} %get-tuple-element.205, bf16[112,40,256]{2,1,0:T(8,128)(2,1)} %get-tuple-element.211, s32[]{:T(128)} %bitcast.318, s32[]{:T(128)} %bitcast.319), kind=kLoop, calls=%fused_computation.clone.1 | loop fusion | bytes 147468 | tf_op jit(solution)/shard_map/vmap()/gather
  76.8 2.2 %bitcast_dynamic-update-slice_fusion.2 = bf16[32,9,16,256]{3,2,1,0:T(8,128)(2,1)S(1)} fusion(bf16[32,9,16,256]{3,2,1,0:T(8,128)(2,1)S(1)} %get-tuple-element.208, s32[]{:T(128)} %get-tuple-element.205, bf16[112,40,256]{2,1,0:T(8,128)(2,1)} %get-tuple-element.211, s32[]{:T(128)} %bitcast.318, s32[]{:T(128)} %bitcast.319), kind=kLoop, calls=%fused_computation.clone.1 | loop fusion | bytes 147468 | tf_op jit(solution)/shard_map/vmap()/gather
  139.4 5.3 %collective-permute-done.5 = f32[256,128]{1,0:T(8,128)S(1)} collective-permute-done((f32[256,128]{1,0:T(8,128)S(1)}, f32[256,128]{1,0:T(8,128)S(1)}, u32[]{:S(2)}, u32[]{:S(2)}) %collective-permute-start.5) | collective-permute-done | bytes 131104 | tf_op jit(solution)/shard_map/ppermute | solution.py:21
  146.4 2.6 %collective-permute-done.6 = f32[128,128]{1,0:T(8,128)S(1)} collective-permute-done((f32[128,128]{1,0:T(8,128)S(1)}, f32[128,128]{1,0:T(8,128)S(1)}, u32[]{:S(2)}, u32[]{:S(2)}) %collective-permute-start.6) | collective-permute-done | bytes 65568 | tf_op jit(solution)/shard_map/ppermute | solution.py:21
  149.0 2.8 %collective-permute-start.7 = (f32[64,128]{1,0:T(8,128)S(1)}, f32[64,128]{1,0:T(8,128)S(1)}, u32[]{:S(2)}, u32[]{:S(2)}) collective-permute-start(f32[64,128]{1,0:T(8,128)S(1)} %constant_dynamic-slice_fusion.1), channel_id=1, source_target_pairs={{0,8},{2,10},{4,12},{6,14},{8,0},{10,2},{12,4},{14,6},{1,9},{3,11}... | collective-permute-start | bytes 98312 | tf_op jit(solution)/shard_map/ppermute | solution.py:21
  153.9 2.8 %collective-permute-start.8 = (f32[64,128]{1,0:T(8,128)S(1)}, f32[64,128]{1,0:T(8,128)S(1)}, u32[]{:S(2)}, u32[]{:S(2)}) collective-permute-start(f32[64,128]{1,0:T(8,128)S(1)} %get-tuple-element.114), channel_id=1, source_target_pairs={{0,8},{2,10},{4,12},{6,14},{8,0},{10,2},{12,4},{14,6},{1,9},{3,11}... | collective-permute-start | bytes 98312 | tf_op jit(solution)/shard_map/ppermute | solution.py:28
  160.8 2.3 %collective-permute-done.9 = f32[128,128]{1,0:T(8,128)S(1)} collective-permute-done((f32[128,128]{1,0:T(8,128)S(1)}, f32[128,128]{1,0:T(8,128)S(1)}, u32[]{:S(2)}, u32[]{:S(2)}) %collective-permute-start.9) | collective-permute-done | bytes 65568 | tf_op jit(solution)/shard_map/ppermute | solution.py:28
  163.7 4.5 %collective-permute-done.10 = f32[256,128]{1,0:T(8,128)S(1)} collective-permute-done((f32[256,128]{1,0:T(8,128)S(1)}, f32[256,128]{1,0:T(8,128)S(1)}, u32[]{:S(2)}, u32[]{:S(2)}) %collective-permute-start.10) | collective-permute-done | bytes 131104 | tf_op jit(solution)/shard_map/ppermute | solution.py:28
  (249 shorter events, 106.0 us)
Async XLA Ops:
  0.6 131.0 %copy-start = (bf16[256,256]{1,0:T(8,128)(2,1)S(1)}, bf16[256,256]{1,0:T(8,128)(2,1)}, u32[]{:S(2)}) copy-start(bf16[256,256]{1,0:T(8,128)(2,1)} %param.18) | copy-start | bytes 393220
  6.5 27.0 %all-to-all-start = ((bf16[32,8,228]{2,1,0:T(8,128)(2,1)}), bf16[32,8,228]{2,1,0:T(8,128)(2,1)S(1)}, u32[]{:S(2)}, u32[]{:S(2)}) async-start(bf16[32,8,228]{2,1,0:T(8,128)(2,1)} %reshape.836), calls=%async_computation | async-start | bytes 262144 | tf_op jit(solution)/shard_map/all_to_all | solution.py:113
  15.2 11.2 %collective-permute-start = (bf16[2,48,4,256]{3,2,1,0:T(4,128)(2,1)S(1)}, bf16[2,48,4,256]{3,2,1,0:T(4,128)(2,1)S(1)}, u32[]{:S(2)}, u32[]{:S(2)}) collective-permute-start(bf16[2,48,4,256]{3,2,1,0:T(4,128)(2,1)S(1)} %get-tuple-element.122), channel_id=1, source_target_pairs={{0,2},{2,4},{4,6},{6,8},{8,10},{10,12},{12,14},{14,0},{1,3},{3,5},... | collective-permute-start | bytes 589832 | tf_op jit(solution)/shard_map/ppermute | solution.py:73
  17.1 11.3 %collective-permute-start.1 = (bf16[2,48,4,256]{3,2,1,0:T(4,128)(2,1)S(1)}, bf16[2,48,4,256]{3,2,1,0:T(4,128)(2,1)S(1)}, u32[]{:S(2)}, u32[]{:S(2)}) collective-permute-start(bf16[2,48,4,256]{3,2,1,0:T(4,128)(2,1)S(1)} %get-tuple-element.123), channel_id=1, source_target_pairs={{2,0},{4,2},{6,4},{8,6},{10,8},{12,10},{14,12},{0,14},{3,1},{5,3},... | collective-permute-start | bytes 589832 | tf_op jit(solution)/shard_map/ppermute | solution.py:75
  30.3 4.6 %collective-permute-start.2 = (bf16[2,4,40,256]{3,2,1,0:T(8,128)(2,1)}, bf16[2,4,40,256]{3,2,1,0:T(8,128)(2,1)}, u32[]{:S(2)}, u32[]{:S(2)}) collective-permute-start(bf16[2,4,40,256]{3,2,1,0:T(8,128)(2,1)} %get-tuple-element.120), channel_id=1, source_target_pairs={{0,1},{2,3},{4,5},{6,7},{8,9},{10,11},{12,13},{14,15},{16,17},{18,... | collective-permute-start | bytes 491528 | tf_op jit(solution)/shard_map/ppermute | solution.py:73
  32.3 3.6 %collective-permute-start.3 = (bf16[2,4,40,256]{3,2,1,0:T(8,128)(2,1)}, bf16[2,4,40,256]{3,2,1,0:T(8,128)(2,1)}, u32[]{:S(2)}, u32[]{:S(2)}) collective-permute-start(bf16[2,4,40,256]{3,2,1,0:T(8,128)(2,1)} %get-tuple-element.121), channel_id=1, source_target_pairs={{1,0},{3,2},{5,4},{7,6},{9,8},{11,10},{13,12},{15,14},{17,16},{19,... | collective-permute-start | bytes 491528 | tf_op jit(solution)/shard_map/ppermute | solution.py:75
  34.7 95.4 %copy-start.3 = (f32[1,256]{1,0:T(1,128)S(1)}, f32[1,256]{1,0:T(1,128)}, u32[]{:S(2)}) copy-start(f32[1,256]{1,0:T(1,128)} %get-tuple-element.126) | copy-start | bytes 3076
  34.7 95.4 %copy-start.4 = (f32[1,256]{1,0:T(1,128)S(1)}, f32[1,256]{1,0:T(1,128)}, u32[]{:S(2)}) copy-start(f32[1,256]{1,0:T(1,128)} %get-tuple-element.127) | copy-start | bytes 3076
  34.7 95.4 %copy-start.5 = (f32[1,256]{1,0:T(1,128)S(1)}, f32[1,256]{1,0:T(1,128)}, u32[]{:S(2)}) copy-start(f32[1,256]{1,0:T(1,128)} %get-tuple-element.128) | copy-start | bytes 3076
  34.7 95.4 %copy-start.6 = (f32[1,256]{1,0:T(1,128)S(1)}, f32[1,256]{1,0:T(1,128)}, u32[]{:S(2)}) copy-start(f32[1,256]{1,0:T(1,128)} %get-tuple-element.129) | copy-start | bytes 3076
  34.7 95.4 %copy-start.7 = (f32[1,256]{1,0:T(1,128)S(1)}, f32[1,256]{1,0:T(1,128)}, u32[]{:S(2)}) copy-start(f32[1,256]{1,0:T(1,128)} %get-tuple-element.130) | copy-start | bytes 3076
  34.7 95.4 %copy-start.8 = (f32[1,256]{1,0:T(1,128)S(1)}, f32[1,256]{1,0:T(1,128)}, u32[]{:S(2)}) copy-start(f32[1,256]{1,0:T(1,128)} %get-tuple-element.131) | copy-start | bytes 3076
  34.7 95.4 %copy-start.9 = (f32[1,256]{1,0:T(1,128)S(1)}, f32[1,256]{1,0:T(1,128)}, u32[]{:S(2)}) copy-start(f32[1,256]{1,0:T(1,128)} %get-tuple-element.132) | copy-start | bytes 3076
  34.7 95.4 %copy-start.10 = (f32[1,256]{1,0:T(1,128)S(1)}, f32[1,256]{1,0:T(1,128)}, u32[]{:S(2)}) copy-start(f32[1,256]{1,0:T(1,128)} %get-tuple-element.133) | copy-start | bytes 3076
  34.7 95.4 %copy-start.11 = (f32[1,256]{1,0:T(1,128)S(1)}, f32[1,256]{1,0:T(1,128)}, u32[]{:S(2)}) copy-start(f32[1,256]{1,0:T(1,128)} %get-tuple-element.134) | copy-start | bytes 3076
  34.7 95.4 %copy-start.12 = (f32[1,256]{1,0:T(1,128)S(1)}, f32[1,256]{1,0:T(1,128)}, u32[]{:S(2)}) copy-start(f32[1,256]{1,0:T(1,128)} %get-tuple-element.135) | copy-start | bytes 3076
  136.6 2.1 %collective-permute-start.4 = (f32[512,128]{1,0:T(8,128)S(1)}, f32[512,128]{1,0:T(8,128)S(1)}, u32[]{:S(2)}, u32[]{:S(2)}) collective-permute-start(f32[512,128]{1,0:T(8,128)S(1)} %constant_dynamic-slice_fusion.4), channel_id=1, source_target_pairs={{0,1},{1,0},{2,3},{3,2},{4,5},{5,4},{6,7},{7,6},{8,9},{9,8},{10,11... | collective-permute-start | bytes 786440 | tf_op jit(solution)/shard_map/ppermute | solution.py:21
  138.8 5.8 %collective-permute-start.5 = (f32[256,128]{1,0:T(8,128)S(1)}, f32[256,128]{1,0:T(8,128)S(1)}, u32[]{:S(2)}, u32[]{:S(2)}) collective-permute-start(f32[256,128]{1,0:T(8,128)S(1)} %constant_dynamic-slice_fusion.3), channel_id=1, source_target_pairs={{0,2},{2,0},{4,6},{6,4},{8,10},{10,8},{12,14},{14,12},{1,3},{3,1},... | collective-permute-start | bytes 393224 | tf_op jit(solution)/shard_map/ppermute | solution.py:21
  144.7 4.3 %collective-permute-start.6 = (f32[128,128]{1,0:T(8,128)S(1)}, f32[128,128]{1,0:T(8,128)S(1)}, u32[]{:S(2)}, u32[]{:S(2)}) collective-permute-start(f32[128,128]{1,0:T(8,128)S(1)} %constant_dynamic-slice_fusion.2), channel_id=1, source_target_pairs={{0,4},{2,6},{4,0},{6,2},{8,12},{10,14},{12,8},{14,10},{1,5},{3,7},... | collective-permute-start | bytes 196616 | tf_op jit(solution)/shard_map/ppermute | solution.py:21
  149.0 4.9 %collective-permute-start.7 = (f32[64,128]{1,0:T(8,128)S(1)}, f32[64,128]{1,0:T(8,128)S(1)}, u32[]{:S(2)}, u32[]{:S(2)}) collective-permute-start(f32[64,128]{1,0:T(8,128)S(1)} %constant_dynamic-slice_fusion.1), channel_id=1, source_target_pairs={{0,8},{2,10},{4,12},{6,14},{8,0},{10,2},{12,4},{14,6},{1,9},{3,11}... | collective-permute-start | bytes 98312 | tf_op jit(solution)/shard_map/ppermute | solution.py:21
  153.9 4.9 %collective-permute-start.8 = (f32[64,128]{1,0:T(8,128)S(1)}, f32[64,128]{1,0:T(8,128)S(1)}, u32[]{:S(2)}, u32[]{:S(2)}) collective-permute-start(f32[64,128]{1,0:T(8,128)S(1)} %get-tuple-element.114), channel_id=1, source_target_pairs={{0,8},{2,10},{4,12},{6,14},{8,0},{10,2},{12,4},{14,6},{1,9},{3,11}... | collective-permute-start | bytes 98312 | tf_op jit(solution)/shard_map/ppermute | solution.py:28
  158.9 4.3 %collective-permute-start.9 = (f32[128,128]{1,0:T(8,128)S(1)}, f32[128,128]{1,0:T(8,128)S(1)}, u32[]{:S(2)}, u32[]{:S(2)}) collective-permute-start(f32[128,128]{1,0:T(8,128)S(1)} %constant_dynamic-update-slice_fusion.6), channel_id=1, source_target_pairs={{0,4},{2,6},{4,0},{6,2},{8,12},{10,14},{12,8},{14,10},{1,5},{3,7},... | collective-permute-start | bytes 196616 | tf_op jit(solution)/shard_map/ppermute | solution.py:28
  163.1 5.0 %collective-permute-start.10 = (f32[256,128]{1,0:T(8,128)S(1)}, f32[256,128]{1,0:T(8,128)S(1)}, u32[]{:S(2)}, u32[]{:S(2)}) collective-permute-start(f32[256,128]{1,0:T(8,128)S(1)} %constant_dynamic-update-slice_fusion.4), channel_id=1, source_target_pairs={{0,2},{2,0},{4,6},{6,4},{8,10},{10,8},{12,14},{14,12},{1,3},{3,1},... | collective-permute-start | bytes 393224 | tf_op jit(solution)/shard_map/ppermute | solution.py:28
  168.2 1.6 collective-permute-start.11
  (22 other events, 2005.5 us)

commit v8 on v3

--- a/solution.py
+++ b/solution.py
@@ -10,6 +10,7 @@
 
 
 LANES = 128
+EXCHANGED = 2
 
 
 def halve(x, axis, bit):
@@ -47,11 +48,15 @@
     unit = 8 * LANES * (2 ** len(steps))
     total = -(-flat.shape[0] // unit) * unit
     x = jnp.pad(flat, (0, total - flat.shape[0])).reshape(-1, LANES)
-    for axis, bit in steps:
+    halved = steps[: max(0, len(steps) - EXCHANGED)]
+    for axis, bit in halved:
         x = halve(x, axis, bit)
+    for axis, bit in steps[len(halved) :]:
+        count = lax.axis_size(axis)
+        x = x + lax.ppermute(x, axis, [(i, i ^ bit) for i in range(count)])
     if rest:
         x = lax.psum(x, tuple(rest))
-    for axis, bit in reversed(steps):
+    for axis, bit in reversed(halved):
         x = double(x, axis, bit)
     flat = x.reshape(-1)
     out = []

time: 104 us -> 98.9 us (0.951)
  starting transfers between devices: 26.9 us -> 21.9 us
    ppermute x0 -> x2, waiting for transfers between devices: none -> 9.67 us  [packed_sum(): x = x + lax.ppermute(x, axis, [(i, i ^ bit) for i in range(count)])]
    ppermute x4 -> x2, waiting for transfers between devices: 10.7 us -> 5.2 us  [halve(): return keep + lax.ppermute(send, axis, [(i, i ^ bit) for i in range(count)])]
    ppermute x4 -> x2, starting transfers between devices: 6.01 us -> 1.12 us  [double(): got = lax.ppermute(x, axis, [(i, i ^ bit) for i in range(count)])]
    ppermute x4 -> x2, waiting for transfers between devices: 9.6 us -> 5.43 us  [double(): got = lax.ppermute(x, axis, [(i, i ^ bit) for i in range(count)])]
    ppermute x4 -> x2, starting transfers between devices: 6.15 us -> 2.39 us  [halve(): return keep + lax.ppermute(send, axis, [(i, i ^ bit) for i in range(count)])]
    ppermute x0 -> x2, starting transfers between devices: none -> 3.58 us  [packed_sum(): x = x + lax.ppermute(x, axis, [(i, i ^ bit) for i in range(count)])]
  transfers between devices with their start and end apart: 13 -> 11, of which waited for: 11 -> 9; matrix products, arithmetic and copies ran while one was open for 5% -> 5% of each run, Pallas kernels for 0% -> 0%
where the time goes in v8:
time: 98.9 us; the launch traced here: 98.5 us
  waiting for transfers between devices  27.7 us (28%)
  starting transfers between devices  21.9 us (22%)
  other arithmetic  21.5 us (22%)
  local copies, waits for them, and re-layouts  18 us (18%)
  matrix products  6.43 us (7%)
  between operations  2.97 us (3%)
    ppermute x2, waiting for transfers between devices, packed_sum(): x = x + lax.ppermute(x, axis, [(i, i ^ bit) for i in range(count)])  9.67 us
    all_to_all x1, starting transfers between devices, local(): lax.all_to_all(send.reshape(slots, TILE, teach_width + 1), ('lon', 'lat')...  7.36 us
    ppermute x2, waiting for transfers between devices, padded_2(): lax.ppermute(tail, axis, [(i, (i + 1) % count) for i in range(ends)])  5.92 us
    gather x1, local copies, waits for them, and re-layouts, gather_windows(): lax.dynamic_slice(padded, (b, h, w, jnp.int32(0)), (1, span, reach, width))  5.74 us
    ppermute x2, waiting for transfers between devices, double(): got = lax.ppermute(x, axis, [(i, i ^ bit) for i in range(count)])  5.43 us
    ppermute x2, waiting for transfers between devices, halve(): return keep + lax.ppermute(send, axis, [(i, i ^ bit) for i in range(count)])  5.2 us
    concatenate x1, other arithmetic, padded_2(): jnp.concatenate([lax.ppermute(tail, axis, [(i, (i + 1) % count) for i in...  4.77 us
    unnamed x22, local copies, waits for them, and re-layouts  4.62 us
  transfers between devices with their start and end apart: 11, of which 9 were waited for; matrix products, arithmetic and copies ran while one was open for 5% of the time, Pallas kernels for 0%

profile of v8, /device:TPU:0, one launch (start us, length us, event | category | flops | bytes accessed | tf_op | source)
XLA Modules:
  0.0 98.5 jit_solution(8016231564589008525)
XLA Ops:
  6.7 7.4 %all-to-all-start = ((bf16[32,8,228]{2,1,0:T(8,128)(2,1)}), bf16[32,8,228]{2,1,0:T(8,128)(2,1)S(1)}, u32[]{:S(2)}, u32[]{:S(2)}) async-start(bf16[32,8,228]{2,1,0:T(8,128)(2,1)} %reshape.832), calls=%async_computation | async-start | bytes 262144 | tf_op jit(solution)/shard_map/all_to_all | solution.py:118
  14.0 1.3 %fusion.93 = (bf16[2,48,4,256]{3,2,1,0:T(4,128)(2,1)S(1)}, bf16[2,48,4,256]{3,2,1,0:T(4,128)(2,1)S(1)}) fusion(bf16[2,48,32,256]{3,2,1,0:T(8,128)(2,1)} %param.15), kind=kLoop, calls=%fused_computation.327 | loop fusion | bytes 786432 | tf_op jit(solution)/shard_map/slice | solution.py:74
  15.5 2.0 %collective-permute-start = (bf16[2,48,4,256]{3,0,2,1:T(2,128)(2,1)S(1)}, bf16[2,48,4,256]{3,0,2,1:T(2,128)(2,1)S(1)}, u32[]{:S(2)}, u32[]{:S(2)}) collective-permute-start(bf16[2,48,4,256]{3,0,2,1:T(2,128)(2,1)S(1)} %copy.519), channel_id=1, source_target_pairs={{0,2},{2,4},{4,6},{6,8},{8,10},{10,12},{12,14},{14,0},{1,3},{3,5},... | collective-permute-start | bytes 589832 | tf_op jit(solution)/shard_map/ppermute | solution.py:78
  17.7 2.9 %collective-permute-start.1 = (bf16[2,48,4,256]{3,0,2,1:T(2,128)(2,1)S(1)}, bf16[2,48,4,256]{3,0,2,1:T(2,128)(2,1)S(1)}, u32[]{:S(2)}, u32[]{:S(2)}) collective-permute-start(bf16[2,48,4,256]{3,0,2,1:T(2,128)(2,1)S(1)} %copy.520), channel_id=1, source_target_pairs={{2,0},{4,2},{6,4},{8,6},{10,8},{12,10},{14,12},{0,14},{3,1},{5,3},... | collective-permute-start | bytes 589832 | tf_op jit(solution)/shard_map/ppermute | solution.py:80
  20.8 5.9 %collective-permute-done = bf16[2,48,4,256]{3,0,2,1:T(2,128)(2,1)S(1)} collective-permute-done((bf16[2,48,4,256]{3,0,2,1:T(2,128)(2,1)S(1)}, bf16[2,48,4,256]{3,0,2,1:T(2,128)(2,1)S(1)}, u32[]{:S(2)}, u32[]{:S(2)}) %collective-permute-start) | collective-permute-done | bytes 196640 | tf_op jit(solution)/shard_map/ppermute | solution.py:78
  26.8 1.7 %constant_dynamic-update-slice_fusion.1 = bf16[2,48,40,256]{3,0,2,1:T(2,128)(2,1)S(1)} fusion(bf16[2,48,40,256]{3,0,2,1:T(2,128)(2,1)S(1)} %constant_dynamic-update-slice_fusion.2, bf16[2,48,32,256]{3,2,1,0:T(8,128)(2,1)S(1)} %copy-done.3), kind=kLoop, calls=%fused_computation.238 | loop fusion | bytes 3145728
  29.2 1.3 %copy-done.2 = bf16[2,48,40,256]{3,0,2,1:T(2,128)(2,1)} copy-done((bf16[2,48,40,256]{3,0,2,1:T(2,128)(2,1)}, bf16[2,48,40,256]{3,0,2,1:T(2,128)(2,1)S(1)}, u32[]{:S(2)}) %copy-start.2) | copy-done | bytes 1966104
  30.8 1.3 %collective-permute-start.2 = (bf16[2,4,40,256]{3,0,2,1:T(2,128)(2,1)S(1)}, bf16[2,4,40,256]{3,0,2,1:T(2,128)(2,1)S(1)}, u32[]{:S(2)}, u32[]{:S(2)}) collective-permute-start(bf16[2,4,40,256]{3,0,2,1:T(2,128)(2,1)S(1)} %get-tuple-element.168), channel_id=1, source_target_pairs={{0,1},{2,3},{4,5},{6,7},{8,9},{10,11},{12,13},{14,15},{16,17},{18,... | collective-permute-start | bytes 491528 | tf_op jit(solution)/shard_map/ppermute | solution.py:78
  32.1 1.3 %collective-permute-start.3 = (bf16[2,4,40,256]{3,0,2,1:T(2,128)(2,1)S(1)}, bf16[2,4,40,256]{3,0,2,1:T(2,128)(2,1)S(1)}, u32[]{:S(2)}, u32[]{:S(2)}) collective-permute-start(bf16[2,4,40,256]{3,0,2,1:T(2,128)(2,1)S(1)} %get-tuple-element.169), channel_id=1, source_target_pairs={{1,0},{3,2},{5,4},{7,6},{9,8},{11,10},{13,12},{15,14},{17,16},{19,... | collective-permute-start | bytes 491528 | tf_op jit(solution)/shard_map/ppermute | solution.py:80
  35.3 4.8 %pad_maximum_fusion = bf16[2,56,40,256]{3,0,2,1:T(2,128)(2,1)S(1)} fusion(bf16[2,4,40,256]{3,0,2,1:T(2,128)(2,1)S(1)} %collective-permute-done.3, bf16[2,48,40,256]{3,0,2,1:T(2,128)(2,1)} %copy-done.2, bf16[2,4,40,256]{3,0,2,1:T(2,128)(2,1)S(1)} %collective-permute-done.2), kind=kLoop, calls=%fused_computation.1 | loop fusion | flops 2293760 | bytes 4587520 | tf_op jit(solution)/shard_map/concatenate | solution.py:76
  40.1 5.7 %gather_fusion = bf16[32,9,16,256]{3,0,2,1:T(8,128)(2,1)} fusion(bf16[2,56,40,256]{3,0,2,1:T(2,128)(2,1)S(1)} %pad_maximum_fusion, s32[32]{0:T(128)S(1)} %fusion.91), kind=kCustom, calls=%fused_computation | custom fusion | bytes 4719104 | tf_op jit(solution)/shard_map/vmap()/gather | solution.py:151
  45.9 2.5 %slice_convert_fusion.20 = (f32[32,1,8,256]{3,0,2,1:T(8,128)S(1)}, f32[32,1,8,256]{3,0,2,1:T(8,128)S(1)}, f32[32,1,8,256]{3,0,2,1:T(8,128)S(1)}, f32[32,1,8,256]...) fusion(bf16[32,9,16,256]{3,0,2,1:T(8,128)(2,1)} %gather_fusion), kind=kLoop, calls=%fused_computation.179 | loop fusion | flops 1245184 | bytes 7471104 | tf_op jit(solution)/shard_map/convert_element_type | solution.py:157
  50.5 3.9 %fusion.39 = bf16[256,256]{1,0:T(8,128)(2,1)S(1)} fusion(f32[32,1,8,256]{3,2,0,1:T(8,128)S(1)} %copy.397, f32[32,1,8,256]{3,2,0,1:T(8,128)S(1)} %copy.396, f32[32,1,8,256]{3,2,0,1:T(8,128)S(1)} %copy.395, f32[32,1,8,256]{3,2,0,1:T(8,128)S(1)} %copy.394, f32[32,1,8,256]{3,2,0,1:T(8,128)S(1)} %copy.393, f32[32,1,8,256]{3,2,0,1:T(8,128)S(1)} %copy.392, ...), kind=kLoop, calls=%fused_computation.85 | loop fusion | flops 4325376 | bytes 8815616 | tf_op jit(solution)/shard_map/convert_element_type | solution.py:173
  57.5 4.1 %fusion.8 = (f32[256]{0:T(256)S(1)}, f32[256]{0:T(256)S(1)}, f32[256]{0:T(256)S(1)}, f32[256]{0:T(256)S(1)}, f32[256]{0:T(256)S(1)}, /*index=5*/f32[256]{0:T(256...) fusion(f32[32,1,8,256]{3,0,2,1:T(8,128)S(1)} %get-tuple-element, ...), kind=kOutput, calls=%fused_computation.24 | convolution fusion | flops 35909120 | bytes 5261312 | tf_op jit(solution)/shard_map/dot_general | solution.py:191
  61.7 2.9 %fusion.25 = (f32[256]{0:T(256)S(1)}, f32[256]{0:T(256)S(1)}, f32[256]{0:T(256)S(1)}, f32[256]{0:T(256)S(1)}, f32[256]{0:T(256)S(1)}, /*index=5*/f32[256]{0:T(25...) fusion(f32[256,256]{1,0:T(8,128)S(1)} %get-tuple-element.218, ...), kind=kLoop, calls=%fused_computation.58 | loop fusion | flops 1962240 | bytes 4209664 | tf_op jit(solution)/shard_map/reduce_sum | solution.py:204
  66.2 1.3 %collective-permute-done.4 = f32[512,128]{1,0:T(8,128)S(1)} collective-permute-done((f32[512,128]{1,0:T(8,128)S(1)}, f32[512,128]{1,0:T(8,128)S(1)}, u32[]{:S(2)}, u32[]{:S(2)}) %collective-permute-start.4) | collective-permute-done | bytes 262176 | tf_op jit(solution)/shard_map/ppermute | solution.py:22
  67.5 2.1 %collective-permute-start.5 = (f32[256,128]{1,0:T(8,128)S(1)}, f32[256,128]{1,0:T(8,128)S(1)}, u32[]{:S(2)}, u32[]{:S(2)}) collective-permute-start(f32[256,128]{1,0:T(8,128)S(1)} %constant_dynamic-slice_fusion), channel_id=1, source_target_pairs={{0,2},{2,0},{4,6},{6,4},{8,10},{10,8},{12,14},{14,12},{1,3},{3,1},... | collective-permute-start | bytes 393224 | tf_op jit(solution)/shard_map/ppermute | solution.py:22
  69.6 3.9 %collective-permute-done.5 = f32[256,128]{1,0:T(8,128)S(1)} collective-permute-done((f32[256,128]{1,0:T(8,128)S(1)}, f32[256,128]{1,0:T(8,128)S(1)}, u32[]{:S(2)}, u32[]{:S(2)}) %collective-permute-start.5) | collective-permute-done | bytes 131104 | tf_op jit(solution)/shard_map/ppermute | solution.py:22
  73.5 1.5 %collective-permute-start.6 = (f32[256,128]{1,0:T(8,128)S(1)}, f32[256,128]{1,0:T(8,128)S(1)}, u32[]{:S(2)}, u32[]{:S(2)}) collective-permute-start(f32[256,128]{1,0:T(8,128)S(1)} %dynamic-slice_add_fusion.1), channel_id=1, source_target_pairs={{0,4},{2,6},{4,0},{6,2},{8,12},{10,14},{12,8},{14,10},{1,5},{3,7},... | collective-permute-start | bytes 393224 | tf_op jit(solution)/shard_map/ppermute | solution.py:56
  75.0 3.7 %collective-permute-done.6 = f32[256,128]{1,0:T(8,128)S(1)} collective-permute-done((f32[256,128]{1,0:T(8,128)S(1)}, f32[256,128]{1,0:T(8,128)S(1)}, u32[]{:S(2)}, u32[]{:S(2)}) %collective-permute-start.6) | collective-permute-done | bytes 131104 | tf_op jit(solution)/shard_map/ppermute | solution.py:56
  78.8 2.1 %collective-permute-start.7 = (f32[256,128]{1,0:T(8,128)S(1)}, f32[256,128]{1,0:T(8,128)S(1)}, u32[]{:S(2)}, u32[]{:S(2)}) collective-permute-start(f32[256,128]{1,0:T(8,128)S(1)} %add.481), channel_id=1, source_target_pairs={{0,8},{2,10},{4,12},{6,14},{8,0},{10,2},{12,4},{14,6},{1,9},{3,11}... | collective-permute-start | bytes 393224 | tf_op jit(solution)/shard_map/ppermute | solution.py:56
  80.8 6.0 %collective-permute-done.7 = f32[256,128]{1,0:T(8,128)S(1)} collective-permute-done((f32[256,128]{1,0:T(8,128)S(1)}, f32[256,128]{1,0:T(8,128)S(1)}, u32[]{:S(2)}, u32[]{:S(2)}) %collective-permute-start.7) | collective-permute-done | bytes 131104 | tf_op jit(solution)/shard_map/ppermute | solution.py:56
  87.9 4.0 %collective-permute-done.8 = f32[256,128]{1,0:T(8,128)S(1)} collective-permute-done((f32[256,128]{1,0:T(8,128)S(1)}, f32[256,128]{1,0:T(8,128)S(1)}, u32[]{:S(2)}, u32[]{:S(2)}) %collective-permute-start.8) | collective-permute-done | bytes 131104 | tf_op jit(solution)/shard_map/ppermute | solution.py:29
  92.1 1.4 %collective-permute-done.9 = f32[512,128]{1,0:T(8,128)S(1)} collective-permute-done((f32[512,128]{1,0:T(8,128)S(1)}, f32[512,128]{1,0:T(8,128)S(1)}, u32[]{:S(2)}, u32[]{:S(2)}) %collective-permute-start.9) | collective-permute-done | bytes 262176 | tf_op jit(solution)/shard_map/ppermute | solution.py:29
  (105 shorter events, 20.7 us)
Async XLA Ops:
  0.6 53.8 %copy-start = (bf16[256,256]{1,0:T(8,128)(2,1)S(1)}, bf16[256,256]{1,0:T(8,128)(2,1)}, u32[]{:S(2)}) copy-start(bf16[256,256]{1,0:T(8,128)(2,1)} %param.18) | copy-start | bytes 393220
  0.6 26.2 %copy-start.3 = (bf16[2,48,32,256]{3,2,1,0:T(8,128)(2,1)S(1)}, bf16[2,48,32,256]{3,2,1,0:T(8,128)(2,1)}, u32[]{:S(2)}) copy-start(bf16[2,48,32,256]{3,2,1,0:T(8,128)(2,1)} %param.15) | copy-start | bytes 4718596
  0.7 19.9 %copy-start.5 = (bf16[9,256]{1,0:T(8,128)(2,1)S(1)}, bf16[9,256]{1,0:T(8,128)(2,1)}, u32[]{:S(2)}) copy-start(bf16[9,256]{1,0:T(8,128)(2,1)} %param.17) | copy-start | bytes 13828
  0.7 19.9 %copy-start.6 = (s32[256]{0:T(256)S(1)}, s32[256]{0:T(256)}, u32[]{:S(2)}) copy-start(s32[256]{0:T(256)} %param.16) | copy-start | bytes 3076
  6.7 26.7 %all-to-all-start = ((bf16[32,8,228]{2,1,0:T(8,128)(2,1)}), bf16[32,8,228]{2,1,0:T(8,128)(2,1)S(1)}, u32[]{:S(2)}, u32[]{:S(2)}) async-start(bf16[32,8,228]{2,1,0:T(8,128)(2,1)} %reshape.832), calls=%async_computation | async-start | bytes 262144 | tf_op jit(solution)/shard_map/all_to_all | solution.py:118
  15.5 11.2 %collective-permute-start = (bf16[2,48,4,256]{3,0,2,1:T(2,128)(2,1)S(1)}, bf16[2,48,4,256]{3,0,2,1:T(2,128)(2,1)S(1)}, u32[]{:S(2)}, u32[]{:S(2)}) collective-permute-start(bf16[2,48,4,256]{3,0,2,1:T(2,128)(2,1)S(1)} %copy.519), channel_id=1, source_target_pairs={{0,2},{2,4},{4,6},{6,8},{8,10},{10,12},{12,14},{14,0},{1,3},{3,5},... | collective-permute-start | bytes 589832 | tf_op jit(solution)/shard_map/ppermute | solution.py:78
  17.7 11.4 %collective-permute-start.1 = (bf16[2,48,4,256]{3,0,2,1:T(2,128)(2,1)S(1)}, bf16[2,48,4,256]{3,0,2,1:T(2,128)(2,1)S(1)}, u32[]{:S(2)}, u32[]{:S(2)}) collective-permute-start(bf16[2,48,4,256]{3,0,2,1:T(2,128)(2,1)S(1)} %copy.520), channel_id=1, source_target_pairs={{2,0},{4,2},{6,4},{8,6},{10,8},{12,10},{14,12},{0,14},{3,1},{5,3},... | collective-permute-start | bytes 589832 | tf_op jit(solution)/shard_map/ppermute | solution.py:80
  29.2 1.3 %copy-start.2 = (bf16[2,48,40,256]{3,0,2,1:T(2,128)(2,1)}, bf16[2,48,40,256]{3,0,2,1:T(2,128)(2,1)S(1)}, u32[]{:S(2)}) copy-start(bf16[2,48,40,256]{3,0,2,1:T(2,128)(2,1)S(1)} %constant_dynamic-update-slice_fusion) | copy-start | bytes 5898244
  30.8 3.7 %collective-permute-start.2 = (bf16[2,4,40,256]{3,0,2,1:T(2,128)(2,1)S(1)}, bf16[2,4,40,256]{3,0,2,1:T(2,128)(2,1)S(1)}, u32[]{:S(2)}, u32[]{:S(2)}) collective-permute-start(bf16[2,4,40,256]{3,0,2,1:T(2,128)(2,1)S(1)} %get-tuple-element.168), channel_id=1, source_target_pairs={{0,1},{2,3},{4,5},{6,7},{8,9},{10,11},{12,13},{14,15},{16,17},{18,... | collective-permute-start | bytes 491528 | tf_op jit(solution)/shard_map/ppermute | solution.py:78
  32.1 3.3 %collective-permute-start.3 = (bf16[2,4,40,256]{3,0,2,1:T(2,128)(2,1)S(1)}, bf16[2,4,40,256]{3,0,2,1:T(2,128)(2,1)S(1)}, u32[]{:S(2)}, u32[]{:S(2)}) collective-permute-start(bf16[2,4,40,256]{3,0,2,1:T(2,128)(2,1)S(1)} %get-tuple-element.169), channel_id=1, source_target_pairs={{1,0},{3,2},{5,4},{7,6},{9,8},{11,10},{13,12},{15,14},{17,16},{19,... | collective-permute-start | bytes 491528 | tf_op jit(solution)/shard_map/ppermute | solution.py:80
  45.9 2.5 %copy-start.1 = (bf16[32,9,16,256]{3,0,2,1:T(8,128)(2,1)S(1)}, bf16[32,9,16,256]{3,0,2,1:T(8,128)(2,1)}, u32[]{:S(2)}) copy-start(bf16[32,9,16,256]{3,0,2,1:T(8,128)(2,1)} %gather_fusion) | copy-start | bytes 7077892
  50.5 4.2 %copy-start.4 = (bf16[256,227]{0,1:T(8,128)(2,1)S(1)}, bf16[256,227]{0,1:T(8,128)(2,1)}, u32[]{:S(2)}) copy-start(bf16[256,227]{0,1:T(8,128)(2,1)} %param.19) | copy-start | bytes 348676
  65.9 1.6 %collective-permute-start.4 = (f32[512,128]{1,0:T(8,128)S(1)}, f32[512,128]{1,0:T(8,128)S(1)}, u32[]{:S(2)}, u32[]{:S(2)}) collective-permute-start(f32[512,128]{1,0:T(8,128)S(1)} %constant_dynamic-slice_fusion.1), channel_id=1, source_target_pairs={{0,1},{1,0},{2,3},{3,2},{4,5},{5,4},{6,7},{7,6},{8,9},{9,8},{10,11... | collective-permute-start | bytes 786440 | tf_op jit(solution)/shard_map/ppermute | solution.py:22
  67.5 6.0 %collective-permute-start.5 = (f32[256,128]{1,0:T(8,128)S(1)}, f32[256,128]{1,0:T(8,128)S(1)}, u32[]{:S(2)}, u32[]{:S(2)}) collective-permute-start(f32[256,128]{1,0:T(8,128)S(1)} %constant_dynamic-slice_fusion), channel_id=1, source_target_pairs={{0,2},{2,0},{4,6},{6,4},{8,10},{10,8},{12,14},{14,12},{1,3},{3,1},... | collective-permute-start | bytes 393224 | tf_op jit(solution)/shard_map/ppermute | solution.py:22
  73.5 5.2 %collective-permute-start.6 = (f32[256,128]{1,0:T(8,128)S(1)}, f32[256,128]{1,0:T(8,128)S(1)}, u32[]{:S(2)}, u32[]{:S(2)}) collective-permute-start(f32[256,128]{1,0:T(8,128)S(1)} %dynamic-slice_add_fusion.1), channel_id=1, source_target_pairs={{0,4},{2,6},{4,0},{6,2},{8,12},{10,14},{12,8},{14,10},{1,5},{3,7},... | collective-permute-start | bytes 393224 | tf_op jit(solution)/shard_map/ppermute | solution.py:56
  78.8 8.0 %collective-permute-start.7 = (f32[256,128]{1,0:T(8,128)S(1)}, f32[256,128]{1,0:T(8,128)S(1)}, u32[]{:S(2)}, u32[]{:S(2)}) collective-permute-start(f32[256,128]{1,0:T(8,128)S(1)} %add.481), channel_id=1, source_target_pairs={{0,8},{2,10},{4,12},{6,14},{8,0},{10,2},{12,4},{14,6},{1,9},{3,11}... | collective-permute-start | bytes 393224 | tf_op jit(solution)/shard_map/ppermute | solution.py:56
  86.9 5.0 %collective-permute-start.8 = (f32[256,128]{1,0:T(8,128)S(1)}, f32[256,128]{1,0:T(8,128)S(1)}, u32[]{:S(2)}, u32[]{:S(2)}) collective-permute-start(f32[256,128]{1,0:T(8,128)S(1)} %get-tuple-element.98), channel_id=1, source_target_pairs={{0,2},{2,0},{4,6},{6,4},{8,10},{10,8},{12,14},{14,12},{1,3},{3,1},... | collective-permute-start | bytes 393224 | tf_op jit(solution)/shard_map/ppermute | solution.py:29
  91.9 1.6 %collective-permute-start.9 = (f32[512,128]{1,0:T(8,128)S(1)}, f32[512,128]{1,0:T(8,128)S(1)}, u32[]{:S(2)}, u32[]{:S(2)}) collective-permute-start(f32[512,128]{1,0:T(8,128)S(1)} %constant_dynamic-update-slice_fusion.5), channel_id=1, source_target_pairs={{0,1},{1,0},{2,3},{3,2},{4,5},{5,4},{6,7},{7,6},{8,9},{9,8},{10,11... | collective-permute-start | bytes 786440 | tf_op jit(solution)/shard_map/ppermute | solution.py:29

commit v9 on v8

--- a/solution.py
+++ b/solution.py
@@ -44,10 +44,15 @@
         while bit < count:
             steps.append((axis, bit))
             bit *= 2
-    flat = jnp.concatenate([jnp.ravel(v).astype(jnp.float32) for v in values])
-    unit = 8 * LANES * (2 ** len(steps))
-    total = -(-flat.shape[0] // unit) * unit
-    x = jnp.pad(flat, (0, total - flat.shape[0])).reshape(-1, LANES)
+    blocks = [jnp.reshape(v, (-1, v.shape[-1]) if v.ndim else (1, 1)) for v in values]
+    cols = -(-max(blk.shape[1] for blk in blocks) // LANES) * LANES
+    blocks = [
+        jnp.pad(blk.astype(jnp.float32), ((0, 0), (0, cols - blk.shape[1]))) for blk in blocks
+    ]
+    x = jnp.concatenate(blocks, axis=0)
+    halvings = max(0, len(steps) - EXCHANGED)
+    unit = 8 * (2**halvings)
+    x = jnp.pad(x, ((0, -(-x.shape[0] // unit) * unit - x.shape[0]), (0, 0)))
     halved = steps[: max(0, len(steps) - EXCHANGED)]
     for axis, bit in halved:
         x = halve(x, axis, bit)
@@ -58,12 +63,13 @@
         x = lax.psum(x, tuple(rest))
     for axis, bit in reversed(halved):
         x = double(x, axis, bit)
-    flat = x.reshape(-1)
     out = []
     offset = 0
-    for v in values:
-        out.append(flat[offset : offset + v.size].reshape(v.shape))
-        offset += v.size
+    for v, blk in zip(values, blocks):
+        rows = blk.shape[0]
+        width = v.shape[-1] if v.ndim else 1
+        out.append(x[offset : offset + rows, :width].reshape(v.shape))
+        offset += rows
     return tuple(out)
 
 
@@ -253,8 +259,8 @@
             (tuple(split(v) for v in place), rows_split(depth_flat), rows_split(grad_u)),
         )
         grad_pw, grad_dw = jnp.sum(outs[0], axis=0), jnp.sum(outs[1], axis=0)
-    grad_dw, grad_pw, grad_head, loss_sum = packed_sum(
-        (grad_dw, grad_pw, grad_head, loss_sum), ("lat", "lon")
+    grad_pw, grad_head, grad_dw, loss_sum = packed_sum(
+        (grad_pw, grad_head, grad_dw, loss_sum), ("lat", "lon")
     )
     return (grad_dw, grad_pw, grad_head, (loss_sum / teach_width).reshape(1))
 

time: 98.9 us -> 106 us (1.072)
  local copies, waits for them, and re-layouts: 18 us -> 28.1 us
  waiting for transfers between devices: 27.7 us -> 25.6 us
    dynamic_update_slice x1 -> x2, local copies, waits for them, and re-layouts: 0.02 us -> 5.19 us  [double(): whole = lax.dynamic_update_slice_in_dim(whole, x, upper * rows, 0)]
    dynamic_update_slice x2, local copies, waits for them, and re-layouts: 0.03 us -> 4.72 us  [double(): return lax.dynamic_update_slice_in_dim(whole, got, (1 - upper) * rows, 0)]
    ppermute x2, waiting for transfers between devices: 5.43 us -> 2.48 us  [double(): got = lax.ppermute(x, axis, [(i, i ^ bit) for i in range(count)])]
    reshape x5 -> x0, local copies, waits for them, and re-layouts: 2.1 us -> none  [the longest x3 1.74 us: packed_sum(): out.append(flat[offset:offset + v.size].reshape(v.shape))]
  transfers between devices with their start and end apart: 11 -> 11, of which waited for: 9 -> 8; matrix products, arithmetic and copies ran while one was open for 5% -> 10% of each run, Pallas kernels for 0% -> 0%
where the time goes in v9:
time: 106 us
  local copies, waits for them, and re-layouts  28.1 us (27%)
  waiting for transfers between devices  25.6 us (24%)
  starting transfers between devices  21.6 us (20%)
  other arithmetic  20.8 us (20%)
  matrix products  6.42 us (6%)
  between operations  2.98 us (3%)
    ppermute x2, waiting for transfers between devices, packed_sum(): x = x + lax.ppermute(x, axis, [(i, i ^ bit) for i in range(count)])  10.3 us
    all_to_all x1, starting transfers between devices, local(): lax.all_to_all(send.reshape(slots, TILE, teach_width + 1), ('lon', 'lat')...  7.36 us
    ppermute x2, waiting for transfers between devices, padded_2(): lax.ppermute(tail, axis, [(i, (i + 1) % count) for i in range(ends)])  5.93 us
    gather x1, local copies, waits for them, and re-layouts, gather_windows(): lax.dynamic_slice(padded, (b, h, w, jnp.int32(0)), (1, span, reach, width))  5.73 us
    ppermute x2, waiting for transfers between devices, halve(): return keep + lax.ppermute(send, axis, [(i, i ^ bit) for i in range(count)])  5.41 us
    dynamic_update_slice x2, local copies, waits for them, and re-layouts, double(): whole = lax.dynamic_update_slice_in_dim(whole, x, upper * rows, 0)  5.19 us
    unnamed x22, local copies, waits for them, and re-layouts  5.19 us
    concatenate x1, other arithmetic, padded_2(): jnp.concatenate([lax.ppermute(tail, axis, [(i, (i + 1) % count) for i in...  4.77 us
  transfers between devices with their start and end apart: 11, of which 8 were waited for; matrix products, arithmetic and copies ran while one was open for 10% of the time, Pallas kernels for 0%

profile of v9, /device:TPU:0, one launch (start us, length us, event | category | flops | bytes accessed | tf_op | source)
XLA Modules:
  0.0 105.6 jit_solution(7983160585161218790)
XLA Ops:
  6.7 7.4 %all-to-all-start = ((bf16[32,8,228]{2,1,0:T(8,128)(2,1)}), bf16[32,8,228]{2,1,0:T(8,128)(2,1)S(1)}, u32[]{:S(2)}, u32[]{:S(2)}) async-start(bf16[32,8,228]{2,1,0:T(8,128)(2,1)} %reshape.804), calls=%async_computation | async-start | bytes 262144 | tf_op jit(solution)/shard_map/all_to_all | solution.py:124
  15.5 2.0 %collective-permute-start = (bf16[2,48,4,256]{3,0,2,1:T(2,128)(2,1)S(1)}, bf16[2,48,4,256]{3,0,2,1:T(2,128)(2,1)S(1)}, u32[]{:S(2)}, u32[]{:S(2)}) collective-permute-start(bf16[2,48,4,256]{3,0,2,1:T(2,128)(2,1)S(1)} %copy.538), channel_id=1, source_target_pairs={{0,2},{2,4},{4,6},{6,8},{8,10},{10,12},{12,14},{14,0},{1,3},{3,5},... | collective-permute-start | bytes 589832 | tf_op jit(solution)/shard_map/ppermute | solution.py:84
  17.7 2.9 %collective-permute-start.1 = (bf16[2,48,4,256]{3,0,2,1:T(2,128)(2,1)S(1)}, bf16[2,48,4,256]{3,0,2,1:T(2,128)(2,1)S(1)}, u32[]{:S(2)}, u32[]{:S(2)}) collective-permute-start(bf16[2,48,4,256]{3,0,2,1:T(2,128)(2,1)S(1)} %copy.539), channel_id=1, source_target_pairs={{2,0},{4,2},{6,4},{8,6},{10,8},{12,10},{14,12},{0,14},{3,1},{5,3},... | collective-permute-start | bytes 589832 | tf_op jit(solution)/shard_map/ppermute | solution.py:86
  20.7 5.9 %collective-permute-done = bf16[2,48,4,256]{3,0,2,1:T(2,128)(2,1)S(1)} collective-permute-done((bf16[2,48,4,256]{3,0,2,1:T(2,128)(2,1)S(1)}, bf16[2,48,4,256]{3,0,2,1:T(2,128)(2,1)S(1)}, u32[]{:S(2)}, u32[]{:S(2)}) %collective-permute-start) | collective-permute-done | bytes 196640 | tf_op jit(solution)/shard_map/ppermute | solution.py:84
  26.8 1.7 %constant_dynamic-update-slice_fusion.1 = bf16[2,48,40,256]{3,0,2,1:T(2,128)(2,1)S(1)} fusion(bf16[2,48,40,256]{3,0,2,1:T(2,128)(2,1)S(1)} %constant_dynamic-update-slice_fusion.2, bf16[2,48,32,256]{3,2,1,0:T(8,128)(2,1)S(1)} %copy-done.3), kind=kLoop, calls=%fused_computation.234 | loop fusion | bytes 3145728
  30.7 1.3 %collective-permute-start.2 = (bf16[2,4,40,256]{3,0,2,1:T(2,128)(2,1)S(1)}, bf16[2,4,40,256]{3,0,2,1:T(2,128)(2,1)S(1)}, u32[]{:S(2)}, u32[]{:S(2)}) collective-permute-start(bf16[2,4,40,256]{3,0,2,1:T(2,128)(2,1)S(1)} %get-tuple-element.170), channel_id=1, source_target_pairs={{0,1},{2,3},{4,5},{6,7},{8,9},{10,11},{12,13},{14,15},{16,17},{18,... | collective-permute-start | bytes 491528 | tf_op jit(solution)/shard_map/ppermute | solution.py:84
  35.3 4.8 %pad_maximum_fusion = bf16[2,56,40,256]{3,0,2,1:T(2,128)(2,1)S(1)} fusion(bf16[2,4,40,256]{3,0,2,1:T(2,128)(2,1)S(1)} %collective-permute-done.3, bf16[2,48,40,256]{3,0,2,1:T(2,128)(2,1)} %copy-done.2, bf16[2,4,40,256]{3,0,2,1:T(2,128)(2,1)S(1)} %collective-permute-done.2), kind=kLoop, calls=%fused_computation.1 | loop fusion | flops 2293760 | bytes 4587520 | tf_op jit(solution)/shard_map/concatenate | solution.py:82
  40.1 5.7 %gather_fusion = bf16[32,9,16,256]{3,0,2,1:T(8,128)(2,1)} fusion(bf16[2,56,40,256]{3,0,2,1:T(2,128)(2,1)S(1)} %pad_maximum_fusion, s32[32]{0:T(128)S(1)} %fusion.91), kind=kCustom, calls=%fused_computation | custom fusion | bytes 4719104 | tf_op jit(solution)/shard_map/vmap()/gather | solution.py:157
  45.9 2.5 %slice_convert_fusion.20 = (f32[32,1,8,256]{3,0,2,1:T(8,128)S(1)}, f32[32,1,8,256]{3,0,2,1:T(8,128)S(1)}, f32[32,1,8,256]{3,0,2,1:T(8,128)S(1)}, f32[32,1,8,256]...) fusion(bf16[32,9,16,256]{3,0,2,1:T(8,128)(2,1)} %gather_fusion), kind=kLoop, calls=%fused_computation.176 | loop fusion | flops 1245184 | bytes 7471104 | tf_op jit(solution)/shard_map/convert_element_type | solution.py:163
  50.5 3.9 %fusion.39 = bf16[256,256]{1,0:T(8,128)(2,1)S(1)} fusion(f32[32,1,8,256]{3,2,0,1:T(8,128)S(1)} %copy.414, f32[32,1,8,256]{3,2,0,1:T(8,128)S(1)} %copy.413, f32[32,1,8,256]{3,2,0,1:T(8,128)S(1)} %copy.412, f32[32,1,8,256]{3,2,0,1:T(8,128)S(1)} %copy.411, f32[32,1,8,256]{3,2,0,1:T(8,128)S(1)} %copy.410, f32[32,1,8,256]{3,2,0,1:T(8,128)S(1)} %copy.409, ...), kind=kLoop, calls=%fused_computation.82 | loop fusion | flops 4325376 | bytes 8815616 | tf_op jit(solution)/shard_map/convert_element_type | solution.py:179
  58.2 4.1 %fusion.8 = (f32[256]{0:T(256)S(1)}, f32[256]{0:T(256)S(1)}, f32[256]{0:T(256)S(1)}, f32[256]{0:T(256)S(1)}, f32[256]{0:T(256)S(1)}, /*index=5*/f32[256]{0:T(256...) fusion(f32[32,1,8,256]{3,0,2,1:T(8,128)S(1)} %get-tuple-element, ...), kind=kOutput, calls=%fused_computation.21 | convolution fusion | flops 35909120 | bytes 5261312 | tf_op jit(solution)/shard_map/dot_general | solution.py:197
  62.3 2.9 %fusion.25 = (f32[256]{0:T(256)S(1)}, f32[256]{0:T(256)S(1)}, f32[256]{0:T(256)S(1)}, f32[256]{0:T(256)S(1)}, f32[256]{0:T(256)S(1)}, /*index=5*/f32[256]{0:T(25...) fusion(f32[256,256]{1,0:T(8,128)S(1)} %get-tuple-element.218, ...), kind=kLoop, calls=%fused_computation.55 | loop fusion | flops 1962240 | bytes 4209664 | tf_op jit(solution)/shard_map/reduce_sum | solution.py:210
  65.7 1.3 %collective-permute-done.4 = f32[272,256]{1,0:T(8,128)S(1)} collective-permute-done((f32[272,256]{1,0:T(8,128)S(1)}, f32[272,256]{1,0:T(8,128)S(1)}, u32[]{:S(2)}, u32[]{:S(2)}) %collective-permute-start.4) | collective-permute-done | bytes 278560 | tf_op jit(solution)/shard_map/ppermute | solution.py:22
  67.1 2.1 %collective-permute-start.5 = (f32[136,256]{1,0:T(8,128)S(1)}, f32[136,256]{1,0:T(8,128)S(1)}, u32[]{:S(2)}, u32[]{:S(2)}) collective-permute-start(f32[136,256]{1,0:T(8,128)S(1)} %constant_dynamic-slice_fusion), channel_id=1, source_target_pairs={{0,2},{2,0},{4,6},{6,4},{8,10},{10,8},{12,14},{14,12},{1,3},{3,1},... | collective-permute-start | bytes 417800 | tf_op jit(solution)/shard_map/ppermute | solution.py:22
  69.2 4.1 %collective-permute-done.5 = f32[136,256]{1,0:T(8,128)S(1)} collective-permute-done((f32[136,256]{1,0:T(8,128)S(1)}, f32[136,256]{1,0:T(8,128)S(1)}, u32[]{:S(2)}, u32[]{:S(2)}) %collective-permute-start.5) | collective-permute-done | bytes 139296 | tf_op jit(solution)/shard_map/ppermute | solution.py:22
  73.3 1.5 %collective-permute-start.6 = (f32[136,256]{1,0:T(8,128)S(1)}, f32[136,256]{1,0:T(8,128)S(1)}, u32[]{:S(2)}, u32[]{:S(2)}) collective-permute-start(f32[136,256]{1,0:T(8,128)S(1)} %dynamic-slice_add_fusion), channel_id=1, source_target_pairs={{0,4},{2,6},{4,0},{6,2},{8,12},{10,14},{12,8},{14,10},{1,5},{3,7},... | collective-permute-start | bytes 417800 | tf_op jit(solution)/shard_map/ppermute | solution.py:61
  74.8 3.9 %collective-permute-done.6 = f32[136,256]{1,0:T(8,128)S(1)} collective-permute-done((f32[136,256]{1,0:T(8,128)S(1)}, f32[136,256]{1,0:T(8,128)S(1)}, u32[]{:S(2)}, u32[]{:S(2)}) %collective-permute-start.6) | collective-permute-done | bytes 139296 | tf_op jit(solution)/shard_map/ppermute | solution.py:61
  78.7 2.0 %collective-permute-start.7 = (f32[136,256]{1,0:T(8,128)S(1)}, f32[136,256]{1,0:T(8,128)S(1)}, u32[]{:S(2)}, u32[]{:S(2)}) collective-permute-start(f32[136,256]{1,0:T(8,128)S(1)} %add.485), channel_id=1, source_target_pairs={{0,8},{2,10},{4,12},{6,14},{8,0},{10,2},{12,4},{14,6},{1,9},{3,11}... | collective-permute-start | bytes 417800 | tf_op jit(solution)/shard_map/ppermute | solution.py:61
  80.7 6.4 %collective-permute-done.7 = f32[136,256]{1,0:T(8,128)S(1)} collective-permute-done((f32[136,256]{1,0:T(8,128)S(1)}, f32[136,256]{1,0:T(8,128)S(1)}, u32[]{:S(2)}, u32[]{:S(2)}) %collective-permute-start.7) | collective-permute-done | bytes 139296 | tf_op jit(solution)/shard_map/ppermute | solution.py:61
  88.2 1.5 %dynamic_update_slice.12 = f32[272,256]{0,1:T(8,128)S(1)} dynamic-update-slice(f32[272,256]{0,1:T(8,128)S(1)} %broadcast_in_dim.26, f32[136,256]{0,1:T(8,128)S(1)} %copy.473, s32[]{:T(128)S(6)} %select_n.115, s32[]{:T(128)} %constant.224.clone.1) | dynamic-update-slice | bytes 278532 | tf_op jit(solution)/shard_map/dynamic_update_slice | solution.py:31
  89.8 2.5 %collective-permute-done.8 = f32[136,256]{1,0:T(8,128)S(1)} collective-permute-done((f32[136,256]{1,0:T(8,128)S(1)}, f32[136,256]{1,0:T(8,128)S(1)}, u32[]{:S(2)}, u32[]{:S(2)}) %collective-permute-start.8) | collective-permute-done | bytes 139296 | tf_op jit(solution)/shard_map/ppermute | solution.py:29
  92.4 1.4 %dynamic_update_slice.13 = f32[272,256]{0,1:T(8,128)S(1)} dynamic-update-slice(f32[272,256]{0,1:T(8,128)S(1)} %dynamic_update_slice.12, f32[136,256]{0,1:T(8,128)S(1)} %copy.474, s32[]{:T(128)S(6)} %select_n.116, s32[]{:T(128)} %constant.224.clone.1) | dynamic-update-slice | bytes 278532 | tf_op jit(solution)/shard_map/dynamic_update_slice | solution.py:32
  93.9 3.7 %dynamic_update_slice.14 = f32[544,256]{0,1:T(8,128)S(1)} dynamic-update-slice(f32[544,256]{0,1:T(8,128)S(1)} %broadcast_in_dim.25, f32[272,256]{0,1:T(8,128)S(1)} %dynamic_update_slice.13, s32[]{:T(128)S(6)} %select_n.112, s32[]{:T(128)} %constant.224.clone.1) | dynamic-update-slice | bytes 557060 | tf_op jit(solution)/shard_map/dynamic_update_slice | solution.py:31
  97.6 3.3 %dynamic_update_slice.15 = f32[544,256]{0,1:T(8,128)S(1)} dynamic-update-slice(f32[544,256]{0,1:T(8,128)S(1)} %dynamic_update_slice.14, f32[272,256]{0,1:T(8,128)S(1)} %collective-permute-done.9, s32[]{:T(128)S(6)} %select_n.113, s32[]{:T(128)} %constant.224.clone.1) | dynamic-update-slice | bytes 557060 | tf_op jit(solution)/shard_map/dynamic_update_slice | solution.py:32
  (104 shorter events, 23.9 us)
Async XLA Ops:
  0.6 53.8 %copy-start = (bf16[256,256]{1,0:T(8,128)(2,1)S(1)}, bf16[256,256]{1,0:T(8,128)(2,1)}, u32[]{:S(2)}) copy-start(bf16[256,256]{1,0:T(8,128)(2,1)} %param.18) | copy-start | bytes 393220
  0.6 26.2 %copy-start.3 = (bf16[2,48,32,256]{3,2,1,0:T(8,128)(2,1)S(1)}, bf16[2,48,32,256]{3,2,1,0:T(8,128)(2,1)}, u32[]{:S(2)}) copy-start(bf16[2,48,32,256]{3,2,1,0:T(8,128)(2,1)} %param.15) | copy-start | bytes 4718596
  0.7 19.9 %copy-start.5 = (bf16[9,256]{1,0:T(8,128)(2,1)S(1)}, bf16[9,256]{1,0:T(8,128)(2,1)}, u32[]{:S(2)}) copy-start(bf16[9,256]{1,0:T(8,128)(2,1)} %param.17) | copy-start | bytes 13828
  0.7 19.9 %copy-start.6 = (s32[256]{0:T(256)S(1)}, s32[256]{0:T(256)}, u32[]{:S(2)}) copy-start(s32[256]{0:T(256)} %param.16) | copy-start | bytes 3076
  6.7 26.7 %all-to-all-start = ((bf16[32,8,228]{2,1,0:T(8,128)(2,1)}), bf16[32,8,228]{2,1,0:T(8,128)(2,1)S(1)}, u32[]{:S(2)}, u32[]{:S(2)}) async-start(bf16[32,8,228]{2,1,0:T(8,128)(2,1)} %reshape.804), calls=%async_computation | async-start | bytes 262144 | tf_op jit(solution)/shard_map/all_to_all | solution.py:124
  15.5 11.2 %collective-permute-start = (bf16[2,48,4,256]{3,0,2,1:T(2,128)(2,1)S(1)}, bf16[2,48,4,256]{3,0,2,1:T(2,128)(2,1)S(1)}, u32[]{:S(2)}, u32[]{:S(2)}) collective-permute-start(bf16[2,48,4,256]{3,0,2,1:T(2,128)(2,1)S(1)} %copy.538), channel_id=1, source_target_pairs={{0,2},{2,4},{4,6},{6,8},{8,10},{10,12},{12,14},{14,0},{1,3},{3,5},... | collective-permute-start | bytes 589832 | tf_op jit(solution)/shard_map/ppermute | solution.py:84
  17.7 11.4 %collective-permute-start.1 = (bf16[2,48,4,256]{3,0,2,1:T(2,128)(2,1)S(1)}, bf16[2,48,4,256]{3,0,2,1:T(2,128)(2,1)S(1)}, u32[]{:S(2)}, u32[]{:S(2)}) collective-permute-start(bf16[2,48,4,256]{3,0,2,1:T(2,128)(2,1)S(1)} %copy.539), channel_id=1, source_target_pairs={{2,0},{4,2},{6,4},{8,6},{10,8},{12,10},{14,12},{0,14},{3,1},{5,3},... | collective-permute-start | bytes 589832 | tf_op jit(solution)/shard_map/ppermute | solution.py:86
  29.2 1.3 %copy-start.2 = (bf16[2,48,40,256]{3,0,2,1:T(2,128)(2,1)}, bf16[2,48,40,256]{3,0,2,1:T(2,128)(2,1)S(1)}, u32[]{:S(2)}) copy-start(bf16[2,48,40,256]{3,0,2,1:T(2,128)(2,1)S(1)} %constant_dynamic-update-slice_fusion) | copy-start | bytes 5898244
  30.7 3.7 %collective-permute-start.2 = (bf16[2,4,40,256]{3,0,2,1:T(2,128)(2,1)S(1)}, bf16[2,4,40,256]{3,0,2,1:T(2,128)(2,1)S(1)}, u32[]{:S(2)}, u32[]{:S(2)}) collective-permute-start(bf16[2,4,40,256]{3,0,2,1:T(2,128)(2,1)S(1)} %get-tuple-element.170), channel_id=1, source_target_pairs={{0,1},{2,3},{4,5},{6,7},{8,9},{10,11},{12,13},{14,15},{16,17},{18,... | collective-permute-start | bytes 491528 | tf_op jit(solution)/shard_map/ppermute | solution.py:84
  32.0 3.3 %collective-permute-start.3 = (bf16[2,4,40,256]{3,0,2,1:T(2,128)(2,1)S(1)}, bf16[2,4,40,256]{3,0,2,1:T(2,128)(2,1)S(1)}, u32[]{:S(2)}, u32[]{:S(2)}) collective-permute-start(bf16[2,4,40,256]{3,0,2,1:T(2,128)(2,1)S(1)} %get-tuple-element.171), channel_id=1, source_target_pairs={{1,0},{3,2},{5,4},{7,6},{9,8},{11,10},{13,12},{15,14},{17,16},{19,... | collective-permute-start | bytes 491528 | tf_op jit(solution)/shard_map/ppermute | solution.py:86
  45.9 2.5 %copy-start.1 = (bf16[32,9,16,256]{3,0,2,1:T(8,128)(2,1)S(1)}, bf16[32,9,16,256]{3,0,2,1:T(8,128)(2,1)}, u32[]{:S(2)}) copy-start(bf16[32,9,16,256]{3,0,2,1:T(8,128)(2,1)} %gather_fusion) | copy-start | bytes 7077892
  50.5 4.2 %copy-start.4 = (bf16[256,227]{0,1:T(8,128)(2,1)S(1)}, bf16[256,227]{0,1:T(8,128)(2,1)}, u32[]{:S(2)}) copy-start(bf16[256,227]{0,1:T(8,128)(2,1)} %param.19) | copy-start | bytes 348676
  65.4 1.6 %collective-permute-start.4 = (f32[272,256]{1,0:T(8,128)S(1)}, f32[272,256]{1,0:T(8,128)S(1)}, u32[]{:S(2)}, u32[]{:S(2)}) collective-permute-start(f32[272,256]{1,0:T(8,128)S(1)} %pad_dynamic-slice_fusion), channel_id=1, source_target_pairs={{0,1},{1,0},{2,3},{3,2},{4,5},{5,4},{6,7},{7,6},{8,9},{9,8},{10,11... | collective-permute-start | bytes 835592 | tf_op jit(solution)/shard_map/ppermute | solution.py:22
  67.1 6.2 %collective-permute-start.5 = (f32[136,256]{1,0:T(8,128)S(1)}, f32[136,256]{1,0:T(8,128)S(1)}, u32[]{:S(2)}, u32[]{:S(2)}) collective-permute-start(f32[136,256]{1,0:T(8,128)S(1)} %constant_dynamic-slice_fusion), channel_id=1, source_target_pairs={{0,2},{2,0},{4,6},{6,4},{8,10},{10,8},{12,14},{14,12},{1,3},{3,1},... | collective-permute-start | bytes 417800 | tf_op jit(solution)/shard_map/ppermute | solution.py:22
  73.3 5.4 %collective-permute-start.6 = (f32[136,256]{1,0:T(8,128)S(1)}, f32[136,256]{1,0:T(8,128)S(1)}, u32[]{:S(2)}, u32[]{:S(2)}) collective-permute-start(f32[136,256]{1,0:T(8,128)S(1)} %dynamic-slice_add_fusion), channel_id=1, source_target_pairs={{0,4},{2,6},{4,0},{6,2},{8,12},{10,14},{12,8},{14,10},{1,5},{3,7},... | collective-permute-start | bytes 417800 | tf_op jit(solution)/shard_map/ppermute | solution.py:61
  78.7 8.4 %collective-permute-start.7 = (f32[136,256]{1,0:T(8,128)S(1)}, f32[136,256]{1,0:T(8,128)S(1)}, u32[]{:S(2)}, u32[]{:S(2)}) collective-permute-start(f32[136,256]{1,0:T(8,128)S(1)} %add.485), channel_id=1, source_target_pairs={{0,8},{2,10},{4,12},{6,14},{8,0},{10,2},{12,4},{14,6},{1,9},{3,11}... | collective-permute-start | bytes 417800 | tf_op jit(solution)/shard_map/ppermute | solution.py:61
  87.1 5.1 %collective-permute-start.8 = (f32[136,256]{1,0:T(8,128)S(1)}, f32[136,256]{1,0:T(8,128)S(1)}, u32[]{:S(2)}, u32[]{:S(2)}) collective-permute-start(f32[136,256]{1,0:T(8,128)S(1)} %add.486), channel_id=1, source_target_pairs={{0,2},{2,0},{4,6},{6,4},{8,10},{10,8},{12,14},{14,12},{1,3},{3,1},... | collective-permute-start | bytes 417800 | tf_op jit(solution)/shard_map/ppermute | solution.py:29
  93.8 3.8 %collective-permute-start.9 = (f32[272,256]{0,1:T(8,128)S(1)}, f32[272,256]{0,1:T(8,128)S(1)}, u32[]{:S(2)}, u32[]{:S(2)}) collective-permute-start(f32[272,256]{0,1:T(8,128)S(1)} %dynamic_update_slice.13), channel_id=1, source_target_pairs={{0,1},{1,0},{2,3},{3,2},{4,5},{5,4},{6,7},{7,6},{8,9},{9,8},{10,11... | collective-permute-start | bytes 835592 | tf_op jit(solution)/shard_map/ppermute | solution.py:29

commit v10 on v8

--- a/solution.py
+++ b/solution.py
@@ -1,6 +1,8 @@
 import jax
 import jax.numpy as jnp
 from jax import lax
+from jax.experimental import pallas as pl
+from jax.experimental.pallas import tpu as pltpu
 from jax.sharding import PartitionSpec as P
 
 DMAX = 4
@@ -11,6 +13,55 @@
 
 LANES = 128
 EXCHANGED = 2
+
+
+def tap_list():
+    taps = [(0, 0)]
+    for dilation in range(1, DMAX + 1):
+        for tap_index in range(9):
+            if tap_index == 4:
+                continue
+            taps.append(((tap_index // 3 - 1) * dilation, (tap_index % 3 - 1) * dilation))
+    return taps
+
+def conv_kernel(win_ref, coef_ref, out_ref):
+    taps = tap_list()
+    def body(s, carry):
+        acc = None
+        for i, (rs, cs) in enumerate(taps):
+            term = coef_ref[i : i + 1, :] * win_ref[s, DMAX + rs, pl.ds(DMAX + cs, TILE), :]
+            acc = term if acc is None else acc + term
+        out_ref[s] = acc
+        return carry
+    lax.fori_loop(0, win_ref.shape[0], body, 0)
+
+def taps_conv(win, coef):
+    slots, _, _, width = win.shape
+    return pl.pallas_call(
+        conv_kernel,
+        out_shape=jax.ShapeDtypeStruct((slots, TILE, width), jnp.float32),
+        in_specs=[pl.BlockSpec(memory_space=pltpu.VMEM)] * 2,
+        out_specs=pl.BlockSpec(memory_space=pltpu.VMEM),
+    )(win, coef)
+
+def grad_kernel(win_ref, gz_ref, out_ref):
+    taps = tap_list()
+    out_ref[...] = jnp.zeros_like(out_ref)
+    def body(s, carry):
+        gz = gz_ref[s]
+        for i, (rs, cs) in enumerate(taps):
+            out_ref[i] += win_ref[s, DMAX + rs, pl.ds(DMAX + cs, TILE), :] * gz
+        return carry
+    lax.fori_loop(0, win_ref.shape[0], body, 0)
+
+def taps_grad(win, gz):
+    slots, _, _, width = win.shape
+    return pl.pallas_call(
+        grad_kernel,
+        out_shape=jax.ShapeDtypeStruct((len(tap_list()), TILE, width), jnp.float32),
+        in_specs=[pl.BlockSpec(memory_space=pltpu.VMEM)] * 2,
+        out_specs=pl.BlockSpec(memory_space=pltpu.VMEM),
+    )(win, gz)
 
 
 def halve(x, axis, bit):
@@ -158,18 +209,16 @@
             jnp.float32
         )
 
+    coef_rows = [kernel[4]]
+    for dilation in range(1, DMAX + 1):
+        for tap_index in range(9):
+            if tap_index != 4:
+                coef_rows.append(kernel[tap_index] * onehot[dilation - 1])
+    coef = jnp.stack(coef_rows)
+
     def forward(windows, tiles, weight):
         center = shifted(windows, 0, 0)
-        accum_sum = center * kernel[4]
-        for dilation in range(1, DMAX + 1):
-            for tap_index in range(9):
-                if tap_index == 4:
-                    continue
-                row_shift = (tap_index // 3 - 1) * dilation
-                col_shift = (tap_index % 3 - 1) * dilation
-                accum_sum = accum_sum + kernel[tap_index] * onehot[dilation - 1] * shifted(
-                    windows, row_shift, col_shift
-                )
+        accum_sum = taps_conv(windows.astype(jnp.float32), coef)
         depth_flat = accum_sum.astype(jnp.bfloat16).reshape(-1, width)
         preact = jnp.dot(depth_flat, pw_weight, preferred_element_type=jnp.float32)
         y_rows = (center.reshape(-1, width) + jax.nn.silu(preact)).astype(jnp.bfloat16)
@@ -190,19 +239,22 @@
         )
         grad_z = jnp.dot(grad_u, pw_weight.T, preferred_element_type=jnp.float32)
         grad_z = grad_z.reshape(windows.shape[0], TILE, width)
+        parts = jnp.sum(taps_grad(windows.astype(jnp.float32), grad_z), axis=1)
         tap_sums = []
+        row = 1
+        rows_of = {}
+        for dilation in range(1, DMAX + 1):
+            for tap_index in range(9):
+                if tap_index != 4:
+                    rows_of[(dilation, tap_index)] = row
+                    row += 1
         for tap_index in range(9):
             if tap_index == 4:
-                part = shifted(windows, 0, 0) * grad_z
-                tap_sums.append(jnp.sum(part.reshape(-1, width), axis=0))
+                tap_sums.append(parts[0])
                 continue
             tap_sum = jnp.zeros((width,), jnp.float32)
             for dilation in range(1, DMAX + 1):
-                row_shift = (tap_index // 3 - 1) * dilation
-                col_shift = (tap_index % 3 - 1) * dilation
-                part = shifted(windows, row_shift, col_shift) * grad_z
-                part = jnp.sum(part.reshape(-1, width), axis=0)
-                tap_sum = tap_sum + onehot[dilation - 1] * part
+                tap_sum = tap_sum + onehot[dilation - 1] * parts[rows_of[(dilation, tap_index)]]
             tap_sums.append(tap_sum)
         return pw_part, jnp.stack(tap_sums, axis=0)
 

time: 98.9 us -> 105 us (1.062)
  Pallas kernels: 0 us -> 10.1 us
  waiting for transfers between devices: 27.7 us -> 24.6 us
  matrix products: 6.43 us -> 4.22 us
  local copies, waits for them, and re-layouts: 18 us -> 19.5 us
    pallas_call x0 -> x2, Pallas kernels: none -> 10.1 us  [the longest x1 5.25 us: taps_conv(): pl.pallas_call(conv_kernel, out_shape=jax.ShapeDtypeStruct((slots, TILE,...]
    convert_element_type x1 -> x2, other arithmetic: 3.9 us -> 8.83 us  [the longest x1 5.32 us: forward(): accum_sum = taps_conv(windows.astype(jnp.float32), coef)]
    convert_element_type x4 -> x1, other arithmetic: 3.86 us -> 0.02 us  [shifted(): source[:, DMAX + row_shift, DMAX + col_shift:DMAX + col_shift + TILE, :]]
    dot_general x1, matrix products: 4.11 us -> 0.95 us  [backward(): grad_z = jnp.dot(grad_u, pw_weight.T, preferred_element_type=jnp.float32)]
    another operation x0 -> x1, local copies, waits for them, and re-layouts: none -> 3.05 us  [local(): coef = jnp.stack(coef_rows)]
    ppermute x2, waiting for transfers between devices: 5.92 us -> 2.88 us  [padded_2(): lax.ppermute(tail, axis, [(i, (i + 1) % count) for i in range(ends)])]
    reduce_sum x1, other arithmetic: 2.86 us -> 1.03 us  [backward(): parts = jnp.sum(taps_grad(windows.astype(jnp.float32), grad_z), axis=1)]
    convert_element_type x10 -> x0, local copies, waits for them, and re-layouts: 1.57 us -> none  [shifted(): source[:, DMAX + row_shift, DMAX + col_shift:DMAX + col_shift + TILE, :]]
  transfers between devices with their start and end apart: 11 -> 11, of which waited for: 9 -> 9; matrix products, arithmetic and copies ran while one was open for 5% -> 8% of each run, Pallas kernels for 0% -> 0%
where the time goes in v10:
time: 105 us; the launch traced here: 104 us
  waiting for transfers between devices  24.6 us (23%)
  starting transfers between devices  22.2 us (21%)
  other arithmetic  20.6 us (20%)
  local copies, waits for them, and re-layouts  19.5 us (19%)
  Pallas kernels  10.1 us (10%)
  matrix products  4.22 us (4%)
  between operations  2.88 us (3%)
    ppermute x2, waiting for transfers between devices, packed_sum(): x = x + lax.ppermute(x, axis, [(i, i ^ bit) for i in range(count)])  9.85 us
    all_to_all x1, starting transfers between devices, local(): lax.all_to_all(send.reshape(slots, TILE, teach_width + 1), ('lon', 'lat')...  7.36 us
    gather x1, local copies, waits for them, and re-layouts, gather_windows(): lax.dynamic_slice(padded, (b, h, w, jnp.int32(0)), (1, span, reach, width))  5.76 us
    ppermute x2, waiting for transfers between devices, double(): got = lax.ppermute(x, axis, [(i, i ^ bit) for i in range(count)])  5.42 us
    convert_element_type x1, other arithmetic, forward(): accum_sum = taps_conv(windows.astype(jnp.float32), coef)  5.32 us
    pallas_call x1, Pallas kernels, taps_conv(): pl.pallas_call(conv_kernel, out_shape=jax.ShapeDtypeStruct((slots, TILE,...  5.25 us
    ppermute x2, waiting for transfers between devices, halve(): return keep + lax.ppermute(send, axis, [(i, i ^ bit) for i in range(count)])  5.18 us
    pallas_call x1, Pallas kernels, taps_grad(): pl.pallas_call(grad_kernel, out_shape=jax.ShapeDtypeStruct((len(tap_list(...  4.85 us
  transfers between devices with their start and end apart: 11, of which 9 were waited for; matrix products, arithmetic and copies ran while one was open for 8% of the time, Pallas kernels for 0%

profile of v10, /device:TPU:0, one launch (start us, length us, event | category | flops | bytes accessed | tf_op | source)
XLA Modules:
  0.0 104.1 jit_solution(12136675894688073682)
XLA Ops:
  6.7 7.4 %all-to-all-start = ((bf16[32,8,228]{2,1,0:T(8,128)(2,1)}), bf16[32,8,228]{2,1,0:T(8,128)(2,1)S(1)}, u32[]{:S(2)}, u32[]{:S(2)}) async-start(bf16[32,8,228]{2,1,0:T(8,128)(2,1)} %reshape.254), calls=%async_computation | async-start | bytes 262144 | tf_op jit(solution)/shard_map/all_to_all | solution.py:169
  14.0 1.3 %fusion.56 = (bf16[2,48,4,256]{3,2,1,0:T(4,128)(2,1)S(1)}, bf16[2,48,4,256]{3,2,1,0:T(4,128)(2,1)S(1)}) fusion(bf16[2,48,32,256]{3,2,1,0:T(8,128)(2,1)} %param.15), kind=kLoop, calls=%fused_computation.186 | loop fusion | bytes 786432 | tf_op jit(solution)/shard_map/slice | solution.py:125
  15.5 2.0 %collective-permute-start = (bf16[2,48,4,256]{3,0,2,1:T(2,128)(2,1)S(1)}, bf16[2,48,4,256]{3,0,2,1:T(2,128)(2,1)S(1)}, u32[]{:S(2)}, u32[]{:S(2)}) collective-permute-start(bf16[2,48,4,256]{3,0,2,1:T(2,128)(2,1)S(1)} %copy.89), channel_id=1, source_target_pairs={{0,2},{2,4},{4,6},{6,8},{8,10},{10,12},{12,14},{14,0},{1,3},{3,5},... | collective-permute-start | bytes 589832 | tf_op jit(solution)/shard_map/ppermute | solution.py:129
  17.7 2.9 %collective-permute-start.1 = (bf16[2,48,4,256]{3,0,2,1:T(2,128)(2,1)S(1)}, bf16[2,48,4,256]{3,0,2,1:T(2,128)(2,1)S(1)}, u32[]{:S(2)}, u32[]{:S(2)}) collective-permute-start(bf16[2,48,4,256]{3,0,2,1:T(2,128)(2,1)S(1)} %copy.90), channel_id=1, source_target_pairs={{2,0},{4,2},{6,4},{8,6},{10,8},{12,10},{14,12},{0,14},{3,1},{5,3},... | collective-permute-start | bytes 589832 | tf_op jit(solution)/shard_map/ppermute | solution.py:131
  20.7 3.1 %stack.4.coef_ref = f32[33,256]{1,0:T(8,128)} concatenate(f32[1,256]{1,0:T(1,128)S(1)} %slice.401, f32[1,256]{1,0:T(1,128)S(1)} %get-tuple-element.113, f32[1,256]{1,0:T(1,128)S(1)} %get-tuple-element.112, f32[1,256]{1,0:T(1,128)S(1)} %get-tuple-element.111, f32[1,256]{1,0:T(1,128)S(1)} %get-tuple-element.110, f32[1,256]{1,0:T(1,128)S(1)} %get-tuple-element.108, ...), dimensions={0} | concatenate | bytes 67584 | tf_op jit(solution)/shard_map/stack | solution.py:217
  23.8 2.9 %collective-permute-done = bf16[2,48,4,256]{3,0,2,1:T(2,128)(2,1)S(1)} collective-permute-done((bf16[2,48,4,256]{3,0,2,1:T(2,128)(2,1)S(1)}, bf16[2,48,4,256]{3,0,2,1:T(2,128)(2,1)S(1)}, u32[]{:S(2)}, u32[]{:S(2)}) %collective-permute-start) | collective-permute-done | bytes 196640 | tf_op jit(solution)/shard_map/ppermute | solution.py:129
  26.8 1.7 %constant_dynamic-update-slice_fusion.1 = bf16[2,48,40,256]{3,0,2,1:T(2,128)(2,1)S(1)} fusion(bf16[2,48,40,256]{3,0,2,1:T(2,128)(2,1)S(1)} %constant_dynamic-update-slice_fusion.2, bf16[2,48,32,256]{3,2,1,0:T(8,128)(2,1)S(1)} %copy-done.3), kind=kLoop, calls=%fused_computation.49 | loop fusion | bytes 3145728
  29.2 1.3 %copy-done.2 = bf16[2,48,40,256]{3,0,2,1:T(2,128)(2,1)} copy-done((bf16[2,48,40,256]{3,0,2,1:T(2,128)(2,1)}, bf16[2,48,40,256]{3,0,2,1:T(2,128)(2,1)S(1)}, u32[]{:S(2)}) %copy-start.2) | copy-done | bytes 1966104
  30.8 1.3 %collective-permute-start.2 = (bf16[2,4,40,256]{3,0,2,1:T(2,128)(2,1)S(1)}, bf16[2,4,40,256]{3,0,2,1:T(2,128)(2,1)S(1)}, u32[]{:S(2)}, u32[]{:S(2)}) collective-permute-start(bf16[2,4,40,256]{3,0,2,1:T(2,128)(2,1)S(1)} %get-tuple-element.69), channel_id=1, source_target_pairs={{0,1},{2,3},{4,5},{6,7},{8,9},{10,11},{12,13},{14,15},{16,17},{18,... | collective-permute-start | bytes 491528 | tf_op jit(solution)/shard_map/ppermute | solution.py:129
  32.1 1.5 %collective-permute-start.3 = (bf16[2,4,40,256]{3,0,2,1:T(2,128)(2,1)S(1)}, bf16[2,4,40,256]{3,0,2,1:T(2,128)(2,1)S(1)}, u32[]{:S(2)}, u32[]{:S(2)}) collective-permute-start(bf16[2,4,40,256]{3,0,2,1:T(2,128)(2,1)S(1)} %get-tuple-element.70), channel_id=1, source_target_pairs={{1,0},{3,2},{5,4},{7,6},{9,8},{11,10},{13,12},{15,14},{17,16},{19,... | collective-permute-start | bytes 491528 | tf_op jit(solution)/shard_map/ppermute | solution.py:131
  35.4 4.6 %pad_maximum_fusion = bf16[2,56,40,256]{3,0,2,1:T(2,128)(2,1)S(1)} fusion(bf16[2,4,40,256]{3,0,2,1:T(2,128)(2,1)S(1)} %collective-permute-done.3, bf16[2,48,40,256]{3,0,2,1:T(2,128)(2,1)} %copy-done.2, bf16[2,4,40,256]{3,0,2,1:T(2,128)(2,1)S(1)} %collective-permute-done.2), kind=kLoop, calls=%fused_computation.3 | loop fusion | flops 2293760 | bytes 4587520 | tf_op jit(solution)/shard_map/concatenate | solution.py:127
  40.0 5.8 %gather_fusion = bf16[32,9,16,256]{3,0,2,1:T(8,128)(2,1)} fusion(bf16[2,56,40,256]{3,0,2,1:T(2,128)(2,1)S(1)} %pad_maximum_fusion, s32[32]{0:T(128)S(1)} %fusion.54), kind=kCustom, calls=%fused_computation | custom fusion | bytes 4719104 | tf_op jit(solution)/shard_map/vmap()/gather | solution.py:202
  45.7 5.3 %copy_convert_fusion.1.win_ref = f32[32,9,16,256]{3,2,1,0:T(8,128)} fusion(bf16[32,9,16,256]{3,0,2,1:T(8,128)(2,1)} %gather_fusion), kind=kLoop, calls=%fused_computation.2 | loop fusion | flops 1179648 | bytes 7077888 | tf_op jit(solution)/shard_map/convert_element_type | solution.py:221
  51.1 5.2 %shard_map.120 = f32[32,8,256]{2,1,0:T(8,128)} custom-call(f32[32,9,16,256]{3,2,1,0:T(8,128)} %copy_convert_fusion.1.win_ref, f32[33,256]{1,0:T(8,128)} %stack.4.coef_ref), custom_call_target="tpu_custom_call" | custom-call | tf_op jit(solution)/shard_map/pallas_call | solution.py:40
  59.0 3.5 %copy_convert_fusion.win_ref = f32[32,9,16,256]{3,2,1,0:T(8,128)} fusion(bf16[32,9,16,256]{3,0,2,1:T(8,128)(2,1)S(1)} %copy-done.1), kind=kLoop, calls=%fused_computation.1 | loop fusion | flops 1179648 | bytes 7077888 | tf_op jit(solution)/shard_map/convert_element_type | solution.py:242
  63.5 4.8 %shard_map.121 = f32[33,8,256]{2,1,0:T(8,128)} custom-call(f32[32,9,16,256]{3,2,1,0:T(8,128)} %copy_convert_fusion.win_ref, f32[32,8,256]{2,1,0:T(8,128)} %convolution_bitcast_fusion.1.gz_ref), custom_call_target="tpu_custom_call" | custom-call | tf_op jit(solution)/shard_map/pallas_call | solution.py:59
  72.9 2.1 %collective-permute-start.5 = (f32[256,128]{1,0:T(8,128)S(1)}, f32[256,128]{1,0:T(8,128)S(1)}, u32[]{:S(2)}, u32[]{:S(2)}) collective-permute-start(f32[256,128]{1,0:T(8,128)S(1)} %constant_dynamic-slice_fusion), channel_id=1, source_target_pairs={{0,2},{2,0},{4,6},{6,4},{8,10},{10,8},{12,14},{14,12},{1,3},{3,1},... | collective-permute-start | bytes 393224 | tf_op jit(solution)/shard_map/ppermute | solution.py:73
  75.0 4.0 %collective-permute-done.5 = f32[256,128]{1,0:T(8,128)S(1)} collective-permute-done((f32[256,128]{1,0:T(8,128)S(1)}, f32[256,128]{1,0:T(8,128)S(1)}, u32[]{:S(2)}, u32[]{:S(2)}) %collective-permute-start.5) | collective-permute-done | bytes 131104 | tf_op jit(solution)/shard_map/ppermute | solution.py:73
  79.1 1.5 %collective-permute-start.6 = (f32[256,128]{1,0:T(8,128)S(1)}, f32[256,128]{1,0:T(8,128)S(1)}, u32[]{:S(2)}, u32[]{:S(2)}) collective-permute-start(f32[256,128]{1,0:T(8,128)S(1)} %dynamic-slice_add_fusion.1), channel_id=1, source_target_pairs={{0,4},{2,6},{4,0},{6,2},{8,12},{10,14},{12,8},{14,10},{1,5},{3,7},... | collective-permute-start | bytes 393224 | tf_op jit(solution)/shard_map/ppermute | solution.py:107
  80.6 3.8 %collective-permute-done.6 = f32[256,128]{1,0:T(8,128)S(1)} collective-permute-done((f32[256,128]{1,0:T(8,128)S(1)}, f32[256,128]{1,0:T(8,128)S(1)}, u32[]{:S(2)}, u32[]{:S(2)}) %collective-permute-start.6) | collective-permute-done | bytes 131104 | tf_op jit(solution)/shard_map/ppermute | solution.py:107
  84.4 2.0 %collective-permute-start.7 = (f32[256,128]{1,0:T(8,128)S(1)}, f32[256,128]{1,0:T(8,128)S(1)}, u32[]{:S(2)}, u32[]{:S(2)}) collective-permute-start(f32[256,128]{1,0:T(8,128)S(1)} %add.321), channel_id=1, source_target_pairs={{0,8},{2,10},{4,12},{6,14},{8,0},{10,2},{12,4},{14,6},{1,9},{3,11}... | collective-permute-start | bytes 393224 | tf_op jit(solution)/shard_map/ppermute | solution.py:107
  86.4 6.1 %collective-permute-done.7 = f32[256,128]{1,0:T(8,128)S(1)} collective-permute-done((f32[256,128]{1,0:T(8,128)S(1)}, f32[256,128]{1,0:T(8,128)S(1)}, u32[]{:S(2)}, u32[]{:S(2)}) %collective-permute-start.7) | collective-permute-done | bytes 131104 | tf_op jit(solution)/shard_map/ppermute | solution.py:107
  93.6 4.0 %collective-permute-done.8 = f32[256,128]{1,0:T(8,128)S(1)} collective-permute-done((f32[256,128]{1,0:T(8,128)S(1)}, f32[256,128]{1,0:T(8,128)S(1)}, u32[]{:S(2)}, u32[]{:S(2)}) %collective-permute-start.8) | collective-permute-done | bytes 131104 | tf_op jit(solution)/shard_map/ppermute | solution.py:80
  97.7 1.4 %collective-permute-done.9 = f32[512,128]{1,0:T(8,128)S(1)} collective-permute-done((f32[512,128]{1,0:T(8,128)S(1)}, f32[512,128]{1,0:T(8,128)S(1)}, u32[]{:S(2)}, u32[]{:S(2)}) %collective-permute-start.9) | collective-permute-done | bytes 262176 | tf_op jit(solution)/shard_map/ppermute | solution.py:80
  (98 shorter events, 21.9 us)
Async XLA Ops:
  0.6 55.7 %copy-start = (bf16[256,256]{1,0:T(8,128)(2,1)S(1)}, bf16[256,256]{1,0:T(8,128)(2,1)}, u32[]{:S(2)}) copy-start(bf16[256,256]{1,0:T(8,128)(2,1)} %param.18) | copy-start | bytes 393220
  0.6 26.2 %copy-start.3 = (bf16[2,48,32,256]{3,2,1,0:T(8,128)(2,1)S(1)}, bf16[2,48,32,256]{3,2,1,0:T(8,128)(2,1)}, u32[]{:S(2)}) copy-start(bf16[2,48,32,256]{3,2,1,0:T(8,128)(2,1)} %param.15) | copy-start | bytes 4718596
  0.7 19.9 %copy-start.6 = (bf16[9,256]{1,0:T(8,128)(2,1)S(1)}, bf16[9,256]{1,0:T(8,128)(2,1)}, u32[]{:S(2)}) copy-start(bf16[9,256]{1,0:T(8,128)(2,1)} %param.17) | copy-start | bytes 13828
  0.7 19.9 %copy-start.7 = (s32[256]{0:T(256)S(1)}, s32[256]{0:T(256)}, u32[]{:S(2)}) copy-start(s32[256]{0:T(256)} %param.16) | copy-start | bytes 3076
  6.7 26.9 %all-to-all-start = ((bf16[32,8,228]{2,1,0:T(8,128)(2,1)}), bf16[32,8,228]{2,1,0:T(8,128)(2,1)S(1)}, u32[]{:S(2)}, u32[]{:S(2)}) async-start(bf16[32,8,228]{2,1,0:T(8,128)(2,1)} %reshape.254), calls=%async_computation | async-start | bytes 262144 | tf_op jit(solution)/shard_map/all_to_all | solution.py:169
  15.5 11.2 %collective-permute-start = (bf16[2,48,4,256]{3,0,2,1:T(2,128)(2,1)S(1)}, bf16[2,48,4,256]{3,0,2,1:T(2,128)(2,1)S(1)}, u32[]{:S(2)}, u32[]{:S(2)}) collective-permute-start(bf16[2,48,4,256]{3,0,2,1:T(2,128)(2,1)S(1)} %copy.89), channel_id=1, source_target_pairs={{0,2},{2,4},{4,6},{6,8},{8,10},{10,12},{12,14},{14,0},{1,3},{3,5},... | collective-permute-start | bytes 589832 | tf_op jit(solution)/shard_map/ppermute | solution.py:129
  17.7 11.4 %collective-permute-start.1 = (bf16[2,48,4,256]{3,0,2,1:T(2,128)(2,1)S(1)}, bf16[2,48,4,256]{3,0,2,1:T(2,128)(2,1)S(1)}, u32[]{:S(2)}, u32[]{:S(2)}) collective-permute-start(bf16[2,48,4,256]{3,0,2,1:T(2,128)(2,1)S(1)} %copy.90), channel_id=1, source_target_pairs={{2,0},{4,2},{6,4},{8,6},{10,8},{12,10},{14,12},{0,14},{3,1},{5,3},... | collective-permute-start | bytes 589832 | tf_op jit(solution)/shard_map/ppermute | solution.py:131
  29.2 1.3 %copy-start.2 = (bf16[2,48,40,256]{3,0,2,1:T(2,128)(2,1)}, bf16[2,48,40,256]{3,0,2,1:T(2,128)(2,1)S(1)}, u32[]{:S(2)}) copy-start(bf16[2,48,40,256]{3,0,2,1:T(2,128)(2,1)S(1)} %constant_dynamic-update-slice_fusion) | copy-start | bytes 5898244
  30.8 3.9 %collective-permute-start.2 = (bf16[2,4,40,256]{3,0,2,1:T(2,128)(2,1)S(1)}, bf16[2,4,40,256]{3,0,2,1:T(2,128)(2,1)S(1)}, u32[]{:S(2)}, u32[]{:S(2)}) collective-permute-start(bf16[2,4,40,256]{3,0,2,1:T(2,128)(2,1)S(1)} %get-tuple-element.69), channel_id=1, source_target_pairs={{0,1},{2,3},{4,5},{6,7},{8,9},{10,11},{12,13},{14,15},{16,17},{18,... | collective-permute-start | bytes 491528 | tf_op jit(solution)/shard_map/ppermute | solution.py:129
  32.1 3.3 %collective-permute-start.3 = (bf16[2,4,40,256]{3,0,2,1:T(2,128)(2,1)S(1)}, bf16[2,4,40,256]{3,0,2,1:T(2,128)(2,1)S(1)}, u32[]{:S(2)}, u32[]{:S(2)}) collective-permute-start(bf16[2,4,40,256]{3,0,2,1:T(2,128)(2,1)S(1)} %get-tuple-element.70), channel_id=1, source_target_pairs={{1,0},{3,2},{5,4},{7,6},{9,8},{11,10},{13,12},{15,14},{17,16},{19,... | collective-permute-start | bytes 491528 | tf_op jit(solution)/shard_map/ppermute | solution.py:131
  45.7 5.3 %copy-start.1 = (bf16[32,9,16,256]{3,0,2,1:T(8,128)(2,1)S(1)}, bf16[32,9,16,256]{3,0,2,1:T(8,128)(2,1)}, u32[]{:S(2)}) copy-start(bf16[32,9,16,256]{3,0,2,1:T(8,128)(2,1)} %gather_fusion) | copy-start | bytes 7077892
  51.1 6.5 %copy-start.5 = (bf16[256,227]{0,1:T(8,128)(2,1)S(1)}, bf16[256,227]{0,1:T(8,128)(2,1)}, u32[]{:S(2)}) copy-start(bf16[256,227]{0,1:T(8,128)(2,1)} %param.19) | copy-start | bytes 348676
  63.5 6.0 %copy-start.4 = (f32[32,8,256]{2,1,0:T(8,128)S(1)}, f32[32,8,256]{2,1,0:T(8,128)}, u32[]{:S(2)}) copy-start(f32[32,8,256]{2,1,0:T(8,128)} %shard_map.120) | copy-start | bytes 786436
  71.2 1.6 %collective-permute-start.4 = (f32[512,128]{1,0:T(8,128)S(1)}, f32[512,128]{1,0:T(8,128)S(1)}, u32[]{:S(2)}, u32[]{:S(2)}) collective-permute-start(f32[512,128]{1,0:T(8,128)S(1)} %constant_dynamic-slice_fusion.1), channel_id=1, source_target_pairs={{0,1},{1,0},{2,3},{3,2},{4,5},{5,4},{6,7},{7,6},{8,9},{9,8},{10,11... | collective-permute-start | bytes 786440 | tf_op jit(solution)/shard_map/ppermute | solution.py:73
  72.9 6.1 %collective-permute-start.5 = (f32[256,128]{1,0:T(8,128)S(1)}, f32[256,128]{1,0:T(8,128)S(1)}, u32[]{:S(2)}, u32[]{:S(2)}) collective-permute-start(f32[256,128]{1,0:T(8,128)S(1)} %constant_dynamic-slice_fusion), channel_id=1, source_target_pairs={{0,2},{2,0},{4,6},{6,4},{8,10},{10,8},{12,14},{14,12},{1,3},{3,1},... | collective-permute-start | bytes 393224 | tf_op jit(solution)/shard_map/ppermute | solution.py:73
  79.1 5.3 %collective-permute-start.6 = (f32[256,128]{1,0:T(8,128)S(1)}, f32[256,128]{1,0:T(8,128)S(1)}, u32[]{:S(2)}, u32[]{:S(2)}) collective-permute-start(f32[256,128]{1,0:T(8,128)S(1)} %dynamic-slice_add_fusion.1), channel_id=1, source_target_pairs={{0,4},{2,6},{4,0},{6,2},{8,12},{10,14},{12,8},{14,10},{1,5},{3,7},... | collective-permute-start | bytes 393224 | tf_op jit(solution)/shard_map/ppermute | solution.py:107
  84.4 8.1 %collective-permute-start.7 = (f32[256,128]{1,0:T(8,128)S(1)}, f32[256,128]{1,0:T(8,128)S(1)}, u32[]{:S(2)}, u32[]{:S(2)}) collective-permute-start(f32[256,128]{1,0:T(8,128)S(1)} %add.321), channel_id=1, source_target_pairs={{0,8},{2,10},{4,12},{6,14},{8,0},{10,2},{12,4},{14,6},{1,9},{3,11}... | collective-permute-start | bytes 393224 | tf_op jit(solution)/shard_map/ppermute | solution.py:107
  92.5 5.0 %collective-permute-start.8 = (f32[256,128]{1,0:T(8,128)S(1)}, f32[256,128]{1,0:T(8,128)S(1)}, u32[]{:S(2)}, u32[]{:S(2)}) collective-permute-start(f32[256,128]{1,0:T(8,128)S(1)} %get-tuple-element.65), channel_id=1, source_target_pairs={{0,2},{2,0},{4,6},{6,4},{8,10},{10,8},{12,14},{14,12},{1,3},{3,1},... | collective-permute-start | bytes 393224 | tf_op jit(solution)/shard_map/ppermute | solution.py:80
  97.6 1.6 %collective-permute-start.9 = (f32[512,128]{1,0:T(8,128)S(1)}, f32[512,128]{1,0:T(8,128)S(1)}, u32[]{:S(2)}, u32[]{:S(2)}) collective-permute-start(f32[512,128]{1,0:T(8,128)S(1)} %constant_dynamic-update-slice_fusion.5), channel_id=1, source_target_pairs={{0,1},{1,0},{2,3},{3,2},{4,5},{5,4},{6,7},{7,6},{8,9},{9,8},{10,11... | collective-permute-start | bytes 786440 | tf_op jit(solution)/shard_map/ppermute | solution.py:80

commit v11 on v8

--- a/solution.py
+++ b/solution.py
@@ -104,11 +104,11 @@
     slot_index = destination * CAP + slot_rank
     slots = devices * CAP
     base = 64
-    column = jnp.zeros((tiles_here, TILE, 1), jnp.float32)
-    column = column.at[:, 0, 0].set((tile_start // base).astype(jnp.float32))
-    column = column.at[:, 1, 0].set((tile_start % base).astype(jnp.float32))
-    column = column.at[:, 2, 0].set(tile_count.astype(jnp.float32))
-    packed = jnp.concatenate([teacher_tiles, column.astype(jnp.bfloat16)], axis=2)
+    blank = jnp.zeros_like(tile_count)
+    column = jnp.stack(
+        [tile_start // base, tile_start % base, tile_count] + [blank] * (TILE - 3), axis=1
+    )
+    packed = jnp.concatenate([teacher_tiles, column.astype(jnp.bfloat16)[:, :, None]], axis=2)
     chooser = (slot_index[None, :] == jnp.arange(slots, dtype=jnp.int32)[:, None]).astype(
         jnp.bfloat16
     )

time: 98.9 us -> 98.5 us (level)
    scatter x2 -> x0, other arithmetic: 1.33 us -> none  [the longest x1 0.67 us: local(): column = column.at[:, 1, 0].set((tile_start % base).astype(jnp.float32))]
where the time goes in v11:
time: 98.5 us; the launch traced here: 98.1 us
  waiting for transfers between devices  27.8 us (28%)
  starting transfers between devices  21.8 us (22%)
  other arithmetic  20.8 us (21%)
  local copies, waits for them, and re-layouts  18.3 us (19%)
  matrix products  6.42 us (7%)
  between operations  2.98 us (3%)
    ppermute x2, waiting for transfers between devices, packed_sum(): x = x + lax.ppermute(x, axis, [(i, i ^ bit) for i in range(count)])  9.77 us
    all_to_all x1, starting transfers between devices, local(): lax.all_to_all(send.reshape(slots, TILE, teach_width + 1), ('lon', 'lat')...  7.36 us
    ppermute x2, waiting for transfers between devices, padded_2(): lax.ppermute(tail, axis, [(i, (i + 1) % count) for i in range(ends)])  5.92 us
    gather x1, local copies, waits for them, and re-layouts, gather_windows(): lax.dynamic_slice(padded, (b, h, w, jnp.int32(0)), (1, span, reach, width))  5.74 us
    ppermute x2, waiting for transfers between devices, double(): got = lax.ppermute(x, axis, [(i, i ^ bit) for i in range(count)])  5.46 us
    ppermute x2, waiting for transfers between devices, halve(): return keep + lax.ppermute(send, axis, [(i, i ^ bit) for i in range(count)])  5.23 us
    concatenate x1, other arithmetic, padded_2(): jnp.concatenate([lax.ppermute(tail, axis, [(i, (i + 1) % count) for i in...  4.77 us
    unnamed x22, local copies, waits for them, and re-layouts  4.62 us
  transfers between devices with their start and end apart: 11, of which 9 were waited for; matrix products, arithmetic and copies ran while one was open for 5% of the time, Pallas kernels for 0%

profile of v11, /device:TPU:0, one launch (start us, length us, event | category | flops | bytes accessed | tf_op | source)
XLA Modules:
  0.0 98.1 jit_solution(6952034299203904824)
XLA Ops:
  6.2 7.4 %all-to-all-start = ((bf16[32,8,228]{2,1,0:T(8,128)(2,1)}), bf16[32,8,228]{2,1,0:T(8,128)(2,1)S(1)}, u32[]{:S(2)}, u32[]{:S(2)}) async-start(bf16[32,8,228]{2,1,0:T(8,128)(2,1)} %reshape.794), calls=%async_computation | async-start | bytes 262144 | tf_op jit(solution)/shard_map/all_to_all | solution.py:118
  13.6 1.3 %fusion.93 = (bf16[2,48,4,256]{3,2,1,0:T(4,128)(2,1)S(1)}, bf16[2,48,4,256]{3,2,1,0:T(4,128)(2,1)S(1)}) fusion(bf16[2,48,32,256]{3,2,1,0:T(8,128)(2,1)} %param.9), kind=kLoop, calls=%fused_computation.326 | loop fusion | bytes 786432 | tf_op jit(solution)/shard_map/slice | solution.py:74
  15.1 2.0 %collective-permute-start = (bf16[2,48,4,256]{3,0,2,1:T(2,128)(2,1)S(1)}, bf16[2,48,4,256]{3,0,2,1:T(2,128)(2,1)S(1)}, u32[]{:S(2)}, u32[]{:S(2)}) collective-permute-start(bf16[2,48,4,256]{3,0,2,1:T(2,128)(2,1)S(1)} %copy.608), channel_id=1, source_target_pairs={{0,2},{2,4},{4,6},{6,8},{8,10},{10,12},{12,14},{14,0},{1,3},{3,5},... | collective-permute-start | bytes 589832 | tf_op jit(solution)/shard_map/ppermute | solution.py:78
  17.3 2.9 %collective-permute-start.1 = (bf16[2,48,4,256]{3,0,2,1:T(2,128)(2,1)S(1)}, bf16[2,48,4,256]{3,0,2,1:T(2,128)(2,1)S(1)}, u32[]{:S(2)}, u32[]{:S(2)}) collective-permute-start(bf16[2,48,4,256]{3,0,2,1:T(2,128)(2,1)S(1)} %copy.609), channel_id=1, source_target_pairs={{2,0},{4,2},{6,4},{8,6},{10,8},{12,10},{14,12},{0,14},{3,1},{5,3},... | collective-permute-start | bytes 589832 | tf_op jit(solution)/shard_map/ppermute | solution.py:80
  20.3 5.9 %collective-permute-done = bf16[2,48,4,256]{3,0,2,1:T(2,128)(2,1)S(1)} collective-permute-done((bf16[2,48,4,256]{3,0,2,1:T(2,128)(2,1)S(1)}, bf16[2,48,4,256]{3,0,2,1:T(2,128)(2,1)S(1)}, u32[]{:S(2)}, u32[]{:S(2)}) %collective-permute-start) | collective-permute-done | bytes 196640 | tf_op jit(solution)/shard_map/ppermute | solution.py:78
  26.4 1.7 %constant_dynamic-update-slice_fusion.1 = bf16[2,48,40,256]{3,0,2,1:T(2,128)(2,1)S(1)} fusion(bf16[2,48,40,256]{3,0,2,1:T(2,128)(2,1)S(1)} %constant_dynamic-update-slice_fusion.2, bf16[2,48,32,256]{3,2,1,0:T(8,128)(2,1)S(1)} %copy-done.3), kind=kLoop, calls=%fused_computation.238 | loop fusion | bytes 3145728
  28.8 1.3 %copy-done.2 = bf16[2,48,40,256]{3,0,2,1:T(2,128)(2,1)} copy-done((bf16[2,48,40,256]{3,0,2,1:T(2,128)(2,1)}, bf16[2,48,40,256]{3,0,2,1:T(2,128)(2,1)S(1)}, u32[]{:S(2)}) %copy-start.2) | copy-done | bytes 1966104
  30.3 1.3 %collective-permute-start.2 = (bf16[2,4,40,256]{3,0,2,1:T(2,128)(2,1)S(1)}, bf16[2,4,40,256]{3,0,2,1:T(2,128)(2,1)S(1)}, u32[]{:S(2)}, u32[]{:S(2)}) collective-permute-start(bf16[2,4,40,256]{3,0,2,1:T(2,128)(2,1)S(1)} %get-tuple-element.136), channel_id=1, source_target_pairs={{0,1},{2,3},{4,5},{6,7},{8,9},{10,11},{12,13},{14,15},{16,17},{18,... | collective-permute-start | bytes 491528 | tf_op jit(solution)/shard_map/ppermute | solution.py:78
  31.6 1.3 %collective-permute-start.3 = (bf16[2,4,40,256]{3,0,2,1:T(2,128)(2,1)S(1)}, bf16[2,4,40,256]{3,0,2,1:T(2,128)(2,1)S(1)}, u32[]{:S(2)}, u32[]{:S(2)}) collective-permute-start(bf16[2,4,40,256]{3,0,2,1:T(2,128)(2,1)S(1)} %get-tuple-element.137), channel_id=1, source_target_pairs={{1,0},{3,2},{5,4},{7,6},{9,8},{11,10},{13,12},{15,14},{17,16},{19,... | collective-permute-start | bytes 491528 | tf_op jit(solution)/shard_map/ppermute | solution.py:80
  34.9 4.8 %pad_maximum_fusion = bf16[2,56,40,256]{3,0,2,1:T(2,128)(2,1)S(1)} fusion(bf16[2,4,40,256]{3,0,2,1:T(2,128)(2,1)S(1)} %collective-permute-done.3, bf16[2,48,40,256]{3,0,2,1:T(2,128)(2,1)} %copy-done.2, bf16[2,4,40,256]{3,0,2,1:T(2,128)(2,1)S(1)} %collective-permute-done.2), kind=kLoop, calls=%fused_computation.1 | loop fusion | flops 2293760 | bytes 4587520 | tf_op jit(solution)/shard_map/concatenate | solution.py:76
  39.7 5.7 %gather_fusion = bf16[32,9,16,256]{3,0,2,1:T(8,128)(2,1)} fusion(bf16[2,56,40,256]{3,0,2,1:T(2,128)(2,1)S(1)} %pad_maximum_fusion, s32[32]{0:T(128)S(1)} %fusion.91), kind=kCustom, calls=%fused_computation | custom fusion | bytes 4719104 | tf_op jit(solution)/shard_map/vmap()/gather | solution.py:151
  45.4 2.5 %slice_convert_fusion.20 = (f32[32,1,8,256]{3,0,2,1:T(8,128)S(1)}, f32[32,1,8,256]{3,0,2,1:T(8,128)S(1)}, f32[32,1,8,256]{3,0,2,1:T(8,128)S(1)}, f32[32,1,8,256]...) fusion(bf16[32,9,16,256]{3,0,2,1:T(8,128)(2,1)} %gather_fusion), kind=kLoop, calls=%fused_computation.179 | loop fusion | flops 1245184 | bytes 7471104 | tf_op jit(solution)/shard_map/convert_element_type | solution.py:157
  50.0 3.9 %fusion.39 = bf16[256,256]{1,0:T(8,128)(2,1)S(1)} fusion(f32[32,1,8,256]{3,2,0,1:T(8,128)S(1)} %copy.486, f32[32,1,8,256]{3,2,0,1:T(8,128)S(1)} %copy.485, f32[32,1,8,256]{3,2,0,1:T(8,128)S(1)} %copy.484, f32[32,1,8,256]{3,2,0,1:T(8,128)S(1)} %copy.483, f32[32,1,8,256]{3,2,0,1:T(8,128)S(1)} %copy.482, f32[32,1,8,256]{3,2,0,1:T(8,128)S(1)} %copy.481, ...), kind=kLoop, calls=%fused_computation.85 | loop fusion | flops 4325376 | bytes 8815616 | tf_op jit(solution)/shard_map/convert_element_type | solution.py:173
  57.1 4.1 %fusion.8 = (f32[256]{0:T(256)S(1)}, f32[256]{0:T(256)S(1)}, f32[256]{0:T(256)S(1)}, f32[256]{0:T(256)S(1)}, f32[256]{0:T(256)S(1)}, /*index=5*/f32[256]{0:T(256...) fusion(f32[32,1,8,256]{3,0,2,1:T(8,128)S(1)} %get-tuple-element, ...), kind=kOutput, calls=%fused_computation.24 | convolution fusion | flops 35909120 | bytes 5261312 | tf_op jit(solution)/shard_map/dot_general | solution.py:191
  61.2 2.9 %fusion.25 = (f32[256]{0:T(256)S(1)}, f32[256]{0:T(256)S(1)}, f32[256]{0:T(256)S(1)}, f32[256]{0:T(256)S(1)}, f32[256]{0:T(256)S(1)}, /*index=5*/f32[256]{0:T(25...) fusion(f32[256,256]{1,0:T(8,128)S(1)} %get-tuple-element.188, ...), kind=kLoop, calls=%fused_computation.58 | loop fusion | flops 1962240 | bytes 4209664 | tf_op jit(solution)/shard_map/reduce_sum | solution.py:204
  65.7 1.3 %collective-permute-done.4 = f32[512,128]{1,0:T(8,128)S(1)} collective-permute-done((f32[512,128]{1,0:T(8,128)S(1)}, f32[512,128]{1,0:T(8,128)S(1)}, u32[]{:S(2)}, u32[]{:S(2)}) %collective-permute-start.4) | collective-permute-done | bytes 262176 | tf_op jit(solution)/shard_map/ppermute | solution.py:22
  67.1 2.1 %collective-permute-start.5 = (f32[256,128]{1,0:T(8,128)S(1)}, f32[256,128]{1,0:T(8,128)S(1)}, u32[]{:S(2)}, u32[]{:S(2)}) collective-permute-start(f32[256,128]{1,0:T(8,128)S(1)} %constant_dynamic-slice_fusion), channel_id=1, source_target_pairs={{0,2},{2,0},{4,6},{6,4},{8,10},{10,8},{12,14},{14,12},{1,3},{3,1},... | collective-permute-start | bytes 393224 | tf_op jit(solution)/shard_map/ppermute | solution.py:22
  69.2 3.9 %collective-permute-done.5 = f32[256,128]{1,0:T(8,128)S(1)} collective-permute-done((f32[256,128]{1,0:T(8,128)S(1)}, f32[256,128]{1,0:T(8,128)S(1)}, u32[]{:S(2)}, u32[]{:S(2)}) %collective-permute-start.5) | collective-permute-done | bytes 131104 | tf_op jit(solution)/shard_map/ppermute | solution.py:22
  73.1 1.5 %collective-permute-start.6 = (f32[256,128]{1,0:T(8,128)S(1)}, f32[256,128]{1,0:T(8,128)S(1)}, u32[]{:S(2)}, u32[]{:S(2)}) collective-permute-start(f32[256,128]{1,0:T(8,128)S(1)} %dynamic-slice_add_fusion.1), channel_id=1, source_target_pairs={{0,4},{2,6},{4,0},{6,2},{8,12},{10,14},{12,8},{14,10},{1,5},{3,7},... | collective-permute-start | bytes 393224 | tf_op jit(solution)/shard_map/ppermute | solution.py:56
  74.6 3.8 %collective-permute-done.6 = f32[256,128]{1,0:T(8,128)S(1)} collective-permute-done((f32[256,128]{1,0:T(8,128)S(1)}, f32[256,128]{1,0:T(8,128)S(1)}, u32[]{:S(2)}, u32[]{:S(2)}) %collective-permute-start.6) | collective-permute-done | bytes 131104 | tf_op jit(solution)/shard_map/ppermute | solution.py:56
  78.4 2.0 %collective-permute-start.7 = (f32[256,128]{1,0:T(8,128)S(1)}, f32[256,128]{1,0:T(8,128)S(1)}, u32[]{:S(2)}, u32[]{:S(2)}) collective-permute-start(f32[256,128]{1,0:T(8,128)S(1)} %add.473), channel_id=1, source_target_pairs={{0,8},{2,10},{4,12},{6,14},{8,0},{10,2},{12,4},{14,6},{1,9},{3,11}... | collective-permute-start | bytes 393224 | tf_op jit(solution)/shard_map/ppermute | solution.py:56
  80.4 6.0 %collective-permute-done.7 = f32[256,128]{1,0:T(8,128)S(1)} collective-permute-done((f32[256,128]{1,0:T(8,128)S(1)}, f32[256,128]{1,0:T(8,128)S(1)}, u32[]{:S(2)}, u32[]{:S(2)}) %collective-permute-start.7) | collective-permute-done | bytes 131104 | tf_op jit(solution)/shard_map/ppermute | solution.py:56
  87.5 4.0 %collective-permute-done.8 = f32[256,128]{1,0:T(8,128)S(1)} collective-permute-done((f32[256,128]{1,0:T(8,128)S(1)}, f32[256,128]{1,0:T(8,128)S(1)}, u32[]{:S(2)}, u32[]{:S(2)}) %collective-permute-start.8) | collective-permute-done | bytes 131104 | tf_op jit(solution)/shard_map/ppermute | solution.py:29
  91.7 1.4 %collective-permute-done.9 = f32[512,128]{1,0:T(8,128)S(1)} collective-permute-done((f32[512,128]{1,0:T(8,128)S(1)}, f32[512,128]{1,0:T(8,128)S(1)}, u32[]{:S(2)}, u32[]{:S(2)}) %collective-permute-start.9) | collective-permute-done | bytes 262176 | tf_op jit(solution)/shard_map/ppermute | solution.py:29
  (108 shorter events, 20.2 us)
Async XLA Ops:
  0.6 53.3 %copy-start = (bf16[256,256]{1,0:T(8,128)(2,1)S(1)}, bf16[256,256]{1,0:T(8,128)(2,1)}, u32[]{:S(2)}) copy-start(bf16[256,256]{1,0:T(8,128)(2,1)} %param.12) | copy-start | bytes 393220
  0.6 25.7 %copy-start.3 = (bf16[2,48,32,256]{3,2,1,0:T(8,128)(2,1)S(1)}, bf16[2,48,32,256]{3,2,1,0:T(8,128)(2,1)}, u32[]{:S(2)}) copy-start(bf16[2,48,32,256]{3,2,1,0:T(8,128)(2,1)} %param.9) | copy-start | bytes 4718596
  0.7 19.5 %copy-start.5 = (bf16[9,256]{1,0:T(8,128)(2,1)S(1)}, bf16[9,256]{1,0:T(8,128)(2,1)}, u32[]{:S(2)}) copy-start(bf16[9,256]{1,0:T(8,128)(2,1)} %param.11) | copy-start | bytes 13828
  0.7 19.5 %copy-start.6 = (s32[256]{0:T(256)S(1)}, s32[256]{0:T(256)}, u32[]{:S(2)}) copy-start(s32[256]{0:T(256)} %param.10) | copy-start | bytes 3076
  6.2 26.7 %all-to-all-start = ((bf16[32,8,228]{2,1,0:T(8,128)(2,1)}), bf16[32,8,228]{2,1,0:T(8,128)(2,1)S(1)}, u32[]{:S(2)}, u32[]{:S(2)}) async-start(bf16[32,8,228]{2,1,0:T(8,128)(2,1)} %reshape.794), calls=%async_computation | async-start | bytes 262144 | tf_op jit(solution)/shard_map/all_to_all | solution.py:118
  15.1 11.2 %collective-permute-start = (bf16[2,48,4,256]{3,0,2,1:T(2,128)(2,1)S(1)}, bf16[2,48,4,256]{3,0,2,1:T(2,128)(2,1)S(1)}, u32[]{:S(2)}, u32[]{:S(2)}) collective-permute-start(bf16[2,48,4,256]{3,0,2,1:T(2,128)(2,1)S(1)} %copy.608), channel_id=1, source_target_pairs={{0,2},{2,4},{4,6},{6,8},{8,10},{10,12},{12,14},{14,0},{1,3},{3,5},... | collective-permute-start | bytes 589832 | tf_op jit(solution)/shard_map/ppermute | solution.py:78
  17.3 11.4 %collective-permute-start.1 = (bf16[2,48,4,256]{3,0,2,1:T(2,128)(2,1)S(1)}, bf16[2,48,4,256]{3,0,2,1:T(2,128)(2,1)S(1)}, u32[]{:S(2)}, u32[]{:S(2)}) collective-permute-start(bf16[2,48,4,256]{3,0,2,1:T(2,128)(2,1)S(1)} %copy.609), channel_id=1, source_target_pairs={{2,0},{4,2},{6,4},{8,6},{10,8},{12,10},{14,12},{0,14},{3,1},{5,3},... | collective-permute-start | bytes 589832 | tf_op jit(solution)/shard_map/ppermute | solution.py:80
  28.8 1.3 %copy-start.2 = (bf16[2,48,40,256]{3,0,2,1:T(2,128)(2,1)}, bf16[2,48,40,256]{3,0,2,1:T(2,128)(2,1)S(1)}, u32[]{:S(2)}) copy-start(bf16[2,48,40,256]{3,0,2,1:T(2,128)(2,1)S(1)} %constant_dynamic-update-slice_fusion) | copy-start | bytes 5898244
  30.3 3.7 %collective-permute-start.2 = (bf16[2,4,40,256]{3,0,2,1:T(2,128)(2,1)S(1)}, bf16[2,4,40,256]{3,0,2,1:T(2,128)(2,1)S(1)}, u32[]{:S(2)}, u32[]{:S(2)}) collective-permute-start(bf16[2,4,40,256]{3,0,2,1:T(2,128)(2,1)S(1)} %get-tuple-element.136), channel_id=1, source_target_pairs={{0,1},{2,3},{4,5},{6,7},{8,9},{10,11},{12,13},{14,15},{16,17},{18,... | collective-permute-start | bytes 491528 | tf_op jit(solution)/shard_map/ppermute | solution.py:78
  31.6 3.3 %collective-permute-start.3 = (bf16[2,4,40,256]{3,0,2,1:T(2,128)(2,1)S(1)}, bf16[2,4,40,256]{3,0,2,1:T(2,128)(2,1)S(1)}, u32[]{:S(2)}, u32[]{:S(2)}) collective-permute-start(bf16[2,4,40,256]{3,0,2,1:T(2,128)(2,1)S(1)} %get-tuple-element.137), channel_id=1, source_target_pairs={{1,0},{3,2},{5,4},{7,6},{9,8},{11,10},{13,12},{15,14},{17,16},{19,... | collective-permute-start | bytes 491528 | tf_op jit(solution)/shard_map/ppermute | solution.py:80
  45.4 2.5 %copy-start.1 = (bf16[32,9,16,256]{3,0,2,1:T(8,128)(2,1)S(1)}, bf16[32,9,16,256]{3,0,2,1:T(8,128)(2,1)}, u32[]{:S(2)}) copy-start(bf16[32,9,16,256]{3,0,2,1:T(8,128)(2,1)} %gather_fusion) | copy-start | bytes 7077892
  50.0 4.2 %copy-start.4 = (bf16[256,227]{0,1:T(8,128)(2,1)S(1)}, bf16[256,227]{0,1:T(8,128)(2,1)}, u32[]{:S(2)}) copy-start(bf16[256,227]{0,1:T(8,128)(2,1)} %param.13) | copy-start | bytes 348676
  65.4 1.6 %collective-permute-start.4 = (f32[512,128]{1,0:T(8,128)S(1)}, f32[512,128]{1,0:T(8,128)S(1)}, u32[]{:S(2)}, u32[]{:S(2)}) collective-permute-start(f32[512,128]{1,0:T(8,128)S(1)} %constant_dynamic-slice_fusion.1), channel_id=1, source_target_pairs={{0,1},{1,0},{2,3},{3,2},{4,5},{5,4},{6,7},{7,6},{8,9},{9,8},{10,11... | collective-permute-start | bytes 786440 | tf_op jit(solution)/shard_map/ppermute | solution.py:22
  67.1 6.0 %collective-permute-start.5 = (f32[256,128]{1,0:T(8,128)S(1)}, f32[256,128]{1,0:T(8,128)S(1)}, u32[]{:S(2)}, u32[]{:S(2)}) collective-permute-start(f32[256,128]{1,0:T(8,128)S(1)} %constant_dynamic-slice_fusion), channel_id=1, source_target_pairs={{0,2},{2,0},{4,6},{6,4},{8,10},{10,8},{12,14},{14,12},{1,3},{3,1},... | collective-permute-start | bytes 393224 | tf_op jit(solution)/shard_map/ppermute | solution.py:22
  73.1 5.2 %collective-permute-start.6 = (f32[256,128]{1,0:T(8,128)S(1)}, f32[256,128]{1,0:T(8,128)S(1)}, u32[]{:S(2)}, u32[]{:S(2)}) collective-permute-start(f32[256,128]{1,0:T(8,128)S(1)} %dynamic-slice_add_fusion.1), channel_id=1, source_target_pairs={{0,4},{2,6},{4,0},{6,2},{8,12},{10,14},{12,8},{14,10},{1,5},{3,7},... | collective-permute-start | bytes 393224 | tf_op jit(solution)/shard_map/ppermute | solution.py:56
  78.4 8.1 %collective-permute-start.7 = (f32[256,128]{1,0:T(8,128)S(1)}, f32[256,128]{1,0:T(8,128)S(1)}, u32[]{:S(2)}, u32[]{:S(2)}) collective-permute-start(f32[256,128]{1,0:T(8,128)S(1)} %add.473), channel_id=1, source_target_pairs={{0,8},{2,10},{4,12},{6,14},{8,0},{10,2},{12,4},{14,6},{1,9},{3,11}... | collective-permute-start | bytes 393224 | tf_op jit(solution)/shard_map/ppermute | solution.py:56
  86.5 5.0 %collective-permute-start.8 = (f32[256,128]{1,0:T(8,128)S(1)}, f32[256,128]{1,0:T(8,128)S(1)}, u32[]{:S(2)}, u32[]{:S(2)}) collective-permute-start(f32[256,128]{1,0:T(8,128)S(1)} %get-tuple-element.66), channel_id=1, source_target_pairs={{0,2},{2,0},{4,6},{6,4},{8,10},{10,8},{12,14},{14,12},{1,3},{3,1},... | collective-permute-start | bytes 393224 | tf_op jit(solution)/shard_map/ppermute | solution.py:29
  91.5 1.6 %collective-permute-start.9 = (f32[512,128]{1,0:T(8,128)S(1)}, f32[512,128]{1,0:T(8,128)S(1)}, u32[]{:S(2)}, u32[]{:S(2)}) collective-permute-start(f32[512,128]{1,0:T(8,128)S(1)} %constant_dynamic-update-slice_fusion.5), channel_id=1, source_target_pairs={{0,1},{1,0},{2,3},{3,2},{4,5},{5,4},{6,7},{7,6},{8,9},{9,8},{10,11... | collective-permute-start | bytes 786440 | tf_op jit(solution)/shard_map/ppermute | solution.py:29

commit v12 on v11

--- a/solution.py
+++ b/solution.py
@@ -94,7 +94,6 @@
     lon_count = lax.axis_size("lon")
     devices = lon_count * lat_count
     lon_padded = padded_2(acts, (("lon", 2),), DMAX, True)
-    padded = padded_2(lon_padded, (("lat", 1),), DMAX, False)
     tiles_here = teacher_tiles.shape[0]
     destination = tile_dest[:, 0]
     positions = jnp.arange(tiles_here, dtype=jnp.int32)
@@ -115,6 +114,8 @@
     send = jnp.dot(
         chooser, packed.reshape(tiles_here, -1), preferred_element_type=jnp.float32
     ).astype(jnp.bfloat16)
+    send, lon_padded = lax.optimization_barrier((send, lon_padded))
+    padded = padded_2(lon_padded, (("lat", 1),), DMAX, False)
     recv = lax.all_to_all(
         send.reshape(slots, TILE, teach_width + 1),
         ("lon", "lat"),

time: 98.5 us -> 119 us (1.21)
  local copies, waits for them, and re-layouts: 18.3 us -> 30.4 us
  other arithmetic: 20.8 us -> 31.8 us
  starting transfers between devices: 21.8 us -> 16.2 us
  waiting for transfers between devices: 27.8 us -> 31.3 us
    convert_element_type x10, local copies, waits for them, and re-layouts: 1.57 us -> 8.64 us  [shifted(): source[:, DMAX + row_shift, DMAX + col_shift:DMAX + col_shift + TILE, :]]
    ppermute x2, waiting for transfers between devices: 5.92 us -> 1.66 us  [padded_2(): lax.ppermute(tail, axis, [(i, (i + 1) % count) for i in range(ends)])]
    convert_element_type x1, other arithmetic: 3.9 us -> 7.16 us  [forward(): depth_flat = accum_sum.astype(jnp.bfloat16).reshape(-1, width)]
    all_to_all x1, waiting for transfers between devices: 0.01 us -> 3.12 us  [local(): lax.all_to_all(send.reshape(slots, TILE, teach_width + 1), ('lon', 'lat')...]
    ppermute x2, starting transfers between devices: 3.52 us -> 0.55 us  [packed_sum(): x = x + lax.ppermute(x, axis, [(i, i ^ bit) for i in range(count)])]
    concatenate x1 -> x2, other arithmetic: 4.77 us -> 7.61 us  [padded_2(): jnp.concatenate([lax.ppermute(tail, axis, [(i, (i + 1) % count) for i in...]
    convert_element_type x4, other arithmetic: 3.86 us -> 6.42 us  [shifted(): source[:, DMAX + row_shift, DMAX + col_shift:DMAX + col_shift + TILE, :]]
    mul x4, other arithmetic: 0.05 us -> 2.51 us  [forward(): kernel[tap_index] * onehot[dilation - 1]]
  transfers between devices with their start and end apart: 11 -> 11, of which waited for: 9 -> 9; matrix products, arithmetic and copies ran while one was open for 5% -> 8% of each run, Pallas kernels for 0% -> 0%
where the time goes in v12:
time: 119 us
  other arithmetic  31.8 us (27%)
  waiting for transfers between devices  31.3 us (26%)
  local copies, waits for them, and re-layouts  30.4 us (26%)
  starting transfers between devices  16.2 us (14%)
  matrix products  6.12 us (5%)
  between operations  3.01 us (3%)
    ppermute x2, waiting for transfers between devices, packed_sum(): x = x + lax.ppermute(x, axis, [(i, i ^ bit) for i in range(count)])  11.5 us
    convert_element_type x10, local copies, waits for them, and re-layouts, shifted(): source[:, DMAX + row_shift, DMAX + col_shift:DMAX + col_shift + TILE, :]  8.64 us
    concatenate x2, other arithmetic, padded_2(): jnp.concatenate([lax.ppermute(tail, axis, [(i, (i + 1) % count) for i in...  7.61 us
    convert_element_type x1, other arithmetic, forward(): depth_flat = accum_sum.astype(jnp.bfloat16).reshape(-1, width)  7.16 us
    ppermute x2, waiting for transfers between devices, halve(): return keep + lax.ppermute(send, axis, [(i, i ^ bit) for i in range(count)])  7.01 us
    convert_element_type x4, other arithmetic, shifted(): source[:, DMAX + row_shift, DMAX + col_shift:DMAX + col_shift + TILE, :]  6.42 us
    all_to_all x1, starting transfers between devices, local(): lax.all_to_all(send.reshape(slots, TILE, teach_width + 1), ('lon', 'lat')...  6.04 us
    unnamed x37, local copies, waits for them, and re-layouts  5.98 us
  transfers between devices with their start and end apart: 11, of which 9 were waited for; matrix products, arithmetic and copies ran while one was open for 8% of the time, Pallas kernels for 0%

profile of v12, /device:TPU:0, one launch (start us, length us, event | category | flops | bytes accessed | tf_op | source)
XLA Modules:
  0.0 118.8 jit_solution(3043819191441170966)
XLA Ops:
  0.7 3.1 %copy.473 = bf16[2,48,32,256]{3,0,2,1:T(2,128)(2,1)S(1)} copy(bf16[2,48,32,256]{3,2,1,0:T(8,128)(2,1)} %param.9) | data formatting | bytes 3145728 | tf_op args[0]
  4.1 3.0 %collective-permute-start = (bf16[2,48,4,256]{3,0,2,1:T(2,128)(2,1)S(1)}, bf16[2,48,4,256]{3,0,2,1:T(2,128)(2,1)S(1)}, u32[]{:S(2)}, u32[]{:S(2)}) collective-permute-start(bf16[2,48,4,256]{3,0,2,1:T(2,128)(2,1)S(1)} %get-tuple-element.142), channel_id=1, source_target_pairs={{0,2},{2,4},{4,6},{6,8},{8,10},{10,12},{12,14},{14,0},{1,3},{3,5},... | collective-permute-start | bytes 589832 | tf_op jit(solution)/shard_map/ppermute | solution.py:78
  7.1 3.1 %collective-permute-start.1 = (bf16[2,48,4,256]{3,0,2,1:T(2,128)(2,1)S(1)}, bf16[2,48,4,256]{3,0,2,1:T(2,128)(2,1)S(1)}, u32[]{:S(2)}, u32[]{:S(2)}) collective-permute-start(bf16[2,48,4,256]{3,0,2,1:T(2,128)(2,1)S(1)} %get-tuple-element.143), channel_id=1, source_target_pairs={{2,0},{4,2},{6,4},{8,6},{10,8},{12,10},{14,12},{0,14},{3,1},{5,3},... | collective-permute-start | bytes 589832 | tf_op jit(solution)/shard_map/ppermute | solution.py:80
  13.8 1.7 %collective-permute-done = bf16[2,48,4,256]{3,0,2,1:T(2,128)(2,1)S(1)} collective-permute-done((bf16[2,48,4,256]{3,0,2,1:T(2,128)(2,1)S(1)}, bf16[2,48,4,256]{3,0,2,1:T(2,128)(2,1)S(1)}, u32[]{:S(2)}, u32[]{:S(2)}) %collective-permute-start) | collective-permute-done | bytes 196640 | tf_op jit(solution)/shard_map/ppermute | solution.py:78
  15.5 2.2 %collective-permute-done.1 = bf16[2,48,4,256]{3,0,2,1:T(2,128)(2,1)S(1)} collective-permute-done((bf16[2,48,4,256]{3,0,2,1:T(2,128)(2,1)S(1)}, bf16[2,48,4,256]{3,0,2,1:T(2,128)(2,1)S(1)}, u32[]{:S(2)}, u32[]{:S(2)}) %collective-permute-start.1) | collective-permute-done | bytes 196640 | tf_op jit(solution)/shard_map/ppermute | solution.py:80
  17.7 2.8 %pad_maximum_fusion.1 = bf16[2,48,40,256]{3,0,2,1:T(2,128)(2,1)S(1)} fusion(bf16[2,48,4,256]{3,0,2,1:T(2,128)(2,1)S(1)} %collective-permute-done.1, bf16[2,48,32,256]{3,0,2,1:T(2,128)(2,1)S(1)} %copy.473, bf16[2,48,4,256]{3,0,2,1:T(2,128)(2,1)S(1)} %collective-permute-done), kind=kLoop, calls=%fused_computation.3 | loop fusion | flops 1966080 | bytes 3932160 | tf_op jit(solution)/shard_map/concatenate | solution.py:76
  26.1 6.0 %all-to-all-start = ((bf16[32,8,228]{2,1,0:T(8,128)(2,1)}), bf16[32,8,228]{2,1,0:T(8,128)(2,1)S(1)}, u32[]{:S(2)}, u32[]{:S(2)}) async-start(bf16[32,8,228]{2,1,0:T(8,128)(2,1)} %reshape.794), calls=%async_computation | async-start | bytes 262144 | tf_op jit(solution)/shard_map/all_to_all | solution.py:119
  32.2 4.8 %pad_maximum_fusion = bf16[2,56,40,256]{3,0,2,1:T(2,128)(2,1)S(1)} fusion(bf16[2,4,40,256]{3,0,2,1:T(2,128)(2,1)S(1)} %collective-permute-done.3, bf16[2,48,40,256]{3,0,2,1:T(2,128)(2,1)} %copy-done.2, bf16[2,4,40,256]{3,0,2,1:T(2,128)(2,1)S(1)} %collective-permute-done.2), kind=kLoop, calls=%fused_computation.1 | loop fusion | flops 2293760 | bytes 4587520 | tf_op jit(solution)/shard_map/concatenate | solution.py:76
  37.0 3.1 %all-to-all-done = bf16[32,8,228]{2,1,0:T(8,128)(2,1)S(1)} async-done(((bf16[32,8,228]{2,1,0:T(8,128)(2,1)}), bf16[32,8,228]{2,1,0:T(8,128)(2,1)S(1)}, u32[]{:S(2)}, u32[]{:S(2)}) %all-to-all-start) | async-done | bytes 116768 | tf_op jit(solution)/shard_map/all_to_all | solution.py:119
  40.9 5.7 %gather_fusion = bf16[32,9,16,256]{3,0,2,1:T(8,128)(2,1)} fusion(bf16[2,56,40,256]{3,0,2,1:T(2,128)(2,1)S(1)} %pad_maximum_fusion, s32[32]{0:T(128)S(1)} %fusion.91), kind=kCustom, calls=%fused_computation | custom fusion | bytes 4719104 | tf_op jit(solution)/shard_map/vmap()/gather | solution.py:152
  46.6 3.9 %slice_convert_fusion.20 = (f32[32,1,8,256]{3,0,2,1:T(8,128)S(1)}, f32[32,1,8,256]{3,0,2,1:T(8,128)S(1)}, f32[32,1,8,256]{3,0,2,1:T(8,128)S(1)}, f32[32,1,8,256]...) fusion(bf16[32,9,16,256]{3,0,2,1:T(8,128)(2,1)} %gather_fusion), kind=kLoop, calls=%fused_computation.180 | loop fusion | flops 1245184 | bytes 7471104 | tf_op jit(solution)/shard_map/convert_element_type | solution.py:158
  61.1 1.3 %div.70 = f32[256]{0:T(256)} reshape(f32[32,8]{1,0:T(8,128)} %get-tuple-element.185) | data formatting | bytes 2048 | tf_op jit(solution)/shard_map/div | solution.py:139
  62.4 1.6 %fusion.74 = f32[256,227]{1,0:T(8,128)} fusion(bf16[32,8,228]{2,1,0:T(8,128)(2,1)} %copy-done.6), kind=kLoop, calls=%fused_computation.159 | loop fusion | flops 58112 | bytes 348672 | tf_op jit(solution)/shard_map/convert_element_type | solution.py:179
  64.1 1.8 %copy.510 = f32[256,227]{0,1:T(8,128)} copy(f32[256,227]{1,0:T(8,128)} %fusion.74) | data formatting | bytes 464896 | tf_op jit(solution)/shard_map/convert_element_type | solution.py:179
  66.6 1.3 %iota_add_fusion = s32[32,8]{1,0:T(8,128)} fusion(s32[32]{0:T(128)} %bitcast.509), kind=kLoop, calls=%fused_computation.236 | loop fusion | flops 256 | bytes 1152 | tf_op jit(solution)/shard_map/add | solution.py:227
  69.0 7.2 %fusion.39 = bf16[256,256]{1,0:T(8,128)(2,1)S(1)} fusion(f32[32,1,8,256]{3,2,0,1:T(8,128)} %copy.486, f32[32,1,8,256]{3,2,0,1:T(8,128)} %copy.485, f32[32,1,8,256]{3,2,0,1:T(8,128)} %copy.484, f32[32,1,8,256]{3,2,0,1:T(8,128)} %copy.483, f32[32,1,8,256]{3,2,0,1:T(8,128)} %copy.482, f32[32,1,8,256]{3,2,0,1:T(8,128)} %copy.481, f32[32,1,8,256]{3,2,0,1:T(8,128)} %copy.480, ...), kind=kLoop, calls=%fused_computation.86 | loop fusion | flops 4325376 | bytes 8815616 | tf_op jit(solution)/shard_map/convert_element_type | solution.py:174
  79.7 3.8 %fusion.8 = (f32[256]{0:T(256)S(1)}, f32[256]{0:T(256)S(1)}, f32[256]{0:T(256)S(1)}, f32[256]{0:T(256)S(1)}, f32[256]{0:T(256)S(1)}, /*index=5*/f32[256]{0:T(256...) fusion(f32[32,1,8,256]{3,0,2,1:T(8,128)S(1)} %get-tuple-element, ...), kind=kOutput, calls=%fused_computation.25 | convolution fusion | flops 35909120 | bytes 5261312 | tf_op jit(solution)/shard_map/dot_general | solution.py:192
  83.5 2.9 %fusion.25 = (f32[256]{0:T(256)S(1)}, f32[256]{0:T(256)S(1)}, f32[256]{0:T(256)S(1)}, f32[256]{0:T(256)S(1)}, f32[256]{0:T(256)S(1)}, /*index=5*/f32[256]{0:T(25...) fusion(f32[256,256]{1,0:T(8,128)S(1)} %get-tuple-element.192, ...), kind=kLoop, calls=%fused_computation.59 | loop fusion | flops 1962240 | bytes 4209664 | tf_op jit(solution)/shard_map/reduce_sum | solution.py:205
  87.8 1.5 %collective-permute-done.4 = f32[512,128]{1,0:T(8,128)S(1)} collective-permute-done((f32[512,128]{1,0:T(8,128)S(1)}, f32[512,128]{1,0:T(8,128)S(1)}, u32[]{:S(2)}, u32[]{:S(2)}) %collective-permute-start.4) | collective-permute-done | bytes 262176 | tf_op jit(solution)/shard_map/ppermute | solution.py:22
  89.5 5.5 %collective-permute-done.5 = f32[256,128]{1,0:T(8,128)S(1)} collective-permute-done((f32[256,128]{1,0:T(8,128)S(1)}, f32[256,128]{1,0:T(8,128)S(1)}, u32[]{:S(2)}, u32[]{:S(2)}) %collective-permute-start.5) | collective-permute-done | bytes 131104 | tf_op jit(solution)/shard_map/ppermute | solution.py:22
  95.1 5.0 %collective-permute-done.6 = f32[256,128]{1,0:T(8,128)S(1)} collective-permute-done((f32[256,128]{1,0:T(8,128)S(1)}, f32[256,128]{1,0:T(8,128)S(1)}, u32[]{:S(2)}, u32[]{:S(2)}) %collective-permute-start.6) | collective-permute-done | bytes 131104 | tf_op jit(solution)/shard_map/ppermute | solution.py:56
  100.6 6.6 %collective-permute-done.7 = f32[256,128]{1,0:T(8,128)S(1)} collective-permute-done((f32[256,128]{1,0:T(8,128)S(1)}, f32[256,128]{1,0:T(8,128)S(1)}, u32[]{:S(2)}, u32[]{:S(2)}) %collective-permute-start.7) | collective-permute-done | bytes 131104 | tf_op jit(solution)/shard_map/ppermute | solution.py:56
  107.9 4.4 %collective-permute-done.8 = f32[256,128]{1,0:T(8,128)S(1)} collective-permute-done((f32[256,128]{1,0:T(8,128)S(1)}, f32[256,128]{1,0:T(8,128)S(1)}, u32[]{:S(2)}, u32[]{:S(2)}) %collective-permute-start.8) | collective-permute-done | bytes 131104 | tf_op jit(solution)/shard_map/ppermute | solution.py:29
  112.4 1.4 %collective-permute-done.9 = f32[512,128]{1,0:T(8,128)S(1)} collective-permute-done((f32[512,128]{1,0:T(8,128)S(1)}, f32[512,128]{1,0:T(8,128)S(1)}, u32[]{:S(2)}, u32[]{:S(2)}) %collective-permute-start.9) | collective-permute-done | bytes 262176 | tf_op jit(solution)/shard_map/ppermute | solution.py:29
  (123 shorter events, 32.1 us)
Async XLA Ops:
  0.6 75.5 %copy-start = (bf16[256,256]{1,0:T(8,128)(2,1)S(1)}, bf16[256,256]{1,0:T(8,128)(2,1)}, u32[]{:S(2)}) copy-start(bf16[256,256]{1,0:T(8,128)(2,1)} %param.12) | copy-start | bytes 393220
  0.6 9.6 %copy-start.9 = (bf16[9,256]{1,0:T(8,128)(2,1)S(1)}, bf16[9,256]{1,0:T(8,128)(2,1)}, u32[]{:S(2)}) copy-start(bf16[9,256]{1,0:T(8,128)(2,1)} %param.11) | copy-start | bytes 13828
  0.7 9.6 %copy-start.12 = (s32[256]{0:T(256)S(1)}, s32[256]{0:T(256)}, u32[]{:S(2)}) copy-start(s32[256]{0:T(256)} %param.10) | copy-start | bytes 3076
  0.7 11.5 %copy-start.13 = (s32[16]{0:T(128)S(1)}, s32[16]{0:T(128)}, u32[]{:S(2)}) copy-start(s32[16]{0:T(128)} %param.16) | copy-start | bytes 196
  0.7 11.7 %copy-start.14 = (s32[16]{0:T(128)S(1)}, s32[16]{0:T(128)}, u32[]{:S(2)}) copy-start(s32[16]{0:T(128)} %param.17) | copy-start | bytes 196
  0.7 11.9 %copy-start.8 = (bf16[16,8,227]{2,1,0:T(8,128)(2,1)S(1)}, bf16[16,8,227]{2,1,0:T(8,128)(2,1)}, u32[]{:S(2)}) copy-start(bf16[16,8,227]{2,1,0:T(8,128)(2,1)} %param.14) | copy-start | bytes 174340
  0.7 12.1 %copy-start.15 = (s32[16,1]{0,1:T(1,128)S(1)}, s32[16,1]{0,1:T(1,128)}, u32[]{:S(2)}) copy-start(s32[16,1]{0,1:T(1,128)} %param.15) | copy-start | bytes 196
  4.1 11.4 %collective-permute-start = (bf16[2,48,4,256]{3,0,2,1:T(2,128)(2,1)S(1)}, bf16[2,48,4,256]{3,0,2,1:T(2,128)(2,1)S(1)}, u32[]{:S(2)}, u32[]{:S(2)}) collective-permute-start(bf16[2,48,4,256]{3,0,2,1:T(2,128)(2,1)S(1)} %get-tuple-element.142), channel_id=1, source_target_pairs={{0,2},{2,4},{4,6},{6,8},{8,10},{10,12},{12,14},{14,0},{1,3},{3,5},... | collective-permute-start | bytes 589832 | tf_op jit(solution)/shard_map/ppermute | solution.py:78
  7.1 10.6 %collective-permute-start.1 = (bf16[2,48,4,256]{3,0,2,1:T(2,128)(2,1)S(1)}, bf16[2,48,4,256]{3,0,2,1:T(2,128)(2,1)S(1)}, u32[]{:S(2)}, u32[]{:S(2)}) collective-permute-start(bf16[2,48,4,256]{3,0,2,1:T(2,128)(2,1)S(1)} %get-tuple-element.143), channel_id=1, source_target_pairs={{2,0},{4,2},{6,4},{8,6},{10,8},{12,10},{14,12},{0,14},{3,1},{5,3},... | collective-permute-start | bytes 589832 | tf_op jit(solution)/shard_map/ppermute | solution.py:80
  22.0 10.2 %collective-permute-start.2 = (bf16[2,4,40,256]{3,0,2,1:T(2,128)(2,1)S(1)}, bf16[2,4,40,256]{3,0,2,1:T(2,128)(2,1)S(1)}, u32[]{:S(2)}, u32[]{:S(2)}) collective-permute-start(bf16[2,4,40,256]{3,0,2,1:T(2,128)(2,1)S(1)} %get-tuple-element.140), channel_id=1, source_target_pairs={{0,1},{2,3},{4,5},{6,7},{8,9},{10,11},{12,13},{14,15},{16,17},{18,... | collective-permute-start | bytes 491528 | tf_op jit(solution)/shard_map/ppermute | solution.py:78
  23.3 8.9 %collective-permute-start.3 = (bf16[2,4,40,256]{3,0,2,1:T(2,128)(2,1)S(1)}, bf16[2,4,40,256]{3,0,2,1:T(2,128)(2,1)S(1)}, u32[]{:S(2)}, u32[]{:S(2)}) collective-permute-start(bf16[2,4,40,256]{3,0,2,1:T(2,128)(2,1)S(1)} %get-tuple-element.141), channel_id=1, source_target_pairs={{1,0},{3,2},{5,4},{7,6},{9,8},{11,10},{13,12},{15,14},{17,16},{19,... | collective-permute-start | bytes 491528 | tf_op jit(solution)/shard_map/ppermute | solution.py:80
  26.1 14.0 %all-to-all-start = ((bf16[32,8,228]{2,1,0:T(8,128)(2,1)}), bf16[32,8,228]{2,1,0:T(8,128)(2,1)S(1)}, u32[]{:S(2)}, u32[]{:S(2)}) async-start(bf16[32,8,228]{2,1,0:T(8,128)(2,1)} %reshape.794), calls=%async_computation | async-start | bytes 262144 | tf_op jit(solution)/shard_map/all_to_all | solution.py:119
  46.6 3.9 %copy-start.1 = (bf16[32,9,16,256]{3,0,2,1:T(8,128)(2,1)S(1)}, bf16[32,9,16,256]{3,0,2,1:T(8,128)(2,1)}, u32[]{:S(2)}) copy-start(bf16[32,9,16,256]{3,0,2,1:T(8,128)(2,1)} %gather_fusion) | copy-start | bytes 7077892
  51.8 7.8 %copy-start.3 = (f32[32,1,8,256]{3,0,2,1:T(8,128)}, f32[32,1,8,256]{3,0,2,1:T(8,128)S(1)}, u32[]{:S(2)}) copy-start(f32[32,1,8,256]{3,0,2,1:T(8,128)S(1)} %get-tuple-element.139) | copy-start | bytes 786436
  69.0 7.2 %copy-start.4 = (f32[32,1,8,256]{3,0,2,1:T(8,128)S(1)}, f32[32,1,8,256]{3,0,2,1:T(8,128)}, u32[]{:S(2)}) copy-start(f32[32,1,8,256]{3,0,2,1:T(8,128)} %copy-done.3) | copy-start | bytes 786436
  69.0 7.5 %copy-start.5 = (f32[256,227]{0,1:T(8,128)S(1)}, f32[256,227]{0,1:T(8,128)}, u32[]{:S(2)}) copy-start(f32[256,227]{0,1:T(8,128)} %copy.510) | copy-start | bytes 697348
  69.0 7.5 %copy-start.7 = (bf16[256,227]{0,1:T(8,128)(2,1)S(1)}, bf16[256,227]{0,1:T(8,128)(2,1)}, u32[]{:S(2)}) copy-start(bf16[256,227]{0,1:T(8,128)(2,1)} %param.13) | copy-start | bytes 348676
  69.0 7.5 %copy-start.10 = (f32[256]{0:T(256)S(1)}, f32[256]{0:T(256)}, u32[]{:S(2)}) copy-start(f32[256]{0:T(256)} %div.70) | copy-start | bytes 3076
  87.7 1.6 %collective-permute-start.4 = (f32[512,128]{1,0:T(8,128)S(1)}, f32[512,128]{1,0:T(8,128)S(1)}, u32[]{:S(2)}, u32[]{:S(2)}) collective-permute-start(f32[512,128]{1,0:T(8,128)S(1)} %constant_dynamic-slice_fusion.1), channel_id=1, source_target_pairs={{0,1},{1,0},{2,3},{3,2},{4,5},{5,4},{6,7},{7,6},{8,9},{9,8},{10,11... | collective-permute-start | bytes 786440 | tf_op jit(solution)/shard_map/ppermute | solution.py:22
  89.4 5.6 %collective-permute-start.5 = (f32[256,128]{1,0:T(8,128)S(1)}, f32[256,128]{1,0:T(8,128)S(1)}, u32[]{:S(2)}, u32[]{:S(2)}) collective-permute-start(f32[256,128]{1,0:T(8,128)S(1)} %constant_dynamic-slice_fusion), channel_id=1, source_target_pairs={{0,2},{2,0},{4,6},{6,4},{8,10},{10,8},{12,14},{14,12},{1,3},{3,1},... | collective-permute-start | bytes 393224 | tf_op jit(solution)/shard_map/ppermute | solution.py:22
  95.0 5.0 %collective-permute-start.6 = (f32[256,128]{1,0:T(8,128)S(1)}, f32[256,128]{1,0:T(8,128)S(1)}, u32[]{:S(2)}, u32[]{:S(2)}) collective-permute-start(f32[256,128]{1,0:T(8,128)S(1)} %dynamic-slice_add_fusion.1), channel_id=1, source_target_pairs={{0,4},{2,6},{4,0},{6,2},{8,12},{10,14},{12,8},{14,10},{1,5},{3,7},... | collective-permute-start | bytes 393224 | tf_op jit(solution)/shard_map/ppermute | solution.py:56
  100.1 7.1 %collective-permute-start.7 = (f32[256,128]{1,0:T(8,128)S(1)}, f32[256,128]{1,0:T(8,128)S(1)}, u32[]{:S(2)}, u32[]{:S(2)}) collective-permute-start(f32[256,128]{1,0:T(8,128)S(1)} %add.473), channel_id=1, source_target_pairs={{0,8},{2,10},{4,12},{6,14},{8,0},{10,2},{12,4},{14,6},{1,9},{3,11}... | collective-permute-start | bytes 393224 | tf_op jit(solution)/shard_map/ppermute | solution.py:56
  107.2 5.0 %collective-permute-start.8 = (f32[256,128]{1,0:T(8,128)S(1)}, f32[256,128]{1,0:T(8,128)S(1)}, u32[]{:S(2)}, u32[]{:S(2)}) collective-permute-start(f32[256,128]{1,0:T(8,128)S(1)} %get-tuple-element.70), channel_id=1, source_target_pairs={{0,2},{2,0},{4,6},{6,4},{8,10},{10,8},{12,14},{14,12},{1,3},{3,1},... | collective-permute-start | bytes 393224 | tf_op jit(solution)/shard_map/ppermute | solution.py:29
  112.2 1.6 %collective-permute-start.9 = (f32[512,128]{1,0:T(8,128)S(1)}, f32[512,128]{1,0:T(8,128)S(1)}, u32[]{:S(2)}, u32[]{:S(2)}) collective-permute-start(f32[512,128]{1,0:T(8,128)S(1)} %constant_dynamic-update-slice_fusion.2), channel_id=1, source_target_pairs={{0,1},{1,0},{2,3},{3,2},{4,5},{5,4},{6,7},{7,6},{8,9},{9,8},{10,11... | collective-permute-start | bytes 786440 | tf_op jit(solution)/shard_map/ppermute | solution.py:29
  (3 other events, 2.5 us)

commit v13 on v11

--- a/solution.py
+++ b/solution.py
@@ -253,8 +253,8 @@
             (tuple(split(v) for v in place), rows_split(depth_flat), rows_split(grad_u)),
         )
         grad_pw, grad_dw = jnp.sum(outs[0], axis=0), jnp.sum(outs[1], axis=0)
-    grad_dw, grad_pw, grad_head, loss_sum = packed_sum(
-        (grad_dw, grad_pw, grad_head, loss_sum), ("lat", "lon")
+    grad_pw, grad_head, grad_dw, loss_sum = packed_sum(
+        (grad_pw, grad_head, grad_dw, loss_sum), ("lat", "lon")
     )
     return (grad_dw, grad_pw, grad_head, (loss_sum / teach_width).reshape(1))
 

time: 98.5 us -> 105 us (1.066)
  other arithmetic: 20.8 us -> 23.4 us
  local copies, waits for them, and re-layouts: 18.3 us -> 20.9 us
  matrix products: 6.42 us -> 7.95 us
    convert_element_type x4, other arithmetic: 3.86 us -> 6.45 us  [shifted(): source[:, DMAX + row_shift, DMAX + col_shift:DMAX + col_shift + TILE, :]]
    reshape x2, local copies, waits for them, and re-layouts: 0.36 us -> 2 us  [packed_sum(): flat = jnp.concatenate([jnp.ravel(v).astype(jnp.float32) for v in values])]
    unnamed x22 -> x56, local copies, waits for them, and re-layouts: 4.62 us -> 5.62 us
where the time goes in v13:
time: 105 us
  waiting for transfers between devices  27.7 us (26%)
  other arithmetic  23.4 us (22%)
  starting transfers between devices  21.9 us (21%)
  local copies, waits for them, and re-layouts  20.9 us (20%)
  matrix products  7.95 us (8%)
  between operations  3.18 us (3%)
    ppermute x2, waiting for transfers between devices, packed_sum(): x = x + lax.ppermute(x, axis, [(i, i ^ bit) for i in range(count)])  9.72 us
    all_to_all x1, starting transfers between devices, local(): lax.all_to_all(send.reshape(slots, TILE, teach_width + 1), ('lon', 'lat')...  7.36 us
    convert_element_type x4, other arithmetic, shifted(): source[:, DMAX + row_shift, DMAX + col_shift:DMAX + col_shift + TILE, :]  6.45 us
    ppermute x2, waiting for transfers between devices, padded_2(): lax.ppermute(tail, axis, [(i, (i + 1) % count) for i in range(ends)])  5.93 us
    gather x1, local copies, waits for them, and re-layouts, gather_windows(): lax.dynamic_slice(padded, (b, h, w, jnp.int32(0)), (1, span, reach, width))  5.74 us
    unnamed x56, local copies, waits for them, and re-layouts  5.62 us
    ppermute x2, waiting for transfers between devices, double(): got = lax.ppermute(x, axis, [(i, i ^ bit) for i in range(count)])  5.44 us
    ppermute x2, waiting for transfers between devices, halve(): return keep + lax.ppermute(send, axis, [(i, i ^ bit) for i in range(count)])  5.17 us
  transfers between devices with their start and end apart: 11, of which 9 were waited for; matrix products, arithmetic and copies ran while one was open for 5% of the time, Pallas kernels for 0%

profile of v13, /device:TPU:0, one launch (start us, length us, event | category | flops | bytes accessed | tf_op | source)
XLA Modules:
  0.0 105.0 jit_solution(2750442396431654835)
XLA Ops:
  6.2 7.4 %all-to-all-start = ((bf16[32,8,228]{2,1,0:T(8,128)(2,1)}), bf16[32,8,228]{2,1,0:T(8,128)(2,1)S(1)}, u32[]{:S(2)}, u32[]{:S(2)}) async-start(bf16[32,8,228]{2,1,0:T(8,128)(2,1)} %reshape.794), calls=%async_computation | async-start | bytes 262144 | tf_op jit(solution)/shard_map/all_to_all | solution.py:118
  15.1 2.0 %collective-permute-start = (bf16[2,48,4,256]{3,0,2,1:T(2,128)(2,1)S(1)}, bf16[2,48,4,256]{3,0,2,1:T(2,128)(2,1)S(1)}, u32[]{:S(2)}, u32[]{:S(2)}) collective-permute-start(bf16[2,48,4,256]{3,0,2,1:T(2,128)(2,1)S(1)} %copy.608), channel_id=1, source_target_pairs={{0,2},{2,4},{4,6},{6,8},{8,10},{10,12},{12,14},{14,0},{1,3},{3,5},... | collective-permute-start | bytes 589832 | tf_op jit(solution)/shard_map/ppermute | solution.py:78
  17.3 2.9 %collective-permute-start.1 = (bf16[2,48,4,256]{3,0,2,1:T(2,128)(2,1)S(1)}, bf16[2,48,4,256]{3,0,2,1:T(2,128)(2,1)S(1)}, u32[]{:S(2)}, u32[]{:S(2)}) collective-permute-start(bf16[2,48,4,256]{3,0,2,1:T(2,128)(2,1)S(1)} %copy.609), channel_id=1, source_target_pairs={{2,0},{4,2},{6,4},{8,6},{10,8},{12,10},{14,12},{0,14},{3,1},{5,3},... | collective-permute-start | bytes 589832 | tf_op jit(solution)/shard_map/ppermute | solution.py:80
  20.3 5.9 %collective-permute-done = bf16[2,48,4,256]{3,0,2,1:T(2,128)(2,1)S(1)} collective-permute-done((bf16[2,48,4,256]{3,0,2,1:T(2,128)(2,1)S(1)}, bf16[2,48,4,256]{3,0,2,1:T(2,128)(2,1)S(1)}, u32[]{:S(2)}, u32[]{:S(2)}) %collective-permute-start) | collective-permute-done | bytes 196640 | tf_op jit(solution)/shard_map/ppermute | solution.py:78
  26.4 1.7 %constant_dynamic-update-slice_fusion.1 = bf16[2,48,40,256]{3,0,2,1:T(2,128)(2,1)S(1)} fusion(bf16[2,48,40,256]{3,0,2,1:T(2,128)(2,1)S(1)} %constant_dynamic-update-slice_fusion.2, bf16[2,48,32,256]{3,2,1,0:T(8,128)(2,1)S(1)} %copy-done.3), kind=kLoop, calls=%fused_computation.238 | loop fusion | bytes 3145728
  30.3 1.3 %collective-permute-start.2 = (bf16[2,4,40,256]{3,0,2,1:T(2,128)(2,1)S(1)}, bf16[2,4,40,256]{3,0,2,1:T(2,128)(2,1)S(1)}, u32[]{:S(2)}, u32[]{:S(2)}) collective-permute-start(bf16[2,4,40,256]{3,0,2,1:T(2,128)(2,1)S(1)} %get-tuple-element.136), channel_id=1, source_target_pairs={{0,1},{2,3},{4,5},{6,7},{8,9},{10,11},{12,13},{14,15},{16,17},{18,... | collective-permute-start | bytes 491528 | tf_op jit(solution)/shard_map/ppermute | solution.py:78
  31.6 1.3 %collective-permute-start.3 = (bf16[2,4,40,256]{3,0,2,1:T(2,128)(2,1)S(1)}, bf16[2,4,40,256]{3,0,2,1:T(2,128)(2,1)S(1)}, u32[]{:S(2)}, u32[]{:S(2)}) collective-permute-start(bf16[2,4,40,256]{3,0,2,1:T(2,128)(2,1)S(1)} %get-tuple-element.137), channel_id=1, source_target_pairs={{1,0},{3,2},{5,4},{7,6},{9,8},{11,10},{13,12},{15,14},{17,16},{19,... | collective-permute-start | bytes 491528 | tf_op jit(solution)/shard_map/ppermute | solution.py:80
  34.9 4.8 %pad_maximum_fusion = bf16[2,56,40,256]{3,0,2,1:T(2,128)(2,1)S(1)} fusion(bf16[2,4,40,256]{3,0,2,1:T(2,128)(2,1)S(1)} %collective-permute-done.3, bf16[2,48,40,256]{3,0,2,1:T(2,128)(2,1)} %copy-done.2, bf16[2,4,40,256]{3,0,2,1:T(2,128)(2,1)S(1)} %collective-permute-done.2), kind=kLoop, calls=%fused_computation.1 | loop fusion | flops 2293760 | bytes 4587520 | tf_op jit(solution)/shard_map/concatenate | solution.py:76
  39.7 5.7 %gather_fusion = bf16[32,9,16,256]{3,0,2,1:T(8,128)(2,1)} fusion(bf16[2,56,40,256]{3,0,2,1:T(2,128)(2,1)S(1)} %pad_maximum_fusion, s32[32]{0:T(128)S(1)} %fusion.91), kind=kCustom, calls=%fused_computation | custom fusion | bytes 4719104 | tf_op jit(solution)/shard_map/vmap()/gather | solution.py:151
  45.4 2.5 %slice_convert_fusion.20 = (f32[32,1,8,256]{3,0,2,1:T(8,128)S(1)}, f32[32,1,8,256]{3,0,2,1:T(8,128)S(1)}, f32[32,1,8,256]{3,0,2,1:T(8,128)S(1)}, f32[32,1,8,256]...) fusion(bf16[32,9,16,256]{3,0,2,1:T(8,128)(2,1)} %gather_fusion), kind=kLoop, calls=%fused_computation.179 | loop fusion | flops 1245184 | bytes 7471104 | tf_op jit(solution)/shard_map/convert_element_type | solution.py:157
  50.0 3.9 %fusion.39 = bf16[256,256]{1,0:T(8,128)(2,1)S(1)} fusion(f32[32,1,8,256]{3,2,0,1:T(8,128)S(1)} %copy.486, f32[32,1,8,256]{3,2,0,1:T(8,128)S(1)} %copy.485, f32[32,1,8,256]{3,2,0,1:T(8,128)S(1)} %copy.484, f32[32,1,8,256]{3,2,0,1:T(8,128)S(1)} %copy.483, f32[32,1,8,256]{3,2,0,1:T(8,128)S(1)} %copy.482, f32[32,1,8,256]{3,2,0,1:T(8,128)S(1)} %copy.481, ...), kind=kLoop, calls=%fused_computation.85 | loop fusion | flops 4325376 | bytes 8815616 | tf_op jit(solution)/shard_map/convert_element_type | solution.py:173
  56.6 1.6 %slice_convert_fusion.50 = (f32[32,1,8,256]{3,0,2,1:T(8,128)S(1)}, f32[32,1,8,256]{3,0,2,1:T(8,128)S(1)}, f32[32,1,8,256]{3,0,2,1:T(8,128)S(1)}, f32[32,1,8,256]...) fusion(bf16[32,9,16,256]{3,0,2,1:T(8,128)(2,1)S(1)} %copy-done.1), kind=kLoop, calls=%fused_computation.210 | loop fusion | flops 1245184 | bytes 7471104 | tf_op jit(solution)/shard_map/convert_element_type | solution.py:157
  58.3 1.9 %slice_convert_fusion.65 = (f32[32,1,8,256]{3,0,2,1:T(8,128)}, f32[32,1,8,256]{3,0,2,1:T(8,128)}, f32[32,1,8,256]{3,0,2,1:T(8,128)}, f32[32,1,8,256]{3,0,2,1:T(8...) fusion(bf16[32,9,16,256]{3,0,2,1:T(8,128)(2,1)S(1)} %copy-done.1), kind=kLoop, calls=%fused_computation.225 | loop fusion | flops 917504 | bytes 5505024 | tf_op jit(solution)/shard_map/convert_element_type | solution.py:157
  61.4 2.0 %reshape.796 = f32[58112]{0:T(1024)} reshape(f32[256,227]{1,0:T(8,128)} %fusion.77) | data formatting | bytes 464896 | tf_op jit(solution)/shard_map/reshape | solution.py:47
  63.6 4.9 %fusion.8 = (f32[256]{0:T(256)S(1)}, f32[256]{0:T(256)S(1)}, f32[256]{0:T(256)S(1)}, f32[256]{0:T(256)S(1)}, f32[256]{0:T(256)S(1)}, /*index=5*/f32[256]{0:T(256...) fusion(f32[32,1,8,256]{3,0,2,1:T(8,128)S(1)} %get-tuple-element, ...), kind=kOutput, calls=%fused_computation.24 | convolution fusion | flops 35909120 | bytes 5261312 | tf_op jit(solution)/shard_map/dot_general | solution.py:191
  68.6 2.9 %fusion.25 = (f32[256]{0:T(256)S(1)}, f32[256]{0:T(256)S(1)}, f32[256]{0:T(256)S(1)}, f32[256]{0:T(256)S(1)}, f32[256]{0:T(256)S(1)}, /*index=5*/f32[256]{0:T(25...) fusion(f32[256,256]{1,0:T(8,128)S(1)} %get-tuple-element.188, ...), kind=kLoop, calls=%fused_computation.58 | loop fusion | flops 1962240 | bytes 4209664 | tf_op jit(solution)/shard_map/reduce_sum | solution.py:204
  74.0 2.1 %collective-permute-start.5 = (f32[256,128]{1,0:T(8,128)S(1)}, f32[256,128]{1,0:T(8,128)S(1)}, u32[]{:S(2)}, u32[]{:S(2)}) collective-permute-start(f32[256,128]{1,0:T(8,128)S(1)} %constant_dynamic-slice_fusion), channel_id=1, source_target_pairs={{0,2},{2,0},{4,6},{6,4},{8,10},{10,8},{12,14},{14,12},{1,3},{3,1},... | collective-permute-start | bytes 393224 | tf_op jit(solution)/shard_map/ppermute | solution.py:22
  76.2 3.9 %collective-permute-done.5 = f32[256,128]{1,0:T(8,128)S(1)} collective-permute-done((f32[256,128]{1,0:T(8,128)S(1)}, f32[256,128]{1,0:T(8,128)S(1)}, u32[]{:S(2)}, u32[]{:S(2)}) %collective-permute-start.5) | collective-permute-done | bytes 131104 | tf_op jit(solution)/shard_map/ppermute | solution.py:22
  80.1 1.5 %collective-permute-start.6 = (f32[256,128]{1,0:T(8,128)S(1)}, f32[256,128]{1,0:T(8,128)S(1)}, u32[]{:S(2)}, u32[]{:S(2)}) collective-permute-start(f32[256,128]{1,0:T(8,128)S(1)} %dynamic-slice_add_fusion.1), channel_id=1, source_target_pairs={{0,4},{2,6},{4,0},{6,2},{8,12},{10,14},{12,8},{14,10},{1,5},{3,7},... | collective-permute-start | bytes 393224 | tf_op jit(solution)/shard_map/ppermute | solution.py:56
  81.6 3.7 %collective-permute-done.6 = f32[256,128]{1,0:T(8,128)S(1)} collective-permute-done((f32[256,128]{1,0:T(8,128)S(1)}, f32[256,128]{1,0:T(8,128)S(1)}, u32[]{:S(2)}, u32[]{:S(2)}) %collective-permute-start.6) | collective-permute-done | bytes 131104 | tf_op jit(solution)/shard_map/ppermute | solution.py:56
  85.3 2.0 %collective-permute-start.7 = (f32[256,128]{1,0:T(8,128)S(1)}, f32[256,128]{1,0:T(8,128)S(1)}, u32[]{:S(2)}, u32[]{:S(2)}) collective-permute-start(f32[256,128]{1,0:T(8,128)S(1)} %add.473), channel_id=1, source_target_pairs={{0,8},{2,10},{4,12},{6,14},{8,0},{10,2},{12,4},{14,6},{1,9},{3,11}... | collective-permute-start | bytes 393224 | tf_op jit(solution)/shard_map/ppermute | solution.py:56
  87.4 6.0 %collective-permute-done.7 = f32[256,128]{1,0:T(8,128)S(1)} collective-permute-done((f32[256,128]{1,0:T(8,128)S(1)}, f32[256,128]{1,0:T(8,128)S(1)}, u32[]{:S(2)}, u32[]{:S(2)}) %collective-permute-start.7) | collective-permute-done | bytes 131104 | tf_op jit(solution)/shard_map/ppermute | solution.py:56
  94.5 4.0 %collective-permute-done.8 = f32[256,128]{1,0:T(8,128)S(1)} collective-permute-done((f32[256,128]{1,0:T(8,128)S(1)}, f32[256,128]{1,0:T(8,128)S(1)}, u32[]{:S(2)}, u32[]{:S(2)}) %collective-permute-start.8) | collective-permute-done | bytes 131104 | tf_op jit(solution)/shard_map/ppermute | solution.py:29
  98.6 1.4 %collective-permute-done.9 = f32[512,128]{1,0:T(8,128)S(1)} collective-permute-done((f32[512,128]{1,0:T(8,128)S(1)}, f32[512,128]{1,0:T(8,128)S(1)}, u32[]{:S(2)}, u32[]{:S(2)}) %collective-permute-start.9) | collective-permute-done | bytes 262176 | tf_op jit(solution)/shard_map/ppermute | solution.py:29
  (142 shorter events, 24.5 us)
Async XLA Ops:
  0.6 53.3 %copy-start = (bf16[256,256]{1,0:T(8,128)(2,1)S(1)}, bf16[256,256]{1,0:T(8,128)(2,1)}, u32[]{:S(2)}) copy-start(bf16[256,256]{1,0:T(8,128)(2,1)} %param.12) | copy-start | bytes 393220
  0.6 25.7 %copy-start.3 = (bf16[2,48,32,256]{3,2,1,0:T(8,128)(2,1)S(1)}, bf16[2,48,32,256]{3,2,1,0:T(8,128)(2,1)}, u32[]{:S(2)}) copy-start(bf16[2,48,32,256]{3,2,1,0:T(8,128)(2,1)} %param.9) | copy-start | bytes 4718596
  0.7 19.5 %copy-start.22 = (bf16[9,256]{1,0:T(8,128)(2,1)S(1)}, bf16[9,256]{1,0:T(8,128)(2,1)}, u32[]{:S(2)}) copy-start(bf16[9,256]{1,0:T(8,128)(2,1)} %param.11) | copy-start | bytes 13828
  0.7 19.5 %copy-start.23 = (s32[256]{0:T(256)S(1)}, s32[256]{0:T(256)}, u32[]{:S(2)}) copy-start(s32[256]{0:T(256)} %param.10) | copy-start | bytes 3076
  6.2 26.7 %all-to-all-start = ((bf16[32,8,228]{2,1,0:T(8,128)(2,1)}), bf16[32,8,228]{2,1,0:T(8,128)(2,1)S(1)}, u32[]{:S(2)}, u32[]{:S(2)}) async-start(bf16[32,8,228]{2,1,0:T(8,128)(2,1)} %reshape.794), calls=%async_computation | async-start | bytes 262144 | tf_op jit(solution)/shard_map/all_to_all | solution.py:118
  15.1 11.2 %collective-permute-start = (bf16[2,48,4,256]{3,0,2,1:T(2,128)(2,1)S(1)}, bf16[2,48,4,256]{3,0,2,1:T(2,128)(2,1)S(1)}, u32[]{:S(2)}, u32[]{:S(2)}) collective-permute-start(bf16[2,48,4,256]{3,0,2,1:T(2,128)(2,1)S(1)} %copy.608), channel_id=1, source_target_pairs={{0,2},{2,4},{4,6},{6,8},{8,10},{10,12},{12,14},{14,0},{1,3},{3,5},... | collective-permute-start | bytes 589832 | tf_op jit(solution)/shard_map/ppermute | solution.py:78
  17.3 11.4 %collective-permute-start.1 = (bf16[2,48,4,256]{3,0,2,1:T(2,128)(2,1)S(1)}, bf16[2,48,4,256]{3,0,2,1:T(2,128)(2,1)S(1)}, u32[]{:S(2)}, u32[]{:S(2)}) collective-permute-start(bf16[2,48,4,256]{3,0,2,1:T(2,128)(2,1)S(1)} %copy.609), channel_id=1, source_target_pairs={{2,0},{4,2},{6,4},{8,6},{10,8},{12,10},{14,12},{0,14},{3,1},{5,3},... | collective-permute-start | bytes 589832 | tf_op jit(solution)/shard_map/ppermute | solution.py:80
  30.3 3.7 %collective-permute-start.2 = (bf16[2,4,40,256]{3,0,2,1:T(2,128)(2,1)S(1)}, bf16[2,4,40,256]{3,0,2,1:T(2,128)(2,1)S(1)}, u32[]{:S(2)}, u32[]{:S(2)}) collective-permute-start(bf16[2,4,40,256]{3,0,2,1:T(2,128)(2,1)S(1)} %get-tuple-element.136), channel_id=1, source_target_pairs={{0,1},{2,3},{4,5},{6,7},{8,9},{10,11},{12,13},{14,15},{16,17},{18,... | collective-permute-start | bytes 491528 | tf_op jit(solution)/shard_map/ppermute | solution.py:78
  31.6 3.3 %collective-permute-start.3 = (bf16[2,4,40,256]{3,0,2,1:T(2,128)(2,1)S(1)}, bf16[2,4,40,256]{3,0,2,1:T(2,128)(2,1)S(1)}, u32[]{:S(2)}, u32[]{:S(2)}) collective-permute-start(bf16[2,4,40,256]{3,0,2,1:T(2,128)(2,1)S(1)} %get-tuple-element.137), channel_id=1, source_target_pairs={{1,0},{3,2},{5,4},{7,6},{9,8},{11,10},{13,12},{15,14},{17,16},{19,... | collective-permute-start | bytes 491528 | tf_op jit(solution)/shard_map/ppermute | solution.py:80
  63.5 5.1 %copy-start.9 = (f32[32,1,8,256]{3,0,2,1:T(8,128)S(1)}, f32[32,1,8,256]{3,0,2,1:T(8,128)}, u32[]{:S(2)}) copy-start(f32[32,1,8,256]{3,0,2,1:T(8,128)} %get-tuple-element.93) | copy-start | bytes 786436
  63.5 5.1 %copy-start.10 = (f32[32,1,8,256]{3,0,2,1:T(8,128)S(1)}, f32[32,1,8,256]{3,0,2,1:T(8,128)}, u32[]{:S(2)}) copy-start(f32[32,1,8,256]{3,0,2,1:T(8,128)} %get-tuple-element.94) | copy-start | bytes 786436
  63.5 5.1 %copy-start.11 = (f32[32,1,8,256]{3,0,2,1:T(8,128)S(1)}, f32[32,1,8,256]{3,0,2,1:T(8,128)}, u32[]{:S(2)}) copy-start(f32[32,1,8,256]{3,0,2,1:T(8,128)} %get-tuple-element.95) | copy-start | bytes 786436
  63.5 5.1 %copy-start.12 = (f32[32,1,8,256]{3,0,2,1:T(8,128)S(1)}, f32[32,1,8,256]{3,0,2,1:T(8,128)}, u32[]{:S(2)}) copy-start(f32[32,1,8,256]{3,0,2,1:T(8,128)} %get-tuple-element.96) | copy-start | bytes 786436
  63.5 5.1 %copy-start.13 = (f32[32,1,8,256]{3,0,2,1:T(8,128)S(1)}, f32[32,1,8,256]{3,0,2,1:T(8,128)}, u32[]{:S(2)}) copy-start(f32[32,1,8,256]{3,0,2,1:T(8,128)} %get-tuple-element.97) | copy-start | bytes 786436
  63.5 5.1 %copy-start.14 = (f32[32,1,8,256]{3,0,2,1:T(8,128)S(1)}, f32[32,1,8,256]{3,0,2,1:T(8,128)}, u32[]{:S(2)}) copy-start(f32[32,1,8,256]{3,0,2,1:T(8,128)} %get-tuple-element.98) | copy-start | bytes 786436
  63.5 5.1 %copy-start.15 = (f32[32,1,8,256]{3,0,2,1:T(8,128)S(1)}, f32[32,1,8,256]{3,0,2,1:T(8,128)}, u32[]{:S(2)}) copy-start(f32[32,1,8,256]{3,0,2,1:T(8,128)} %get-tuple-element.99) | copy-start | bytes 786436
  63.5 5.1 %copy-start.16 = (f32[32,1,8,256]{3,0,2,1:T(8,128)S(1)}, f32[32,1,8,256]{3,0,2,1:T(8,128)}, u32[]{:S(2)}) copy-start(f32[32,1,8,256]{3,0,2,1:T(8,128)} %get-tuple-element.100) | copy-start | bytes 786436
  63.5 5.1 %copy-start.17 = (f32[32,1,8,256]{3,0,2,1:T(8,128)S(1)}, f32[32,1,8,256]{3,0,2,1:T(8,128)}, u32[]{:S(2)}) copy-start(f32[32,1,8,256]{3,0,2,1:T(8,128)} %get-tuple-element.101) | copy-start | bytes 786436
  72.4 1.6 %collective-permute-start.4 = (f32[512,128]{1,0:T(8,128)S(1)}, f32[512,128]{1,0:T(8,128)S(1)}, u32[]{:S(2)}, u32[]{:S(2)}) collective-permute-start(f32[512,128]{1,0:T(8,128)S(1)} %constant_dynamic-slice_fusion.1), channel_id=1, source_target_pairs={{0,1},{1,0},{2,3},{3,2},{4,5},{5,4},{6,7},{7,6},{8,9},{9,8},{10,11... | collective-permute-start | bytes 786440 | tf_op jit(solution)/shard_map/ppermute | solution.py:22
  74.0 6.0 %collective-permute-start.5 = (f32[256,128]{1,0:T(8,128)S(1)}, f32[256,128]{1,0:T(8,128)S(1)}, u32[]{:S(2)}, u32[]{:S(2)}) collective-permute-start(f32[256,128]{1,0:T(8,128)S(1)} %constant_dynamic-slice_fusion), channel_id=1, source_target_pairs={{0,2},{2,0},{4,6},{6,4},{8,10},{10,8},{12,14},{14,12},{1,3},{3,1},... | collective-permute-start | bytes 393224 | tf_op jit(solution)/shard_map/ppermute | solution.py:22
  80.1 5.2 %collective-permute-start.6 = (f32[256,128]{1,0:T(8,128)S(1)}, f32[256,128]{1,0:T(8,128)S(1)}, u32[]{:S(2)}, u32[]{:S(2)}) collective-permute-start(f32[256,128]{1,0:T(8,128)S(1)} %dynamic-slice_add_fusion.1), channel_id=1, source_target_pairs={{0,4},{2,6},{4,0},{6,2},{8,12},{10,14},{12,8},{14,10},{1,5},{3,7},... | collective-permute-start | bytes 393224 | tf_op jit(solution)/shard_map/ppermute | solution.py:56
  85.3 8.0 %collective-permute-start.7 = (f32[256,128]{1,0:T(8,128)S(1)}, f32[256,128]{1,0:T(8,128)S(1)}, u32[]{:S(2)}, u32[]{:S(2)}) collective-permute-start(f32[256,128]{1,0:T(8,128)S(1)} %add.473), channel_id=1, source_target_pairs={{0,8},{2,10},{4,12},{6,14},{8,0},{10,2},{12,4},{14,6},{1,9},{3,11}... | collective-permute-start | bytes 393224 | tf_op jit(solution)/shard_map/ppermute | solution.py:56
  93.4 5.0 %collective-permute-start.8 = (f32[256,128]{1,0:T(8,128)S(1)}, f32[256,128]{1,0:T(8,128)S(1)}, u32[]{:S(2)}, u32[]{:S(2)}) collective-permute-start(f32[256,128]{1,0:T(8,128)S(1)} %get-tuple-element.66), channel_id=1, source_target_pairs={{0,2},{2,0},{4,6},{6,4},{8,10},{10,8},{12,14},{14,12},{1,3},{3,1},... | collective-permute-start | bytes 393224 | tf_op jit(solution)/shard_map/ppermute | solution.py:29
  98.5 1.6 %collective-permute-start.9 = (f32[512,128]{1,0:T(8,128)S(1)}, f32[512,128]{1,0:T(8,128)S(1)}, u32[]{:S(2)}, u32[]{:S(2)}) collective-permute-start(f32[512,128]{1,0:T(8,128)S(1)} %constant_dynamic-update-slice_fusion.5), channel_id=1, source_target_pairs={{0,1},{1,0},{2,3},{3,2},{4,5},{5,4},{6,7},{7,6},{8,9},{9,8},{10,11... | collective-permute-start | bytes 786440 | tf_op jit(solution)/shard_map/ppermute | solution.py:29
  (11 other events, 43.3 us)

commit v14 on v11

--- a/solution.py
+++ b/solution.py
@@ -193,17 +193,15 @@
         tap_sums = []
         for tap_index in range(9):
             if tap_index == 4:
-                part = shifted(windows, 0, 0) * grad_z
-                tap_sums.append(jnp.sum(part.reshape(-1, width), axis=0))
-                continue
-            tap_sum = jnp.zeros((width,), jnp.float32)
-            for dilation in range(1, DMAX + 1):
-                row_shift = (tap_index // 3 - 1) * dilation
-                col_shift = (tap_index % 3 - 1) * dilation
-                part = shifted(windows, row_shift, col_shift) * grad_z
-                part = jnp.sum(part.reshape(-1, width), axis=0)
-                tap_sum = tap_sum + onehot[dilation - 1] * part
-            tap_sums.append(tap_sum)
+                chosen = shifted(windows, 0, 0)
+            else:
+                chosen = None
+                for dilation in range(1, DMAX + 1):
+                    row_shift = (tap_index // 3 - 1) * dilation
+                    col_shift = (tap_index % 3 - 1) * dilation
+                    term = onehot[dilation - 1] * shifted(windows, row_shift, col_shift)
+                    chosen = term if chosen is None else chosen + term
+            tap_sums.append(jnp.sum((chosen * grad_z).reshape(-1, width), axis=0))
         return pw_part, jnp.stack(tap_sums, axis=0)
 
     slots = recv_start.shape[0]

time: 98.5 us -> 98.1 us (level)
  matrix products: 6.42 us -> 3.92 us
  other arithmetic: 20.8 us -> 22.9 us
    dot_general x1, matrix products: 4.11 us -> 1.62 us  [backward(): grad_z = jnp.dot(grad_u, pw_weight.T, preferred_element_type=jnp.float32)]
    reduce_sum x1 -> x2, other arithmetic: 2.86 us -> 5 us  [backward(): tap_sums.append(jnp.sum((chosen * grad_z).reshape(-1, width), axis=0))]
where the time goes in v14:
time: 98.1 us; the launch traced here: 97.6 us
  waiting for transfers between devices  27.8 us (28%)
  other arithmetic  22.9 us (23%)
  starting transfers between devices  21.9 us (22%)
  local copies, waits for them, and re-layouts  18.3 us (19%)
  matrix products  3.92 us (4%)
  between operations  2.91 us (3%)
    ppermute x2, waiting for transfers between devices, packed_sum(): x = x + lax.ppermute(x, axis, [(i, i ^ bit) for i in range(count)])  9.7 us
    all_to_all x1, starting transfers between devices, local(): lax.all_to_all(send.reshape(slots, TILE, teach_width + 1), ('lon', 'lat')...  7.36 us
    ppermute x2, waiting for transfers between devices, padded_2(): lax.ppermute(tail, axis, [(i, (i + 1) % count) for i in range(ends)])  5.98 us
    gather x1, local copies, waits for them, and re-layouts, gather_windows(): lax.dynamic_slice(padded, (b, h, w, jnp.int32(0)), (1, span, reach, width))  5.74 us
    ppermute x2, waiting for transfers between devices, double(): got = lax.ppermute(x, axis, [(i, i ^ bit) for i in range(count)])  5.44 us
    ppermute x2, waiting for transfers between devices, halve(): return keep + lax.ppermute(send, axis, [(i, i ^ bit) for i in range(count)])  5.19 us
    reduce_sum x2, other arithmetic, backward(): tap_sums.append(jnp.sum((chosen * grad_z).reshape(-1, width), axis=0))  5 us
    concatenate x1, other arithmetic, padded_2(): jnp.concatenate([lax.ppermute(tail, axis, [(i, (i + 1) % count) for i in...  4.77 us
  transfers between devices with their start and end apart: 11, of which 9 were waited for; matrix products, arithmetic and copies ran while one was open for 5% of the time, Pallas kernels for 0%

profile of v14, /device:TPU:0, one launch (start us, length us, event | category | flops | bytes accessed | tf_op | source)
XLA Modules:
  0.0 97.6 jit_solution(10368418812177400818)
XLA Ops:
  6.2 7.4 %all-to-all-start = ((bf16[32,8,228]{2,1,0:T(8,128)(2,1)}), bf16[32,8,228]{2,1,0:T(8,128)(2,1)S(1)}, u32[]{:S(2)}, u32[]{:S(2)}) async-start(bf16[32,8,228]{2,1,0:T(8,128)(2,1)} %reshape.710), calls=%async_computation | async-start | bytes 262144 | tf_op jit(solution)/shard_map/all_to_all | solution.py:118
  13.6 1.3 %fusion.101 = (bf16[2,48,4,256]{3,2,1,0:T(4,128)(2,1)S(1)}, bf16[2,48,4,256]{3,2,1,0:T(4,128)(2,1)S(1)}) fusion(bf16[2,48,32,256]{3,2,1,0:T(8,128)(2,1)} %param.9), kind=kLoop, calls=%fused_computation.294 | loop fusion | bytes 786432 | tf_op jit(solution)/shard_map/slice | solution.py:74
  15.1 2.0 %collective-permute-start = (bf16[2,48,4,256]{3,0,2,1:T(2,128)(2,1)S(1)}, bf16[2,48,4,256]{3,0,2,1:T(2,128)(2,1)S(1)}, u32[]{:S(2)}, u32[]{:S(2)}) collective-permute-start(bf16[2,48,4,256]{3,0,2,1:T(2,128)(2,1)S(1)} %copy.608), channel_id=1, source_target_pairs={{0,2},{2,4},{4,6},{6,8},{8,10},{10,12},{12,14},{14,0},{1,3},{3,5},... | collective-permute-start | bytes 589832 | tf_op jit(solution)/shard_map/ppermute | solution.py:78
  17.3 2.9 %collective-permute-start.1 = (bf16[2,48,4,256]{3,0,2,1:T(2,128)(2,1)S(1)}, bf16[2,48,4,256]{3,0,2,1:T(2,128)(2,1)S(1)}, u32[]{:S(2)}, u32[]{:S(2)}) collective-permute-start(bf16[2,48,4,256]{3,0,2,1:T(2,128)(2,1)S(1)} %copy.609), channel_id=1, source_target_pairs={{2,0},{4,2},{6,4},{8,6},{10,8},{12,10},{14,12},{0,14},{3,1},{5,3},... | collective-permute-start | bytes 589832 | tf_op jit(solution)/shard_map/ppermute | solution.py:80
  20.3 6.0 %collective-permute-done = bf16[2,48,4,256]{3,0,2,1:T(2,128)(2,1)S(1)} collective-permute-done((bf16[2,48,4,256]{3,0,2,1:T(2,128)(2,1)S(1)}, bf16[2,48,4,256]{3,0,2,1:T(2,128)(2,1)S(1)}, u32[]{:S(2)}, u32[]{:S(2)}) %collective-permute-start) | collective-permute-done | bytes 196640 | tf_op jit(solution)/shard_map/ppermute | solution.py:78
  26.4 1.7 %constant_dynamic-update-slice_fusion.1 = bf16[2,48,40,256]{3,0,2,1:T(2,128)(2,1)S(1)} fusion(bf16[2,48,40,256]{3,0,2,1:T(2,128)(2,1)S(1)} %constant_dynamic-update-slice_fusion.2, bf16[2,48,32,256]{3,2,1,0:T(8,128)(2,1)S(1)} %copy-done.3), kind=kLoop, calls=%fused_computation.246 | loop fusion | bytes 3145728
  28.8 1.3 %copy-done.2 = bf16[2,48,40,256]{3,0,2,1:T(2,128)(2,1)} copy-done((bf16[2,48,40,256]{3,0,2,1:T(2,128)(2,1)}, bf16[2,48,40,256]{3,0,2,1:T(2,128)(2,1)S(1)}, u32[]{:S(2)}) %copy-start.2) | copy-done | bytes 1966104
  30.3 1.3 %collective-permute-start.2 = (bf16[2,4,40,256]{3,0,2,1:T(2,128)(2,1)S(1)}, bf16[2,4,40,256]{3,0,2,1:T(2,128)(2,1)S(1)}, u32[]{:S(2)}, u32[]{:S(2)}) collective-permute-start(bf16[2,4,40,256]{3,0,2,1:T(2,128)(2,1)S(1)} %get-tuple-element.112), channel_id=1, source_target_pairs={{0,1},{2,3},{4,5},{6,7},{8,9},{10,11},{12,13},{14,15},{16,17},{18,... | collective-permute-start | bytes 491528 | tf_op jit(solution)/shard_map/ppermute | solution.py:78
  31.6 1.3 %collective-permute-start.3 = (bf16[2,4,40,256]{3,0,2,1:T(2,128)(2,1)S(1)}, bf16[2,4,40,256]{3,0,2,1:T(2,128)(2,1)S(1)}, u32[]{:S(2)}, u32[]{:S(2)}) collective-permute-start(bf16[2,4,40,256]{3,0,2,1:T(2,128)(2,1)S(1)} %get-tuple-element.113), channel_id=1, source_target_pairs={{1,0},{3,2},{5,4},{7,6},{9,8},{11,10},{13,12},{15,14},{17,16},{19,... | collective-permute-start | bytes 491528 | tf_op jit(solution)/shard_map/ppermute | solution.py:80
  34.9 4.8 %pad_maximum_fusion = bf16[2,56,40,256]{3,0,2,1:T(2,128)(2,1)S(1)} fusion(bf16[2,4,40,256]{3,0,2,1:T(2,128)(2,1)S(1)} %collective-permute-done.3, bf16[2,48,40,256]{3,0,2,1:T(2,128)(2,1)} %copy-done.2, bf16[2,4,40,256]{3,0,2,1:T(2,128)(2,1)S(1)} %collective-permute-done.2), kind=kLoop, calls=%fused_computation.1 | loop fusion | flops 2293760 | bytes 4587520 | tf_op jit(solution)/shard_map/concatenate | solution.py:76
  39.7 5.7 %gather_fusion = bf16[32,9,16,256]{3,0,2,1:T(8,128)(2,1)} fusion(bf16[2,56,40,256]{3,0,2,1:T(2,128)(2,1)S(1)} %pad_maximum_fusion, s32[32]{0:T(128)S(1)} %fusion.99), kind=kCustom, calls=%fused_computation | custom fusion | bytes 4719104 | tf_op jit(solution)/shard_map/vmap()/gather | solution.py:151
  45.5 2.5 %slice_convert_fusion.20 = (f32[32,1,8,256]{3,0,2,1:T(8,128)S(1)}, f32[32,1,8,256]{3,0,2,1:T(8,128)S(1)}, f32[32,1,8,256]{3,0,2,1:T(8,128)S(1)}, f32[32,1,8,256]...) fusion(bf16[32,9,16,256]{3,0,2,1:T(8,128)(2,1)} %gather_fusion), kind=kLoop, calls=%fused_computation.187 | loop fusion | flops 1245184 | bytes 7471104 | tf_op jit(solution)/shard_map/convert_element_type | solution.py:157
  50.1 3.9 %fusion.47 = bf16[256,256]{1,0:T(8,128)(2,1)S(1)} fusion(f32[32,1,8,256]{3,2,0,1:T(8,128)S(1)} %copy.486, f32[32,1,8,256]{3,2,0,1:T(8,128)S(1)} %copy.485, f32[32,1,8,256]{3,2,0,1:T(8,128)S(1)} %copy.484, f32[32,1,8,256]{3,2,0,1:T(8,128)S(1)} %copy.483, f32[32,1,8,256]{3,2,0,1:T(8,128)S(1)} %copy.482, f32[32,1,8,256]{3,2,0,1:T(8,128)S(1)} %copy.481, ...), kind=kLoop, calls=%fused_computation.93 | loop fusion | flops 4325376 | bytes 8815616 | tf_op jit(solution)/shard_map/convert_element_type | solution.py:173
  57.1 1.6 %fusion.38 = (f32[256]{0:T(256)S(1)}, f32[256]{0:T(256)S(1)}, f32[256,256]{1,0:T(8,128)S(1)}) fusion(f32[32,1,8,256]{3,0,2,1:T(8,128)S(1)} %get-tuple-element.71, f32[32,1,8,256]{3,0,2,1:T(8,128)S(1)} %get-tuple-element.72, f32[32,1,8,256]{3,0,2,1:T(8,128)S(1)} %get-tuple-element.73, f32[32,1,8,256]{3,0,2,1:T(8,128)S(1)} %get-tuple-element.74, ...), kind=kOutput, calls=%fused_computation.76 | convolution fusion | flops 34733568 | bytes 2627584 | tf_op jit(solution)/shard_map/dot_general | solution.py:191
  58.7 2.4 %fusion.22 = (f32[256]{0:T(256)S(1)}, f32[256]{0:T(256)S(1)}, f32[256]{0:T(256)S(1)}) fusion(f32[256,256]{1,0:T(8,128)S(1)} %get-tuple-element.169, f32[32,1,8,256]{3,0,2,1:T(8,128)S(1)} %get-tuple-element.59, f32[32,1,8,256]{3,0,2,1:T(8,128)S(1)} %get-tuple-element.60, f32[32,1,8,256]{3,0,2,1:T(8,128)S(1)} %get-tuple-element.61, ...), kind=kLoop, calls=%fused_computation.47 | loop fusion | flops 1768704 | bytes 3415040 | tf_op jit(solution)/shard_map/reduce_sum | solution.py:204
  61.1 2.6 %fusion.7 = (f32[256]{0:T(256)S(1)}, f32[256]{0:T(256)S(1)}, f32[256]{0:T(256)S(1)}, f32[256]{0:T(256)S(1)}) fusion(f32[256,256]{1,0:T(8,128)S(1)} %get-tuple-element.169, f32[32,1,8,256]{3,0,2,1:T(8,128)S(1)} %get-tuple-element.47, f32[32,1,8,256]{3,0,2,1:T(8,128)S(1)} %get-tuple-element.48, f32[32,1,8,256]{3,0,2,1:T(8,128)S(1)} %get-tuple-element.49, ...), kind=kLoop, calls=%fused_computation.20 | loop fusion | flops 1899520 | bytes 3678208 | tf_op jit(solution)/shard_map/reduce_sum | solution.py:204
  66.7 2.1 %collective-permute-start.5 = (f32[256,128]{1,0:T(8,128)S(1)}, f32[256,128]{1,0:T(8,128)S(1)}, u32[]{:S(2)}, u32[]{:S(2)}) collective-permute-start(f32[256,128]{1,0:T(8,128)S(1)} %constant_dynamic-slice_fusion), channel_id=1, source_target_pairs={{0,2},{2,0},{4,6},{6,4},{8,10},{10,8},{12,14},{14,12},{1,3},{3,1},... | collective-permute-start | bytes 393224 | tf_op jit(solution)/shard_map/ppermute | solution.py:22
  68.8 3.9 %collective-permute-done.5 = f32[256,128]{1,0:T(8,128)S(1)} collective-permute-done((f32[256,128]{1,0:T(8,128)S(1)}, f32[256,128]{1,0:T(8,128)S(1)}, u32[]{:S(2)}, u32[]{:S(2)}) %collective-permute-start.5) | collective-permute-done | bytes 131104 | tf_op jit(solution)/shard_map/ppermute | solution.py:22
  72.7 1.5 %collective-permute-start.6 = (f32[256,128]{1,0:T(8,128)S(1)}, f32[256,128]{1,0:T(8,128)S(1)}, u32[]{:S(2)}, u32[]{:S(2)}) collective-permute-start(f32[256,128]{1,0:T(8,128)S(1)} %dynamic-slice_add_fusion.1), channel_id=1, source_target_pairs={{0,4},{2,6},{4,0},{6,2},{8,12},{10,14},{12,8},{14,10},{1,5},{3,7},... | collective-permute-start | bytes 393224 | tf_op jit(solution)/shard_map/ppermute | solution.py:56
  74.2 3.7 %collective-permute-done.6 = f32[256,128]{1,0:T(8,128)S(1)} collective-permute-done((f32[256,128]{1,0:T(8,128)S(1)}, f32[256,128]{1,0:T(8,128)S(1)}, u32[]{:S(2)}, u32[]{:S(2)}) %collective-permute-start.6) | collective-permute-done | bytes 131104 | tf_op jit(solution)/shard_map/ppermute | solution.py:56
  77.9 2.1 %collective-permute-start.7 = (f32[256,128]{1,0:T(8,128)S(1)}, f32[256,128]{1,0:T(8,128)S(1)}, u32[]{:S(2)}, u32[]{:S(2)}) collective-permute-start(f32[256,128]{1,0:T(8,128)S(1)} %add.473), channel_id=1, source_target_pairs={{0,8},{2,10},{4,12},{6,14},{8,0},{10,2},{12,4},{14,6},{1,9},{3,11}... | collective-permute-start | bytes 393224 | tf_op jit(solution)/shard_map/ppermute | solution.py:56
  80.0 6.0 %collective-permute-done.7 = f32[256,128]{1,0:T(8,128)S(1)} collective-permute-done((f32[256,128]{1,0:T(8,128)S(1)}, f32[256,128]{1,0:T(8,128)S(1)}, u32[]{:S(2)}, u32[]{:S(2)}) %collective-permute-start.7) | collective-permute-done | bytes 131104 | tf_op jit(solution)/shard_map/ppermute | solution.py:56
  87.1 4.0 %collective-permute-done.8 = f32[256,128]{1,0:T(8,128)S(1)} collective-permute-done((f32[256,128]{1,0:T(8,128)S(1)}, f32[256,128]{1,0:T(8,128)S(1)}, u32[]{:S(2)}, u32[]{:S(2)}) %collective-permute-start.8) | collective-permute-done | bytes 131104 | tf_op jit(solution)/shard_map/ppermute | solution.py:29
  91.2 1.4 %collective-permute-done.9 = f32[512,128]{1,0:T(8,128)S(1)} collective-permute-done((f32[512,128]{1,0:T(8,128)S(1)}, f32[512,128]{1,0:T(8,128)S(1)}, u32[]{:S(2)}, u32[]{:S(2)}) %collective-permute-start.9) | collective-permute-done | bytes 262176 | tf_op jit(solution)/shard_map/ppermute | solution.py:29
  (102 shorter events, 21.4 us)
Async XLA Ops:
  0.6 53.3 %copy-start = (bf16[256,256]{1,0:T(8,128)(2,1)S(1)}, bf16[256,256]{1,0:T(8,128)(2,1)}, u32[]{:S(2)}) copy-start(bf16[256,256]{1,0:T(8,128)(2,1)} %param.12) | copy-start | bytes 393220
  0.6 25.7 %copy-start.3 = (bf16[2,48,32,256]{3,2,1,0:T(8,128)(2,1)S(1)}, bf16[2,48,32,256]{3,2,1,0:T(8,128)(2,1)}, u32[]{:S(2)}) copy-start(bf16[2,48,32,256]{3,2,1,0:T(8,128)(2,1)} %param.9) | copy-start | bytes 4718596
  0.7 19.5 %copy-start.5 = (bf16[9,256]{1,0:T(8,128)(2,1)S(1)}, bf16[9,256]{1,0:T(8,128)(2,1)}, u32[]{:S(2)}) copy-start(bf16[9,256]{1,0:T(8,128)(2,1)} %param.11) | copy-start | bytes 13828
  0.7 19.5 %copy-start.6 = (s32[256]{0:T(256)S(1)}, s32[256]{0:T(256)}, u32[]{:S(2)}) copy-start(s32[256]{0:T(256)} %param.10) | copy-start | bytes 3076
  6.2 26.7 %all-to-all-start = ((bf16[32,8,228]{2,1,0:T(8,128)(2,1)}), bf16[32,8,228]{2,1,0:T(8,128)(2,1)S(1)}, u32[]{:S(2)}, u32[]{:S(2)}) async-start(bf16[32,8,228]{2,1,0:T(8,128)(2,1)} %reshape.710), calls=%async_computation | async-start | bytes 262144 | tf_op jit(solution)/shard_map/all_to_all | solution.py:118
  15.1 11.2 %collective-permute-start = (bf16[2,48,4,256]{3,0,2,1:T(2,128)(2,1)S(1)}, bf16[2,48,4,256]{3,0,2,1:T(2,128)(2,1)S(1)}, u32[]{:S(2)}, u32[]{:S(2)}) collective-permute-start(bf16[2,48,4,256]{3,0,2,1:T(2,128)(2,1)S(1)} %copy.608), channel_id=1, source_target_pairs={{0,2},{2,4},{4,6},{6,8},{8,10},{10,12},{12,14},{14,0},{1,3},{3,5},... | collective-permute-start | bytes 589832 | tf_op jit(solution)/shard_map/ppermute | solution.py:78
  17.3 11.4 %collective-permute-start.1 = (bf16[2,48,4,256]{3,0,2,1:T(2,128)(2,1)S(1)}, bf16[2,48,4,256]{3,0,2,1:T(2,128)(2,1)S(1)}, u32[]{:S(2)}, u32[]{:S(2)}) collective-permute-start(bf16[2,48,4,256]{3,0,2,1:T(2,128)(2,1)S(1)} %copy.609), channel_id=1, source_target_pairs={{2,0},{4,2},{6,4},{8,6},{10,8},{12,10},{14,12},{0,14},{3,1},{5,3},... | collective-permute-start | bytes 589832 | tf_op jit(solution)/shard_map/ppermute | solution.py:80
  28.8 1.3 %copy-start.2 = (bf16[2,48,40,256]{3,0,2,1:T(2,128)(2,1)}, bf16[2,48,40,256]{3,0,2,1:T(2,128)(2,1)S(1)}, u32[]{:S(2)}) copy-start(bf16[2,48,40,256]{3,0,2,1:T(2,128)(2,1)S(1)} %constant_dynamic-update-slice_fusion) | copy-start | bytes 5898244
  30.3 3.7 %collective-permute-start.2 = (bf16[2,4,40,256]{3,0,2,1:T(2,128)(2,1)S(1)}, bf16[2,4,40,256]{3,0,2,1:T(2,128)(2,1)S(1)}, u32[]{:S(2)}, u32[]{:S(2)}) collective-permute-start(bf16[2,4,40,256]{3,0,2,1:T(2,128)(2,1)S(1)} %get-tuple-element.112), channel_id=1, source_target_pairs={{0,1},{2,3},{4,5},{6,7},{8,9},{10,11},{12,13},{14,15},{16,17},{18,... | collective-permute-start | bytes 491528 | tf_op jit(solution)/shard_map/ppermute | solution.py:78
  31.6 3.3 %collective-permute-start.3 = (bf16[2,4,40,256]{3,0,2,1:T(2,128)(2,1)S(1)}, bf16[2,4,40,256]{3,0,2,1:T(2,128)(2,1)S(1)}, u32[]{:S(2)}, u32[]{:S(2)}) collective-permute-start(bf16[2,4,40,256]{3,0,2,1:T(2,128)(2,1)S(1)} %get-tuple-element.113), channel_id=1, source_target_pairs={{1,0},{3,2},{5,4},{7,6},{9,8},{11,10},{13,12},{15,14},{17,16},{19,... | collective-permute-start | bytes 491528 | tf_op jit(solution)/shard_map/ppermute | solution.py:80
  45.4 2.5 %copy-start.1 = (bf16[32,9,16,256]{3,0,2,1:T(8,128)(2,1)S(1)}, bf16[32,9,16,256]{3,0,2,1:T(8,128)(2,1)}, u32[]{:S(2)}) copy-start(bf16[32,9,16,256]{3,0,2,1:T(8,128)(2,1)} %gather_fusion) | copy-start | bytes 7077892
  50.0 4.2 %copy-start.4 = (bf16[256,227]{0,1:T(8,128)(2,1)S(1)}, bf16[256,227]{0,1:T(8,128)(2,1)}, u32[]{:S(2)}) copy-start(bf16[256,227]{0,1:T(8,128)(2,1)} %param.13) | copy-start | bytes 348676
  65.0 1.6 %collective-permute-start.4 = (f32[512,128]{1,0:T(8,128)S(1)}, f32[512,128]{1,0:T(8,128)S(1)}, u32[]{:S(2)}, u32[]{:S(2)}) collective-permute-start(f32[512,128]{1,0:T(8,128)S(1)} %constant_dynamic-slice_fusion.1), channel_id=1, source_target_pairs={{0,1},{1,0},{2,3},{3,2},{4,5},{5,4},{6,7},{7,6},{8,9},{9,8},{10,11... | collective-permute-start | bytes 786440 | tf_op jit(solution)/shard_map/ppermute | solution.py:22
  66.7 6.0 %collective-permute-start.5 = (f32[256,128]{1,0:T(8,128)S(1)}, f32[256,128]{1,0:T(8,128)S(1)}, u32[]{:S(2)}, u32[]{:S(2)}) collective-permute-start(f32[256,128]{1,0:T(8,128)S(1)} %constant_dynamic-slice_fusion), channel_id=1, source_target_pairs={{0,2},{2,0},{4,6},{6,4},{8,10},{10,8},{12,14},{14,12},{1,3},{3,1},... | collective-permute-start | bytes 393224 | tf_op jit(solution)/shard_map/ppermute | solution.py:22
  72.7 5.2 %collective-permute-start.6 = (f32[256,128]{1,0:T(8,128)S(1)}, f32[256,128]{1,0:T(8,128)S(1)}, u32[]{:S(2)}, u32[]{:S(2)}) collective-permute-start(f32[256,128]{1,0:T(8,128)S(1)} %dynamic-slice_add_fusion.1), channel_id=1, source_target_pairs={{0,4},{2,6},{4,0},{6,2},{8,12},{10,14},{12,8},{14,10},{1,5},{3,7},... | collective-permute-start | bytes 393224 | tf_op jit(solution)/shard_map/ppermute | solution.py:56
  77.9 8.0 %collective-permute-start.7 = (f32[256,128]{1,0:T(8,128)S(1)}, f32[256,128]{1,0:T(8,128)S(1)}, u32[]{:S(2)}, u32[]{:S(2)}) collective-permute-start(f32[256,128]{1,0:T(8,128)S(1)} %add.473), channel_id=1, source_target_pairs={{0,8},{2,10},{4,12},{6,14},{8,0},{10,2},{12,4},{14,6},{1,9},{3,11}... | collective-permute-start | bytes 393224 | tf_op jit(solution)/shard_map/ppermute | solution.py:56
  86.0 5.0 %collective-permute-start.8 = (f32[256,128]{1,0:T(8,128)S(1)}, f32[256,128]{1,0:T(8,128)S(1)}, u32[]{:S(2)}, u32[]{:S(2)}) collective-permute-start(f32[256,128]{1,0:T(8,128)S(1)} %get-tuple-element.42), channel_id=1, source_target_pairs={{0,2},{2,0},{4,6},{6,4},{8,10},{10,8},{12,14},{14,12},{1,3},{3,1},... | collective-permute-start | bytes 393224 | tf_op jit(solution)/shard_map/ppermute | solution.py:29
  91.1 1.6 %collective-permute-start.9 = (f32[512,128]{1,0:T(8,128)S(1)}, f32[512,128]{1,0:T(8,128)S(1)}, u32[]{:S(2)}, u32[]{:S(2)}) collective-permute-start(f32[512,128]{1,0:T(8,128)S(1)} %constant_dynamic-update-slice_fusion.5), channel_id=1, source_target_pairs={{0,1},{1,0},{2,3},{3,2},{4,5},{5,4},{6,7},{7,6},{8,9},{9,8},{10,11... | collective-permute-start | bytes 786440 | tf_op jit(solution)/shard_map/ppermute | solution.py:29

commit v15 on v14

--- a/solution.py
+++ b/solution.py
@@ -179,7 +179,7 @@
         loss_part = jnp.sum(weight * residual * residual)
         grad_pred = (2.0 * weight * residual).astype(jnp.bfloat16)
         head_part = lax.dot_general(
-            y_rows, grad_pred, (((0,), (0,)), ((), ())), preferred_element_type=jnp.float32
+            grad_pred, y_rows, (((0,), (0,)), ((), ())), preferred_element_type=jnp.float32
         )
         grad_rows = jnp.dot(grad_pred, head_weight.T, preferred_element_type=jnp.float32)
         return depth_flat, preact, grad_rows, loss_part, head_part
@@ -254,6 +254,7 @@
     grad_dw, grad_pw, grad_head, loss_sum = packed_sum(
         (grad_dw, grad_pw, grad_head, loss_sum), ("lat", "lon")
     )
+    grad_head = grad_head.T
     return (grad_dw, grad_pw, grad_head, (loss_sum / teach_width).reshape(1))
 
 

time: 98.1 us -> 97.3 us (level)
    unnamed x22 -> x21, local copies, waits for them, and re-layouts: 4.63 us -> 3.81 us
where the time goes in v15:
time: 97.3 us; the launch traced here: 96.9 us
  waiting for transfers between devices  27.8 us (29%)
  other arithmetic  22.9 us (24%)
  starting transfers between devices  21.8 us (22%)
  local copies, waits for them, and re-layouts  17.5 us (18%)
  matrix products  3.92 us (4%)
  between operations  2.9 us (3%)
    ppermute x2, waiting for transfers between devices, packed_sum(): x = x + lax.ppermute(x, axis, [(i, i ^ bit) for i in range(count)])  9.71 us
    all_to_all x1, starting transfers between devices, local(): lax.all_to_all(send.reshape(slots, TILE, teach_width + 1), ('lon', 'lat')...  7.36 us
    ppermute x2, waiting for transfers between devices, padded_2(): lax.ppermute(tail, axis, [(i, (i + 1) % count) for i in range(ends)])  5.98 us
    gather x1, local copies, waits for them, and re-layouts, gather_windows(): lax.dynamic_slice(padded, (b, h, w, jnp.int32(0)), (1, span, reach, width))  5.74 us
    ppermute x2, waiting for transfers between devices, double(): got = lax.ppermute(x, axis, [(i, i ^ bit) for i in range(count)])  5.43 us
    ppermute x2, waiting for transfers between devices, halve(): return keep + lax.ppermute(send, axis, [(i, i ^ bit) for i in range(count)])  5.21 us
    reduce_sum x2, other arithmetic, backward(): tap_sums.append(jnp.sum((chosen * grad_z).reshape(-1, width), axis=0))  5 us
    concatenate x1, other arithmetic, padded_2(): jnp.concatenate([lax.ppermute(tail, axis, [(i, (i + 1) % count) for i in...  4.77 us
  transfers between devices with their start and end apart: 11, of which 9 were waited for; matrix products, arithmetic and copies ran while one was open for 5% of the time, Pallas kernels for 0%

profile of v15, /device:TPU:0, one launch (start us, length us, event | category | flops | bytes accessed | tf_op | source)
XLA Modules:
  0.0 96.9 jit_solution(14767206487668319517)
XLA Ops:
  6.2 7.4 %all-to-all-start = ((bf16[32,8,228]{2,1,0:T(8,128)(2,1)}), bf16[32,8,228]{2,1,0:T(8,128)(2,1)S(1)}, u32[]{:S(2)}, u32[]{:S(2)}) async-start(bf16[32,8,228]{2,1,0:T(8,128)(2,1)} %reshape.710), calls=%async_computation | async-start | bytes 262144 | tf_op jit(solution)/shard_map/all_to_all | solution.py:118
  13.6 1.3 %fusion.101 = (bf16[2,48,4,256]{3,2,1,0:T(4,128)(2,1)S(1)}, bf16[2,48,4,256]{3,2,1,0:T(4,128)(2,1)S(1)}) fusion(bf16[2,48,32,256]{3,2,1,0:T(8,128)(2,1)} %param.9), kind=kLoop, calls=%fused_computation.294 | loop fusion | bytes 786432 | tf_op jit(solution)/shard_map/slice | solution.py:74
  15.1 2.0 %collective-permute-start = (bf16[2,48,4,256]{3,0,2,1:T(2,128)(2,1)S(1)}, bf16[2,48,4,256]{3,0,2,1:T(2,128)(2,1)S(1)}, u32[]{:S(2)}, u32[]{:S(2)}) collective-permute-start(bf16[2,48,4,256]{3,0,2,1:T(2,128)(2,1)S(1)} %copy.595), channel_id=1, source_target_pairs={{0,2},{2,4},{4,6},{6,8},{8,10},{10,12},{12,14},{14,0},{1,3},{3,5},... | collective-permute-start | bytes 589832 | tf_op jit(solution)/shard_map/ppermute | solution.py:78
  17.3 2.9 %collective-permute-start.1 = (bf16[2,48,4,256]{3,0,2,1:T(2,128)(2,1)S(1)}, bf16[2,48,4,256]{3,0,2,1:T(2,128)(2,1)S(1)}, u32[]{:S(2)}, u32[]{:S(2)}) collective-permute-start(bf16[2,48,4,256]{3,0,2,1:T(2,128)(2,1)S(1)} %copy.596), channel_id=1, source_target_pairs={{2,0},{4,2},{6,4},{8,6},{10,8},{12,10},{14,12},{0,14},{3,1},{5,3},... | collective-permute-start | bytes 589832 | tf_op jit(solution)/shard_map/ppermute | solution.py:80
  20.3 6.0 %collective-permute-done = bf16[2,48,4,256]{3,0,2,1:T(2,128)(2,1)S(1)} collective-permute-done((bf16[2,48,4,256]{3,0,2,1:T(2,128)(2,1)S(1)}, bf16[2,48,4,256]{3,0,2,1:T(2,128)(2,1)S(1)}, u32[]{:S(2)}, u32[]{:S(2)}) %collective-permute-start) | collective-permute-done | bytes 196640 | tf_op jit(solution)/shard_map/ppermute | solution.py:78
  26.4 1.7 %constant_dynamic-update-slice_fusion.1 = bf16[2,48,40,256]{3,0,2,1:T(2,128)(2,1)S(1)} fusion(bf16[2,48,40,256]{3,0,2,1:T(2,128)(2,1)S(1)} %constant_dynamic-update-slice_fusion.2, bf16[2,48,32,256]{3,2,1,0:T(8,128)(2,1)S(1)} %copy-done.3), kind=kLoop, calls=%fused_computation.246 | loop fusion | bytes 3145728
  30.3 1.3 %collective-permute-start.2 = (bf16[2,4,40,256]{3,0,2,1:T(2,128)(2,1)S(1)}, bf16[2,4,40,256]{3,0,2,1:T(2,128)(2,1)S(1)}, u32[]{:S(2)}, u32[]{:S(2)}) collective-permute-start(bf16[2,4,40,256]{3,0,2,1:T(2,128)(2,1)S(1)} %get-tuple-element.88), channel_id=1, source_target_pairs={{0,1},{2,3},{4,5},{6,7},{8,9},{10,11},{12,13},{14,15},{16,17},{18,... | collective-permute-start | bytes 491528 | tf_op jit(solution)/shard_map/ppermute | solution.py:78
  31.6 1.3 %collective-permute-start.3 = (bf16[2,4,40,256]{3,0,2,1:T(2,128)(2,1)S(1)}, bf16[2,4,40,256]{3,0,2,1:T(2,128)(2,1)S(1)}, u32[]{:S(2)}, u32[]{:S(2)}) collective-permute-start(bf16[2,4,40,256]{3,0,2,1:T(2,128)(2,1)S(1)} %get-tuple-element.89), channel_id=1, source_target_pairs={{1,0},{3,2},{5,4},{7,6},{9,8},{11,10},{13,12},{15,14},{17,16},{19,... | collective-permute-start | bytes 491528 | tf_op jit(solution)/shard_map/ppermute | solution.py:80
  34.9 4.8 %pad_maximum_fusion = bf16[2,56,40,256]{3,0,2,1:T(2,128)(2,1)S(1)} fusion(bf16[2,4,40,256]{3,0,2,1:T(2,128)(2,1)S(1)} %collective-permute-done.3, bf16[2,48,40,256]{3,0,2,1:T(2,128)(2,1)} %copy-done.2, bf16[2,4,40,256]{3,0,2,1:T(2,128)(2,1)S(1)} %collective-permute-done.2), kind=kLoop, calls=%fused_computation.1 | loop fusion | flops 2293760 | bytes 4587520 | tf_op jit(solution)/shard_map/concatenate | solution.py:76
  39.7 5.7 %gather_fusion = bf16[32,9,16,256]{3,0,2,1:T(8,128)(2,1)} fusion(bf16[2,56,40,256]{3,0,2,1:T(2,128)(2,1)S(1)} %pad_maximum_fusion, s32[32]{0:T(128)S(1)} %fusion.99), kind=kCustom, calls=%fused_computation | custom fusion | bytes 4719104 | tf_op jit(solution)/shard_map/vmap()/gather | solution.py:151
  45.5 2.5 %slice_convert_fusion.20 = (f32[32,1,8,256]{3,0,2,1:T(8,128)S(1)}, f32[32,1,8,256]{3,0,2,1:T(8,128)S(1)}, f32[32,1,8,256]{3,0,2,1:T(8,128)S(1)}, f32[32,1,8,256]...) fusion(bf16[32,9,16,256]{3,0,2,1:T(8,128)(2,1)} %gather_fusion), kind=kLoop, calls=%fused_computation.187 | loop fusion | flops 1245184 | bytes 7471104 | tf_op jit(solution)/shard_map/convert_element_type | solution.py:157
  50.1 3.9 %fusion.47 = bf16[256,256]{1,0:T(8,128)(2,1)S(1)} fusion(f32[32,1,8,256]{3,2,0,1:T(8,128)S(1)} %copy.476, f32[32,1,8,256]{3,2,0,1:T(8,128)S(1)} %copy.475, f32[32,1,8,256]{3,2,0,1:T(8,128)S(1)} %copy.474, f32[32,1,8,256]{3,2,0,1:T(8,128)S(1)} %copy.473, f32[32,1,8,256]{3,2,0,1:T(8,128)S(1)} %copy.472, f32[32,1,8,256]{3,2,0,1:T(8,128)S(1)} %copy.471, ...), kind=kLoop, calls=%fused_computation.93 | loop fusion | flops 4325376 | bytes 8815616 | tf_op jit(solution)/shard_map/convert_element_type | solution.py:173
  57.1 1.6 %fusion.38 = (f32[256]{0:T(256)S(1)}, f32[256]{0:T(256)S(1)}, f32[256,256]{1,0:T(8,128)S(1)}) fusion(f32[32,1,8,256]{3,0,2,1:T(8,128)S(1)} %get-tuple-element.47, f32[32,1,8,256]{3,0,2,1:T(8,128)S(1)} %get-tuple-element.48, f32[32,1,8,256]{3,0,2,1:T(8,128)S(1)} %get-tuple-element.49, f32[32,1,8,256]{3,0,2,1:T(8,128)S(1)} %get-tuple-element.50, ...), kind=kOutput, calls=%fused_computation.76 | convolution fusion | flops 34733568 | bytes 2627584 | tf_op jit(solution)/shard_map/dot_general | solution.py:191
  58.7 2.4 %fusion.22 = (f32[256]{0:T(256)S(1)}, f32[256]{0:T(256)S(1)}, f32[256]{0:T(256)S(1)}) fusion(f32[256,256]{1,0:T(8,128)S(1)} %get-tuple-element.145, f32[32,1,8,256]{3,0,2,1:T(8,128)S(1)} %get-tuple-element.35, f32[32,1,8,256]{3,0,2,1:T(8,128)S(1)} %get-tuple-element.36, f32[32,1,8,256]{3,0,2,1:T(8,128)S(1)} %get-tuple-element.37, ...), kind=kLoop, calls=%fused_computation.47 | loop fusion | flops 1768704 | bytes 3415040 | tf_op jit(solution)/shard_map/reduce_sum | solution.py:204
  61.1 2.6 %fusion.7 = (f32[256]{0:T(256)S(1)}, f32[256]{0:T(256)S(1)}, f32[256]{0:T(256)S(1)}, f32[256]{0:T(256)S(1)}) fusion(f32[256,256]{1,0:T(8,128)S(1)} %get-tuple-element.145, f32[32,1,8,256]{3,0,2,1:T(8,128)S(1)} %get-tuple-element.23, f32[32,1,8,256]{3,0,2,1:T(8,128)S(1)} %get-tuple-element.24, f32[32,1,8,256]{3,0,2,1:T(8,128)S(1)} %get-tuple-element.25, ...), kind=kLoop, calls=%fused_computation.20 | loop fusion | flops 1899520 | bytes 3678208 | tf_op jit(solution)/shard_map/reduce_sum | solution.py:204
  65.0 1.3 %collective-permute-done.4 = f32[512,128]{1,0:T(8,128)S(1)} collective-permute-done((f32[512,128]{1,0:T(8,128)S(1)}, f32[512,128]{1,0:T(8,128)S(1)}, u32[]{:S(2)}, u32[]{:S(2)}) %collective-permute-start.4) | collective-permute-done | bytes 262176 | tf_op jit(solution)/shard_map/ppermute | solution.py:22
  66.3 2.1 %collective-permute-start.5 = (f32[256,128]{1,0:T(8,128)S(1)}, f32[256,128]{1,0:T(8,128)S(1)}, u32[]{:S(2)}, u32[]{:S(2)}) collective-permute-start(f32[256,128]{1,0:T(8,128)S(1)} %constant_dynamic-slice_fusion), channel_id=1, source_target_pairs={{0,2},{2,0},{4,6},{6,4},{8,10},{10,8},{12,14},{14,12},{1,3},{3,1},... | collective-permute-start | bytes 393224 | tf_op jit(solution)/shard_map/ppermute | solution.py:22
  68.4 3.9 %collective-permute-done.5 = f32[256,128]{1,0:T(8,128)S(1)} collective-permute-done((f32[256,128]{1,0:T(8,128)S(1)}, f32[256,128]{1,0:T(8,128)S(1)}, u32[]{:S(2)}, u32[]{:S(2)}) %collective-permute-start.5) | collective-permute-done | bytes 131104 | tf_op jit(solution)/shard_map/ppermute | solution.py:22
  72.3 1.5 %collective-permute-start.6 = (f32[256,128]{1,0:T(8,128)S(1)}, f32[256,128]{1,0:T(8,128)S(1)}, u32[]{:S(2)}, u32[]{:S(2)}) collective-permute-start(f32[256,128]{1,0:T(8,128)S(1)} %dynamic-slice_add_fusion.1), channel_id=1, source_target_pairs={{0,4},{2,6},{4,0},{6,2},{8,12},{10,14},{12,8},{14,10},{1,5},{3,7},... | collective-permute-start | bytes 393224 | tf_op jit(solution)/shard_map/ppermute | solution.py:56
  73.8 3.7 %collective-permute-done.6 = f32[256,128]{1,0:T(8,128)S(1)} collective-permute-done((f32[256,128]{1,0:T(8,128)S(1)}, f32[256,128]{1,0:T(8,128)S(1)}, u32[]{:S(2)}, u32[]{:S(2)}) %collective-permute-start.6) | collective-permute-done | bytes 131104 | tf_op jit(solution)/shard_map/ppermute | solution.py:56
  77.6 2.1 %collective-permute-start.7 = (f32[256,128]{1,0:T(8,128)S(1)}, f32[256,128]{1,0:T(8,128)S(1)}, u32[]{:S(2)}, u32[]{:S(2)}) collective-permute-start(f32[256,128]{1,0:T(8,128)S(1)} %add.473), channel_id=1, source_target_pairs={{0,8},{2,10},{4,12},{6,14},{8,0},{10,2},{12,4},{14,6},{1,9},{3,11}... | collective-permute-start | bytes 393224 | tf_op jit(solution)/shard_map/ppermute | solution.py:56
  79.6 6.0 %collective-permute-done.7 = f32[256,128]{1,0:T(8,128)S(1)} collective-permute-done((f32[256,128]{1,0:T(8,128)S(1)}, f32[256,128]{1,0:T(8,128)S(1)}, u32[]{:S(2)}, u32[]{:S(2)}) %collective-permute-start.7) | collective-permute-done | bytes 131104 | tf_op jit(solution)/shard_map/ppermute | solution.py:56
  86.7 4.0 %collective-permute-done.8 = f32[256,128]{1,0:T(8,128)S(1)} collective-permute-done((f32[256,128]{1,0:T(8,128)S(1)}, f32[256,128]{1,0:T(8,128)S(1)}, u32[]{:S(2)}, u32[]{:S(2)}) %collective-permute-start.8) | collective-permute-done | bytes 131104 | tf_op jit(solution)/shard_map/ppermute | solution.py:29
  90.9 1.4 %collective-permute-done.9 = f32[512,128]{1,0:T(8,128)S(1)} collective-permute-done((f32[512,128]{1,0:T(8,128)S(1)}, f32[512,128]{1,0:T(8,128)S(1)}, u32[]{:S(2)}, u32[]{:S(2)}) %collective-permute-start.9) | collective-permute-done | bytes 262176 | tf_op jit(solution)/shard_map/ppermute | solution.py:29
  (101 shorter events, 20.7 us)
Async XLA Ops:
  0.6 53.3 %copy-start = (bf16[256,256]{1,0:T(8,128)(2,1)S(1)}, bf16[256,256]{1,0:T(8,128)(2,1)}, u32[]{:S(2)}) copy-start(bf16[256,256]{1,0:T(8,128)(2,1)} %param.12) | copy-start | bytes 393220
  0.6 25.7 %copy-start.3 = (bf16[2,48,32,256]{3,2,1,0:T(8,128)(2,1)S(1)}, bf16[2,48,32,256]{3,2,1,0:T(8,128)(2,1)}, u32[]{:S(2)}) copy-start(bf16[2,48,32,256]{3,2,1,0:T(8,128)(2,1)} %param.9) | copy-start | bytes 4718596
  0.7 19.5 %copy-start.5 = (bf16[9,256]{1,0:T(8,128)(2,1)S(1)}, bf16[9,256]{1,0:T(8,128)(2,1)}, u32[]{:S(2)}) copy-start(bf16[9,256]{1,0:T(8,128)(2,1)} %param.11) | copy-start | bytes 13828
  0.7 19.5 %copy-start.6 = (s32[256]{0:T(256)S(1)}, s32[256]{0:T(256)}, u32[]{:S(2)}) copy-start(s32[256]{0:T(256)} %param.10) | copy-start | bytes 3076
  6.2 26.7 %all-to-all-start = ((bf16[32,8,228]{2,1,0:T(8,128)(2,1)}), bf16[32,8,228]{2,1,0:T(8,128)(2,1)S(1)}, u32[]{:S(2)}, u32[]{:S(2)}) async-start(bf16[32,8,228]{2,1,0:T(8,128)(2,1)} %reshape.710), calls=%async_computation | async-start | bytes 262144 | tf_op jit(solution)/shard_map/all_to_all | solution.py:118
  15.1 11.2 %collective-permute-start = (bf16[2,48,4,256]{3,0,2,1:T(2,128)(2,1)S(1)}, bf16[2,48,4,256]{3,0,2,1:T(2,128)(2,1)S(1)}, u32[]{:S(2)}, u32[]{:S(2)}) collective-permute-start(bf16[2,48,4,256]{3,0,2,1:T(2,128)(2,1)S(1)} %copy.595), channel_id=1, source_target_pairs={{0,2},{2,4},{4,6},{6,8},{8,10},{10,12},{12,14},{14,0},{1,3},{3,5},... | collective-permute-start | bytes 589832 | tf_op jit(solution)/shard_map/ppermute | solution.py:78
  17.3 11.4 %collective-permute-start.1 = (bf16[2,48,4,256]{3,0,2,1:T(2,128)(2,1)S(1)}, bf16[2,48,4,256]{3,0,2,1:T(2,128)(2,1)S(1)}, u32[]{:S(2)}, u32[]{:S(2)}) collective-permute-start(bf16[2,48,4,256]{3,0,2,1:T(2,128)(2,1)S(1)} %copy.596), channel_id=1, source_target_pairs={{2,0},{4,2},{6,4},{8,6},{10,8},{12,10},{14,12},{0,14},{3,1},{5,3},... | collective-permute-start | bytes 589832 | tf_op jit(solution)/shard_map/ppermute | solution.py:80
  28.8 1.3 %copy-start.2 = (bf16[2,48,40,256]{3,0,2,1:T(2,128)(2,1)}, bf16[2,48,40,256]{3,0,2,1:T(2,128)(2,1)S(1)}, u32[]{:S(2)}) copy-start(bf16[2,48,40,256]{3,0,2,1:T(2,128)(2,1)S(1)} %constant_dynamic-update-slice_fusion) | copy-start | bytes 5898244
  30.3 3.7 %collective-permute-start.2 = (bf16[2,4,40,256]{3,0,2,1:T(2,128)(2,1)S(1)}, bf16[2,4,40,256]{3,0,2,1:T(2,128)(2,1)S(1)}, u32[]{:S(2)}, u32[]{:S(2)}) collective-permute-start(bf16[2,4,40,256]{3,0,2,1:T(2,128)(2,1)S(1)} %get-tuple-element.88), channel_id=1, source_target_pairs={{0,1},{2,3},{4,5},{6,7},{8,9},{10,11},{12,13},{14,15},{16,17},{18,... | collective-permute-start | bytes 491528 | tf_op jit(solution)/shard_map/ppermute | solution.py:78
  31.6 3.3 %collective-permute-start.3 = (bf16[2,4,40,256]{3,0,2,1:T(2,128)(2,1)S(1)}, bf16[2,4,40,256]{3,0,2,1:T(2,128)(2,1)S(1)}, u32[]{:S(2)}, u32[]{:S(2)}) collective-permute-start(bf16[2,4,40,256]{3,0,2,1:T(2,128)(2,1)S(1)} %get-tuple-element.89), channel_id=1, source_target_pairs={{1,0},{3,2},{5,4},{7,6},{9,8},{11,10},{13,12},{15,14},{17,16},{19,... | collective-permute-start | bytes 491528 | tf_op jit(solution)/shard_map/ppermute | solution.py:80
  45.4 2.5 %copy-start.1 = (bf16[32,9,16,256]{3,0,2,1:T(8,128)(2,1)S(1)}, bf16[32,9,16,256]{3,0,2,1:T(8,128)(2,1)}, u32[]{:S(2)}) copy-start(bf16[32,9,16,256]{3,0,2,1:T(8,128)(2,1)} %gather_fusion) | copy-start | bytes 7077892
  50.0 4.2 %copy-start.4 = (bf16[256,227]{0,1:T(8,128)(2,1)S(1)}, bf16[256,227]{0,1:T(8,128)(2,1)}, u32[]{:S(2)}) copy-start(bf16[256,227]{0,1:T(8,128)(2,1)} %param.13) | copy-start | bytes 348676
  64.7 1.6 %collective-permute-start.4 = (f32[512,128]{1,0:T(8,128)S(1)}, f32[512,128]{1,0:T(8,128)S(1)}, u32[]{:S(2)}, u32[]{:S(2)}) collective-permute-start(f32[512,128]{1,0:T(8,128)S(1)} %constant_dynamic-slice_fusion.1), channel_id=1, source_target_pairs={{0,1},{1,0},{2,3},{3,2},{4,5},{5,4},{6,7},{7,6},{8,9},{9,8},{10,11... | collective-permute-start | bytes 786440 | tf_op jit(solution)/shard_map/ppermute | solution.py:22
  66.3 6.0 %collective-permute-start.5 = (f32[256,128]{1,0:T(8,128)S(1)}, f32[256,128]{1,0:T(8,128)S(1)}, u32[]{:S(2)}, u32[]{:S(2)}) collective-permute-start(f32[256,128]{1,0:T(8,128)S(1)} %constant_dynamic-slice_fusion), channel_id=1, source_target_pairs={{0,2},{2,0},{4,6},{6,4},{8,10},{10,8},{12,14},{14,12},{1,3},{3,1},... | collective-permute-start | bytes 393224 | tf_op jit(solution)/shard_map/ppermute | solution.py:22
  72.3 5.2 %collective-permute-start.6 = (f32[256,128]{1,0:T(8,128)S(1)}, f32[256,128]{1,0:T(8,128)S(1)}, u32[]{:S(2)}, u32[]{:S(2)}) collective-permute-start(f32[256,128]{1,0:T(8,128)S(1)} %dynamic-slice_add_fusion.1), channel_id=1, source_target_pairs={{0,4},{2,6},{4,0},{6,2},{8,12},{10,14},{12,8},{14,10},{1,5},{3,7},... | collective-permute-start | bytes 393224 | tf_op jit(solution)/shard_map/ppermute | solution.py:56
  77.6 8.0 %collective-permute-start.7 = (f32[256,128]{1,0:T(8,128)S(1)}, f32[256,128]{1,0:T(8,128)S(1)}, u32[]{:S(2)}, u32[]{:S(2)}) collective-permute-start(f32[256,128]{1,0:T(8,128)S(1)} %add.473), channel_id=1, source_target_pairs={{0,8},{2,10},{4,12},{6,14},{8,0},{10,2},{12,4},{14,6},{1,9},{3,11}... | collective-permute-start | bytes 393224 | tf_op jit(solution)/shard_map/ppermute | solution.py:56
  85.7 5.0 %collective-permute-start.8 = (f32[256,128]{1,0:T(8,128)S(1)}, f32[256,128]{1,0:T(8,128)S(1)}, u32[]{:S(2)}, u32[]{:S(2)}) collective-permute-start(f32[256,128]{1,0:T(8,128)S(1)} %get-tuple-element.18), channel_id=1, source_target_pairs={{0,2},{2,0},{4,6},{6,4},{8,10},{10,8},{12,14},{14,12},{1,3},{3,1},... | collective-permute-start | bytes 393224 | tf_op jit(solution)/shard_map/ppermute | solution.py:29
  90.7 1.6 %collective-permute-start.9 = (f32[512,128]{1,0:T(8,128)S(1)}, f32[512,128]{1,0:T(8,128)S(1)}, u32[]{:S(2)}, u32[]{:S(2)}) collective-permute-start(f32[512,128]{1,0:T(8,128)S(1)} %constant_dynamic-update-slice_fusion.5), channel_id=1, source_target_pairs={{0,1},{1,0},{2,3},{3,2},{4,5},{5,4},{6,7},{7,6},{8,9},{9,8},{10,11... | collective-permute-start | bytes 786440 | tf_op jit(solution)/shard_map/ppermute | solution.py:29

commit v16 on v15

--- a/solution.py
+++ b/solution.py
@@ -112,16 +112,10 @@
     chooser = (slot_index[None, :] == jnp.arange(slots, dtype=jnp.int32)[:, None]).astype(
         jnp.bfloat16
     )
-    send = jnp.dot(
-        chooser, packed.reshape(tiles_here, -1), preferred_element_type=jnp.float32
+    send = jnp.einsum(
+        "st,tre->sre", chooser, packed, preferred_element_type=jnp.float32
     ).astype(jnp.bfloat16)
-    recv = lax.all_to_all(
-        send.reshape(slots, TILE, teach_width + 1),
-        ("lon", "lat"),
-        split_axis=0,
-        concat_axis=0,
-        tiled=True,
-    )
+    recv = lax.all_to_all(send, ("lon", "lat"), split_axis=0, concat_axis=0, tiled=True)
     recv_tiles = recv[:, :, :teach_width]
     meta = recv[:, :3, teach_width].astype(jnp.int32)
     recv_start = meta[:, 0] * base + meta[:, 1]

time: 97.3 us -> 97 us (level)
    reshape x2 -> x0, local copies, waits for them, and re-layouts: 1.02 us -> none  [the longest x1 0.89 us: local(): send.reshape(slots, TILE, teach_width + 1)]
    unnamed x21 -> x26, local copies, waits for them, and re-layouts: 3.81 us -> 4.69 us
where the time goes in v16:
time: 97 us; the launch traced here: 96.6 us
  waiting for transfers between devices  27.8 us (29%)
  other arithmetic  22 us (23%)
  starting transfers between devices  21.8 us (22%)
  local copies, waits for them, and re-layouts  18 us (19%)
  matrix products  4.04 us (4%)
  between operations  2.9 us (3%)
    ppermute x2, waiting for transfers between devices, packed_sum(): x = x + lax.ppermute(x, axis, [(i, i ^ bit) for i in range(count)])  9.76 us
    all_to_all x1, starting transfers between devices, local(): lax.all_to_all(send, ('lon', 'lat'), split_axis=0, concat_axis=0, tiled=T...  7.36 us
    ppermute x2, waiting for transfers between devices, padded_2(): lax.ppermute(tail, axis, [(i, (i + 1) % count) for i in range(ends)])  5.98 us
    gather x1, local copies, waits for them, and re-layouts, gather_windows(): lax.dynamic_slice(padded, (b, h, w, jnp.int32(0)), (1, span, reach, width))  5.74 us
    ppermute x2, waiting for transfers between devices, double(): got = lax.ppermute(x, axis, [(i, i ^ bit) for i in range(count)])  5.46 us
    ppermute x2, waiting for transfers between devices, halve(): return keep + lax.ppermute(send, axis, [(i, i ^ bit) for i in range(count)])  5.2 us
    reduce_sum x2, other arithmetic, backward(): tap_sums.append(jnp.sum((chosen * grad_z).reshape(-1, width), axis=0))  5 us
    concatenate x1, other arithmetic, padded_2(): jnp.concatenate([lax.ppermute(tail, axis, [(i, (i + 1) % count) for i in...  4.77 us
  transfers between devices with their start and end apart: 11, of which 9 were waited for; matrix products, arithmetic and copies ran while one was open for 5% of the time, Pallas kernels for 0%

profile of v16, /device:TPU:0, one launch (start us, length us, event | category | flops | bytes accessed | tf_op | source)
XLA Modules:
  0.0 96.6 jit_solution(17303952239172506312)
XLA Ops:
  5.9 7.4 %all-to-all-start = ((bf16[32,8,228]{2,1,0:T(8,128)(2,1)}), bf16[32,8,228]{2,1,0:T(8,128)(2,1)S(1)}, u32[]{:S(2)}, u32[]{:S(2)}) async-start(bf16[32,8,228]{2,1,0:T(8,128)(2,1)} %copy.321), calls=%async_computation | async-start | bytes 262144 | tf_op jit(solution)/shard_map/all_to_all | solution.py:118
  13.3 1.3 %fusion.107 = (bf16[2,48,4,256]{3,2,1,0:T(4,128)(2,1)S(1)}, bf16[2,48,4,256]{3,2,1,0:T(4,128)(2,1)S(1)}) fusion(bf16[2,48,32,256]{3,2,1,0:T(8,128)(2,1)} %param.9), kind=kLoop, calls=%fused_computation.303 | loop fusion | bytes 786432 | tf_op jit(solution)/shard_map/slice | solution.py:74
  14.8 2.0 %collective-permute-start = (bf16[2,48,4,256]{3,0,2,1:T(2,128)(2,1)S(1)}, bf16[2,48,4,256]{3,0,2,1:T(2,128)(2,1)S(1)}, u32[]{:S(2)}, u32[]{:S(2)}) collective-permute-start(bf16[2,48,4,256]{3,0,2,1:T(2,128)(2,1)S(1)} %copy.451), channel_id=1, source_target_pairs={{0,2},{2,4},{4,6},{6,8},{8,10},{10,12},{12,14},{14,0},{1,3},{3,5},... | collective-permute-start | bytes 589832 | tf_op jit(solution)/shard_map/ppermute | solution.py:78
  17.0 2.9 %collective-permute-start.1 = (bf16[2,48,4,256]{3,0,2,1:T(2,128)(2,1)S(1)}, bf16[2,48,4,256]{3,0,2,1:T(2,128)(2,1)S(1)}, u32[]{:S(2)}, u32[]{:S(2)}) collective-permute-start(bf16[2,48,4,256]{3,0,2,1:T(2,128)(2,1)S(1)} %copy.452), channel_id=1, source_target_pairs={{2,0},{4,2},{6,4},{8,6},{10,8},{12,10},{14,12},{0,14},{3,1},{5,3},... | collective-permute-start | bytes 589832 | tf_op jit(solution)/shard_map/ppermute | solution.py:80
  20.0 6.0 %collective-permute-done = bf16[2,48,4,256]{3,0,2,1:T(2,128)(2,1)S(1)} collective-permute-done((bf16[2,48,4,256]{3,0,2,1:T(2,128)(2,1)S(1)}, bf16[2,48,4,256]{3,0,2,1:T(2,128)(2,1)S(1)}, u32[]{:S(2)}, u32[]{:S(2)}) %collective-permute-start) | collective-permute-done | bytes 196640 | tf_op jit(solution)/shard_map/ppermute | solution.py:78
  26.1 1.7 %constant_dynamic-update-slice_fusion.1 = bf16[2,48,40,256]{3,0,2,1:T(2,128)(2,1)S(1)} fusion(bf16[2,48,40,256]{3,0,2,1:T(2,128)(2,1)S(1)} %constant_dynamic-update-slice_fusion.2, bf16[2,48,32,256]{3,2,1,0:T(8,128)(2,1)S(1)} %copy-done.3), kind=kLoop, calls=%fused_computation.245 | loop fusion | bytes 3145728
  28.5 1.3 %copy-done.2 = bf16[2,48,40,256]{3,0,2,1:T(2,128)(2,1)} copy-done((bf16[2,48,40,256]{3,0,2,1:T(2,128)(2,1)}, bf16[2,48,40,256]{3,0,2,1:T(2,128)(2,1)S(1)}, u32[]{:S(2)}) %copy-start.2) | copy-done | bytes 1966104
  30.0 1.3 %collective-permute-start.2 = (bf16[2,4,40,256]{3,0,2,1:T(2,128)(2,1)S(1)}, bf16[2,4,40,256]{3,0,2,1:T(2,128)(2,1)S(1)}, u32[]{:S(2)}, u32[]{:S(2)}) collective-permute-start(bf16[2,4,40,256]{3,0,2,1:T(2,128)(2,1)S(1)} %get-tuple-element.88), channel_id=1, source_target_pairs={{0,1},{2,3},{4,5},{6,7},{8,9},{10,11},{12,13},{14,15},{16,17},{18,... | collective-permute-start | bytes 491528 | tf_op jit(solution)/shard_map/ppermute | solution.py:78
  31.3 1.3 %collective-permute-start.3 = (bf16[2,4,40,256]{3,0,2,1:T(2,128)(2,1)S(1)}, bf16[2,4,40,256]{3,0,2,1:T(2,128)(2,1)S(1)}, u32[]{:S(2)}, u32[]{:S(2)}) collective-permute-start(bf16[2,4,40,256]{3,0,2,1:T(2,128)(2,1)S(1)} %get-tuple-element.89), channel_id=1, source_target_pairs={{1,0},{3,2},{5,4},{7,6},{9,8},{11,10},{13,12},{15,14},{17,16},{19,... | collective-permute-start | bytes 491528 | tf_op jit(solution)/shard_map/ppermute | solution.py:80
  34.6 4.8 %pad_maximum_fusion = bf16[2,56,40,256]{3,0,2,1:T(2,128)(2,1)S(1)} fusion(bf16[2,4,40,256]{3,0,2,1:T(2,128)(2,1)S(1)} %collective-permute-done.3, bf16[2,48,40,256]{3,0,2,1:T(2,128)(2,1)} %copy-done.2, bf16[2,4,40,256]{3,0,2,1:T(2,128)(2,1)S(1)} %collective-permute-done.2), kind=kLoop, calls=%fused_computation.1 | loop fusion | flops 2293760 | bytes 4587520 | tf_op jit(solution)/shard_map/concatenate | solution.py:76
  39.4 5.7 %gather_fusion = bf16[32,9,16,256]{3,0,2,1:T(8,128)(2,1)} fusion(bf16[2,56,40,256]{3,0,2,1:T(2,128)(2,1)S(1)} %pad_maximum_fusion, s32[32]{0:T(128)S(1)} %fusion.104), kind=kCustom, calls=%fused_computation | custom fusion | bytes 4719104 | tf_op jit(solution)/shard_map/vmap()/gather | solution.py:145
  45.2 2.5 %slice_convert_fusion.20 = (f32[32,1,8,256]{3,0,2,1:T(8,128)S(1)}, f32[32,1,8,256]{3,0,2,1:T(8,128)S(1)}, f32[32,1,8,256]{3,0,2,1:T(8,128)S(1)}, f32[32,1,8,256]...) fusion(bf16[32,9,16,256]{3,0,2,1:T(8,128)(2,1)} %gather_fusion), kind=kLoop, calls=%fused_computation.187 | loop fusion | flops 1245184 | bytes 7471104 | tf_op jit(solution)/shard_map/convert_element_type | solution.py:151
  49.8 3.9 %fusion.47 = bf16[256,256]{1,0:T(8,128)(2,1)S(1)} fusion(f32[32,1,8,256]{3,2,0,1:T(8,128)S(1)} %copy.332, f32[32,1,8,256]{3,2,0,1:T(8,128)S(1)} %copy.331, f32[32,1,8,256]{3,2,0,1:T(8,128)S(1)} %copy.330, f32[32,1,8,256]{3,2,0,1:T(8,128)S(1)} %copy.329, f32[32,1,8,256]{3,2,0,1:T(8,128)S(1)} %copy.328, f32[32,1,8,256]{3,2,0,1:T(8,128)S(1)} %copy.327, ...), kind=kLoop, calls=%fused_computation.93 | loop fusion | flops 4325376 | bytes 8815616 | tf_op jit(solution)/shard_map/convert_element_type | solution.py:167
  56.8 1.6 %fusion.38 = (f32[256]{0:T(256)S(1)}, f32[256]{0:T(256)S(1)}, f32[256,256]{1,0:T(8,128)S(1)}) fusion(f32[32,1,8,256]{3,0,2,1:T(8,128)S(1)} %get-tuple-element.47, f32[32,1,8,256]{3,0,2,1:T(8,128)S(1)} %get-tuple-element.48, f32[32,1,8,256]{3,0,2,1:T(8,128)S(1)} %get-tuple-element.49, f32[32,1,8,256]{3,0,2,1:T(8,128)S(1)} %get-tuple-element.50, ...), kind=kOutput, calls=%fused_computation.76 | convolution fusion | flops 34733568 | bytes 2627584 | tf_op jit(solution)/shard_map/dot_general | solution.py:185
  58.4 2.4 %fusion.22 = (f32[256]{0:T(256)S(1)}, f32[256]{0:T(256)S(1)}, f32[256]{0:T(256)S(1)}) fusion(f32[256,256]{1,0:T(8,128)S(1)} %get-tuple-element.145, f32[32,1,8,256]{3,0,2,1:T(8,128)S(1)} %get-tuple-element.35, f32[32,1,8,256]{3,0,2,1:T(8,128)S(1)} %get-tuple-element.36, f32[32,1,8,256]{3,0,2,1:T(8,128)S(1)} %get-tuple-element.37, ...), kind=kLoop, calls=%fused_computation.47 | loop fusion | flops 1768704 | bytes 3415040 | tf_op jit(solution)/shard_map/reduce_sum | solution.py:198
  60.8 2.6 %fusion.7 = (f32[256]{0:T(256)S(1)}, f32[256]{0:T(256)S(1)}, f32[256]{0:T(256)S(1)}, f32[256]{0:T(256)S(1)}) fusion(f32[256,256]{1,0:T(8,128)S(1)} %get-tuple-element.145, f32[32,1,8,256]{3,0,2,1:T(8,128)S(1)} %get-tuple-element.23, f32[32,1,8,256]{3,0,2,1:T(8,128)S(1)} %get-tuple-element.24, f32[32,1,8,256]{3,0,2,1:T(8,128)S(1)} %get-tuple-element.25, ...), kind=kLoop, calls=%fused_computation.20 | loop fusion | flops 1899520 | bytes 3678208 | tf_op jit(solution)/shard_map/reduce_sum | solution.py:198
  66.0 2.1 %collective-permute-start.5 = (f32[256,128]{1,0:T(8,128)S(1)}, f32[256,128]{1,0:T(8,128)S(1)}, u32[]{:S(2)}, u32[]{:S(2)}) collective-permute-start(f32[256,128]{1,0:T(8,128)S(1)} %constant_dynamic-slice_fusion), channel_id=1, source_target_pairs={{0,2},{2,0},{4,6},{6,4},{8,10},{10,8},{12,14},{14,12},{1,3},{3,1},... | collective-permute-start | bytes 393224 | tf_op jit(solution)/shard_map/ppermute | solution.py:22
  68.1 3.9 %collective-permute-done.5 = f32[256,128]{1,0:T(8,128)S(1)} collective-permute-done((f32[256,128]{1,0:T(8,128)S(1)}, f32[256,128]{1,0:T(8,128)S(1)}, u32[]{:S(2)}, u32[]{:S(2)}) %collective-permute-start.5) | collective-permute-done | bytes 131104 | tf_op jit(solution)/shard_map/ppermute | solution.py:22
  72.1 1.5 %collective-permute-start.6 = (f32[256,128]{1,0:T(8,128)S(1)}, f32[256,128]{1,0:T(8,128)S(1)}, u32[]{:S(2)}, u32[]{:S(2)}) collective-permute-start(f32[256,128]{1,0:T(8,128)S(1)} %dynamic-slice_add_fusion.1), channel_id=1, source_target_pairs={{0,4},{2,6},{4,0},{6,2},{8,12},{10,14},{12,8},{14,10},{1,5},{3,7},... | collective-permute-start | bytes 393224 | tf_op jit(solution)/shard_map/ppermute | solution.py:56
  73.6 3.7 %collective-permute-done.6 = f32[256,128]{1,0:T(8,128)S(1)} collective-permute-done((f32[256,128]{1,0:T(8,128)S(1)}, f32[256,128]{1,0:T(8,128)S(1)}, u32[]{:S(2)}, u32[]{:S(2)}) %collective-permute-start.6) | collective-permute-done | bytes 131104 | tf_op jit(solution)/shard_map/ppermute | solution.py:56
  77.3 2.0 %collective-permute-start.7 = (f32[256,128]{1,0:T(8,128)S(1)}, f32[256,128]{1,0:T(8,128)S(1)}, u32[]{:S(2)}, u32[]{:S(2)}) collective-permute-start(f32[256,128]{1,0:T(8,128)S(1)} %add.473), channel_id=1, source_target_pairs={{0,8},{2,10},{4,12},{6,14},{8,0},{10,2},{12,4},{14,6},{1,9},{3,11}... | collective-permute-start | bytes 393224 | tf_op jit(solution)/shard_map/ppermute | solution.py:56
  79.4 6.0 %collective-permute-done.7 = f32[256,128]{1,0:T(8,128)S(1)} collective-permute-done((f32[256,128]{1,0:T(8,128)S(1)}, f32[256,128]{1,0:T(8,128)S(1)}, u32[]{:S(2)}, u32[]{:S(2)}) %collective-permute-start.7) | collective-permute-done | bytes 131104 | tf_op jit(solution)/shard_map/ppermute | solution.py:56
  86.4 4.0 %collective-permute-done.8 = f32[256,128]{1,0:T(8,128)S(1)} collective-permute-done((f32[256,128]{1,0:T(8,128)S(1)}, f32[256,128]{1,0:T(8,128)S(1)}, u32[]{:S(2)}, u32[]{:S(2)}) %collective-permute-start.8) | collective-permute-done | bytes 131104 | tf_op jit(solution)/shard_map/ppermute | solution.py:29
  90.6 1.4 %collective-permute-done.9 = f32[512,128]{1,0:T(8,128)S(1)} collective-permute-done((f32[512,128]{1,0:T(8,128)S(1)}, f32[512,128]{1,0:T(8,128)S(1)}, u32[]{:S(2)}, u32[]{:S(2)}) %collective-permute-start.9) | collective-permute-done | bytes 262176 | tf_op jit(solution)/shard_map/ppermute | solution.py:29
  (102 shorter events, 20.3 us)
Async XLA Ops:
  0.6 53.0 %copy-start = (bf16[256,256]{1,0:T(8,128)(2,1)S(1)}, bf16[256,256]{1,0:T(8,128)(2,1)}, u32[]{:S(2)}) copy-start(bf16[256,256]{1,0:T(8,128)(2,1)} %param.12) | copy-start | bytes 393220
  0.6 25.4 %copy-start.3 = (bf16[2,48,32,256]{3,2,1,0:T(8,128)(2,1)S(1)}, bf16[2,48,32,256]{3,2,1,0:T(8,128)(2,1)}, u32[]{:S(2)}) copy-start(bf16[2,48,32,256]{3,2,1,0:T(8,128)(2,1)} %param.9) | copy-start | bytes 4718596
  0.7 19.2 %copy-start.5 = (bf16[9,256]{1,0:T(8,128)(2,1)S(1)}, bf16[9,256]{1,0:T(8,128)(2,1)}, u32[]{:S(2)}) copy-start(bf16[9,256]{1,0:T(8,128)(2,1)} %param.11) | copy-start | bytes 13828
  0.7 19.2 %copy-start.6 = (s32[256]{0:T(256)S(1)}, s32[256]{0:T(256)}, u32[]{:S(2)}) copy-start(s32[256]{0:T(256)} %param.10) | copy-start | bytes 3076
  5.9 26.7 %all-to-all-start = ((bf16[32,8,228]{2,1,0:T(8,128)(2,1)}), bf16[32,8,228]{2,1,0:T(8,128)(2,1)S(1)}, u32[]{:S(2)}, u32[]{:S(2)}) async-start(bf16[32,8,228]{2,1,0:T(8,128)(2,1)} %copy.321), calls=%async_computation | async-start | bytes 262144 | tf_op jit(solution)/shard_map/all_to_all | solution.py:118
  14.8 11.2 %collective-permute-start = (bf16[2,48,4,256]{3,0,2,1:T(2,128)(2,1)S(1)}, bf16[2,48,4,256]{3,0,2,1:T(2,128)(2,1)S(1)}, u32[]{:S(2)}, u32[]{:S(2)}) collective-permute-start(bf16[2,48,4,256]{3,0,2,1:T(2,128)(2,1)S(1)} %copy.451), channel_id=1, source_target_pairs={{0,2},{2,4},{4,6},{6,8},{8,10},{10,12},{12,14},{14,0},{1,3},{3,5},... | collective-permute-start | bytes 589832 | tf_op jit(solution)/shard_map/ppermute | solution.py:78
  17.0 11.4 %collective-permute-start.1 = (bf16[2,48,4,256]{3,0,2,1:T(2,128)(2,1)S(1)}, bf16[2,48,4,256]{3,0,2,1:T(2,128)(2,1)S(1)}, u32[]{:S(2)}, u32[]{:S(2)}) collective-permute-start(bf16[2,48,4,256]{3,0,2,1:T(2,128)(2,1)S(1)} %copy.452), channel_id=1, source_target_pairs={{2,0},{4,2},{6,4},{8,6},{10,8},{12,10},{14,12},{0,14},{3,1},{5,3},... | collective-permute-start | bytes 589832 | tf_op jit(solution)/shard_map/ppermute | solution.py:80
  28.5 1.3 %copy-start.2 = (bf16[2,48,40,256]{3,0,2,1:T(2,128)(2,1)}, bf16[2,48,40,256]{3,0,2,1:T(2,128)(2,1)S(1)}, u32[]{:S(2)}) copy-start(bf16[2,48,40,256]{3,0,2,1:T(2,128)(2,1)S(1)} %constant_dynamic-update-slice_fusion) | copy-start | bytes 5898244
  30.0 3.7 %collective-permute-start.2 = (bf16[2,4,40,256]{3,0,2,1:T(2,128)(2,1)S(1)}, bf16[2,4,40,256]{3,0,2,1:T(2,128)(2,1)S(1)}, u32[]{:S(2)}, u32[]{:S(2)}) collective-permute-start(bf16[2,4,40,256]{3,0,2,1:T(2,128)(2,1)S(1)} %get-tuple-element.88), channel_id=1, source_target_pairs={{0,1},{2,3},{4,5},{6,7},{8,9},{10,11},{12,13},{14,15},{16,17},{18,... | collective-permute-start | bytes 491528 | tf_op jit(solution)/shard_map/ppermute | solution.py:78
  31.3 3.3 %collective-permute-start.3 = (bf16[2,4,40,256]{3,0,2,1:T(2,128)(2,1)S(1)}, bf16[2,4,40,256]{3,0,2,1:T(2,128)(2,1)S(1)}, u32[]{:S(2)}, u32[]{:S(2)}) collective-permute-start(bf16[2,4,40,256]{3,0,2,1:T(2,128)(2,1)S(1)} %get-tuple-element.89), channel_id=1, source_target_pairs={{1,0},{3,2},{5,4},{7,6},{9,8},{11,10},{13,12},{15,14},{17,16},{19,... | collective-permute-start | bytes 491528 | tf_op jit(solution)/shard_map/ppermute | solution.py:80
  45.2 2.5 %copy-start.1 = (bf16[32,9,16,256]{3,0,2,1:T(8,128)(2,1)S(1)}, bf16[32,9,16,256]{3,0,2,1:T(8,128)(2,1)}, u32[]{:S(2)}) copy-start(bf16[32,9,16,256]{3,0,2,1:T(8,128)(2,1)} %gather_fusion) | copy-start | bytes 7077892
  49.8 4.2 %copy-start.4 = (bf16[256,227]{0,1:T(8,128)(2,1)S(1)}, bf16[256,227]{0,1:T(8,128)(2,1)}, u32[]{:S(2)}) copy-start(bf16[256,227]{0,1:T(8,128)(2,1)} %param.13) | copy-start | bytes 348676
  64.4 1.6 %collective-permute-start.4 = (f32[512,128]{1,0:T(8,128)S(1)}, f32[512,128]{1,0:T(8,128)S(1)}, u32[]{:S(2)}, u32[]{:S(2)}) collective-permute-start(f32[512,128]{1,0:T(8,128)S(1)} %constant_dynamic-slice_fusion.1), channel_id=1, source_target_pairs={{0,1},{1,0},{2,3},{3,2},{4,5},{5,4},{6,7},{7,6},{8,9},{9,8},{10,11... | collective-permute-start | bytes 786440 | tf_op jit(solution)/shard_map/ppermute | solution.py:22
  66.0 6.0 %collective-permute-start.5 = (f32[256,128]{1,0:T(8,128)S(1)}, f32[256,128]{1,0:T(8,128)S(1)}, u32[]{:S(2)}, u32[]{:S(2)}) collective-permute-start(f32[256,128]{1,0:T(8,128)S(1)} %constant_dynamic-slice_fusion), channel_id=1, source_target_pairs={{0,2},{2,0},{4,6},{6,4},{8,10},{10,8},{12,14},{14,12},{1,3},{3,1},... | collective-permute-start | bytes 393224 | tf_op jit(solution)/shard_map/ppermute | solution.py:22
  72.1 5.2 %collective-permute-start.6 = (f32[256,128]{1,0:T(8,128)S(1)}, f32[256,128]{1,0:T(8,128)S(1)}, u32[]{:S(2)}, u32[]{:S(2)}) collective-permute-start(f32[256,128]{1,0:T(8,128)S(1)} %dynamic-slice_add_fusion.1), channel_id=1, source_target_pairs={{0,4},{2,6},{4,0},{6,2},{8,12},{10,14},{12,8},{14,10},{1,5},{3,7},... | collective-permute-start | bytes 393224 | tf_op jit(solution)/shard_map/ppermute | solution.py:56
  77.3 8.1 %collective-permute-start.7 = (f32[256,128]{1,0:T(8,128)S(1)}, f32[256,128]{1,0:T(8,128)S(1)}, u32[]{:S(2)}, u32[]{:S(2)}) collective-permute-start(f32[256,128]{1,0:T(8,128)S(1)} %add.473), channel_id=1, source_target_pairs={{0,8},{2,10},{4,12},{6,14},{8,0},{10,2},{12,4},{14,6},{1,9},{3,11}... | collective-permute-start | bytes 393224 | tf_op jit(solution)/shard_map/ppermute | solution.py:56
  85.4 5.0 %collective-permute-start.8 = (f32[256,128]{1,0:T(8,128)S(1)}, f32[256,128]{1,0:T(8,128)S(1)}, u32[]{:S(2)}, u32[]{:S(2)}) collective-permute-start(f32[256,128]{1,0:T(8,128)S(1)} %get-tuple-element.18), channel_id=1, source_target_pairs={{0,2},{2,0},{4,6},{6,4},{8,10},{10,8},{12,14},{14,12},{1,3},{3,1},... | collective-permute-start | bytes 393224 | tf_op jit(solution)/shard_map/ppermute | solution.py:29
  90.5 1.6 %collective-permute-start.9 = (f32[512,128]{1,0:T(8,128)S(1)}, f32[512,128]{1,0:T(8,128)S(1)}, u32[]{:S(2)}, u32[]{:S(2)}) collective-permute-start(f32[512,128]{1,0:T(8,128)S(1)} %constant_dynamic-update-slice_fusion.10), channel_id=1, source_target_pairs={{0,1},{1,0},{2,3},{3,2},{4,5},{5,4},{6,7},{7,6},{8,9},{9,8},{10,11... | collective-permute-start | bytes 786440 | tf_op jit(solution)/shard_map/ppermute | solution.py:29

commit v17 on v16

--- a/solution.py
+++ b/solution.py
@@ -236,8 +236,7 @@
     grad_u = (grad_y * sigmoid_u * (1.0 + preact * (1.0 - sigmoid_u))).astype(jnp.bfloat16)
     grad_u = jnp.where(repeated[:, None], jnp.zeros_like(grad_u), grad_u)
     if chunks == 1:
-        windows_again, grad_u = lax.optimization_barrier((windows, grad_u))
-        grad_pw, grad_dw = backward(windows_again, depth_flat, grad_u)
+        grad_pw, grad_dw = backward(windows, depth_flat, grad_u)
     else:
         rows_split = lambda v: v.reshape((chunks, chunk * TILE) + v.shape[1:])
         outs = lax.map(

time: 97 us -> 96.1 us (level)
    convert_element_type x4 -> x2, other arithmetic: 3.87 us -> 2.98 us  [shifted(): source[:, DMAX + row_shift, DMAX + col_shift:DMAX + col_shift + TILE, :]]
where the time goes in v17:
time: 96.1 us; the launch traced here: 95.6 us
  waiting for transfers between devices  27.7 us (29%)
  starting transfers between devices  21.9 us (23%)
  other arithmetic  21.1 us (22%)
  local copies, waits for them, and re-layouts  18 us (19%)
  matrix products  4.04 us (4%)
  between operations  2.88 us (3%)
    ppermute x2, waiting for transfers between devices, packed_sum(): x = x + lax.ppermute(x, axis, [(i, i ^ bit) for i in range(count)])  9.63 us
    all_to_all x1, starting transfers between devices, local(): lax.all_to_all(send, ('lon', 'lat'), split_axis=0, concat_axis=0, tiled=T...  7.36 us
    ppermute x2, waiting for transfers between devices, padded_2(): lax.ppermute(tail, axis, [(i, (i + 1) % count) for i in range(ends)])  5.98 us
    gather x1, local copies, waits for them, and re-layouts, gather_windows(): lax.dynamic_slice(padded, (b, h, w, jnp.int32(0)), (1, span, reach, width))  5.73 us
    ppermute x2, waiting for transfers between devices, double(): got = lax.ppermute(x, axis, [(i, i ^ bit) for i in range(count)])  5.42 us
    ppermute x2, waiting for transfers between devices, halve(): return keep + lax.ppermute(send, axis, [(i, i ^ bit) for i in range(count)])  5.18 us
    reduce_sum x2, other arithmetic, backward(): tap_sums.append(jnp.sum((chosen * grad_z).reshape(-1, width), axis=0))  5 us
    concatenate x1, other arithmetic, padded_2(): jnp.concatenate([lax.ppermute(tail, axis, [(i, (i + 1) % count) for i in...  4.77 us
  transfers between devices with their start and end apart: 11, of which 9 were waited for; matrix products, arithmetic and copies ran while one was open for 5% of the time, Pallas kernels for 0%

profile of v17, /device:TPU:0, one launch (start us, length us, event | category | flops | bytes accessed | tf_op | source)
XLA Modules:
  0.0 95.6 jit_solution(16485345360124994436)
XLA Ops:
  5.9 7.4 %all-to-all-start = ((bf16[32,8,228]{2,1,0:T(8,128)(2,1)}), bf16[32,8,228]{2,1,0:T(8,128)(2,1)S(1)}, u32[]{:S(2)}, u32[]{:S(2)}) async-start(bf16[32,8,228]{2,1,0:T(8,128)(2,1)} %copy.189), calls=%async_computation | async-start | bytes 262144 | tf_op jit(solution)/shard_map/all_to_all | solution.py:118
  13.3 1.3 %fusion.107 = (bf16[2,48,4,256]{3,2,1,0:T(4,128)(2,1)S(1)}, bf16[2,48,4,256]{3,2,1,0:T(4,128)(2,1)S(1)}) fusion(bf16[2,48,32,256]{3,2,1,0:T(8,128)(2,1)} %param.9), kind=kLoop, calls=%fused_computation.270 | loop fusion | bytes 786432 | tf_op jit(solution)/shard_map/slice | solution.py:74
  14.8 2.0 %collective-permute-start = (bf16[2,48,4,256]{3,0,2,1:T(2,128)(2,1)S(1)}, bf16[2,48,4,256]{3,0,2,1:T(2,128)(2,1)S(1)}, u32[]{:S(2)}, u32[]{:S(2)}) collective-permute-start(bf16[2,48,4,256]{3,0,2,1:T(2,128)(2,1)S(1)} %copy.286), channel_id=1, source_target_pairs={{0,2},{2,4},{4,6},{6,8},{8,10},{10,12},{12,14},{14,0},{1,3},{3,5},... | collective-permute-start | bytes 589832 | tf_op jit(solution)/shard_map/ppermute | solution.py:78
  17.0 2.9 %collective-permute-start.1 = (bf16[2,48,4,256]{3,0,2,1:T(2,128)(2,1)S(1)}, bf16[2,48,4,256]{3,0,2,1:T(2,128)(2,1)S(1)}, u32[]{:S(2)}, u32[]{:S(2)}) collective-permute-start(bf16[2,48,4,256]{3,0,2,1:T(2,128)(2,1)S(1)} %copy.287), channel_id=1, source_target_pairs={{2,0},{4,2},{6,4},{8,6},{10,8},{12,10},{14,12},{0,14},{3,1},{5,3},... | collective-permute-start | bytes 589832 | tf_op jit(solution)/shard_map/ppermute | solution.py:80
  20.0 6.0 %collective-permute-done = bf16[2,48,4,256]{3,0,2,1:T(2,128)(2,1)S(1)} collective-permute-done((bf16[2,48,4,256]{3,0,2,1:T(2,128)(2,1)S(1)}, bf16[2,48,4,256]{3,0,2,1:T(2,128)(2,1)S(1)}, u32[]{:S(2)}, u32[]{:S(2)}) %collective-permute-start) | collective-permute-done | bytes 196640 | tf_op jit(solution)/shard_map/ppermute | solution.py:78
  26.1 1.7 %constant_dynamic-update-slice_fusion.1 = bf16[2,48,40,256]{3,0,2,1:T(2,128)(2,1)S(1)} fusion(bf16[2,48,40,256]{3,0,2,1:T(2,128)(2,1)S(1)} %constant_dynamic-update-slice_fusion.2, bf16[2,48,32,256]{3,2,1,0:T(8,128)(2,1)S(1)} %copy-done.3), kind=kLoop, calls=%fused_computation.212 | loop fusion | bytes 3145728
  30.0 1.3 %collective-permute-start.2 = (bf16[2,4,40,256]{3,0,2,1:T(2,128)(2,1)S(1)}, bf16[2,4,40,256]{3,0,2,1:T(2,128)(2,1)S(1)}, u32[]{:S(2)}, u32[]{:S(2)}) collective-permute-start(bf16[2,4,40,256]{3,0,2,1:T(2,128)(2,1)S(1)} %get-tuple-element.51), channel_id=1, source_target_pairs={{0,1},{2,3},{4,5},{6,7},{8,9},{10,11},{12,13},{14,15},{16,17},{18,... | collective-permute-start | bytes 491528 | tf_op jit(solution)/shard_map/ppermute | solution.py:78
  31.3 1.3 %collective-permute-start.3 = (bf16[2,4,40,256]{3,0,2,1:T(2,128)(2,1)S(1)}, bf16[2,4,40,256]{3,0,2,1:T(2,128)(2,1)S(1)}, u32[]{:S(2)}, u32[]{:S(2)}) collective-permute-start(bf16[2,4,40,256]{3,0,2,1:T(2,128)(2,1)S(1)} %get-tuple-element.52), channel_id=1, source_target_pairs={{1,0},{3,2},{5,4},{7,6},{9,8},{11,10},{13,12},{15,14},{17,16},{19,... | collective-permute-start | bytes 491528 | tf_op jit(solution)/shard_map/ppermute | solution.py:80
  34.6 4.8 %pad_maximum_fusion = bf16[2,56,40,256]{3,0,2,1:T(2,128)(2,1)S(1)} fusion(bf16[2,4,40,256]{3,0,2,1:T(2,128)(2,1)S(1)} %collective-permute-done.3, bf16[2,48,40,256]{3,0,2,1:T(2,128)(2,1)} %copy-done.2, bf16[2,4,40,256]{3,0,2,1:T(2,128)(2,1)S(1)} %collective-permute-done.2), kind=kLoop, calls=%fused_computation.1 | loop fusion | flops 2293760 | bytes 4587520 | tf_op jit(solution)/shard_map/concatenate | solution.py:76
  39.4 5.7 %gather_fusion = bf16[32,9,16,256]{3,0,2,1:T(8,128)(2,1)} fusion(bf16[2,56,40,256]{3,0,2,1:T(2,128)(2,1)S(1)} %pad_maximum_fusion, s32[32]{0:T(128)S(1)} %fusion.104), kind=kCustom, calls=%fused_computation | custom fusion | bytes 4719104 | tf_op jit(solution)/shard_map/vmap()/gather | solution.py:145
  45.1 2.5 %slice_convert_fusion.20 = (f32[32,1,8,256]{3,0,2,1:T(8,128)S(1)}, f32[32,1,8,256]{3,0,2,1:T(8,128)S(1)}, f32[32,1,8,256]{3,0,2,1:T(8,128)S(1)}, f32[32,1,8,256]...) fusion(bf16[32,9,16,256]{3,0,2,1:T(8,128)(2,1)} %gather_fusion), kind=kLoop, calls=%fused_computation.187 | loop fusion | flops 1245184 | bytes 7471104 | tf_op jit(solution)/shard_map/convert_element_type | solution.py:151
  49.8 3.9 %fusion.6 = bf16[256,256]{1,0:T(8,128)(2,1)S(1)} fusion(f32[32,1,8,256]{3,2,0,1:T(8,128)S(1)} %copy.200, f32[32,1,8,256]{3,2,0,1:T(8,128)S(1)} %copy.199, f32[32,1,8,256]{3,2,0,1:T(8,128)S(1)} %copy.198, f32[32,1,8,256]{3,2,0,1:T(8,128)S(1)} %copy.197, f32[32,1,8,256]{3,2,0,1:T(8,128)S(1)} %copy.196, f32[32,1,8,256]{3,2,0,1:T(8,128)S(1)} %copy.195, ...), kind=kLoop, calls=%fused_computation.20 | loop fusion | flops 4325376 | bytes 8815616 | tf_op jit(solution)/shard_map/convert_element_type | solution.py:167
  55.4 1.6 %fusion.33 = (f32[256]{0:T(256)S(1)}, f32[256]{0:T(256)S(1)}, f32[256,256]{1,0:T(8,128)S(1)}) fusion(f32[32,1,8,256]{3,0,2,1:T(8,128)S(1)} %get-tuple-element.24, f32[32,1,8,256]{3,0,2,1:T(8,128)S(1)} %get-tuple-element.31, f32[32,1,8,256]{3,0,2,1:T(8,128)S(1)} %get-tuple-element.18, f32[32,1,8,256]{3,0,2,1:T(8,128)S(1)} %get-tuple-element.44, ...), kind=kOutput, calls=%fused_computation.59 | convolution fusion | flops 34733568 | bytes 2627584 | tf_op jit(solution)/shard_map/dot_general | solution.py:185
  57.1 2.6 %fusion.9 = (f32[256]{0:T(256)S(1)}, f32[256]{0:T(256)S(1)}, f32[256]{0:T(256)S(1)}, f32[256]{0:T(256)S(1)}) fusion(f32[256,256]{1,0:T(8,128)S(1)} %get-tuple-element.108, f32[32,1,8,256]{3,0,2,1:T(8,128)S(1)} %get-tuple-element.50, f32[32,1,8,256]{3,0,2,1:T(8,128)S(1)} %get-tuple-element.25, f32[32,1,8,256]{3,0,2,1:T(8,128)S(1)} %get-tuple-element.32, ...), kind=kLoop, calls=%fused_computation.23 | loop fusion | flops 1899520 | bytes 3678208 | tf_op jit(solution)/shard_map/reduce_sum | solution.py:198
  59.7 2.4 %fusion.21 = (f32[256]{0:T(256)S(1)}, f32[256]{0:T(256)S(1)}, f32[256]{0:T(256)S(1)}) fusion(f32[256,256]{1,0:T(8,128)S(1)} %get-tuple-element.108, f32[32,1,8,256]{3,0,2,1:T(8,128)S(1)} %get-tuple-element.21, f32[32,1,8,256]{3,0,2,1:T(8,128)S(1)} %get-tuple-element.28, f32[32,1,8,256]{3,0,2,1:T(8,128)S(1)} %get-tuple-element.35, ...), kind=kLoop, calls=%fused_computation.41 | loop fusion | flops 1768704 | bytes 3415040 | tf_op jit(solution)/shard_map/reduce_sum | solution.py:198
  63.8 1.3 %collective-permute-done.4 = f32[512,128]{1,0:T(8,128)S(1)} collective-permute-done((f32[512,128]{1,0:T(8,128)S(1)}, f32[512,128]{1,0:T(8,128)S(1)}, u32[]{:S(2)}, u32[]{:S(2)}) %collective-permute-start.4) | collective-permute-done | bytes 262176 | tf_op jit(solution)/shard_map/ppermute | solution.py:22
  65.1 2.1 %collective-permute-start.5 = (f32[256,128]{1,0:T(8,128)S(1)}, f32[256,128]{1,0:T(8,128)S(1)}, u32[]{:S(2)}, u32[]{:S(2)}) collective-permute-start(f32[256,128]{1,0:T(8,128)S(1)} %constant_dynamic-slice_fusion), channel_id=1, source_target_pairs={{0,2},{2,0},{4,6},{6,4},{8,10},{10,8},{12,14},{14,12},{1,3},{3,1},... | collective-permute-start | bytes 393224 | tf_op jit(solution)/shard_map/ppermute | solution.py:22
  67.2 3.9 %collective-permute-done.5 = f32[256,128]{1,0:T(8,128)S(1)} collective-permute-done((f32[256,128]{1,0:T(8,128)S(1)}, f32[256,128]{1,0:T(8,128)S(1)}, u32[]{:S(2)}, u32[]{:S(2)}) %collective-permute-start.5) | collective-permute-done | bytes 131104 | tf_op jit(solution)/shard_map/ppermute | solution.py:22
  71.1 1.5 %collective-permute-start.6 = (f32[256,128]{1,0:T(8,128)S(1)}, f32[256,128]{1,0:T(8,128)S(1)}, u32[]{:S(2)}, u32[]{:S(2)}) collective-permute-start(f32[256,128]{1,0:T(8,128)S(1)} %dynamic-slice_add_fusion.1), channel_id=1, source_target_pairs={{0,4},{2,6},{4,0},{6,2},{8,12},{10,14},{12,8},{14,10},{1,5},{3,7},... | collective-permute-start | bytes 393224 | tf_op jit(solution)/shard_map/ppermute | solution.py:56
  72.6 3.7 %collective-permute-done.6 = f32[256,128]{1,0:T(8,128)S(1)} collective-permute-done((f32[256,128]{1,0:T(8,128)S(1)}, f32[256,128]{1,0:T(8,128)S(1)}, u32[]{:S(2)}, u32[]{:S(2)}) %collective-permute-start.6) | collective-permute-done | bytes 131104 | tf_op jit(solution)/shard_map/ppermute | solution.py:56
  76.4 2.1 %collective-permute-start.7 = (f32[256,128]{1,0:T(8,128)S(1)}, f32[256,128]{1,0:T(8,128)S(1)}, u32[]{:S(2)}, u32[]{:S(2)}) collective-permute-start(f32[256,128]{1,0:T(8,128)S(1)} %add.473), channel_id=1, source_target_pairs={{0,8},{2,10},{4,12},{6,14},{8,0},{10,2},{12,4},{14,6},{1,9},{3,11}... | collective-permute-start | bytes 393224 | tf_op jit(solution)/shard_map/ppermute | solution.py:56
  78.4 5.9 %collective-permute-done.7 = f32[256,128]{1,0:T(8,128)S(1)} collective-permute-done((f32[256,128]{1,0:T(8,128)S(1)}, f32[256,128]{1,0:T(8,128)S(1)}, u32[]{:S(2)}, u32[]{:S(2)}) %collective-permute-start.7) | collective-permute-done | bytes 131104 | tf_op jit(solution)/shard_map/ppermute | solution.py:56
  85.5 4.0 %collective-permute-done.8 = f32[256,128]{1,0:T(8,128)S(1)} collective-permute-done((f32[256,128]{1,0:T(8,128)S(1)}, f32[256,128]{1,0:T(8,128)S(1)}, u32[]{:S(2)}, u32[]{:S(2)}) %collective-permute-start.8) | collective-permute-done | bytes 131104 | tf_op jit(solution)/shard_map/ppermute | solution.py:29
  89.6 1.4 %collective-permute-done.9 = f32[512,128]{1,0:T(8,128)S(1)} collective-permute-done((f32[512,128]{1,0:T(8,128)S(1)}, f32[512,128]{1,0:T(8,128)S(1)}, u32[]{:S(2)}, u32[]{:S(2)}) %collective-permute-start.9) | collective-permute-done | bytes 262176 | tf_op jit(solution)/shard_map/ppermute | solution.py:29
  (100 shorter events, 19.5 us)
Async XLA Ops:
  0.6 53.1 %copy-start = (bf16[256,256]{1,0:T(8,128)(2,1)S(1)}, bf16[256,256]{1,0:T(8,128)(2,1)}, u32[]{:S(2)}) copy-start(bf16[256,256]{1,0:T(8,128)(2,1)} %param.12) | copy-start | bytes 393220
  0.6 25.4 %copy-start.3 = (bf16[2,48,32,256]{3,2,1,0:T(8,128)(2,1)S(1)}, bf16[2,48,32,256]{3,2,1,0:T(8,128)(2,1)}, u32[]{:S(2)}) copy-start(bf16[2,48,32,256]{3,2,1,0:T(8,128)(2,1)} %param.9) | copy-start | bytes 4718596
  0.7 19.2 %copy-start.5 = (bf16[9,256]{1,0:T(8,128)(2,1)S(1)}, bf16[9,256]{1,0:T(8,128)(2,1)}, u32[]{:S(2)}) copy-start(bf16[9,256]{1,0:T(8,128)(2,1)} %param.11) | copy-start | bytes 13828
  0.7 19.2 %copy-start.6 = (s32[256]{0:T(256)S(1)}, s32[256]{0:T(256)}, u32[]{:S(2)}) copy-start(s32[256]{0:T(256)} %param.10) | copy-start | bytes 3076
  5.9 26.7 %all-to-all-start = ((bf16[32,8,228]{2,1,0:T(8,128)(2,1)}), bf16[32,8,228]{2,1,0:T(8,128)(2,1)S(1)}, u32[]{:S(2)}, u32[]{:S(2)}) async-start(bf16[32,8,228]{2,1,0:T(8,128)(2,1)} %copy.189), calls=%async_computation | async-start | bytes 262144 | tf_op jit(solution)/shard_map/all_to_all | solution.py:118
  14.8 11.2 %collective-permute-start = (bf16[2,48,4,256]{3,0,2,1:T(2,128)(2,1)S(1)}, bf16[2,48,4,256]{3,0,2,1:T(2,128)(2,1)S(1)}, u32[]{:S(2)}, u32[]{:S(2)}) collective-permute-start(bf16[2,48,4,256]{3,0,2,1:T(2,128)(2,1)S(1)} %copy.286), channel_id=1, source_target_pairs={{0,2},{2,4},{4,6},{6,8},{8,10},{10,12},{12,14},{14,0},{1,3},{3,5},... | collective-permute-start | bytes 589832 | tf_op jit(solution)/shard_map/ppermute | solution.py:78
  17.0 11.4 %collective-permute-start.1 = (bf16[2,48,4,256]{3,0,2,1:T(2,128)(2,1)S(1)}, bf16[2,48,4,256]{3,0,2,1:T(2,128)(2,1)S(1)}, u32[]{:S(2)}, u32[]{:S(2)}) collective-permute-start(bf16[2,48,4,256]{3,0,2,1:T(2,128)(2,1)S(1)} %copy.287), channel_id=1, source_target_pairs={{2,0},{4,2},{6,4},{8,6},{10,8},{12,10},{14,12},{0,14},{3,1},{5,3},... | collective-permute-start | bytes 589832 | tf_op jit(solution)/shard_map/ppermute | solution.py:80
  28.5 1.3 %copy-start.2 = (bf16[2,48,40,256]{3,0,2,1:T(2,128)(2,1)}, bf16[2,48,40,256]{3,0,2,1:T(2,128)(2,1)S(1)}, u32[]{:S(2)}) copy-start(bf16[2,48,40,256]{3,0,2,1:T(2,128)(2,1)S(1)} %constant_dynamic-update-slice_fusion) | copy-start | bytes 5898244
  30.0 3.7 %collective-permute-start.2 = (bf16[2,4,40,256]{3,0,2,1:T(2,128)(2,1)S(1)}, bf16[2,4,40,256]{3,0,2,1:T(2,128)(2,1)S(1)}, u32[]{:S(2)}, u32[]{:S(2)}) collective-permute-start(bf16[2,4,40,256]{3,0,2,1:T(2,128)(2,1)S(1)} %get-tuple-element.51), channel_id=1, source_target_pairs={{0,1},{2,3},{4,5},{6,7},{8,9},{10,11},{12,13},{14,15},{16,17},{18,... | collective-permute-start | bytes 491528 | tf_op jit(solution)/shard_map/ppermute | solution.py:78
  31.3 3.3 %collective-permute-start.3 = (bf16[2,4,40,256]{3,0,2,1:T(2,128)(2,1)S(1)}, bf16[2,4,40,256]{3,0,2,1:T(2,128)(2,1)S(1)}, u32[]{:S(2)}, u32[]{:S(2)}) collective-permute-start(bf16[2,4,40,256]{3,0,2,1:T(2,128)(2,1)S(1)} %get-tuple-element.52), channel_id=1, source_target_pairs={{1,0},{3,2},{5,4},{7,6},{9,8},{11,10},{13,12},{15,14},{17,16},{19,... | collective-permute-start | bytes 491528 | tf_op jit(solution)/shard_map/ppermute | solution.py:80
  45.1 2.5 %copy-start.1 = (bf16[32,9,16,256]{3,0,2,1:T(8,128)(2,1)S(1)}, bf16[32,9,16,256]{3,0,2,1:T(8,128)(2,1)}, u32[]{:S(2)}) copy-start(bf16[32,9,16,256]{3,0,2,1:T(8,128)(2,1)} %gather_fusion) | copy-start | bytes 7077892
  49.8 4.2 %copy-start.4 = (bf16[256,227]{0,1:T(8,128)(2,1)S(1)}, bf16[256,227]{0,1:T(8,128)(2,1)}, u32[]{:S(2)}) copy-start(bf16[256,227]{0,1:T(8,128)(2,1)} %param.13) | copy-start | bytes 348676
  63.4 1.6 %collective-permute-start.4 = (f32[512,128]{1,0:T(8,128)S(1)}, f32[512,128]{1,0:T(8,128)S(1)}, u32[]{:S(2)}, u32[]{:S(2)}) collective-permute-start(f32[512,128]{1,0:T(8,128)S(1)} %constant_dynamic-slice_fusion.1), channel_id=1, source_target_pairs={{0,1},{1,0},{2,3},{3,2},{4,5},{5,4},{6,7},{7,6},{8,9},{9,8},{10,11... | collective-permute-start | bytes 786440 | tf_op jit(solution)/shard_map/ppermute | solution.py:22
  65.1 6.0 %collective-permute-start.5 = (f32[256,128]{1,0:T(8,128)S(1)}, f32[256,128]{1,0:T(8,128)S(1)}, u32[]{:S(2)}, u32[]{:S(2)}) collective-permute-start(f32[256,128]{1,0:T(8,128)S(1)} %constant_dynamic-slice_fusion), channel_id=1, source_target_pairs={{0,2},{2,0},{4,6},{6,4},{8,10},{10,8},{12,14},{14,12},{1,3},{3,1},... | collective-permute-start | bytes 393224 | tf_op jit(solution)/shard_map/ppermute | solution.py:22
  71.1 5.2 %collective-permute-start.6 = (f32[256,128]{1,0:T(8,128)S(1)}, f32[256,128]{1,0:T(8,128)S(1)}, u32[]{:S(2)}, u32[]{:S(2)}) collective-permute-start(f32[256,128]{1,0:T(8,128)S(1)} %dynamic-slice_add_fusion.1), channel_id=1, source_target_pairs={{0,4},{2,6},{4,0},{6,2},{8,12},{10,14},{12,8},{14,10},{1,5},{3,7},... | collective-permute-start | bytes 393224 | tf_op jit(solution)/shard_map/ppermute | solution.py:56
  76.4 8.0 %collective-permute-start.7 = (f32[256,128]{1,0:T(8,128)S(1)}, f32[256,128]{1,0:T(8,128)S(1)}, u32[]{:S(2)}, u32[]{:S(2)}) collective-permute-start(f32[256,128]{1,0:T(8,128)S(1)} %add.473), channel_id=1, source_target_pairs={{0,8},{2,10},{4,12},{6,14},{8,0},{10,2},{12,4},{14,6},{1,9},{3,11}... | collective-permute-start | bytes 393224 | tf_op jit(solution)/shard_map/ppermute | solution.py:56
  84.4 5.0 %collective-permute-start.8 = (f32[256,128]{1,0:T(8,128)S(1)}, f32[256,128]{1,0:T(8,128)S(1)}, u32[]{:S(2)}, u32[]{:S(2)}) collective-permute-start(f32[256,128]{1,0:T(8,128)S(1)} %get-tuple-element.14), channel_id=1, source_target_pairs={{0,2},{2,0},{4,6},{6,4},{8,10},{10,8},{12,14},{14,12},{1,3},{3,1},... | collective-permute-start | bytes 393224 | tf_op jit(solution)/shard_map/ppermute | solution.py:29
  89.5 1.6 %collective-permute-start.9 = (f32[512,128]{1,0:T(8,128)S(1)}, f32[512,128]{1,0:T(8,128)S(1)}, u32[]{:S(2)}, u32[]{:S(2)}) collective-permute-start(f32[512,128]{1,0:T(8,128)S(1)} %constant_dynamic-update-slice_fusion.10), channel_id=1, source_target_pairs={{0,1},{1,0},{2,3},{3,2},{4,5},{5,4},{6,7},{7,6},{8,9},{9,8},{10,11... | collective-permute-start | bytes 786440 | tf_op jit(solution)/shard_map/ppermute | solution.py:29

commit v18 on v17

--- a/solution.py
+++ b/solution.py
@@ -152,18 +152,23 @@
             jnp.float32
         )
 
+    def chosen_tap(windows, tap_index):
+        if tap_index == 4:
+            return shifted(windows, 0, 0)
+        chosen = None
+        for dilation in range(1, DMAX + 1):
+            row_shift = (tap_index // 3 - 1) * dilation
+            col_shift = (tap_index % 3 - 1) * dilation
+            term = onehot[dilation - 1] * shifted(windows, row_shift, col_shift)
+            chosen = term if chosen is None else chosen + term
+        return chosen
+
     def forward(windows, tiles, weight):
         center = shifted(windows, 0, 0)
         accum_sum = center * kernel[4]
-        for dilation in range(1, DMAX + 1):
-            for tap_index in range(9):
-                if tap_index == 4:
-                    continue
-                row_shift = (tap_index // 3 - 1) * dilation
-                col_shift = (tap_index % 3 - 1) * dilation
-                accum_sum = accum_sum + kernel[tap_index] * onehot[dilation - 1] * shifted(
-                    windows, row_shift, col_shift
-                )
+        for tap_index in range(9):
+            if tap_index != 4:
+                accum_sum = accum_sum + kernel[tap_index] * chosen_tap(windows, tap_index)
         depth_flat = accum_sum.astype(jnp.bfloat16).reshape(-1, width)
         preact = jnp.dot(depth_flat, pw_weight, preferred_element_type=jnp.float32)
         y_rows = (center.reshape(-1, width) + jax.nn.silu(preact)).astype(jnp.bfloat16)
@@ -186,15 +191,7 @@
         grad_z = grad_z.reshape(windows.shape[0], TILE, width)
         tap_sums = []
         for tap_index in range(9):
-            if tap_index == 4:
-                chosen = shifted(windows, 0, 0)
-            else:
-                chosen = None
-                for dilation in range(1, DMAX + 1):
-                    row_shift = (tap_index // 3 - 1) * dilation
-                    col_shift = (tap_index % 3 - 1) * dilation
-                    term = onehot[dilation - 1] * shifted(windows, row_shift, col_shift)
-                    chosen = term if chosen is None else chosen + term
+            chosen = chosen_tap(windows, tap_index)
             tap_sums.append(jnp.sum((chosen * grad_z).reshape(-1, width), axis=0))
         return pw_part, jnp.stack(tap_sums, axis=0)
 

time: 96.1 us -> 92.3 us (0.960)
  local copies, waits for them, and re-layouts: 18 us -> 16.4 us
  other arithmetic: 21.1 us -> 20 us
  matrix products: 4.04 us -> 2.95 us
    reduce_sum x2 -> x0, other arithmetic: 5 us -> none  [backward(): tap_sums.append(jnp.sum((chosen * grad_z).reshape(-1, width), axis=0))]
    add x0 -> x1, other arithmetic: none -> 2.26 us  [chosen_tap(): chosen = term if chosen is None else chosen + term]
    convert_element_type x1, other arithmetic: 3.9 us -> 5.49 us  [forward(): depth_flat = accum_sum.astype(jnp.bfloat16).reshape(-1, width)]
    convert_element_type x10 -> x0, local copies, waits for them, and re-layouts: 1.57 us -> none  [shifted(): source[:, DMAX + row_shift, DMAX + col_shift:DMAX + col_shift + TILE, :]]
    dot_general x1, matrix products: 1.64 us -> 0.53 us  [backward(): grad_z = jnp.dot(grad_u, pw_weight.T, preferred_element_type=jnp.float32)]
  transfers between devices with their start and end apart: 11 -> 11, of which waited for: 9 -> 9; matrix products, arithmetic and copies ran while one was open for 5% -> 6% of each run, Pallas kernels for 0% -> 0%
where the time goes in v18:
time: 92.3 us; the launch traced here: 91.8 us
  waiting for transfers between devices  27.8 us (30%)
  starting transfers between devices  21.9 us (24%)
  other arithmetic  20 us (22%)
  local copies, waits for them, and re-layouts  16.4 us (18%)
  matrix products  2.95 us (3%)
  between operations  2.84 us (3%)
    ppermute x2, waiting for transfers between devices, packed_sum(): x = x + lax.ppermute(x, axis, [(i, i ^ bit) for i in range(count)])  9.68 us
    all_to_all x1, starting transfers between devices, local(): lax.all_to_all(send, ('lon', 'lat'), split_axis=0, concat_axis=0, tiled=T...  7.36 us
    ppermute x2, waiting for transfers between devices, padded_2(): lax.ppermute(tail, axis, [(i, (i + 1) % count) for i in range(ends)])  6 us
    gather x1, local copies, waits for them, and re-layouts, gather_windows(): lax.dynamic_slice(padded, (b, h, w, jnp.int32(0)), (1, span, reach, width))  5.74 us
    convert_element_type x1, other arithmetic, forward(): depth_flat = accum_sum.astype(jnp.bfloat16).reshape(-1, width)  5.49 us
    ppermute x2, waiting for transfers between devices, double(): got = lax.ppermute(x, axis, [(i, i ^ bit) for i in range(count)])  5.45 us
    ppermute x2, waiting for transfers between devices, halve(): return keep + lax.ppermute(send, axis, [(i, i ^ bit) for i in range(count)])  5.2 us
    concatenate x1, other arithmetic, padded_2(): jnp.concatenate([lax.ppermute(tail, axis, [(i, (i + 1) % count) for i in...  4.77 us
  transfers between devices with their start and end apart: 11, of which 9 were waited for; matrix products, arithmetic and copies ran while one was open for 6% of the time, Pallas kernels for 0%

profile of v18, /device:TPU:0, one launch (start us, length us, event | category | flops | bytes accessed | tf_op | source)
XLA Modules:
  0.0 91.8 jit_solution(8912018338073383265)
XLA Ops:
  5.9 7.4 %all-to-all-start = ((bf16[32,8,228]{2,1,0:T(8,128)(2,1)}), bf16[32,8,228]{2,1,0:T(8,128)(2,1)S(1)}, u32[]{:S(2)}, u32[]{:S(2)}) async-start(bf16[32,8,228]{2,1,0:T(8,128)(2,1)} %copy.189), calls=%async_computation | async-start | bytes 262144 | tf_op jit(solution)/shard_map/all_to_all | solution.py:118
  13.3 1.3 %fusion.72 = (bf16[2,48,4,256]{3,2,1,0:T(4,128)(2,1)S(1)}, bf16[2,48,4,256]{3,2,1,0:T(4,128)(2,1)S(1)}) fusion(bf16[2,48,32,256]{3,2,1,0:T(8,128)(2,1)} %param.9), kind=kLoop, calls=%fused_computation.206 | loop fusion | bytes 786432 | tf_op jit(solution)/shard_map/slice | solution.py:74
  14.8 2.0 %collective-permute-start = (bf16[2,48,4,256]{3,0,2,1:T(2,128)(2,1)S(1)}, bf16[2,48,4,256]{3,0,2,1:T(2,128)(2,1)S(1)}, u32[]{:S(2)}, u32[]{:S(2)}) collective-permute-start(bf16[2,48,4,256]{3,0,2,1:T(2,128)(2,1)S(1)} %copy.266), channel_id=1, source_target_pairs={{0,2},{2,4},{4,6},{6,8},{8,10},{10,12},{12,14},{14,0},{1,3},{3,5},... | collective-permute-start | bytes 589832 | tf_op jit(solution)/shard_map/ppermute | solution.py:78
  17.0 2.9 %collective-permute-start.1 = (bf16[2,48,4,256]{3,0,2,1:T(2,128)(2,1)S(1)}, bf16[2,48,4,256]{3,0,2,1:T(2,128)(2,1)S(1)}, u32[]{:S(2)}, u32[]{:S(2)}) collective-permute-start(bf16[2,48,4,256]{3,0,2,1:T(2,128)(2,1)S(1)} %copy.267), channel_id=1, source_target_pairs={{2,0},{4,2},{6,4},{8,6},{10,8},{12,10},{14,12},{0,14},{3,1},{5,3},... | collective-permute-start | bytes 589832 | tf_op jit(solution)/shard_map/ppermute | solution.py:80
  20.0 6.0 %collective-permute-done = bf16[2,48,4,256]{3,0,2,1:T(2,128)(2,1)S(1)} collective-permute-done((bf16[2,48,4,256]{3,0,2,1:T(2,128)(2,1)S(1)}, bf16[2,48,4,256]{3,0,2,1:T(2,128)(2,1)S(1)}, u32[]{:S(2)}, u32[]{:S(2)}) %collective-permute-start) | collective-permute-done | bytes 196640 | tf_op jit(solution)/shard_map/ppermute | solution.py:78
  26.1 1.7 %constant_dynamic-update-slice_fusion.1 = bf16[2,48,40,256]{3,0,2,1:T(2,128)(2,1)S(1)} fusion(bf16[2,48,40,256]{3,0,2,1:T(2,128)(2,1)S(1)} %constant_dynamic-update-slice_fusion.2, bf16[2,48,32,256]{3,2,1,0:T(8,128)(2,1)S(1)} %copy-done.3), kind=kLoop, calls=%fused_computation.148 | loop fusion | bytes 3145728
  28.5 1.3 %copy-done.2 = bf16[2,48,40,256]{3,0,2,1:T(2,128)(2,1)} copy-done((bf16[2,48,40,256]{3,0,2,1:T(2,128)(2,1)}, bf16[2,48,40,256]{3,0,2,1:T(2,128)(2,1)S(1)}, u32[]{:S(2)}) %copy-start.2) | copy-done | bytes 1966104
  30.0 1.3 %collective-permute-start.2 = (bf16[2,4,40,256]{3,0,2,1:T(2,128)(2,1)S(1)}, bf16[2,4,40,256]{3,0,2,1:T(2,128)(2,1)S(1)}, u32[]{:S(2)}, u32[]{:S(2)}) collective-permute-start(bf16[2,4,40,256]{3,0,2,1:T(2,128)(2,1)S(1)} %get-tuple-element.57), channel_id=1, source_target_pairs={{0,1},{2,3},{4,5},{6,7},{8,9},{10,11},{12,13},{14,15},{16,17},{18,... | collective-permute-start | bytes 491528 | tf_op jit(solution)/shard_map/ppermute | solution.py:78
  31.3 1.3 %collective-permute-start.3 = (bf16[2,4,40,256]{3,0,2,1:T(2,128)(2,1)S(1)}, bf16[2,4,40,256]{3,0,2,1:T(2,128)(2,1)S(1)}, u32[]{:S(2)}, u32[]{:S(2)}) collective-permute-start(bf16[2,4,40,256]{3,0,2,1:T(2,128)(2,1)S(1)} %get-tuple-element.58), channel_id=1, source_target_pairs={{1,0},{3,2},{5,4},{7,6},{9,8},{11,10},{13,12},{15,14},{17,16},{19,... | collective-permute-start | bytes 491528 | tf_op jit(solution)/shard_map/ppermute | solution.py:80
  34.6 4.8 %pad_maximum_fusion = bf16[2,56,40,256]{3,0,2,1:T(2,128)(2,1)S(1)} fusion(bf16[2,4,40,256]{3,0,2,1:T(2,128)(2,1)S(1)} %collective-permute-done.3, bf16[2,48,40,256]{3,0,2,1:T(2,128)(2,1)} %copy-done.2, bf16[2,4,40,256]{3,0,2,1:T(2,128)(2,1)S(1)} %collective-permute-done.2), kind=kLoop, calls=%fused_computation.1 | loop fusion | flops 2293760 | bytes 4587520 | tf_op jit(solution)/shard_map/concatenate | solution.py:76
  39.4 5.7 %gather_fusion = bf16[32,9,16,256]{3,0,2,1:T(8,128)(2,1)} fusion(bf16[2,56,40,256]{3,0,2,1:T(2,128)(2,1)S(1)} %pad_maximum_fusion, s32[32]{0:T(128)S(1)} %fusion.64), kind=kCustom, calls=%fused_computation | custom fusion | bytes 4719104 | tf_op jit(solution)/shard_map/vmap()/gather | solution.py:145
  45.1 2.6 %slice_convert_fusion.15 = (f32[32,1,8,256]{3,0,2,1:T(8,128)S(1)}, f32[32,1,8,256]{3,0,2,1:T(8,128)S(1)}, f32[32,1,8,256]{3,0,2,1:T(8,128)S(1)}, f32[32,1,8,256]...) fusion(bf16[32,9,16,256]{3,0,2,1:T(8,128)(2,1)} %gather_fusion), kind=kLoop, calls=%fused_computation.118 | loop fusion | flops 1245184 | bytes 7471104 | tf_op jit(solution)/shard_map/convert_element_type | solution.py:151
  48.2 2.3 %fusion.11 = (f32[256,256]{1,0:T(8,128)S(1)}, f32[256,256]{1,0:T(8,128)S(1)}, f32[256,256]{1,0:T(8,128)S(1)}) fusion(f32[32,1,8,256]{3,0,2,1:T(8,128)S(1)} %get-tuple-element.32, f32[32,1,8,256]{3,0,2,1:T(8,128)S(1)} %get-tuple-element.33, f32[32,1,8,256]{3,0,2,1:T(8,128)S(1)} %get-tuple-element.34, f32[32,1,8,256]{3,0,2,1:T(8,128)S(1)} %get-tuple-element.35, ...), kind=kLoop, calls=%fused_computation.32 | loop fusion | flops 1376256 | bytes 3936256 | tf_op jit(solution)/shard_map/add | solution.py:163
  50.5 5.5 %fusion.34 = (bf16[256,256]{1,0:T(8,128)(2,1)S(1)}, f32[256,256]{1,0:T(8,128)S(1)}, f32[256,256]{1,0:T(8,128)S(1)}, f32[256,256]{1,0:T(8,128)S(1)}, f32[256,256]{1,0:T(8,128)S(1)}, /*index=5*/f32[256,256]{1,0:T(8,128)S(1)}) fusion(f32[256,256]{1,0:T(8,128)S(1)} %get-tuple-element.72, f32[256,256]{1,0:T(8,128)S(1)} %get-tuple-element.71, ...), kind=kLoop, calls=%fused_computation.77 | loop fusion | flops 3473408 | bytes 7746560 | tf_op jit(solution)/shard_map/convert_element_type | solution.py:172
  59.9 1.3 %collective-permute-done.4 = f32[512,128]{1,0:T(8,128)S(1)} collective-permute-done((f32[512,128]{1,0:T(8,128)S(1)}, f32[512,128]{1,0:T(8,128)S(1)}, u32[]{:S(2)}, u32[]{:S(2)}) %collective-permute-start.4) | collective-permute-done | bytes 262176 | tf_op jit(solution)/shard_map/ppermute | solution.py:22
  61.3 2.1 %collective-permute-start.5 = (f32[256,128]{1,0:T(8,128)S(1)}, f32[256,128]{1,0:T(8,128)S(1)}, u32[]{:S(2)}, u32[]{:S(2)}) collective-permute-start(f32[256,128]{1,0:T(8,128)S(1)} %constant_dynamic-slice_fusion), channel_id=1, source_target_pairs={{0,2},{2,0},{4,6},{6,4},{8,10},{10,8},{12,14},{14,12},{1,3},{3,1},... | collective-permute-start | bytes 393224 | tf_op jit(solution)/shard_map/ppermute | solution.py:22
  63.4 3.9 %collective-permute-done.5 = f32[256,128]{1,0:T(8,128)S(1)} collective-permute-done((f32[256,128]{1,0:T(8,128)S(1)}, f32[256,128]{1,0:T(8,128)S(1)}, u32[]{:S(2)}, u32[]{:S(2)}) %collective-permute-start.5) | collective-permute-done | bytes 131104 | tf_op jit(solution)/shard_map/ppermute | solution.py:22
  67.3 1.5 %collective-permute-start.6 = (f32[256,128]{1,0:T(8,128)S(1)}, f32[256,128]{1,0:T(8,128)S(1)}, u32[]{:S(2)}, u32[]{:S(2)}) collective-permute-start(f32[256,128]{1,0:T(8,128)S(1)} %dynamic-slice_add_fusion.1), channel_id=1, source_target_pairs={{0,4},{2,6},{4,0},{6,2},{8,12},{10,14},{12,8},{14,10},{1,5},{3,7},... | collective-permute-start | bytes 393224 | tf_op jit(solution)/shard_map/ppermute | solution.py:56
  68.8 3.7 %collective-permute-done.6 = f32[256,128]{1,0:T(8,128)S(1)} collective-permute-done((f32[256,128]{1,0:T(8,128)S(1)}, f32[256,128]{1,0:T(8,128)S(1)}, u32[]{:S(2)}, u32[]{:S(2)}) %collective-permute-start.6) | collective-permute-done | bytes 131104 | tf_op jit(solution)/shard_map/ppermute | solution.py:56
  72.5 2.1 %collective-permute-start.7 = (f32[256,128]{1,0:T(8,128)S(1)}, f32[256,128]{1,0:T(8,128)S(1)}, u32[]{:S(2)}, u32[]{:S(2)}) collective-permute-start(f32[256,128]{1,0:T(8,128)S(1)} %add.401), channel_id=1, source_target_pairs={{0,8},{2,10},{4,12},{6,14},{8,0},{10,2},{12,4},{14,6},{1,9},{3,11}... | collective-permute-start | bytes 393224 | tf_op jit(solution)/shard_map/ppermute | solution.py:56
  74.6 6.0 %collective-permute-done.7 = f32[256,128]{1,0:T(8,128)S(1)} collective-permute-done((f32[256,128]{1,0:T(8,128)S(1)}, f32[256,128]{1,0:T(8,128)S(1)}, u32[]{:S(2)}, u32[]{:S(2)}) %collective-permute-start.7) | collective-permute-done | bytes 131104 | tf_op jit(solution)/shard_map/ppermute | solution.py:56
  80.6 1.0 %collective-permute-start.8 = (f32[256,128]{1,0:T(8,128)S(1)}, f32[256,128]{1,0:T(8,128)S(1)}, u32[]{:S(2)}, u32[]{:S(2)}) collective-permute-start(f32[256,128]{1,0:T(8,128)S(1)} %get-tuple-element.14), channel_id=1, source_target_pairs={{0,2},{2,0},{4,6},{6,4},{8,10},{10,8},{12,14},{14,12},{1,3},{3,1},... | collective-permute-start | bytes 393224 | tf_op jit(solution)/shard_map/ppermute | solution.py:29
  81.7 4.0 %collective-permute-done.8 = f32[256,128]{1,0:T(8,128)S(1)} collective-permute-done((f32[256,128]{1,0:T(8,128)S(1)}, f32[256,128]{1,0:T(8,128)S(1)}, u32[]{:S(2)}, u32[]{:S(2)}) %collective-permute-start.8) | collective-permute-done | bytes 131104 | tf_op jit(solution)/shard_map/ppermute | solution.py:29
  85.8 1.4 %collective-permute-done.9 = f32[512,128]{1,0:T(8,128)S(1)} collective-permute-done((f32[512,128]{1,0:T(8,128)S(1)}, f32[512,128]{1,0:T(8,128)S(1)}, u32[]{:S(2)}, u32[]{:S(2)}) %collective-permute-start.9) | collective-permute-done | bytes 262176 | tf_op jit(solution)/shard_map/ppermute | solution.py:29
  (88 shorter events, 16.1 us)
Async XLA Ops:
  0.6 55.3 %copy-start = (bf16[256,256]{1,0:T(8,128)(2,1)S(1)}, bf16[256,256]{1,0:T(8,128)(2,1)}, u32[]{:S(2)}) copy-start(bf16[256,256]{1,0:T(8,128)(2,1)} %param.12) | copy-start | bytes 393220
  0.6 25.4 %copy-start.3 = (bf16[2,48,32,256]{3,2,1,0:T(8,128)(2,1)S(1)}, bf16[2,48,32,256]{3,2,1,0:T(8,128)(2,1)}, u32[]{:S(2)}) copy-start(bf16[2,48,32,256]{3,2,1,0:T(8,128)(2,1)} %param.9) | copy-start | bytes 4718596
  0.7 19.2 %copy-start.5 = (bf16[9,256]{1,0:T(8,128)(2,1)S(1)}, bf16[9,256]{1,0:T(8,128)(2,1)}, u32[]{:S(2)}) copy-start(bf16[9,256]{1,0:T(8,128)(2,1)} %param.11) | copy-start | bytes 13828
  0.7 19.2 %copy-start.6 = (s32[256]{0:T(256)S(1)}, s32[256]{0:T(256)}, u32[]{:S(2)}) copy-start(s32[256]{0:T(256)} %param.10) | copy-start | bytes 3076
  5.9 26.7 %all-to-all-start = ((bf16[32,8,228]{2,1,0:T(8,128)(2,1)}), bf16[32,8,228]{2,1,0:T(8,128)(2,1)S(1)}, u32[]{:S(2)}, u32[]{:S(2)}) async-start(bf16[32,8,228]{2,1,0:T(8,128)(2,1)} %copy.189), calls=%async_computation | async-start | bytes 262144 | tf_op jit(solution)/shard_map/all_to_all | solution.py:118
  14.8 11.2 %collective-permute-start = (bf16[2,48,4,256]{3,0,2,1:T(2,128)(2,1)S(1)}, bf16[2,48,4,256]{3,0,2,1:T(2,128)(2,1)S(1)}, u32[]{:S(2)}, u32[]{:S(2)}) collective-permute-start(bf16[2,48,4,256]{3,0,2,1:T(2,128)(2,1)S(1)} %copy.266), channel_id=1, source_target_pairs={{0,2},{2,4},{4,6},{6,8},{8,10},{10,12},{12,14},{14,0},{1,3},{3,5},... | collective-permute-start | bytes 589832 | tf_op jit(solution)/shard_map/ppermute | solution.py:78
  17.0 11.4 %collective-permute-start.1 = (bf16[2,48,4,256]{3,0,2,1:T(2,128)(2,1)S(1)}, bf16[2,48,4,256]{3,0,2,1:T(2,128)(2,1)S(1)}, u32[]{:S(2)}, u32[]{:S(2)}) collective-permute-start(bf16[2,48,4,256]{3,0,2,1:T(2,128)(2,1)S(1)} %copy.267), channel_id=1, source_target_pairs={{2,0},{4,2},{6,4},{8,6},{10,8},{12,10},{14,12},{0,14},{3,1},{5,3},... | collective-permute-start | bytes 589832 | tf_op jit(solution)/shard_map/ppermute | solution.py:80
  28.5 1.3 %copy-start.2 = (bf16[2,48,40,256]{3,0,2,1:T(2,128)(2,1)}, bf16[2,48,40,256]{3,0,2,1:T(2,128)(2,1)S(1)}, u32[]{:S(2)}) copy-start(bf16[2,48,40,256]{3,0,2,1:T(2,128)(2,1)S(1)} %constant_dynamic-update-slice_fusion) | copy-start | bytes 5898244
  30.0 3.7 %collective-permute-start.2 = (bf16[2,4,40,256]{3,0,2,1:T(2,128)(2,1)S(1)}, bf16[2,4,40,256]{3,0,2,1:T(2,128)(2,1)S(1)}, u32[]{:S(2)}, u32[]{:S(2)}) collective-permute-start(bf16[2,4,40,256]{3,0,2,1:T(2,128)(2,1)S(1)} %get-tuple-element.57), channel_id=1, source_target_pairs={{0,1},{2,3},{4,5},{6,7},{8,9},{10,11},{12,13},{14,15},{16,17},{18,... | collective-permute-start | bytes 491528 | tf_op jit(solution)/shard_map/ppermute | solution.py:78
  31.3 3.3 %collective-permute-start.3 = (bf16[2,4,40,256]{3,0,2,1:T(2,128)(2,1)S(1)}, bf16[2,4,40,256]{3,0,2,1:T(2,128)(2,1)S(1)}, u32[]{:S(2)}, u32[]{:S(2)}) collective-permute-start(bf16[2,4,40,256]{3,0,2,1:T(2,128)(2,1)S(1)} %get-tuple-element.58), channel_id=1, source_target_pairs={{1,0},{3,2},{5,4},{7,6},{9,8},{11,10},{13,12},{15,14},{17,16},{19,... | collective-permute-start | bytes 491528 | tf_op jit(solution)/shard_map/ppermute | solution.py:80
  45.1 2.6 %copy-start.1 = (bf16[32,9,16,256]{3,0,2,1:T(8,128)(2,1)S(1)}, bf16[32,9,16,256]{3,0,2,1:T(8,128)(2,1)}, u32[]{:S(2)}) copy-start(bf16[32,9,16,256]{3,0,2,1:T(8,128)(2,1)} %gather_fusion) | copy-start | bytes 7077892
  50.5 5.8 %copy-start.4 = (bf16[256,227]{0,1:T(8,128)(2,1)S(1)}, bf16[256,227]{0,1:T(8,128)(2,1)}, u32[]{:S(2)}) copy-start(bf16[256,227]{0,1:T(8,128)(2,1)} %param.13) | copy-start | bytes 348676
  59.6 1.6 %collective-permute-start.4 = (f32[512,128]{1,0:T(8,128)S(1)}, f32[512,128]{1,0:T(8,128)S(1)}, u32[]{:S(2)}, u32[]{:S(2)}) collective-permute-start(f32[512,128]{1,0:T(8,128)S(1)} %constant_dynamic-slice_fusion.1), channel_id=1, source_target_pairs={{0,1},{1,0},{2,3},{3,2},{4,5},{5,4},{6,7},{7,6},{8,9},{9,8},{10,11... | collective-permute-start | bytes 786440 | tf_op jit(solution)/shard_map/ppermute | solution.py:22
  61.3 6.0 %collective-permute-start.5 = (f32[256,128]{1,0:T(8,128)S(1)}, f32[256,128]{1,0:T(8,128)S(1)}, u32[]{:S(2)}, u32[]{:S(2)}) collective-permute-start(f32[256,128]{1,0:T(8,128)S(1)} %constant_dynamic-slice_fusion), channel_id=1, source_target_pairs={{0,2},{2,0},{4,6},{6,4},{8,10},{10,8},{12,14},{14,12},{1,3},{3,1},... | collective-permute-start | bytes 393224 | tf_op jit(solution)/shard_map/ppermute | solution.py:22
  67.3 5.2 %collective-permute-start.6 = (f32[256,128]{1,0:T(8,128)S(1)}, f32[256,128]{1,0:T(8,128)S(1)}, u32[]{:S(2)}, u32[]{:S(2)}) collective-permute-start(f32[256,128]{1,0:T(8,128)S(1)} %dynamic-slice_add_fusion.1), channel_id=1, source_target_pairs={{0,4},{2,6},{4,0},{6,2},{8,12},{10,14},{12,8},{14,10},{1,5},{3,7},... | collective-permute-start | bytes 393224 | tf_op jit(solution)/shard_map/ppermute | solution.py:56
  72.5 8.0 %collective-permute-start.7 = (f32[256,128]{1,0:T(8,128)S(1)}, f32[256,128]{1,0:T(8,128)S(1)}, u32[]{:S(2)}, u32[]{:S(2)}) collective-permute-start(f32[256,128]{1,0:T(8,128)S(1)} %add.401), channel_id=1, source_target_pairs={{0,8},{2,10},{4,12},{6,14},{8,0},{10,2},{12,4},{14,6},{1,9},{3,11}... | collective-permute-start | bytes 393224 | tf_op jit(solution)/shard_map/ppermute | solution.py:56
  80.6 5.0 %collective-permute-start.8 = (f32[256,128]{1,0:T(8,128)S(1)}, f32[256,128]{1,0:T(8,128)S(1)}, u32[]{:S(2)}, u32[]{:S(2)}) collective-permute-start(f32[256,128]{1,0:T(8,128)S(1)} %get-tuple-element.14), channel_id=1, source_target_pairs={{0,2},{2,0},{4,6},{6,4},{8,10},{10,8},{12,14},{14,12},{1,3},{3,1},... | collective-permute-start | bytes 393224 | tf_op jit(solution)/shard_map/ppermute | solution.py:29
  85.7 1.6 %collective-permute-start.9 = (f32[512,128]{1,0:T(8,128)S(1)}, f32[512,128]{1,0:T(8,128)S(1)}, u32[]{:S(2)}, u32[]{:S(2)}) collective-permute-start(f32[512,128]{1,0:T(8,128)S(1)} %constant_dynamic-update-slice_fusion.10), channel_id=1, source_target_pairs={{0,1},{1,0},{2,3},{3,2},{4,5},{5,4},{6,7},{7,6},{8,9},{9,8},{10,11... | collective-permute-start | bytes 786440 | tf_op jit(solution)/shard_map/ppermute | solution.py:29

commit v19 on v18

--- a/solution.py
+++ b/solution.py
@@ -159,9 +159,10 @@
         for dilation in range(1, DMAX + 1):
             row_shift = (tap_index // 3 - 1) * dilation
             col_shift = (tap_index % 3 - 1) * dilation
-            term = onehot[dilation - 1] * shifted(windows, row_shift, col_shift)
+            piece = windows[:, DMAX + row_shift, DMAX + col_shift : DMAX + col_shift + TILE, :]
+            term = onehot[dilation - 1].astype(jnp.bfloat16) * piece
             chosen = term if chosen is None else chosen + term
-        return chosen
+        return chosen.astype(jnp.float32)
 
     def forward(windows, tiles, weight):
         center = shifted(windows, 0, 0)

time: 92.3 us -> 90.4 us (0.979)
  other arithmetic: 20 us -> 15.6 us
  local copies, waits for them, and re-layouts: 16.4 us -> 19 us
    convert_element_type x3 -> x0, other arithmetic: 3.1 us -> none  [the longest x2 3.03 us: shifted(): source[:, DMAX + row_shift, DMAX + col_shift:DMAX + col_shift + TILE, :]]
    add x1 -> x0, other arithmetic: 2.26 us -> none  [chosen_tap(): chosen = term if chosen is None else chosen + term]
    slice x1 -> x2, local copies, waits for them, and re-layouts: 0.01 us -> 2.13 us  [the longest x1 2.1 us: chosen_tap(): windows[:, DMAX + row_shift, DMAX + col_shift:DMAX + col_shift + TILE, :]]
where the time goes in v19:
time: 90.4 us; the launch traced here: 90 us
  waiting for transfers between devices  27.8 us (31%)
  starting transfers between devices  21.8 us (24%)
  local copies, waits for them, and re-layouts  19 us (21%)
  other arithmetic  15.6 us (17%)
  matrix products  2.92 us (3%)
  between operations  2.83 us (3%)
    ppermute x2, waiting for transfers between devices, packed_sum(): x = x + lax.ppermute(x, axis, [(i, i ^ bit) for i in range(count)])  9.75 us
    all_to_all x1, starting transfers between devices, local(): lax.all_to_all(send, ('lon', 'lat'), split_axis=0, concat_axis=0, tiled=T...  7.36 us
    convert_element_type x1, other arithmetic, forward(): depth_flat = accum_sum.astype(jnp.bfloat16).reshape(-1, width)  6.21 us
    ppermute x2, waiting for transfers between devices, padded_2(): lax.ppermute(tail, axis, [(i, (i + 1) % count) for i in range(ends)])  5.97 us
    gather x1, local copies, waits for them, and re-layouts, gather_windows(): lax.dynamic_slice(padded, (b, h, w, jnp.int32(0)), (1, span, reach, width))  5.74 us
    ppermute x2, waiting for transfers between devices, double(): got = lax.ppermute(x, axis, [(i, i ^ bit) for i in range(count)])  5.46 us
    ppermute x2, waiting for transfers between devices, halve(): return keep + lax.ppermute(send, axis, [(i, i ^ bit) for i in range(count)])  5.22 us
    unnamed x26, local copies, waits for them, and re-layouts  5.08 us
  transfers between devices with their start and end apart: 11, of which 9 were waited for; matrix products, arithmetic and copies ran while one was open for 6% of the time, Pallas kernels for 0%

profile of v19, /device:TPU:0, one launch (start us, length us, event | category | flops | bytes accessed | tf_op | source)
XLA Modules:
  0.0 90.0 jit_solution(3065455628119013261)
XLA Ops:
  3.3 0.9 %convert_reduce_fusion = s32[16]{0:T(128)S(1)} fusion(s32[16]{0:T(128)} %bitcast.289), kind=kLoop, calls=%fused_computation.142 | loop fusion | flops 1264 | bytes 128 | tf_op jit(solution)/shard_map/reduce_sum | solution.py:103
  5.9 7.4 %all-to-all-start = ((bf16[32,8,228]{2,1,0:T(8,128)(2,1)}), bf16[32,8,228]{2,1,0:T(8,128)(2,1)S(1)}, u32[]{:S(2)}, u32[]{:S(2)}) async-start(bf16[32,8,228]{2,1,0:T(8,128)(2,1)} %copy.189), calls=%async_computation | async-start | bytes 262144 | tf_op jit(solution)/shard_map/all_to_all | solution.py:118
  13.3 1.3 %fusion.85 = (bf16[2,48,4,256]{3,2,1,0:T(4,128)(2,1)S(1)}, bf16[2,48,4,256]{3,2,1,0:T(4,128)(2,1)S(1)}) fusion(bf16[2,48,32,256]{3,2,1,0:T(8,128)(2,1)} %param.9), kind=kLoop, calls=%fused_computation.196 | loop fusion | bytes 786432 | tf_op jit(solution)/shard_map/slice | solution.py:74
  14.8 2.0 %collective-permute-start = (bf16[2,48,4,256]{3,0,2,1:T(2,128)(2,1)S(1)}, bf16[2,48,4,256]{3,0,2,1:T(2,128)(2,1)S(1)}, u32[]{:S(2)}, u32[]{:S(2)}) collective-permute-start(bf16[2,48,4,256]{3,0,2,1:T(2,128)(2,1)S(1)} %copy.266), channel_id=1, source_target_pairs={{0,2},{2,4},{4,6},{6,8},{8,10},{10,12},{12,14},{14,0},{1,3},{3,5},... | collective-permute-start | bytes 589832 | tf_op jit(solution)/shard_map/ppermute | solution.py:78
  17.0 2.9 %collective-permute-start.1 = (bf16[2,48,4,256]{3,0,2,1:T(2,128)(2,1)S(1)}, bf16[2,48,4,256]{3,0,2,1:T(2,128)(2,1)S(1)}, u32[]{:S(2)}, u32[]{:S(2)}) collective-permute-start(bf16[2,48,4,256]{3,0,2,1:T(2,128)(2,1)S(1)} %copy.267), channel_id=1, source_target_pairs={{2,0},{4,2},{6,4},{8,6},{10,8},{12,10},{14,12},{0,14},{3,1},{5,3},... | collective-permute-start | bytes 589832 | tf_op jit(solution)/shard_map/ppermute | solution.py:80
  20.0 6.0 %collective-permute-done = bf16[2,48,4,256]{3,0,2,1:T(2,128)(2,1)S(1)} collective-permute-done((bf16[2,48,4,256]{3,0,2,1:T(2,128)(2,1)S(1)}, bf16[2,48,4,256]{3,0,2,1:T(2,128)(2,1)S(1)}, u32[]{:S(2)}, u32[]{:S(2)}) %collective-permute-start) | collective-permute-done | bytes 196640 | tf_op jit(solution)/shard_map/ppermute | solution.py:78
  26.1 1.7 %constant_dynamic-update-slice_fusion.1 = bf16[2,48,40,256]{3,0,2,1:T(2,128)(2,1)S(1)} fusion(bf16[2,48,40,256]{3,0,2,1:T(2,128)(2,1)S(1)} %constant_dynamic-update-slice_fusion.2, bf16[2,48,32,256]{3,2,1,0:T(8,128)(2,1)S(1)} %copy-done.3), kind=kLoop, calls=%fused_computation.132 | loop fusion | bytes 3145728
  28.5 1.3 %copy-done.2 = bf16[2,48,40,256]{3,0,2,1:T(2,128)(2,1)} copy-done((bf16[2,48,40,256]{3,0,2,1:T(2,128)(2,1)}, bf16[2,48,40,256]{3,0,2,1:T(2,128)(2,1)S(1)}, u32[]{:S(2)}) %copy-start.2) | copy-done | bytes 1966104
  30.0 1.3 %collective-permute-start.2 = (bf16[2,4,40,256]{3,0,2,1:T(2,128)(2,1)S(1)}, bf16[2,4,40,256]{3,0,2,1:T(2,128)(2,1)S(1)}, u32[]{:S(2)}, u32[]{:S(2)}) collective-permute-start(bf16[2,4,40,256]{3,0,2,1:T(2,128)(2,1)S(1)} %get-tuple-element.64), channel_id=1, source_target_pairs={{0,1},{2,3},{4,5},{6,7},{8,9},{10,11},{12,13},{14,15},{16,17},{18,... | collective-permute-start | bytes 491528 | tf_op jit(solution)/shard_map/ppermute | solution.py:78
  31.3 1.3 %collective-permute-start.3 = (bf16[2,4,40,256]{3,0,2,1:T(2,128)(2,1)S(1)}, bf16[2,4,40,256]{3,0,2,1:T(2,128)(2,1)S(1)}, u32[]{:S(2)}, u32[]{:S(2)}) collective-permute-start(bf16[2,4,40,256]{3,0,2,1:T(2,128)(2,1)S(1)} %get-tuple-element.65), channel_id=1, source_target_pairs={{1,0},{3,2},{5,4},{7,6},{9,8},{11,10},{13,12},{15,14},{17,16},{19,... | collective-permute-start | bytes 491528 | tf_op jit(solution)/shard_map/ppermute | solution.py:80
  34.6 4.8 %pad_maximum_fusion = bf16[2,56,40,256]{3,0,2,1:T(2,128)(2,1)S(1)} fusion(bf16[2,4,40,256]{3,0,2,1:T(2,128)(2,1)S(1)} %collective-permute-done.3, bf16[2,48,40,256]{3,0,2,1:T(2,128)(2,1)} %copy-done.2, bf16[2,4,40,256]{3,0,2,1:T(2,128)(2,1)S(1)} %collective-permute-done.2), kind=kLoop, calls=%fused_computation.1 | loop fusion | flops 2293760 | bytes 4587520 | tf_op jit(solution)/shard_map/concatenate | solution.py:76
  39.4 5.7 %gather_fusion = bf16[32,9,16,256]{3,0,2,1:T(8,128)(2,1)} fusion(bf16[2,56,40,256]{3,0,2,1:T(2,128)(2,1)S(1)} %pad_maximum_fusion, s32[32]{0:T(128)S(1)} %fusion.72), kind=kCustom, calls=%fused_computation | custom fusion | bytes 4719104 | tf_op jit(solution)/shard_map/vmap()/gather | solution.py:145
  45.1 2.1 %fusion.82 = (bf16[32,1,8,256]{3,0,2,1:T(8,128)(2,1)S(1)}, bf16[32,1,8,256]{3,0,2,1:T(8,128)(2,1)S(1)}, bf16[32,1,8,256]{3,0,2,1:T(8,128)(2,1)S(1)}, bf16[32,1,8...) fusion(bf16[32,9,16,256]{3,0,2,1:T(8,128)(2,1)} %gather_fusion), kind=kLoop, calls=%fused_computation.193 | loop fusion | bytes 4980736 | tf_op jit(solution)/shard_map/slice | solution.py:162
  47.9 6.2 %fusion.13 = (bf16[256,256]{1,0:T(8,128)(2,1)S(1)}, bf16[256,256]{1,0:T(8,128)(2,1)S(1)}, bf16[256,256]{1,0:T(8,128)(2,1)S(1)}, bf16[256,256]{1,0:T(8,128)(2,1)S...) fusion(f32[32,1,8,256]{3,0,2,1:T(8,128)S(1)} %get-tuple-element, ...), kind=kLoop, calls=%fused_computation.41 | loop fusion | flops 5373952 | bytes 5647360 | tf_op jit(solution)/shard_map/convert_element_type | solution.py:173
  58.0 1.3 %collective-permute-done.4 = f32[512,128]{1,0:T(8,128)S(1)} collective-permute-done((f32[512,128]{1,0:T(8,128)S(1)}, f32[512,128]{1,0:T(8,128)S(1)}, u32[]{:S(2)}, u32[]{:S(2)}) %collective-permute-start.4) | collective-permute-done | bytes 262176 | tf_op jit(solution)/shard_map/ppermute | solution.py:22
  59.4 2.1 %collective-permute-start.5 = (f32[256,128]{1,0:T(8,128)S(1)}, f32[256,128]{1,0:T(8,128)S(1)}, u32[]{:S(2)}, u32[]{:S(2)}) collective-permute-start(f32[256,128]{1,0:T(8,128)S(1)} %constant_dynamic-slice_fusion), channel_id=1, source_target_pairs={{0,2},{2,0},{4,6},{6,4},{8,10},{10,8},{12,14},{14,12},{1,3},{3,1},... | collective-permute-start | bytes 393224 | tf_op jit(solution)/shard_map/ppermute | solution.py:22
  61.5 3.9 %collective-permute-done.5 = f32[256,128]{1,0:T(8,128)S(1)} collective-permute-done((f32[256,128]{1,0:T(8,128)S(1)}, f32[256,128]{1,0:T(8,128)S(1)}, u32[]{:S(2)}, u32[]{:S(2)}) %collective-permute-start.5) | collective-permute-done | bytes 131104 | tf_op jit(solution)/shard_map/ppermute | solution.py:22
  65.4 1.5 %collective-permute-start.6 = (f32[256,128]{1,0:T(8,128)S(1)}, f32[256,128]{1,0:T(8,128)S(1)}, u32[]{:S(2)}, u32[]{:S(2)}) collective-permute-start(f32[256,128]{1,0:T(8,128)S(1)} %dynamic-slice_add_fusion.1), channel_id=1, source_target_pairs={{0,4},{2,6},{4,0},{6,2},{8,12},{10,14},{12,8},{14,10},{1,5},{3,7},... | collective-permute-start | bytes 393224 | tf_op jit(solution)/shard_map/ppermute | solution.py:56
  66.9 3.7 %collective-permute-done.6 = f32[256,128]{1,0:T(8,128)S(1)} collective-permute-done((f32[256,128]{1,0:T(8,128)S(1)}, f32[256,128]{1,0:T(8,128)S(1)}, u32[]{:S(2)}, u32[]{:S(2)}) %collective-permute-start.6) | collective-permute-done | bytes 131104 | tf_op jit(solution)/shard_map/ppermute | solution.py:56
  70.7 2.0 %collective-permute-start.7 = (f32[256,128]{1,0:T(8,128)S(1)}, f32[256,128]{1,0:T(8,128)S(1)}, u32[]{:S(2)}, u32[]{:S(2)}) collective-permute-start(f32[256,128]{1,0:T(8,128)S(1)} %add.401), channel_id=1, source_target_pairs={{0,8},{2,10},{4,12},{6,14},{8,0},{10,2},{12,4},{14,6},{1,9},{3,11}... | collective-permute-start | bytes 393224 | tf_op jit(solution)/shard_map/ppermute | solution.py:56
  72.7 6.0 %collective-permute-done.7 = f32[256,128]{1,0:T(8,128)S(1)} collective-permute-done((f32[256,128]{1,0:T(8,128)S(1)}, f32[256,128]{1,0:T(8,128)S(1)}, u32[]{:S(2)}, u32[]{:S(2)}) %collective-permute-start.7) | collective-permute-done | bytes 131104 | tf_op jit(solution)/shard_map/ppermute | solution.py:56
  78.8 1.0 %collective-permute-start.8 = (f32[256,128]{1,0:T(8,128)S(1)}, f32[256,128]{1,0:T(8,128)S(1)}, u32[]{:S(2)}, u32[]{:S(2)}) collective-permute-start(f32[256,128]{1,0:T(8,128)S(1)} %get-tuple-element.18), channel_id=1, source_target_pairs={{0,2},{2,0},{4,6},{6,4},{8,10},{10,8},{12,14},{14,12},{1,3},{3,1},... | collective-permute-start | bytes 393224 | tf_op jit(solution)/shard_map/ppermute | solution.py:29
  79.8 4.0 %collective-permute-done.8 = f32[256,128]{1,0:T(8,128)S(1)} collective-permute-done((f32[256,128]{1,0:T(8,128)S(1)}, f32[256,128]{1,0:T(8,128)S(1)}, u32[]{:S(2)}, u32[]{:S(2)}) %collective-permute-start.8) | collective-permute-done | bytes 131104 | tf_op jit(solution)/shard_map/ppermute | solution.py:29
  84.0 1.4 %collective-permute-done.9 = f32[512,128]{1,0:T(8,128)S(1)} collective-permute-done((f32[512,128]{1,0:T(8,128)S(1)}, f32[512,128]{1,0:T(8,128)S(1)}, u32[]{:S(2)}, u32[]{:S(2)}) %collective-permute-start.9) | collective-permute-done | bytes 262176 | tf_op jit(solution)/shard_map/ppermute | solution.py:29
  (87 shorter events, 15.3 us)
Async XLA Ops:
  0.6 53.5 %copy-start = (bf16[256,256]{1,0:T(8,128)(2,1)S(1)}, bf16[256,256]{1,0:T(8,128)(2,1)}, u32[]{:S(2)}) copy-start(bf16[256,256]{1,0:T(8,128)(2,1)} %param.12) | copy-start | bytes 393220
  0.6 25.4 %copy-start.3 = (bf16[2,48,32,256]{3,2,1,0:T(8,128)(2,1)S(1)}, bf16[2,48,32,256]{3,2,1,0:T(8,128)(2,1)}, u32[]{:S(2)}) copy-start(bf16[2,48,32,256]{3,2,1,0:T(8,128)(2,1)} %param.9) | copy-start | bytes 4718596
  0.7 19.2 %copy-start.6 = (s32[256]{0:T(256)S(1)}, s32[256]{0:T(256)}, u32[]{:S(2)}) copy-start(s32[256]{0:T(256)} %param.10) | copy-start | bytes 3076
  0.7 19.3 %copy-start.5 = (bf16[9,256]{1,0:T(8,128)(2,1)S(1)}, bf16[9,256]{1,0:T(8,128)(2,1)}, u32[]{:S(2)}) copy-start(bf16[9,256]{1,0:T(8,128)(2,1)} %param.11) | copy-start | bytes 13828
  5.9 26.7 %all-to-all-start = ((bf16[32,8,228]{2,1,0:T(8,128)(2,1)}), bf16[32,8,228]{2,1,0:T(8,128)(2,1)S(1)}, u32[]{:S(2)}, u32[]{:S(2)}) async-start(bf16[32,8,228]{2,1,0:T(8,128)(2,1)} %copy.189), calls=%async_computation | async-start | bytes 262144 | tf_op jit(solution)/shard_map/all_to_all | solution.py:118
  14.8 11.2 %collective-permute-start = (bf16[2,48,4,256]{3,0,2,1:T(2,128)(2,1)S(1)}, bf16[2,48,4,256]{3,0,2,1:T(2,128)(2,1)S(1)}, u32[]{:S(2)}, u32[]{:S(2)}) collective-permute-start(bf16[2,48,4,256]{3,0,2,1:T(2,128)(2,1)S(1)} %copy.266), channel_id=1, source_target_pairs={{0,2},{2,4},{4,6},{6,8},{8,10},{10,12},{12,14},{14,0},{1,3},{3,5},... | collective-permute-start | bytes 589832 | tf_op jit(solution)/shard_map/ppermute | solution.py:78
  17.0 11.4 %collective-permute-start.1 = (bf16[2,48,4,256]{3,0,2,1:T(2,128)(2,1)S(1)}, bf16[2,48,4,256]{3,0,2,1:T(2,128)(2,1)S(1)}, u32[]{:S(2)}, u32[]{:S(2)}) collective-permute-start(bf16[2,48,4,256]{3,0,2,1:T(2,128)(2,1)S(1)} %copy.267), channel_id=1, source_target_pairs={{2,0},{4,2},{6,4},{8,6},{10,8},{12,10},{14,12},{0,14},{3,1},{5,3},... | collective-permute-start | bytes 589832 | tf_op jit(solution)/shard_map/ppermute | solution.py:80
  28.5 1.3 %copy-start.2 = (bf16[2,48,40,256]{3,0,2,1:T(2,128)(2,1)}, bf16[2,48,40,256]{3,0,2,1:T(2,128)(2,1)S(1)}, u32[]{:S(2)}) copy-start(bf16[2,48,40,256]{3,0,2,1:T(2,128)(2,1)S(1)} %constant_dynamic-update-slice_fusion) | copy-start | bytes 5898244
  30.0 3.7 %collective-permute-start.2 = (bf16[2,4,40,256]{3,0,2,1:T(2,128)(2,1)S(1)}, bf16[2,4,40,256]{3,0,2,1:T(2,128)(2,1)S(1)}, u32[]{:S(2)}, u32[]{:S(2)}) collective-permute-start(bf16[2,4,40,256]{3,0,2,1:T(2,128)(2,1)S(1)} %get-tuple-element.64), channel_id=1, source_target_pairs={{0,1},{2,3},{4,5},{6,7},{8,9},{10,11},{12,13},{14,15},{16,17},{18,... | collective-permute-start | bytes 491528 | tf_op jit(solution)/shard_map/ppermute | solution.py:78
  31.3 3.3 %collective-permute-start.3 = (bf16[2,4,40,256]{3,0,2,1:T(2,128)(2,1)S(1)}, bf16[2,4,40,256]{3,0,2,1:T(2,128)(2,1)S(1)}, u32[]{:S(2)}, u32[]{:S(2)}) collective-permute-start(bf16[2,4,40,256]{3,0,2,1:T(2,128)(2,1)S(1)} %get-tuple-element.65), channel_id=1, source_target_pairs={{1,0},{3,2},{5,4},{7,6},{9,8},{11,10},{13,12},{15,14},{17,16},{19,... | collective-permute-start | bytes 491528 | tf_op jit(solution)/shard_map/ppermute | solution.py:80
  45.1 2.5 %copy-start.1 = (bf16[32,9,16,256]{3,0,2,1:T(8,128)(2,1)S(1)}, bf16[32,9,16,256]{3,0,2,1:T(8,128)(2,1)}, u32[]{:S(2)}) copy-start(bf16[32,9,16,256]{3,0,2,1:T(8,128)(2,1)} %gather_fusion) | copy-start | bytes 7077892
  47.9 6.5 %copy-start.4 = (bf16[256,227]{0,1:T(8,128)(2,1)S(1)}, bf16[256,227]{0,1:T(8,128)(2,1)}, u32[]{:S(2)}) copy-start(bf16[256,227]{0,1:T(8,128)(2,1)} %param.13) | copy-start | bytes 348676
  57.7 1.6 %collective-permute-start.4 = (f32[512,128]{1,0:T(8,128)S(1)}, f32[512,128]{1,0:T(8,128)S(1)}, u32[]{:S(2)}, u32[]{:S(2)}) collective-permute-start(f32[512,128]{1,0:T(8,128)S(1)} %constant_dynamic-slice_fusion.1), channel_id=1, source_target_pairs={{0,1},{1,0},{2,3},{3,2},{4,5},{5,4},{6,7},{7,6},{8,9},{9,8},{10,11... | collective-permute-start | bytes 786440 | tf_op jit(solution)/shard_map/ppermute | solution.py:22
  59.4 6.0 %collective-permute-start.5 = (f32[256,128]{1,0:T(8,128)S(1)}, f32[256,128]{1,0:T(8,128)S(1)}, u32[]{:S(2)}, u32[]{:S(2)}) collective-permute-start(f32[256,128]{1,0:T(8,128)S(1)} %constant_dynamic-slice_fusion), channel_id=1, source_target_pairs={{0,2},{2,0},{4,6},{6,4},{8,10},{10,8},{12,14},{14,12},{1,3},{3,1},... | collective-permute-start | bytes 393224 | tf_op jit(solution)/shard_map/ppermute | solution.py:22
  65.4 5.2 %collective-permute-start.6 = (f32[256,128]{1,0:T(8,128)S(1)}, f32[256,128]{1,0:T(8,128)S(1)}, u32[]{:S(2)}, u32[]{:S(2)}) collective-permute-start(f32[256,128]{1,0:T(8,128)S(1)} %dynamic-slice_add_fusion.1), channel_id=1, source_target_pairs={{0,4},{2,6},{4,0},{6,2},{8,12},{10,14},{12,8},{14,10},{1,5},{3,7},... | collective-permute-start | bytes 393224 | tf_op jit(solution)/shard_map/ppermute | solution.py:56
  70.7 8.1 %collective-permute-start.7 = (f32[256,128]{1,0:T(8,128)S(1)}, f32[256,128]{1,0:T(8,128)S(1)}, u32[]{:S(2)}, u32[]{:S(2)}) collective-permute-start(f32[256,128]{1,0:T(8,128)S(1)} %add.401), channel_id=1, source_target_pairs={{0,8},{2,10},{4,12},{6,14},{8,0},{10,2},{12,4},{14,6},{1,9},{3,11}... | collective-permute-start | bytes 393224 | tf_op jit(solution)/shard_map/ppermute | solution.py:56
  78.8 5.0 %collective-permute-start.8 = (f32[256,128]{1,0:T(8,128)S(1)}, f32[256,128]{1,0:T(8,128)S(1)}, u32[]{:S(2)}, u32[]{:S(2)}) collective-permute-start(f32[256,128]{1,0:T(8,128)S(1)} %get-tuple-element.18), channel_id=1, source_target_pairs={{0,2},{2,0},{4,6},{6,4},{8,10},{10,8},{12,14},{14,12},{1,3},{3,1},... | collective-permute-start | bytes 393224 | tf_op jit(solution)/shard_map/ppermute | solution.py:29
  83.8 1.6 %collective-permute-start.9 = (f32[512,128]{1,0:T(8,128)S(1)}, f32[512,128]{1,0:T(8,128)S(1)}, u32[]{:S(2)}, u32[]{:S(2)}) collective-permute-start(f32[512,128]{1,0:T(8,128)S(1)} %constant_dynamic-update-slice_fusion.10), channel_id=1, source_target_pairs={{0,1},{1,0},{2,3},{3,2},{4,5},{5,4},{6,7},{7,6},{8,9},{9,8},{10,11... | collective-permute-start | bytes 786440 | tf_op jit(solution)/shard_map/ppermute | solution.py:29

commit v20 on v19

--- a/solution.py
+++ b/solution.py
@@ -156,12 +156,14 @@
         if tap_index == 4:
             return shifted(windows, 0, 0)
         chosen = None
-        for dilation in range(1, DMAX + 1):
+        for dilation in range(DMAX, 0, -1):
             row_shift = (tap_index // 3 - 1) * dilation
             col_shift = (tap_index % 3 - 1) * dilation
             piece = windows[:, DMAX + row_shift, DMAX + col_shift : DMAX + col_shift + TILE, :]
-            term = onehot[dilation - 1].astype(jnp.bfloat16) * piece
-            chosen = term if chosen is None else chosen + term
+            if chosen is None:
+                chosen = jnp.where(rates == dilation, piece, jnp.zeros_like(piece))
+            else:
+                chosen = jnp.where(rates == dilation, piece, chosen)
         return chosen.astype(jnp.float32)
 
     def forward(windows, tiles, weight):

time: 90.4 us -> 92.7 us (1.025)
  other arithmetic: 15.6 us -> 17.9 us
    convert_element_type x1, other arithmetic: 6.21 us -> 8.57 us  [forward(): depth_flat = accum_sum.astype(jnp.bfloat16).reshape(-1, width)]
  transfers between devices with their start and end apart: 11 -> 11, of which waited for: 9 -> 9; matrix products, arithmetic and copies ran while one was open for 6% -> 5% of each run, Pallas kernels for 0% -> 0%
where the time goes in v20:
time: 92.7 us; the launch traced here: 92.3 us
  waiting for transfers between devices  27.8 us (30%)
  starting transfers between devices  21.9 us (24%)
  local copies, waits for them, and re-layouts  18.9 us (20%)
  other arithmetic  17.9 us (19%)
  matrix products  2.92 us (3%)
  between operations  2.83 us (3%)
    ppermute x2, waiting for transfers between devices, packed_sum(): x = x + lax.ppermute(x, axis, [(i, i ^ bit) for i in range(count)])  9.68 us
    convert_element_type x1, other arithmetic, forward(): depth_flat = accum_sum.astype(jnp.bfloat16).reshape(-1, width)  8.57 us
    all_to_all x1, starting transfers between devices, local(): lax.all_to_all(send, ('lon', 'lat'), split_axis=0, concat_axis=0, tiled=T...  7.36 us
    ppermute x2, waiting for transfers between devices, padded_2(): lax.ppermute(tail, axis, [(i, (i + 1) % count) for i in range(ends)])  6.06 us
    gather x1, local copies, waits for them, and re-layouts, gather_windows(): lax.dynamic_slice(padded, (b, h, w, jnp.int32(0)), (1, span, reach, width))  5.73 us
    ppermute x2, waiting for transfers between devices, double(): got = lax.ppermute(x, axis, [(i, i ^ bit) for i in range(count)])  5.43 us
    ppermute x2, waiting for transfers between devices, halve(): return keep + lax.ppermute(send, axis, [(i, i ^ bit) for i in range(count)])  5.19 us
    unnamed x26, local copies, waits for them, and re-layouts  5.08 us
  transfers between devices with their start and end apart: 11, of which 9 were waited for; matrix products, arithmetic and copies ran while one was open for 5% of the time, Pallas kernels for 0%

profile of v20, /device:TPU:0, one launch (start us, length us, event | category | flops | bytes accessed | tf_op | source)
XLA Modules:
  0.0 92.3 jit_solution(11015830477776135499)
XLA Ops:
  3.3 0.9 convert_reduce_fusion
  5.9 7.4 %all-to-all-start = ((bf16[32,8,228]{2,1,0:T(8,128)(2,1)}), bf16[32,8,228]{2,1,0:T(8,128)(2,1)S(1)}, u32[]{:S(2)}, u32[]{:S(2)}) async-start(bf16[32,8,228]{2,1,0:T(8,128)(2,1)} %copy.189), calls=%async_computation | async-start | bytes 262144 | tf_op jit(solution)/shard_map/all_to_all | solution.py:118
  13.3 1.3 %fusion.85 = (bf16[2,48,4,256]{3,2,1,0:T(4,128)(2,1)S(1)}, bf16[2,48,4,256]{3,2,1,0:T(4,128)(2,1)S(1)}) fusion(bf16[2,48,32,256]{3,2,1,0:T(8,128)(2,1)} %param.9), kind=kLoop, calls=%fused_computation.170 | loop fusion | bytes 786432 | tf_op jit(solution)/shard_map/slice | solution.py:74
  14.8 2.0 %collective-permute-start = (bf16[2,48,4,256]{3,0,2,1:T(2,128)(2,1)S(1)}, bf16[2,48,4,256]{3,0,2,1:T(2,128)(2,1)S(1)}, u32[]{:S(2)}, u32[]{:S(2)}) collective-permute-start(bf16[2,48,4,256]{3,0,2,1:T(2,128)(2,1)S(1)} %copy.266), channel_id=1, source_target_pairs={{0,2},{2,4},{4,6},{6,8},{8,10},{10,12},{12,14},{14,0},{1,3},{3,5},... | collective-permute-start | bytes 589832 | tf_op jit(solution)/shard_map/ppermute | solution.py:78
  17.0 2.9 %collective-permute-start.1 = (bf16[2,48,4,256]{3,0,2,1:T(2,128)(2,1)S(1)}, bf16[2,48,4,256]{3,0,2,1:T(2,128)(2,1)S(1)}, u32[]{:S(2)}, u32[]{:S(2)}) collective-permute-start(bf16[2,48,4,256]{3,0,2,1:T(2,128)(2,1)S(1)} %copy.267), channel_id=1, source_target_pairs={{2,0},{4,2},{6,4},{8,6},{10,8},{12,10},{14,12},{0,14},{3,1},{5,3},... | collective-permute-start | bytes 589832 | tf_op jit(solution)/shard_map/ppermute | solution.py:80
  19.9 6.1 %collective-permute-done = bf16[2,48,4,256]{3,0,2,1:T(2,128)(2,1)S(1)} collective-permute-done((bf16[2,48,4,256]{3,0,2,1:T(2,128)(2,1)S(1)}, bf16[2,48,4,256]{3,0,2,1:T(2,128)(2,1)S(1)}, u32[]{:S(2)}, u32[]{:S(2)}) %collective-permute-start) | collective-permute-done | bytes 196640 | tf_op jit(solution)/shard_map/ppermute | solution.py:78
  26.1 1.7 %constant_dynamic-update-slice_fusion.1 = bf16[2,48,40,256]{3,0,2,1:T(2,128)(2,1)S(1)} fusion(bf16[2,48,40,256]{3,0,2,1:T(2,128)(2,1)S(1)} %constant_dynamic-update-slice_fusion.2, bf16[2,48,32,256]{3,2,1,0:T(8,128)(2,1)S(1)} %copy-done.3), kind=kLoop, calls=%fused_computation.108 | loop fusion | bytes 3145728
  28.5 1.3 %copy-done.2 = bf16[2,48,40,256]{3,0,2,1:T(2,128)(2,1)} copy-done((bf16[2,48,40,256]{3,0,2,1:T(2,128)(2,1)}, bf16[2,48,40,256]{3,0,2,1:T(2,128)(2,1)S(1)}, u32[]{:S(2)}) %copy-start.2) | copy-done | bytes 1966104
  30.0 1.3 %collective-permute-start.2 = (bf16[2,4,40,256]{3,0,2,1:T(2,128)(2,1)S(1)}, bf16[2,4,40,256]{3,0,2,1:T(2,128)(2,1)S(1)}, u32[]{:S(2)}, u32[]{:S(2)}) collective-permute-start(bf16[2,4,40,256]{3,0,2,1:T(2,128)(2,1)S(1)} %get-tuple-element.60), channel_id=1, source_target_pairs={{0,1},{2,3},{4,5},{6,7},{8,9},{10,11},{12,13},{14,15},{16,17},{18,... | collective-permute-start | bytes 491528 | tf_op jit(solution)/shard_map/ppermute | solution.py:78
  31.3 1.3 %collective-permute-start.3 = (bf16[2,4,40,256]{3,0,2,1:T(2,128)(2,1)S(1)}, bf16[2,4,40,256]{3,0,2,1:T(2,128)(2,1)S(1)}, u32[]{:S(2)}, u32[]{:S(2)}) collective-permute-start(bf16[2,4,40,256]{3,0,2,1:T(2,128)(2,1)S(1)} %get-tuple-element.61), channel_id=1, source_target_pairs={{1,0},{3,2},{5,4},{7,6},{9,8},{11,10},{13,12},{15,14},{17,16},{19,... | collective-permute-start | bytes 491528 | tf_op jit(solution)/shard_map/ppermute | solution.py:80
  34.6 4.8 %pad_maximum_fusion = bf16[2,56,40,256]{3,0,2,1:T(2,128)(2,1)S(1)} fusion(bf16[2,4,40,256]{3,0,2,1:T(2,128)(2,1)S(1)} %collective-permute-done.3, bf16[2,48,40,256]{3,0,2,1:T(2,128)(2,1)} %copy-done.2, bf16[2,4,40,256]{3,0,2,1:T(2,128)(2,1)S(1)} %collective-permute-done.2), kind=kLoop, calls=%fused_computation.1 | loop fusion | flops 2293760 | bytes 4587520 | tf_op jit(solution)/shard_map/concatenate | solution.py:76
  39.4 5.7 %gather_fusion = bf16[32,9,16,256]{3,0,2,1:T(8,128)(2,1)} fusion(bf16[2,56,40,256]{3,0,2,1:T(2,128)(2,1)S(1)} %pad_maximum_fusion, s32[32]{0:T(128)S(1)} %fusion.72), kind=kCustom, calls=%fused_computation | custom fusion | bytes 4719104 | tf_op jit(solution)/shard_map/vmap()/gather | solution.py:145
  45.1 2.1 %fusion.82 = (bf16[32,1,8,256]{3,0,2,1:T(8,128)(2,1)S(1)}, bf16[32,1,8,256]{3,0,2,1:T(8,128)(2,1)S(1)}, bf16[32,1,8,256]{3,0,2,1:T(8,128)(2,1)S(1)}, bf16[32,1,8...) fusion(bf16[32,9,16,256]{3,0,2,1:T(8,128)(2,1)} %gather_fusion), kind=kLoop, calls=%fused_computation.167 | loop fusion | bytes 4980736 | tf_op jit(solution)/shard_map/slice | solution.py:162
  47.9 8.6 %fusion.13 = (bf16[256,256]{1,0:T(8,128)(2,1)S(1)}, bf16[256,256]{1,0:T(8,128)(2,1)S(1)}, bf16[256,256]{1,0:T(8,128)(2,1)S(1)}, bf16[256,256]{1,0:T(8,128)(2,1)S...) fusion(f32[32,1,8,256]{3,0,2,1:T(8,128)S(1)} %get-tuple-element, ...), kind=kLoop, calls=%fused_computation.41 | loop fusion | flops 3801088 | bytes 5646336 | tf_op jit(solution)/shard_map/convert_element_type | solution.py:175
  60.4 1.3 %collective-permute-done.4 = f32[512,128]{1,0:T(8,128)S(1)} collective-permute-done((f32[512,128]{1,0:T(8,128)S(1)}, f32[512,128]{1,0:T(8,128)S(1)}, u32[]{:S(2)}, u32[]{:S(2)}) %collective-permute-start.4) | collective-permute-done | bytes 262176 | tf_op jit(solution)/shard_map/ppermute | solution.py:22
  61.8 2.1 %collective-permute-start.5 = (f32[256,128]{1,0:T(8,128)S(1)}, f32[256,128]{1,0:T(8,128)S(1)}, u32[]{:S(2)}, u32[]{:S(2)}) collective-permute-start(f32[256,128]{1,0:T(8,128)S(1)} %constant_dynamic-slice_fusion), channel_id=1, source_target_pairs={{0,2},{2,0},{4,6},{6,4},{8,10},{10,8},{12,14},{14,12},{1,3},{3,1},... | collective-permute-start | bytes 393224 | tf_op jit(solution)/shard_map/ppermute | solution.py:22
  63.9 3.9 %collective-permute-done.5 = f32[256,128]{1,0:T(8,128)S(1)} collective-permute-done((f32[256,128]{1,0:T(8,128)S(1)}, f32[256,128]{1,0:T(8,128)S(1)}, u32[]{:S(2)}, u32[]{:S(2)}) %collective-permute-start.5) | collective-permute-done | bytes 131104 | tf_op jit(solution)/shard_map/ppermute | solution.py:22
  67.8 1.5 %collective-permute-start.6 = (f32[256,128]{1,0:T(8,128)S(1)}, f32[256,128]{1,0:T(8,128)S(1)}, u32[]{:S(2)}, u32[]{:S(2)}) collective-permute-start(f32[256,128]{1,0:T(8,128)S(1)} %dynamic-slice_add_fusion.1), channel_id=1, source_target_pairs={{0,4},{2,6},{4,0},{6,2},{8,12},{10,14},{12,8},{14,10},{1,5},{3,7},... | collective-permute-start | bytes 393224 | tf_op jit(solution)/shard_map/ppermute | solution.py:56
  69.3 3.7 %collective-permute-done.6 = f32[256,128]{1,0:T(8,128)S(1)} collective-permute-done((f32[256,128]{1,0:T(8,128)S(1)}, f32[256,128]{1,0:T(8,128)S(1)}, u32[]{:S(2)}, u32[]{:S(2)}) %collective-permute-start.6) | collective-permute-done | bytes 131104 | tf_op jit(solution)/shard_map/ppermute | solution.py:56
  73.0 2.1 %collective-permute-start.7 = (f32[256,128]{1,0:T(8,128)S(1)}, f32[256,128]{1,0:T(8,128)S(1)}, u32[]{:S(2)}, u32[]{:S(2)}) collective-permute-start(f32[256,128]{1,0:T(8,128)S(1)} %add.225), channel_id=1, source_target_pairs={{0,8},{2,10},{4,12},{6,14},{8,0},{10,2},{12,4},{14,6},{1,9},{3,11}... | collective-permute-start | bytes 393224 | tf_op jit(solution)/shard_map/ppermute | solution.py:56
  75.1 6.0 %collective-permute-done.7 = f32[256,128]{1,0:T(8,128)S(1)} collective-permute-done((f32[256,128]{1,0:T(8,128)S(1)}, f32[256,128]{1,0:T(8,128)S(1)}, u32[]{:S(2)}, u32[]{:S(2)}) %collective-permute-start.7) | collective-permute-done | bytes 131104 | tf_op jit(solution)/shard_map/ppermute | solution.py:56
  81.1 1.0 %collective-permute-start.8 = (f32[256,128]{1,0:T(8,128)S(1)}, f32[256,128]{1,0:T(8,128)S(1)}, u32[]{:S(2)}, u32[]{:S(2)}) collective-permute-start(f32[256,128]{1,0:T(8,128)S(1)} %get-tuple-element.14), channel_id=1, source_target_pairs={{0,2},{2,0},{4,6},{6,4},{8,10},{10,8},{12,14},{14,12},{1,3},{3,1},... | collective-permute-start | bytes 393224 | tf_op jit(solution)/shard_map/ppermute | solution.py:29
  82.2 4.0 %collective-permute-done.8 = f32[256,128]{1,0:T(8,128)S(1)} collective-permute-done((f32[256,128]{1,0:T(8,128)S(1)}, f32[256,128]{1,0:T(8,128)S(1)}, u32[]{:S(2)}, u32[]{:S(2)}) %collective-permute-start.8) | collective-permute-done | bytes 131104 | tf_op jit(solution)/shard_map/ppermute | solution.py:29
  86.3 1.4 %collective-permute-done.9 = f32[512,128]{1,0:T(8,128)S(1)} collective-permute-done((f32[512,128]{1,0:T(8,128)S(1)}, f32[512,128]{1,0:T(8,128)S(1)}, u32[]{:S(2)}, u32[]{:S(2)}) %collective-permute-start.9) | collective-permute-done | bytes 262176 | tf_op jit(solution)/shard_map/ppermute | solution.py:29
  (85 shorter events, 15.2 us)
Async XLA Ops:
  0.6 55.8 %copy-start = (bf16[256,256]{1,0:T(8,128)(2,1)S(1)}, bf16[256,256]{1,0:T(8,128)(2,1)}, u32[]{:S(2)}) copy-start(bf16[256,256]{1,0:T(8,128)(2,1)} %param.12) | copy-start | bytes 393220
  0.6 25.4 %copy-start.3 = (bf16[2,48,32,256]{3,2,1,0:T(8,128)(2,1)S(1)}, bf16[2,48,32,256]{3,2,1,0:T(8,128)(2,1)}, u32[]{:S(2)}) copy-start(bf16[2,48,32,256]{3,2,1,0:T(8,128)(2,1)} %param.9) | copy-start | bytes 4718596
  0.7 19.2 %copy-start.5 = (bf16[9,256]{1,0:T(8,128)(2,1)S(1)}, bf16[9,256]{1,0:T(8,128)(2,1)}, u32[]{:S(2)}) copy-start(bf16[9,256]{1,0:T(8,128)(2,1)} %param.11) | copy-start | bytes 13828
  0.7 19.2 %copy-start.6 = (s32[256]{0:T(256)S(1)}, s32[256]{0:T(256)}, u32[]{:S(2)}) copy-start(s32[256]{0:T(256)} %param.10) | copy-start | bytes 3076
  5.9 26.7 %all-to-all-start = ((bf16[32,8,228]{2,1,0:T(8,128)(2,1)}), bf16[32,8,228]{2,1,0:T(8,128)(2,1)S(1)}, u32[]{:S(2)}, u32[]{:S(2)}) async-start(bf16[32,8,228]{2,1,0:T(8,128)(2,1)} %copy.189), calls=%async_computation | async-start | bytes 262144 | tf_op jit(solution)/shard_map/all_to_all | solution.py:118
  14.8 11.2 %collective-permute-start = (bf16[2,48,4,256]{3,0,2,1:T(2,128)(2,1)S(1)}, bf16[2,48,4,256]{3,0,2,1:T(2,128)(2,1)S(1)}, u32[]{:S(2)}, u32[]{:S(2)}) collective-permute-start(bf16[2,48,4,256]{3,0,2,1:T(2,128)(2,1)S(1)} %copy.266), channel_id=1, source_target_pairs={{0,2},{2,4},{4,6},{6,8},{8,10},{10,12},{12,14},{14,0},{1,3},{3,5},... | collective-permute-start | bytes 589832 | tf_op jit(solution)/shard_map/ppermute | solution.py:78
  17.0 11.4 %collective-permute-start.1 = (bf16[2,48,4,256]{3,0,2,1:T(2,128)(2,1)S(1)}, bf16[2,48,4,256]{3,0,2,1:T(2,128)(2,1)S(1)}, u32[]{:S(2)}, u32[]{:S(2)}) collective-permute-start(bf16[2,48,4,256]{3,0,2,1:T(2,128)(2,1)S(1)} %copy.267), channel_id=1, source_target_pairs={{2,0},{4,2},{6,4},{8,6},{10,8},{12,10},{14,12},{0,14},{3,1},{5,3},... | collective-permute-start | bytes 589832 | tf_op jit(solution)/shard_map/ppermute | solution.py:80
  28.5 1.3 %copy-start.2 = (bf16[2,48,40,256]{3,0,2,1:T(2,128)(2,1)}, bf16[2,48,40,256]{3,0,2,1:T(2,128)(2,1)S(1)}, u32[]{:S(2)}) copy-start(bf16[2,48,40,256]{3,0,2,1:T(2,128)(2,1)S(1)} %constant_dynamic-update-slice_fusion) | copy-start | bytes 5898244
  30.0 3.7 %collective-permute-start.2 = (bf16[2,4,40,256]{3,0,2,1:T(2,128)(2,1)S(1)}, bf16[2,4,40,256]{3,0,2,1:T(2,128)(2,1)S(1)}, u32[]{:S(2)}, u32[]{:S(2)}) collective-permute-start(bf16[2,4,40,256]{3,0,2,1:T(2,128)(2,1)S(1)} %get-tuple-element.60), channel_id=1, source_target_pairs={{0,1},{2,3},{4,5},{6,7},{8,9},{10,11},{12,13},{14,15},{16,17},{18,... | collective-permute-start | bytes 491528 | tf_op jit(solution)/shard_map/ppermute | solution.py:78
  31.3 3.3 %collective-permute-start.3 = (bf16[2,4,40,256]{3,0,2,1:T(2,128)(2,1)S(1)}, bf16[2,4,40,256]{3,0,2,1:T(2,128)(2,1)S(1)}, u32[]{:S(2)}, u32[]{:S(2)}) collective-permute-start(bf16[2,4,40,256]{3,0,2,1:T(2,128)(2,1)S(1)} %get-tuple-element.61), channel_id=1, source_target_pairs={{1,0},{3,2},{5,4},{7,6},{9,8},{11,10},{13,12},{15,14},{17,16},{19,... | collective-permute-start | bytes 491528 | tf_op jit(solution)/shard_map/ppermute | solution.py:80
  45.1 2.5 %copy-start.1 = (bf16[32,9,16,256]{3,0,2,1:T(8,128)(2,1)S(1)}, bf16[32,9,16,256]{3,0,2,1:T(8,128)(2,1)}, u32[]{:S(2)}) copy-start(bf16[32,9,16,256]{3,0,2,1:T(8,128)(2,1)} %gather_fusion) | copy-start | bytes 7077892
  47.9 8.9 %copy-start.4 = (bf16[256,227]{0,1:T(8,128)(2,1)S(1)}, bf16[256,227]{0,1:T(8,128)(2,1)}, u32[]{:S(2)}) copy-start(bf16[256,227]{0,1:T(8,128)(2,1)} %param.13) | copy-start | bytes 348676
  60.1 1.6 %collective-permute-start.4 = (f32[512,128]{1,0:T(8,128)S(1)}, f32[512,128]{1,0:T(8,128)S(1)}, u32[]{:S(2)}, u32[]{:S(2)}) collective-permute-start(f32[512,128]{1,0:T(8,128)S(1)} %constant_dynamic-slice_fusion.1), channel_id=1, source_target_pairs={{0,1},{1,0},{2,3},{3,2},{4,5},{5,4},{6,7},{7,6},{8,9},{9,8},{10,11... | collective-permute-start | bytes 786440 | tf_op jit(solution)/shard_map/ppermute | solution.py:22
  61.8 6.0 %collective-permute-start.5 = (f32[256,128]{1,0:T(8,128)S(1)}, f32[256,128]{1,0:T(8,128)S(1)}, u32[]{:S(2)}, u32[]{:S(2)}) collective-permute-start(f32[256,128]{1,0:T(8,128)S(1)} %constant_dynamic-slice_fusion), channel_id=1, source_target_pairs={{0,2},{2,0},{4,6},{6,4},{8,10},{10,8},{12,14},{14,12},{1,3},{3,1},... | collective-permute-start | bytes 393224 | tf_op jit(solution)/shard_map/ppermute | solution.py:22
  67.8 5.2 %collective-permute-start.6 = (f32[256,128]{1,0:T(8,128)S(1)}, f32[256,128]{1,0:T(8,128)S(1)}, u32[]{:S(2)}, u32[]{:S(2)}) collective-permute-start(f32[256,128]{1,0:T(8,128)S(1)} %dynamic-slice_add_fusion.1), channel_id=1, source_target_pairs={{0,4},{2,6},{4,0},{6,2},{8,12},{10,14},{12,8},{14,10},{1,5},{3,7},... | collective-permute-start | bytes 393224 | tf_op jit(solution)/shard_map/ppermute | solution.py:56
  73.0 8.0 %collective-permute-start.7 = (f32[256,128]{1,0:T(8,128)S(1)}, f32[256,128]{1,0:T(8,128)S(1)}, u32[]{:S(2)}, u32[]{:S(2)}) collective-permute-start(f32[256,128]{1,0:T(8,128)S(1)} %add.225), channel_id=1, source_target_pairs={{0,8},{2,10},{4,12},{6,14},{8,0},{10,2},{12,4},{14,6},{1,9},{3,11}... | collective-permute-start | bytes 393224 | tf_op jit(solution)/shard_map/ppermute | solution.py:56
  81.1 5.0 %collective-permute-start.8 = (f32[256,128]{1,0:T(8,128)S(1)}, f32[256,128]{1,0:T(8,128)S(1)}, u32[]{:S(2)}, u32[]{:S(2)}) collective-permute-start(f32[256,128]{1,0:T(8,128)S(1)} %get-tuple-element.14), channel_id=1, source_target_pairs={{0,2},{2,0},{4,6},{6,4},{8,10},{10,8},{12,14},{14,12},{1,3},{3,1},... | collective-permute-start | bytes 393224 | tf_op jit(solution)/shard_map/ppermute | solution.py:29
  86.2 1.6 %collective-permute-start.9 = (f32[512,128]{1,0:T(8,128)S(1)}, f32[512,128]{1,0:T(8,128)S(1)}, u32[]{:S(2)}, u32[]{:S(2)}) collective-permute-start(f32[512,128]{1,0:T(8,128)S(1)} %constant_dynamic-update-slice_fusion.10), channel_id=1, source_target_pairs={{0,1},{1,0},{2,3},{3,2},{4,5},{5,4},{6,7},{7,6},{8,9},{9,8},{10,11... | collective-permute-start | bytes 786440 | tf_op jit(solution)/shard_map/ppermute | solution.py:29

commit v21 on v19

--- a/solution.py
+++ b/solution.py
@@ -220,7 +220,7 @@
         grad_y = jnp.dot(
             same_cell.astype(jnp.float32),
             grad_rows,
-            precision=lax.Precision.HIGHEST,
+            precision=lax.Precision.HIGH,
             preferred_element_type=jnp.float32,
         )
         repeated = jnp.any(same_cell & (row_ids[None, :] < row_ids[:, None]), axis=1)

time: 90.4 us -> 90.3 us (level)
  no operation moved by 1% of the time
where the time goes in v21:
time: 90.3 us; the launch traced here: 89.9 us
  waiting for transfers between devices  27.7 us (31%)
  starting transfers between devices  21.9 us (24%)
  local copies, waits for them, and re-layouts  19 us (21%)
  other arithmetic  15.6 us (17%)
  matrix products  2.87 us (3%)
  between operations  2.83 us (3%)
    ppermute x2, waiting for transfers between devices, packed_sum(): x = x + lax.ppermute(x, axis, [(i, i ^ bit) for i in range(count)])  9.68 us
    all_to_all x1, starting transfers between devices, local(): lax.all_to_all(send, ('lon', 'lat'), split_axis=0, concat_axis=0, tiled=T...  7.36 us
    convert_element_type x1, other arithmetic, forward(): depth_flat = accum_sum.astype(jnp.bfloat16).reshape(-1, width)  6.21 us
    ppermute x2, waiting for transfers between devices, padded_2(): lax.ppermute(tail, axis, [(i, (i + 1) % count) for i in range(ends)])  5.97 us
    gather x1, local copies, waits for them, and re-layouts, gather_windows(): lax.dynamic_slice(padded, (b, h, w, jnp.int32(0)), (1, span, reach, width))  5.74 us
    ppermute x2, waiting for transfers between devices, double(): got = lax.ppermute(x, axis, [(i, i ^ bit) for i in range(count)])  5.45 us
    ppermute x2, waiting for transfers between devices, halve(): return keep + lax.ppermute(send, axis, [(i, i ^ bit) for i in range(count)])  5.19 us
    unnamed x26, local copies, waits for them, and re-layouts  5.08 us
  transfers between devices with their start and end apart: 11, of which 9 were waited for; matrix products, arithmetic and copies ran while one was open for 6% of the time, Pallas kernels for 0%

profile of v21, /device:TPU:0, one launch (start us, length us, event | category | flops | bytes accessed | tf_op | source)
XLA Modules:
  0.0 89.9 jit_solution(17516858668933138048)
XLA Ops:
  3.3 0.9 %convert_reduce_fusion = s32[16]{0:T(128)S(1)} fusion(s32[16]{0:T(128)} %bitcast.289), kind=kLoop, calls=%fused_computation.142 | loop fusion | flops 1264 | bytes 128 | tf_op jit(solution)/shard_map/reduce_sum | solution.py:103
  5.9 7.4 %all-to-all-start = ((bf16[32,8,228]{2,1,0:T(8,128)(2,1)}), bf16[32,8,228]{2,1,0:T(8,128)(2,1)S(1)}, u32[]{:S(2)}, u32[]{:S(2)}) async-start(bf16[32,8,228]{2,1,0:T(8,128)(2,1)} %copy.189), calls=%async_computation | async-start | bytes 262144 | tf_op jit(solution)/shard_map/all_to_all | solution.py:118
  13.3 1.3 %fusion.85 = (bf16[2,48,4,256]{3,2,1,0:T(4,128)(2,1)S(1)}, bf16[2,48,4,256]{3,2,1,0:T(4,128)(2,1)S(1)}) fusion(bf16[2,48,32,256]{3,2,1,0:T(8,128)(2,1)} %param.9), kind=kLoop, calls=%fused_computation.196 | loop fusion | bytes 786432 | tf_op jit(solution)/shard_map/slice | solution.py:74
  14.8 2.0 %collective-permute-start = (bf16[2,48,4,256]{3,0,2,1:T(2,128)(2,1)S(1)}, bf16[2,48,4,256]{3,0,2,1:T(2,128)(2,1)S(1)}, u32[]{:S(2)}, u32[]{:S(2)}) collective-permute-start(bf16[2,48,4,256]{3,0,2,1:T(2,128)(2,1)S(1)} %copy.266), channel_id=1, source_target_pairs={{0,2},{2,4},{4,6},{6,8},{8,10},{10,12},{12,14},{14,0},{1,3},{3,5},... | collective-permute-start | bytes 589832 | tf_op jit(solution)/shard_map/ppermute | solution.py:78
  17.0 2.9 %collective-permute-start.1 = (bf16[2,48,4,256]{3,0,2,1:T(2,128)(2,1)S(1)}, bf16[2,48,4,256]{3,0,2,1:T(2,128)(2,1)S(1)}, u32[]{:S(2)}, u32[]{:S(2)}) collective-permute-start(bf16[2,48,4,256]{3,0,2,1:T(2,128)(2,1)S(1)} %copy.267), channel_id=1, source_target_pairs={{2,0},{4,2},{6,4},{8,6},{10,8},{12,10},{14,12},{0,14},{3,1},{5,3},... | collective-permute-start | bytes 589832 | tf_op jit(solution)/shard_map/ppermute | solution.py:80
  20.0 6.0 %collective-permute-done = bf16[2,48,4,256]{3,0,2,1:T(2,128)(2,1)S(1)} collective-permute-done((bf16[2,48,4,256]{3,0,2,1:T(2,128)(2,1)S(1)}, bf16[2,48,4,256]{3,0,2,1:T(2,128)(2,1)S(1)}, u32[]{:S(2)}, u32[]{:S(2)}) %collective-permute-start) | collective-permute-done | bytes 196640 | tf_op jit(solution)/shard_map/ppermute | solution.py:78
  26.1 1.7 %constant_dynamic-update-slice_fusion.1 = bf16[2,48,40,256]{3,0,2,1:T(2,128)(2,1)S(1)} fusion(bf16[2,48,40,256]{3,0,2,1:T(2,128)(2,1)S(1)} %constant_dynamic-update-slice_fusion.2, bf16[2,48,32,256]{3,2,1,0:T(8,128)(2,1)S(1)} %copy-done.3), kind=kLoop, calls=%fused_computation.132 | loop fusion | bytes 3145728
  28.5 1.3 %copy-done.2 = bf16[2,48,40,256]{3,0,2,1:T(2,128)(2,1)} copy-done((bf16[2,48,40,256]{3,0,2,1:T(2,128)(2,1)}, bf16[2,48,40,256]{3,0,2,1:T(2,128)(2,1)S(1)}, u32[]{:S(2)}) %copy-start.2) | copy-done | bytes 1966104
  30.0 1.3 %collective-permute-start.2 = (bf16[2,4,40,256]{3,0,2,1:T(2,128)(2,1)S(1)}, bf16[2,4,40,256]{3,0,2,1:T(2,128)(2,1)S(1)}, u32[]{:S(2)}, u32[]{:S(2)}) collective-permute-start(bf16[2,4,40,256]{3,0,2,1:T(2,128)(2,1)S(1)} %get-tuple-element.64), channel_id=1, source_target_pairs={{0,1},{2,3},{4,5},{6,7},{8,9},{10,11},{12,13},{14,15},{16,17},{18,... | collective-permute-start | bytes 491528 | tf_op jit(solution)/shard_map/ppermute | solution.py:78
  31.3 1.3 %collective-permute-start.3 = (bf16[2,4,40,256]{3,0,2,1:T(2,128)(2,1)S(1)}, bf16[2,4,40,256]{3,0,2,1:T(2,128)(2,1)S(1)}, u32[]{:S(2)}, u32[]{:S(2)}) collective-permute-start(bf16[2,4,40,256]{3,0,2,1:T(2,128)(2,1)S(1)} %get-tuple-element.65), channel_id=1, source_target_pairs={{1,0},{3,2},{5,4},{7,6},{9,8},{11,10},{13,12},{15,14},{17,16},{19,... | collective-permute-start | bytes 491528 | tf_op jit(solution)/shard_map/ppermute | solution.py:80
  34.6 4.8 %pad_maximum_fusion = bf16[2,56,40,256]{3,0,2,1:T(2,128)(2,1)S(1)} fusion(bf16[2,4,40,256]{3,0,2,1:T(2,128)(2,1)S(1)} %collective-permute-done.3, bf16[2,48,40,256]{3,0,2,1:T(2,128)(2,1)} %copy-done.2, bf16[2,4,40,256]{3,0,2,1:T(2,128)(2,1)S(1)} %collective-permute-done.2), kind=kLoop, calls=%fused_computation.1 | loop fusion | flops 2293760 | bytes 4587520 | tf_op jit(solution)/shard_map/concatenate | solution.py:76
  39.4 5.7 %gather_fusion = bf16[32,9,16,256]{3,0,2,1:T(8,128)(2,1)} fusion(bf16[2,56,40,256]{3,0,2,1:T(2,128)(2,1)S(1)} %pad_maximum_fusion, s32[32]{0:T(128)S(1)} %fusion.72), kind=kCustom, calls=%fused_computation | custom fusion | bytes 4719104 | tf_op jit(solution)/shard_map/vmap()/gather | solution.py:145
  45.1 2.1 %fusion.82 = (bf16[32,1,8,256]{3,0,2,1:T(8,128)(2,1)S(1)}, bf16[32,1,8,256]{3,0,2,1:T(8,128)(2,1)S(1)}, bf16[32,1,8,256]{3,0,2,1:T(8,128)(2,1)S(1)}, bf16[32,1,8...) fusion(bf16[32,9,16,256]{3,0,2,1:T(8,128)(2,1)} %gather_fusion), kind=kLoop, calls=%fused_computation.193 | loop fusion | bytes 4980736 | tf_op jit(solution)/shard_map/slice | solution.py:162
  47.9 6.2 %fusion.13 = (bf16[256,256]{1,0:T(8,128)(2,1)S(1)}, bf16[256,256]{1,0:T(8,128)(2,1)S(1)}, bf16[256,256]{1,0:T(8,128)(2,1)S(1)}, bf16[256,256]{1,0:T(8,128)(2,1)S...) fusion(f32[32,1,8,256]{3,0,2,1:T(8,128)S(1)} %get-tuple-element, ...), kind=kLoop, calls=%fused_computation.41 | loop fusion | flops 5373952 | bytes 5647360 | tf_op jit(solution)/shard_map/convert_element_type | solution.py:173
  58.0 1.3 %collective-permute-done.4 = f32[512,128]{1,0:T(8,128)S(1)} collective-permute-done((f32[512,128]{1,0:T(8,128)S(1)}, f32[512,128]{1,0:T(8,128)S(1)}, u32[]{:S(2)}, u32[]{:S(2)}) %collective-permute-start.4) | collective-permute-done | bytes 262176 | tf_op jit(solution)/shard_map/ppermute | solution.py:22
  59.4 2.1 %collective-permute-start.5 = (f32[256,128]{1,0:T(8,128)S(1)}, f32[256,128]{1,0:T(8,128)S(1)}, u32[]{:S(2)}, u32[]{:S(2)}) collective-permute-start(f32[256,128]{1,0:T(8,128)S(1)} %constant_dynamic-slice_fusion), channel_id=1, source_target_pairs={{0,2},{2,0},{4,6},{6,4},{8,10},{10,8},{12,14},{14,12},{1,3},{3,1},... | collective-permute-start | bytes 393224 | tf_op jit(solution)/shard_map/ppermute | solution.py:22
  61.5 3.9 %collective-permute-done.5 = f32[256,128]{1,0:T(8,128)S(1)} collective-permute-done((f32[256,128]{1,0:T(8,128)S(1)}, f32[256,128]{1,0:T(8,128)S(1)}, u32[]{:S(2)}, u32[]{:S(2)}) %collective-permute-start.5) | collective-permute-done | bytes 131104 | tf_op jit(solution)/shard_map/ppermute | solution.py:22
  65.4 1.5 %collective-permute-start.6 = (f32[256,128]{1,0:T(8,128)S(1)}, f32[256,128]{1,0:T(8,128)S(1)}, u32[]{:S(2)}, u32[]{:S(2)}) collective-permute-start(f32[256,128]{1,0:T(8,128)S(1)} %dynamic-slice_add_fusion.1), channel_id=1, source_target_pairs={{0,4},{2,6},{4,0},{6,2},{8,12},{10,14},{12,8},{14,10},{1,5},{3,7},... | collective-permute-start | bytes 393224 | tf_op jit(solution)/shard_map/ppermute | solution.py:56
  66.9 3.7 %collective-permute-done.6 = f32[256,128]{1,0:T(8,128)S(1)} collective-permute-done((f32[256,128]{1,0:T(8,128)S(1)}, f32[256,128]{1,0:T(8,128)S(1)}, u32[]{:S(2)}, u32[]{:S(2)}) %collective-permute-start.6) | collective-permute-done | bytes 131104 | tf_op jit(solution)/shard_map/ppermute | solution.py:56
  70.6 2.1 %collective-permute-start.7 = (f32[256,128]{1,0:T(8,128)S(1)}, f32[256,128]{1,0:T(8,128)S(1)}, u32[]{:S(2)}, u32[]{:S(2)}) collective-permute-start(f32[256,128]{1,0:T(8,128)S(1)} %add.401), channel_id=1, source_target_pairs={{0,8},{2,10},{4,12},{6,14},{8,0},{10,2},{12,4},{14,6},{1,9},{3,11}... | collective-permute-start | bytes 393224 | tf_op jit(solution)/shard_map/ppermute | solution.py:56
  72.7 6.0 %collective-permute-done.7 = f32[256,128]{1,0:T(8,128)S(1)} collective-permute-done((f32[256,128]{1,0:T(8,128)S(1)}, f32[256,128]{1,0:T(8,128)S(1)}, u32[]{:S(2)}, u32[]{:S(2)}) %collective-permute-start.7) | collective-permute-done | bytes 131104 | tf_op jit(solution)/shard_map/ppermute | solution.py:56
  78.7 1.0 %collective-permute-start.8 = (f32[256,128]{1,0:T(8,128)S(1)}, f32[256,128]{1,0:T(8,128)S(1)}, u32[]{:S(2)}, u32[]{:S(2)}) collective-permute-start(f32[256,128]{1,0:T(8,128)S(1)} %get-tuple-element.18), channel_id=1, source_target_pairs={{0,2},{2,0},{4,6},{6,4},{8,10},{10,8},{12,14},{14,12},{1,3},{3,1},... | collective-permute-start | bytes 393224 | tf_op jit(solution)/shard_map/ppermute | solution.py:29
  79.7 4.0 %collective-permute-done.8 = f32[256,128]{1,0:T(8,128)S(1)} collective-permute-done((f32[256,128]{1,0:T(8,128)S(1)}, f32[256,128]{1,0:T(8,128)S(1)}, u32[]{:S(2)}, u32[]{:S(2)}) %collective-permute-start.8) | collective-permute-done | bytes 131104 | tf_op jit(solution)/shard_map/ppermute | solution.py:29
  83.9 1.4 %collective-permute-done.9 = f32[512,128]{1,0:T(8,128)S(1)} collective-permute-done((f32[512,128]{1,0:T(8,128)S(1)}, f32[512,128]{1,0:T(8,128)S(1)}, u32[]{:S(2)}, u32[]{:S(2)}) %collective-permute-start.9) | collective-permute-done | bytes 262176 | tf_op jit(solution)/shard_map/ppermute | solution.py:29
  (87 shorter events, 15.3 us)
Async XLA Ops:
  0.6 53.5 %copy-start = (bf16[256,256]{1,0:T(8,128)(2,1)S(1)}, bf16[256,256]{1,0:T(8,128)(2,1)}, u32[]{:S(2)}) copy-start(bf16[256,256]{1,0:T(8,128)(2,1)} %param.12) | copy-start | bytes 393220
  0.6 25.4 %copy-start.3 = (bf16[2,48,32,256]{3,2,1,0:T(8,128)(2,1)S(1)}, bf16[2,48,32,256]{3,2,1,0:T(8,128)(2,1)}, u32[]{:S(2)}) copy-start(bf16[2,48,32,256]{3,2,1,0:T(8,128)(2,1)} %param.9) | copy-start | bytes 4718596
  0.7 19.2 %copy-start.6 = (s32[256]{0:T(256)S(1)}, s32[256]{0:T(256)}, u32[]{:S(2)}) copy-start(s32[256]{0:T(256)} %param.10) | copy-start | bytes 3076
  0.7 19.3 %copy-start.5 = (bf16[9,256]{1,0:T(8,128)(2,1)S(1)}, bf16[9,256]{1,0:T(8,128)(2,1)}, u32[]{:S(2)}) copy-start(bf16[9,256]{1,0:T(8,128)(2,1)} %param.11) | copy-start | bytes 13828
  5.9 26.7 %all-to-all-start = ((bf16[32,8,228]{2,1,0:T(8,128)(2,1)}), bf16[32,8,228]{2,1,0:T(8,128)(2,1)S(1)}, u32[]{:S(2)}, u32[]{:S(2)}) async-start(bf16[32,8,228]{2,1,0:T(8,128)(2,1)} %copy.189), calls=%async_computation | async-start | bytes 262144 | tf_op jit(solution)/shard_map/all_to_all | solution.py:118
  14.8 11.2 %collective-permute-start = (bf16[2,48,4,256]{3,0,2,1:T(2,128)(2,1)S(1)}, bf16[2,48,4,256]{3,0,2,1:T(2,128)(2,1)S(1)}, u32[]{:S(2)}, u32[]{:S(2)}) collective-permute-start(bf16[2,48,4,256]{3,0,2,1:T(2,128)(2,1)S(1)} %copy.266), channel_id=1, source_target_pairs={{0,2},{2,4},{4,6},{6,8},{8,10},{10,12},{12,14},{14,0},{1,3},{3,5},... | collective-permute-start | bytes 589832 | tf_op jit(solution)/shard_map/ppermute | solution.py:78
  17.0 11.4 %collective-permute-start.1 = (bf16[2,48,4,256]{3,0,2,1:T(2,128)(2,1)S(1)}, bf16[2,48,4,256]{3,0,2,1:T(2,128)(2,1)S(1)}, u32[]{:S(2)}, u32[]{:S(2)}) collective-permute-start(bf16[2,48,4,256]{3,0,2,1:T(2,128)(2,1)S(1)} %copy.267), channel_id=1, source_target_pairs={{2,0},{4,2},{6,4},{8,6},{10,8},{12,10},{14,12},{0,14},{3,1},{5,3},... | collective-permute-start | bytes 589832 | tf_op jit(solution)/shard_map/ppermute | solution.py:80
  28.5 1.3 %copy-start.2 = (bf16[2,48,40,256]{3,0,2,1:T(2,128)(2,1)}, bf16[2,48,40,256]{3,0,2,1:T(2,128)(2,1)S(1)}, u32[]{:S(2)}) copy-start(bf16[2,48,40,256]{3,0,2,1:T(2,128)(2,1)S(1)} %constant_dynamic-update-slice_fusion) | copy-start | bytes 5898244
  30.0 3.7 %collective-permute-start.2 = (bf16[2,4,40,256]{3,0,2,1:T(2,128)(2,1)S(1)}, bf16[2,4,40,256]{3,0,2,1:T(2,128)(2,1)S(1)}, u32[]{:S(2)}, u32[]{:S(2)}) collective-permute-start(bf16[2,4,40,256]{3,0,2,1:T(2,128)(2,1)S(1)} %get-tuple-element.64), channel_id=1, source_target_pairs={{0,1},{2,3},{4,5},{6,7},{8,9},{10,11},{12,13},{14,15},{16,17},{18,... | collective-permute-start | bytes 491528 | tf_op jit(solution)/shard_map/ppermute | solution.py:78
  31.3 3.3 %collective-permute-start.3 = (bf16[2,4,40,256]{3,0,2,1:T(2,128)(2,1)S(1)}, bf16[2,4,40,256]{3,0,2,1:T(2,128)(2,1)S(1)}, u32[]{:S(2)}, u32[]{:S(2)}) collective-permute-start(bf16[2,4,40,256]{3,0,2,1:T(2,128)(2,1)S(1)} %get-tuple-element.65), channel_id=1, source_target_pairs={{1,0},{3,2},{5,4},{7,6},{9,8},{11,10},{13,12},{15,14},{17,16},{19,... | collective-permute-start | bytes 491528 | tf_op jit(solution)/shard_map/ppermute | solution.py:80
  45.1 2.5 %copy-start.1 = (bf16[32,9,16,256]{3,0,2,1:T(8,128)(2,1)S(1)}, bf16[32,9,16,256]{3,0,2,1:T(8,128)(2,1)}, u32[]{:S(2)}) copy-start(bf16[32,9,16,256]{3,0,2,1:T(8,128)(2,1)} %gather_fusion) | copy-start | bytes 7077892
  47.9 6.5 %copy-start.4 = (bf16[256,227]{0,1:T(8,128)(2,1)S(1)}, bf16[256,227]{0,1:T(8,128)(2,1)}, u32[]{:S(2)}) copy-start(bf16[256,227]{0,1:T(8,128)(2,1)} %param.13) | copy-start | bytes 348676
  57.7 1.6 %collective-permute-start.4 = (f32[512,128]{1,0:T(8,128)S(1)}, f32[512,128]{1,0:T(8,128)S(1)}, u32[]{:S(2)}, u32[]{:S(2)}) collective-permute-start(f32[512,128]{1,0:T(8,128)S(1)} %constant_dynamic-slice_fusion.1), channel_id=1, source_target_pairs={{0,1},{1,0},{2,3},{3,2},{4,5},{5,4},{6,7},{7,6},{8,9},{9,8},{10,11... | collective-permute-start | bytes 786440 | tf_op jit(solution)/shard_map/ppermute | solution.py:22
  59.4 6.0 %collective-permute-start.5 = (f32[256,128]{1,0:T(8,128)S(1)}, f32[256,128]{1,0:T(8,128)S(1)}, u32[]{:S(2)}, u32[]{:S(2)}) collective-permute-start(f32[256,128]{1,0:T(8,128)S(1)} %constant_dynamic-slice_fusion), channel_id=1, source_target_pairs={{0,2},{2,0},{4,6},{6,4},{8,10},{10,8},{12,14},{14,12},{1,3},{3,1},... | collective-permute-start | bytes 393224 | tf_op jit(solution)/shard_map/ppermute | solution.py:22
  65.4 5.2 %collective-permute-start.6 = (f32[256,128]{1,0:T(8,128)S(1)}, f32[256,128]{1,0:T(8,128)S(1)}, u32[]{:S(2)}, u32[]{:S(2)}) collective-permute-start(f32[256,128]{1,0:T(8,128)S(1)} %dynamic-slice_add_fusion.1), channel_id=1, source_target_pairs={{0,4},{2,6},{4,0},{6,2},{8,12},{10,14},{12,8},{14,10},{1,5},{3,7},... | collective-permute-start | bytes 393224 | tf_op jit(solution)/shard_map/ppermute | solution.py:56
  70.6 8.0 %collective-permute-start.7 = (f32[256,128]{1,0:T(8,128)S(1)}, f32[256,128]{1,0:T(8,128)S(1)}, u32[]{:S(2)}, u32[]{:S(2)}) collective-permute-start(f32[256,128]{1,0:T(8,128)S(1)} %add.401), channel_id=1, source_target_pairs={{0,8},{2,10},{4,12},{6,14},{8,0},{10,2},{12,4},{14,6},{1,9},{3,11}... | collective-permute-start | bytes 393224 | tf_op jit(solution)/shard_map/ppermute | solution.py:56
  78.7 5.0 %collective-permute-start.8 = (f32[256,128]{1,0:T(8,128)S(1)}, f32[256,128]{1,0:T(8,128)S(1)}, u32[]{:S(2)}, u32[]{:S(2)}) collective-permute-start(f32[256,128]{1,0:T(8,128)S(1)} %get-tuple-element.18), channel_id=1, source_target_pairs={{0,2},{2,0},{4,6},{6,4},{8,10},{10,8},{12,14},{14,12},{1,3},{3,1},... | collective-permute-start | bytes 393224 | tf_op jit(solution)/shard_map/ppermute | solution.py:29
  83.8 1.6 %collective-permute-start.9 = (f32[512,128]{1,0:T(8,128)S(1)}, f32[512,128]{1,0:T(8,128)S(1)}, u32[]{:S(2)}, u32[]{:S(2)}) collective-permute-start(f32[512,128]{1,0:T(8,128)S(1)} %constant_dynamic-update-slice_fusion.10), channel_id=1, source_target_pairs={{0,1},{1,0},{2,3},{3,2},{4,5},{5,4},{6,7},{7,6},{8,9},{9,8},{10,11... | collective-permute-start | bytes 786440 | tf_op jit(solution)/shard_map/ppermute | solution.py:29

commit v22 on v19

--- a/solution.py
+++ b/solution.py
@@ -190,11 +190,9 @@
         )
         grad_z = jnp.dot(grad_u, pw_weight.T, preferred_element_type=jnp.float32)
         grad_z = grad_z.reshape(windows.shape[0], TILE, width)
-        tap_sums = []
-        for tap_index in range(9):
-            chosen = chosen_tap(windows, tap_index)
-            tap_sums.append(jnp.sum((chosen * grad_z).reshape(-1, width), axis=0))
-        return pw_part, jnp.stack(tap_sums, axis=0)
+        stacked = jnp.stack([chosen_tap(windows, tap_index) for tap_index in range(9)])
+        tap_sums = jnp.sum((stacked * grad_z[None]).reshape(9, -1, width), axis=1)
+        return pw_part, tap_sums
 
     slots = recv_start.shape[0]
     chunk = min(slots, CHUNK)

time: 90.4 us -> 104 us (1.15)
  other arithmetic: 15.6 us -> 22.8 us
  local copies, waits for them, and re-layouts: 19 us -> 22.9 us
  matrix products: 2.92 us -> 4.73 us
    unnamed x0 -> x7, other arithmetic: none -> 4.25 us
    unnamed x26 -> x63, local copies, waits for them, and re-layouts: 5.08 us -> 7.64 us
    reshape x2, local copies, waits for them, and re-layouts: 0.02 us -> 1.65 us  [packed_sum(): flat = jnp.concatenate([jnp.ravel(v).astype(jnp.float32) for v in values])]
    convert_element_type x1, other arithmetic: 6.21 us -> 7.84 us  [forward(): depth_flat = accum_sum.astype(jnp.bfloat16).reshape(-1, width)]
  transfers between devices with their start and end apart: 11 -> 11, of which waited for: 9 -> 9; matrix products, arithmetic and copies ran while one was open for 6% -> 5% of each run, Pallas kernels for 0% -> 0%
where the time goes in v22:
time: 104 us; the launch traced here: 103 us
  waiting for transfers between devices  27.8 us (27%)
  local copies, waits for them, and re-layouts  22.9 us (22%)
  other arithmetic  22.8 us (22%)
  starting transfers between devices  21.8 us (21%)
  matrix products  4.73 us (5%)
  between operations  3.04 us (3%)
    ppermute x2, waiting for transfers between devices, packed_sum(): x = x + lax.ppermute(x, axis, [(i, i ^ bit) for i in range(count)])  9.71 us
    convert_element_type x1, other arithmetic, forward(): depth_flat = accum_sum.astype(jnp.bfloat16).reshape(-1, width)  7.84 us
    unnamed x63, local copies, waits for them, and re-layouts  7.64 us
    all_to_all x1, starting transfers between devices, local(): lax.all_to_all(send, ('lon', 'lat'), split_axis=0, concat_axis=0, tiled=T...  7.36 us
    ppermute x2, waiting for transfers between devices, padded_2(): lax.ppermute(tail, axis, [(i, (i + 1) % count) for i in range(ends)])  5.98 us
    gather x1, local copies, waits for them, and re-layouts, gather_windows(): lax.dynamic_slice(padded, (b, h, w, jnp.int32(0)), (1, span, reach, width))  5.75 us
    ppermute x2, waiting for transfers between devices, double(): got = lax.ppermute(x, axis, [(i, i ^ bit) for i in range(count)])  5.44 us
    ppermute x2, waiting for transfers between devices, halve(): return keep + lax.ppermute(send, axis, [(i, i ^ bit) for i in range(count)])  5.2 us
  transfers between devices with their start and end apart: 11, of which 9 were waited for; matrix products, arithmetic and copies ran while one was open for 5% of the time, Pallas kernels for 0%

profile of v22, /device:TPU:0, one launch (start us, length us, event | category | flops | bytes accessed | tf_op | source)
XLA Modules:
  0.0 103.1 jit_solution(14281341752387657562)
XLA Ops:
  5.9 7.4 %all-to-all-start = ((bf16[32,8,228]{2,1,0:T(8,128)(2,1)}), bf16[32,8,228]{2,1,0:T(8,128)(2,1)S(1)}, u32[]{:S(2)}, u32[]{:S(2)}) async-start(bf16[32,8,228]{2,1,0:T(8,128)(2,1)} %copy.288), calls=%async_computation | async-start | bytes 262144 | tf_op jit(solution)/shard_map/all_to_all | solution.py:118
  14.8 2.0 %collective-permute-start = (bf16[2,48,4,256]{3,0,2,1:T(2,128)(2,1)S(1)}, bf16[2,48,4,256]{3,0,2,1:T(2,128)(2,1)S(1)}, u32[]{:S(2)}, u32[]{:S(2)}) collective-permute-start(bf16[2,48,4,256]{3,0,2,1:T(2,128)(2,1)S(1)} %copy.430), channel_id=1, source_target_pairs={{0,2},{2,4},{4,6},{6,8},{8,10},{10,12},{12,14},{14,0},{1,3},{3,5},... | collective-permute-start | bytes 589832 | tf_op jit(solution)/shard_map/ppermute | solution.py:78
  17.0 2.9 %collective-permute-start.1 = (bf16[2,48,4,256]{3,0,2,1:T(2,128)(2,1)S(1)}, bf16[2,48,4,256]{3,0,2,1:T(2,128)(2,1)S(1)}, u32[]{:S(2)}, u32[]{:S(2)}) collective-permute-start(bf16[2,48,4,256]{3,0,2,1:T(2,128)(2,1)S(1)} %copy.431), channel_id=1, source_target_pairs={{2,0},{4,2},{6,4},{8,6},{10,8},{12,10},{14,12},{0,14},{3,1},{5,3},... | collective-permute-start | bytes 589832 | tf_op jit(solution)/shard_map/ppermute | solution.py:80
  20.0 6.0 %collective-permute-done = bf16[2,48,4,256]{3,0,2,1:T(2,128)(2,1)S(1)} collective-permute-done((bf16[2,48,4,256]{3,0,2,1:T(2,128)(2,1)S(1)}, bf16[2,48,4,256]{3,0,2,1:T(2,128)(2,1)S(1)}, u32[]{:S(2)}, u32[]{:S(2)}) %collective-permute-start) | collective-permute-done | bytes 196640 | tf_op jit(solution)/shard_map/ppermute | solution.py:78
  26.1 1.7 %constant_dynamic-update-slice_fusion.1 = bf16[2,48,40,256]{3,0,2,1:T(2,128)(2,1)S(1)} fusion(bf16[2,48,40,256]{3,0,2,1:T(2,128)(2,1)S(1)} %constant_dynamic-update-slice_fusion.2, bf16[2,48,32,256]{3,2,1,0:T(8,128)(2,1)S(1)} %copy-done.3), kind=kLoop, calls=%fused_computation.168 | loop fusion | bytes 3145728
  28.5 1.3 %copy-done.2 = bf16[2,48,40,256]{3,0,2,1:T(2,128)(2,1)} copy-done((bf16[2,48,40,256]{3,0,2,1:T(2,128)(2,1)}, bf16[2,48,40,256]{3,0,2,1:T(2,128)(2,1)S(1)}, u32[]{:S(2)}) %copy-start.2) | copy-done | bytes 1966104
  30.0 1.3 %collective-permute-start.2 = (bf16[2,4,40,256]{3,0,2,1:T(2,128)(2,1)S(1)}, bf16[2,4,40,256]{3,0,2,1:T(2,128)(2,1)S(1)}, u32[]{:S(2)}, u32[]{:S(2)}) collective-permute-start(bf16[2,4,40,256]{3,0,2,1:T(2,128)(2,1)S(1)} %get-tuple-element.47), channel_id=1, source_target_pairs={{0,1},{2,3},{4,5},{6,7},{8,9},{10,11},{12,13},{14,15},{16,17},{18,... | collective-permute-start | bytes 491528 | tf_op jit(solution)/shard_map/ppermute | solution.py:78
  31.3 1.3 %collective-permute-start.3 = (bf16[2,4,40,256]{3,0,2,1:T(2,128)(2,1)S(1)}, bf16[2,4,40,256]{3,0,2,1:T(2,128)(2,1)S(1)}, u32[]{:S(2)}, u32[]{:S(2)}) collective-permute-start(bf16[2,4,40,256]{3,0,2,1:T(2,128)(2,1)S(1)} %get-tuple-element.48), channel_id=1, source_target_pairs={{1,0},{3,2},{5,4},{7,6},{9,8},{11,10},{13,12},{15,14},{17,16},{19,... | collective-permute-start | bytes 491528 | tf_op jit(solution)/shard_map/ppermute | solution.py:80
  34.6 4.8 %pad_maximum_fusion = bf16[2,56,40,256]{3,0,2,1:T(2,128)(2,1)S(1)} fusion(bf16[2,4,40,256]{3,0,2,1:T(2,128)(2,1)S(1)} %collective-permute-done.3, bf16[2,48,40,256]{3,0,2,1:T(2,128)(2,1)} %copy-done.2, bf16[2,4,40,256]{3,0,2,1:T(2,128)(2,1)S(1)} %collective-permute-done.2), kind=kLoop, calls=%fused_computation.2 | loop fusion | flops 2293760 | bytes 4587520 | tf_op jit(solution)/shard_map/concatenate | solution.py:76
  39.4 5.8 %gather_fusion = bf16[32,9,16,256]{3,0,2,1:T(8,128)(2,1)} fusion(bf16[2,56,40,256]{3,0,2,1:T(2,128)(2,1)S(1)} %pad_maximum_fusion, s32[32]{0:T(128)S(1)} %fusion.95), kind=kCustom, calls=%fused_computation | custom fusion | bytes 4719104 | tf_op jit(solution)/shard_map/vmap()/gather | solution.py:145
  45.2 1.9 %fusion.98 = (bf16[32,1,8,256]{3,0,2,1:T(8,128)(2,1)S(1)}, bf16[32,1,8,256]{3,0,2,1:T(8,128)(2,1)S(1)}, bf16[32,1,8,256]{3,0,2,1:T(8,128)(2,1)S(1)}, bf16[32,1,8...) fusion(bf16[32,9,16,256]{3,0,2,1:T(8,128)(2,1)} %gather_fusion), kind=kLoop, calls=%fused_computation.234 | loop fusion | bytes 3932160 | tf_op jit(solution)/shard_map/slice | solution.py:162
  48.7 7.8 %fusion.13 = bf16[256,256]{1,0:T(8,128)(2,1)S(1)} fusion(f32[32,1,8,256]{3,0,2,1:T(8,128)S(1)} %get-tuple-element.14, f32[256]{0:T(256)S(1)} %bitcast.444, f32[256]{0:T(256)S(1)} %bitcast.443, f32[256]{0:T(256)S(1)} %bitcast.442, f32[256]{0:T(256)S(1)} %bitcast.441, f32[256]{0:T(256)S(1)} %bitcast.440, f32[256]{0:T(256)S(1)} %bitcast.439, ...), kind=kLoop, calls=%fused_computation.28 | loop fusion | flops 5373952 | bytes 4598784 | tf_op jit(solution)/shard_map/convert_element_type | solution.py:173
  61.9 1.7 %reshape.1066 = f32[58112]{0:T(1024)} reshape(f32[227,256]{1,0:T(8,128)} %fusion.79) | data formatting | bytes 464896 | tf_op jit(solution)/shard_map/reshape | solution.py:47
  63.6 1.8 %copy.359 = f32[32,2,8,128]{3,1,2,0:T(2,128)} copy(f32[32,2,8,128]{3,2,1,0:T(8,128)} %convolution_bitcast_fusion) | data formatting | bytes 524288
  65.4 1.4 %fusion.67 = bf16[9,256,256]{2,1,0:T(8,128)(2,1)S(1)} fusion(bf16[9,256,256]{2,1,0:T(8,128)(2,1)S(1)} %fusion.71, bf16[32,1,8,256]{3,0,2,1:T(8,128)(2,1)} %copy-done.14, bf16[32,1,8,256]{3,0,2,1:T(8,128)(2,1)} %copy-done.15, bf16[32,1,8,256]{3,0,2,1:T(8,128)(2,1)} %copy-done.16, bf16[32,1,8,256]{3,0,2,1:T(8,128)(2,1)} %copy-done.17, ...), kind=kLoop, calls=%fused_computation.145 | loop fusion | flops 1048576 | bytes 657408
  66.8 1.4 %fusion.63 = bf16[9,256,256]{2,1,0:T(8,128)(2,1)S(1)} fusion(bf16[9,256,256]{2,1,0:T(8,128)(2,1)S(1)} %fusion.67, bf16[32,1,8,256]{3,0,2,1:T(8,128)(2,1)} %copy-done.6, bf16[32,1,8,256]{3,0,2,1:T(8,128)(2,1)} %copy-done.7, bf16[32,1,8,256]{3,0,2,1:T(8,128)(2,1)} %copy-done.8, bf16[32,1,8,256]{3,0,2,1:T(8,128)(2,1)} %copy-done.9, ...), kind=kLoop, calls=%fused_computation.137 | loop fusion | flops 1048576 | bytes 657408
  72.6 2.1 %collective-permute-start.5 = (f32[256,128]{1,0:T(8,128)S(1)}, f32[256,128]{1,0:T(8,128)S(1)}, u32[]{:S(2)}, u32[]{:S(2)}) collective-permute-start(f32[256,128]{1,0:T(8,128)S(1)} %constant_dynamic-slice_fusion), channel_id=1, source_target_pairs={{0,2},{2,0},{4,6},{6,4},{8,10},{10,8},{12,14},{14,12},{1,3},{3,1},... | collective-permute-start | bytes 393224 | tf_op jit(solution)/shard_map/ppermute | solution.py:22
  74.7 3.9 %collective-permute-done.5 = f32[256,128]{1,0:T(8,128)S(1)} collective-permute-done((f32[256,128]{1,0:T(8,128)S(1)}, f32[256,128]{1,0:T(8,128)S(1)}, u32[]{:S(2)}, u32[]{:S(2)}) %collective-permute-start.5) | collective-permute-done | bytes 131104 | tf_op jit(solution)/shard_map/ppermute | solution.py:22
  78.6 1.5 %collective-permute-start.6 = (f32[256,128]{1,0:T(8,128)S(1)}, f32[256,128]{1,0:T(8,128)S(1)}, u32[]{:S(2)}, u32[]{:S(2)}) collective-permute-start(f32[256,128]{1,0:T(8,128)S(1)} %dynamic-slice_add_fusion.1), channel_id=1, source_target_pairs={{0,4},{2,6},{4,0},{6,2},{8,12},{10,14},{12,8},{14,10},{1,5},{3,7},... | collective-permute-start | bytes 393224 | tf_op jit(solution)/shard_map/ppermute | solution.py:56
  80.1 3.7 %collective-permute-done.6 = f32[256,128]{1,0:T(8,128)S(1)} collective-permute-done((f32[256,128]{1,0:T(8,128)S(1)}, f32[256,128]{1,0:T(8,128)S(1)}, u32[]{:S(2)}, u32[]{:S(2)}) %collective-permute-start.6) | collective-permute-done | bytes 131104 | tf_op jit(solution)/shard_map/ppermute | solution.py:56
  83.8 2.1 %collective-permute-start.7 = (f32[256,128]{1,0:T(8,128)S(1)}, f32[256,128]{1,0:T(8,128)S(1)}, u32[]{:S(2)}, u32[]{:S(2)}) collective-permute-start(f32[256,128]{1,0:T(8,128)S(1)} %add.641), channel_id=1, source_target_pairs={{0,8},{2,10},{4,12},{6,14},{8,0},{10,2},{12,4},{14,6},{1,9},{3,11}... | collective-permute-start | bytes 393224 | tf_op jit(solution)/shard_map/ppermute | solution.py:56
  85.9 6.0 %collective-permute-done.7 = f32[256,128]{1,0:T(8,128)S(1)} collective-permute-done((f32[256,128]{1,0:T(8,128)S(1)}, f32[256,128]{1,0:T(8,128)S(1)}, u32[]{:S(2)}, u32[]{:S(2)}) %collective-permute-start.7) | collective-permute-done | bytes 131104 | tf_op jit(solution)/shard_map/ppermute | solution.py:56
  93.0 4.0 %collective-permute-done.8 = f32[256,128]{1,0:T(8,128)S(1)} collective-permute-done((f32[256,128]{1,0:T(8,128)S(1)}, f32[256,128]{1,0:T(8,128)S(1)}, u32[]{:S(2)}, u32[]{:S(2)}) %collective-permute-start.8) | collective-permute-done | bytes 131104 | tf_op jit(solution)/shard_map/ppermute | solution.py:29
  97.1 1.4 %collective-permute-done.9 = f32[512,128]{1,0:T(8,128)S(1)} collective-permute-done((f32[512,128]{1,0:T(8,128)S(1)}, f32[512,128]{1,0:T(8,128)S(1)}, u32[]{:S(2)}, u32[]{:S(2)}) %collective-permute-start.9) | collective-permute-done | bytes 262176 | tf_op jit(solution)/shard_map/ppermute | solution.py:29
  (132 shorter events, 25.1 us)
Async XLA Ops:
  0.6 55.9 %copy-start = (bf16[256,256]{1,0:T(8,128)(2,1)S(1)}, bf16[256,256]{1,0:T(8,128)(2,1)}, u32[]{:S(2)}) copy-start(bf16[256,256]{1,0:T(8,128)(2,1)} %param.12) | copy-start | bytes 393220
  0.6 25.4 %copy-start.3 = (bf16[2,48,32,256]{3,2,1,0:T(8,128)(2,1)S(1)}, bf16[2,48,32,256]{3,2,1,0:T(8,128)(2,1)}, u32[]{:S(2)}) copy-start(bf16[2,48,32,256]{3,2,1,0:T(8,128)(2,1)} %param.9) | copy-start | bytes 4718596
  0.7 19.2 %copy-start.24 = (s32[256]{0:T(256)S(1)}, s32[256]{0:T(256)}, u32[]{:S(2)}) copy-start(s32[256]{0:T(256)} %param.10) | copy-start | bytes 3076
  0.7 19.3 %copy-start.23 = (bf16[9,256]{1,0:T(8,128)(2,1)S(1)}, bf16[9,256]{1,0:T(8,128)(2,1)}, u32[]{:S(2)}) copy-start(bf16[9,256]{1,0:T(8,128)(2,1)} %param.11) | copy-start | bytes 13828
  5.9 26.7 %all-to-all-start = ((bf16[32,8,228]{2,1,0:T(8,128)(2,1)}), bf16[32,8,228]{2,1,0:T(8,128)(2,1)S(1)}, u32[]{:S(2)}, u32[]{:S(2)}) async-start(bf16[32,8,228]{2,1,0:T(8,128)(2,1)} %copy.288), calls=%async_computation | async-start | bytes 262144 | tf_op jit(solution)/shard_map/all_to_all | solution.py:118
  14.8 11.2 %collective-permute-start = (bf16[2,48,4,256]{3,0,2,1:T(2,128)(2,1)S(1)}, bf16[2,48,4,256]{3,0,2,1:T(2,128)(2,1)S(1)}, u32[]{:S(2)}, u32[]{:S(2)}) collective-permute-start(bf16[2,48,4,256]{3,0,2,1:T(2,128)(2,1)S(1)} %copy.430), channel_id=1, source_target_pairs={{0,2},{2,4},{4,6},{6,8},{8,10},{10,12},{12,14},{14,0},{1,3},{3,5},... | collective-permute-start | bytes 589832 | tf_op jit(solution)/shard_map/ppermute | solution.py:78
  17.0 11.4 %collective-permute-start.1 = (bf16[2,48,4,256]{3,0,2,1:T(2,128)(2,1)S(1)}, bf16[2,48,4,256]{3,0,2,1:T(2,128)(2,1)S(1)}, u32[]{:S(2)}, u32[]{:S(2)}) collective-permute-start(bf16[2,48,4,256]{3,0,2,1:T(2,128)(2,1)S(1)} %copy.431), channel_id=1, source_target_pairs={{2,0},{4,2},{6,4},{8,6},{10,8},{12,10},{14,12},{0,14},{3,1},{5,3},... | collective-permute-start | bytes 589832 | tf_op jit(solution)/shard_map/ppermute | solution.py:80
  28.5 1.3 %copy-start.2 = (bf16[2,48,40,256]{3,0,2,1:T(2,128)(2,1)}, bf16[2,48,40,256]{3,0,2,1:T(2,128)(2,1)S(1)}, u32[]{:S(2)}) copy-start(bf16[2,48,40,256]{3,0,2,1:T(2,128)(2,1)S(1)} %constant_dynamic-update-slice_fusion) | copy-start | bytes 5898244
  30.0 3.7 %collective-permute-start.2 = (bf16[2,4,40,256]{3,0,2,1:T(2,128)(2,1)S(1)}, bf16[2,4,40,256]{3,0,2,1:T(2,128)(2,1)S(1)}, u32[]{:S(2)}, u32[]{:S(2)}) collective-permute-start(bf16[2,4,40,256]{3,0,2,1:T(2,128)(2,1)S(1)} %get-tuple-element.47), channel_id=1, source_target_pairs={{0,1},{2,3},{4,5},{6,7},{8,9},{10,11},{12,13},{14,15},{16,17},{18,... | collective-permute-start | bytes 491528 | tf_op jit(solution)/shard_map/ppermute | solution.py:78
  31.3 3.3 %collective-permute-start.3 = (bf16[2,4,40,256]{3,0,2,1:T(2,128)(2,1)S(1)}, bf16[2,4,40,256]{3,0,2,1:T(2,128)(2,1)S(1)}, u32[]{:S(2)}, u32[]{:S(2)}) collective-permute-start(bf16[2,4,40,256]{3,0,2,1:T(2,128)(2,1)S(1)} %get-tuple-element.48), channel_id=1, source_target_pairs={{1,0},{3,2},{5,4},{7,6},{9,8},{11,10},{13,12},{15,14},{17,16},{19,... | collective-permute-start | bytes 491528 | tf_op jit(solution)/shard_map/ppermute | solution.py:80
  45.2 2.3 %copy-start.1 = (bf16[32,9,16,256]{3,0,2,1:T(8,128)(2,1)S(1)}, bf16[32,9,16,256]{3,0,2,1:T(8,128)(2,1)}, u32[]{:S(2)}) copy-start(bf16[32,9,16,256]{3,0,2,1:T(8,128)(2,1)} %gather_fusion) | copy-start | bytes 7077892
  48.6 7.9 %copy-start.10 = (bf16[32,1,8,256]{3,0,2,1:T(8,128)(2,1)}, bf16[32,1,8,256]{3,0,2,1:T(8,128)(2,1)S(1)}, u32[]{:S(2)}) copy-start(bf16[32,1,8,256]{3,0,2,1:T(8,128)(2,1)S(1)} %get-tuple-element.30) | copy-start | bytes 393220
  48.6 7.9 %copy-start.12 = (bf16[32,1,8,256]{3,0,2,1:T(8,128)(2,1)}, bf16[32,1,8,256]{3,0,2,1:T(8,128)(2,1)S(1)}, u32[]{:S(2)}) copy-start(bf16[32,1,8,256]{3,0,2,1:T(8,128)(2,1)S(1)} %get-tuple-element.31) | copy-start | bytes 393220
  63.6 4.6 %copy-start.5 = (bf16[32,1,8,256]{3,0,2,1:T(8,128)(2,1)S(1)}, bf16[32,1,8,256]{3,0,2,1:T(8,128)(2,1)}, u32[]{:S(2)}) copy-start(bf16[32,1,8,256]{3,0,2,1:T(8,128)(2,1)} %copy-done.4) | copy-start | bytes 393220
  63.6 4.7 %copy-start.11 = (bf16[32,1,8,256]{3,0,2,1:T(8,128)(2,1)S(1)}, bf16[32,1,8,256]{3,0,2,1:T(8,128)(2,1)}, u32[]{:S(2)}) copy-start(bf16[32,1,8,256]{3,0,2,1:T(8,128)(2,1)} %copy-done.10) | copy-start | bytes 393220
  63.6 4.7 %copy-start.13 = (bf16[32,1,8,256]{3,0,2,1:T(8,128)(2,1)S(1)}, bf16[32,1,8,256]{3,0,2,1:T(8,128)(2,1)}, u32[]{:S(2)}) copy-start(bf16[32,1,8,256]{3,0,2,1:T(8,128)(2,1)} %copy-done.12) | copy-start | bytes 393220
  63.6 5.0 %copy-start.21 = (bf16[32,1,8,256]{3,0,2,1:T(8,128)(2,1)S(1)}, bf16[32,1,8,256]{3,0,2,1:T(8,128)(2,1)}, u32[]{:S(2)}) copy-start(bf16[32,1,8,256]{3,0,2,1:T(8,128)(2,1)} %get-tuple-element.13) | copy-start | bytes 393220
  68.6 1.3 %copy-start.19 = (f32[256,256]{1,0:T(8,128)S(1)}, f32[256,256]{1,0:T(8,128)}, u32[]{:S(2)}) copy-start(f32[256,256]{1,0:T(8,128)} %fusion.102) | copy-start | bytes 786436
  70.9 1.6 %collective-permute-start.4 = (f32[512,128]{1,0:T(8,128)S(1)}, f32[512,128]{1,0:T(8,128)S(1)}, u32[]{:S(2)}, u32[]{:S(2)}) collective-permute-start(f32[512,128]{1,0:T(8,128)S(1)} %constant_dynamic-slice_fusion.1), channel_id=1, source_target_pairs={{0,1},{1,0},{2,3},{3,2},{4,5},{5,4},{6,7},{7,6},{8,9},{9,8},{10,11... | collective-permute-start | bytes 786440 | tf_op jit(solution)/shard_map/ppermute | solution.py:22
  72.6 6.0 %collective-permute-start.5 = (f32[256,128]{1,0:T(8,128)S(1)}, f32[256,128]{1,0:T(8,128)S(1)}, u32[]{:S(2)}, u32[]{:S(2)}) collective-permute-start(f32[256,128]{1,0:T(8,128)S(1)} %constant_dynamic-slice_fusion), channel_id=1, source_target_pairs={{0,2},{2,0},{4,6},{6,4},{8,10},{10,8},{12,14},{14,12},{1,3},{3,1},... | collective-permute-start | bytes 393224 | tf_op jit(solution)/shard_map/ppermute | solution.py:22
  78.6 5.2 %collective-permute-start.6 = (f32[256,128]{1,0:T(8,128)S(1)}, f32[256,128]{1,0:T(8,128)S(1)}, u32[]{:S(2)}, u32[]{:S(2)}) collective-permute-start(f32[256,128]{1,0:T(8,128)S(1)} %dynamic-slice_add_fusion.1), channel_id=1, source_target_pairs={{0,4},{2,6},{4,0},{6,2},{8,12},{10,14},{12,8},{14,10},{1,5},{3,7},... | collective-permute-start | bytes 393224 | tf_op jit(solution)/shard_map/ppermute | solution.py:56
  83.8 8.0 %collective-permute-start.7 = (f32[256,128]{1,0:T(8,128)S(1)}, f32[256,128]{1,0:T(8,128)S(1)}, u32[]{:S(2)}, u32[]{:S(2)}) collective-permute-start(f32[256,128]{1,0:T(8,128)S(1)} %add.641), channel_id=1, source_target_pairs={{0,8},{2,10},{4,12},{6,14},{8,0},{10,2},{12,4},{14,6},{1,9},{3,11}... | collective-permute-start | bytes 393224 | tf_op jit(solution)/shard_map/ppermute | solution.py:56
  91.9 5.0 %collective-permute-start.8 = (f32[256,128]{1,0:T(8,128)S(1)}, f32[256,128]{1,0:T(8,128)S(1)}, u32[]{:S(2)}, u32[]{:S(2)}) collective-permute-start(f32[256,128]{1,0:T(8,128)S(1)} %get-tuple-element.9), channel_id=1, source_target_pairs={{0,2},{2,0},{4,6},{6,4},{8,10},{10,8},{12,14},{14,12},{1,3},{3,1},... | collective-permute-start | bytes 393224 | tf_op jit(solution)/shard_map/ppermute | solution.py:29
  97.0 1.6 %collective-permute-start.9 = (f32[512,128]{1,0:T(8,128)S(1)}, f32[512,128]{1,0:T(8,128)S(1)}, u32[]{:S(2)}, u32[]{:S(2)}) collective-permute-start(f32[512,128]{1,0:T(8,128)S(1)} %constant_dynamic-update-slice_fusion.10), channel_id=1, source_target_pairs={{0,1},{1,0},{2,3},{3,2},{4,5},{5,4},{6,7},{7,6},{8,9},{9,8},{10,11... | collective-permute-start | bytes 786440 | tf_op jit(solution)/shard_map/ppermute | solution.py:29
  (12 other events, 13.3 us)
